TPU v7x, 32 devices: a whole 2x2x4 slice. The times are simulated.
32 devices in a mesh: groups: 2 (over y), seq: 4 (over x, core), fsdp: 4 (over z).
Axes of the slice: x: 2, y: 2, z: 4, core: 2. Of those that a mesh axis runs over, the one named last changes fastest.
Arguments:
- tokens: bfloat16 [16, 512, 1536], P(('groups', 'fsdp'), 'seq'), parts along dimension 0, may hold values from -6 to 6
- in_weight: bfloat16 [1536, 4608], P(None, 'fsdp'), may hold values from -0.15625 to 0.15625
- short_weight: float32 [3, 4608], replicated, may hold values from -3.5 to 3.5
- basis_in: float32 [17, 64], replicated, may hold values from -4 to 4
- basis_bias: float32 [64], replicated, may hold values from -3.140625 to 3.140625
- basis_mid: float32 [64, 64], replicated, may hold values from -1.5 to 1.5
- basis_shift: float32 [64], replicated, may hold values from -3.140625 to 3.140625
- response_out: float32 [2, 64, 1536], P(None, None, 'fsdp'), may hold values from -0.0234375 to 0.0234375
- skip_gain: float32 [1536], P('fsdp'), may hold values from -4 to 4
- block_counts: int32 [16, 4], P(('groups', 'fsdp'), 'seq'), parts along dimension 0, may hold values from 1 to 128, as said below
Outputs:
- mixed: bfloat16 [16, 512, 1536], P(('groups', 'fsdp'), 'seq'), parts along dimension 0
There are 2 independent parts, one for each index of `groups`. A program takes and returns all parts, laid end to end along the dimension named above; an argument that names none is the same for every part. Nothing has to cross between parts.
Inputs may be any that keep to these rules, and one draw needn't show every extreme that they name: `block_counts`: in every table one block holds all 128 tokens and another holds a single token.
All inputs are finite; a program needn't handle non-finite values.
Results may differ from a plain program's by a relative error of at most 0.007.
Values may be sent and summed in bfloat16 or wider, within the bound.
No kernel may reach another device: no remote copies, remote signals or barrier semaphores. Data moves between devices by JAX's collectives and lax.ppermute only.
A program may use at most 128 MiB of HBM per device.

v0:
```python
import jax
import jax.numpy as jnp
from jax import lax
from jax.sharding import PartitionSpec as P


def padded_2(cells, sides, width):
    for axis, dim in sides:
        count = lax.axis_size(axis)
        ends = count - 1
        head = lax.slice_in_dim(cells, 0, width, axis=dim)
        tail = lax.slice_in_dim(cells, cells.shape[dim] - width, cells.shape[dim], axis=dim)
        cells = jnp.concatenate(
            [
                lax.ppermute(tail, axis, [(i, (i + 1) % count) for i in range(ends)]),
                cells,
                lax.ppermute(head, axis, [((i + 1) % count, i) for i in range(ends)]),
            ],
            axis=dim,
        )
    return cells


def filter_basis(lag_values, total_len, basis_in, basis_bias, basis_mid, basis_shift):
    band_count = (basis_in.shape[0] - 1) // 2
    distance = jnp.abs(lag_values)
    periods = (2 ** (jnp.arange(band_count, dtype=jnp.int32) + 2) + 1).astype(jnp.int32)
    angles = (
        2.0
        * jnp.pi
        * (distance[:, None] % periods[None, :]).astype(jnp.float32)
        / periods[None, :].astype(jnp.float32)
    )
    linear = distance.astype(jnp.float32)[:, None] / total_len
    encoded = jnp.concatenate([linear, jnp.cos(angles), jnp.sin(angles)], axis=1)
    hidden = jnp.sin(jnp.dot(encoded, basis_in, precision=lax.Precision.HIGHEST) + basis_bias)
    return jnp.sin(jnp.dot(hidden, basis_mid, precision=lax.Precision.HIGHEST) + basis_shift)


def forward_table(block_len):
    period = 2 * block_len
    frequency = jnp.arange(block_len, dtype=jnp.int32)[:, None]
    samples = jnp.arange(period, dtype=jnp.int32)[None, :]
    phases = 2.0 * jnp.pi / period * (frequency * samples % period).astype(jnp.float32)
    alternate = (1 - 2 * (samples % 2)).astype(jnp.float32)
    real_rows = jnp.cos(phases)
    imag_rows = jnp.where(frequency == 0, alternate, -jnp.sin(phases))
    return jnp.concatenate([real_rows, imag_rows], axis=0)


def inverse_table(block_len):
    period = 2 * block_len
    places = jnp.arange(block_len, dtype=jnp.int32)[:, None]
    frequency = jnp.arange(block_len, dtype=jnp.int32)[None, :]
    phases = 2.0 * jnp.pi / period * (places * frequency % period).astype(jnp.float32)
    alternate = (1 - 2 * (places % 2)).astype(jnp.float32)
    real_cols = jnp.where(frequency == 0, 1.0, 2.0 * jnp.cos(phases)) / period
    imag_cols = jnp.where(frequency == 0, alternate, -2.0 * jnp.sin(phases)) / period
    return jnp.concatenate([real_cols, imag_cols], axis=1)


def packed_product(response, signal, block_len):
    first_slot = (jnp.arange(block_len) == 0)[:, None]
    resp_real = response[..., :block_len, :]
    resp_imag = response[..., block_len:, :]
    sig_real = signal[..., :block_len, :]
    sig_imag = signal[..., block_len:, :]
    cross_term = resp_imag * sig_imag
    prod_real = resp_real * sig_real - jnp.where(first_slot, 0.0, cross_term)
    prod_imag = jnp.where(first_slot, cross_term, resp_real * sig_imag + resp_imag * sig_real)
    return jnp.concatenate([prod_real, prod_imag], axis=-2)


def shards(
    tokens,
    in_weight,
    short_weight,
    basis_in,
    basis_bias,
    basis_mid,
    basis_shift,
    response_out,
    skip_gain,
    block_counts,
):
    seq_dev, block_len, width = tokens.shape
    flat_rows = tokens.reshape(seq_dev * block_len, width)
    projected = jnp.dot(
        flat_rows,
        lax.all_gather(in_weight, "fsdp", axis=1, tiled=True),
        preferred_element_type=jnp.float32,
    ).astype(jnp.bfloat16)
    projected = projected.reshape(seq_dev, block_len, 3 * width)
    padded = padded_2(projected, (("seq", 1),), 1)
    shorted = (
        short_weight[0] * padded[:, :-2]
        + short_weight[1] * padded[:, 1:-1]
        + short_weight[2] * padded[:, 2:]
    )
    query_gate = shorted[:, :, :width]
    key_part = shorted[:, :, width : 2 * width]
    value_part = shorted[:, :, 2 * width :]
    valid_mask = (jnp.arange(block_len, dtype=jnp.int32)[None, :] < block_counts).astype(
        jnp.float32
    )
    carried = (key_part * value_part * valid_mask[:, :, None]).astype(jnp.bfloat16)
    full_out, full_skip = (
        lax.all_gather(response_out, "fsdp", axis=2, tiled=True),
        lax.all_gather(skip_gain, "fsdp", axis=0, tiled=True),
    )
    stacked_out = full_out.reshape(2 * full_out.shape[1], width)
    seq_count = lax.axis_size("seq")
    position = lax.axis_index("seq")
    total_len = float(seq_count * block_len)
    forward = forward_table(block_len)
    forward_half = forward[:, :block_len]
    inverse = inverse_table(block_len)
    circular = jnp.arange(2 * block_len, dtype=jnp.int32)
    wrapped = jnp.where(circular < block_len, circular, circular - 2 * block_len)

    def kernel_response(offset, out_cols):
        lag_values = offset + wrapped
        basis_rows = filter_basis(
            lag_values, total_len, basis_in, basis_bias, basis_mid, basis_shift
        )
        ahead_mask = (lag_values >= 0).astype(jnp.float32)[:, None]
        paired = jnp.concatenate([basis_rows * ahead_mask, basis_rows * (1.0 - ahead_mask)], axis=1)
        return jnp.dot(
            jnp.dot(forward, paired, precision=lax.Precision.HIGHEST),
            out_cols,
            precision=lax.Precision.HIGHEST,
        )

    def add_block(spectrum, block_rows, start):
        offset = position * block_len - start
        response = kernel_response(offset, stacked_out)
        signal = jnp.einsum(
            "fc,scd->sfd",
            forward_half,
            block_rows.astype(jnp.float32),
            precision=lax.Precision.HIGHEST,
        )
        return spectrum + packed_product(response[None], signal, block_len)

    initial = jnp.zeros((seq_dev, 2 * block_len, width), jnp.float32)
    piece = lax.all_gather(carried, "seq", axis=1, tiled=True)
    piece_rows = piece.shape[1]
    block_total = piece_rows // block_len

    def one_block(block_index, carry):
        block_rows = lax.dynamic_slice_in_dim(piece, block_index * block_len, block_len, 1)
        return add_block(carry, block_rows, block_index * block_len)

    spectrum = lax.fori_loop(0, block_total, one_block, initial)
    conv = jnp.einsum("if,sfd->sid", inverse, spectrum, precision=lax.Precision.HIGHEST)
    return (query_gate * (conv + full_skip * carried.astype(jnp.float32))).astype(jnp.bfloat16)


def solution(mesh):
    placed = (
        P(("groups", "fsdp"), "seq", None),
        P(None, "fsdp"),
        P(),
        P(),
        P(),
        P(),
        P(),
        P(None, None, "fsdp"),
        P("fsdp"),
        P(("groups", "fsdp"), "seq"),
    )
    return jax.shard_map(
        shards,
        mesh=mesh,
        in_specs=placed,
        out_specs=P(("groups", "fsdp"), "seq", None),
        check_vma=False,
    )
```

profile of v0, /device:TPU:0, one launch (start us, length us, event | category | flops | bytes accessed | tf_op | source)
XLA Modules:
  0.0 392.8 jit_solution(175382151195454622)
XLA Ops:
  6.5 0.7 all-gather.4.cloned.1.call-update
  7.4 248.2 %all-gather.4.cloned.1.call-done = bf16[1536,4608]{1,0:T(8,128)(2,1)} async-done(((bf16[1536,1152]{1,0:T(8,128)(2,1)}), bf16[1536,4608]{1,0:T(8,128)(2,1)}) %all-gather.4.cloned.1.call-update) | async-done | bytes 14155792 | tf_op jit(solution)/shard_map/all_gather | solution.py:90
  255.6 9.1 %convolution_convert_fusion = bf16[256,4608]{1,0:T(8,128)(2,1)S(1)} fusion(bf16[256,1536]{1,0:T(8,128)(2,1)S(1)} %bitcast.56, bf16[1536,4608]{1,0:T(8,128)(2,1)} %all-gather.4.cloned.1.call-done), kind=kOutput, calls=%fused_computation.57 | convolution fusion | flops 3625058304 | bytes 17301504 | tf_op jit(solution)/shard_map/dot_general | solution.py:88
  264.8 2.0 collective-permute-start
  266.8 1.3 collective-permute-start.1
  268.3 3.0 copy.30
  271.3 2.0 copy.29
  273.3 2.0 copy.34
  275.3 6.3 %multiply_add_fusion = f32[2,128,4608]{1,2,0:T(8,128)S(1)} fusion(bf16[2,128,4608]{1,2,0:T(8,128)(2,1)S(1)} %copy.30, bf16[2,1,4608]{1,2,0:T(8,128)(2,1)} %copy.34, bf16[2,1,4608]{1,2,0:T(8,128)(2,1)} %copy.29, f32[4608]{0:T(1024)S(1)} %get-tuple-element.353, f32[4608]{0:T(1024)S(1)} %get-tuple-element.354, f32[4608]{0:T(1024)S(1)} %get-tuple-element.352), kind=kLoop, calls=%fused_computation.58 | loop fusion | flops 16515072 | bytes 7170048 | tf_op jit(solution)/shard_map/add | solution.py:96
  281.6 2.1 copy-done.2
  283.7 1.0 fusion.31
  284.8 11.9 %all-gather = f32[4,1,384]{2,1,0:T(1,128)S(1)} all-gather(f32[1,1,384]{2,1,0:T(1,128)S(1)} %reshape.183), channel_id=1, replica_groups=mesh['groups'=2,'seq'=4,'fsdp'=4] {'fsdp'}, dimensions={0}, use_global_device_ids=true | all-gather | bytes 7680 | tf_op jit(solution)/shard_map/all_gather | solution.py:109
  296.8 0.5 negate_select_fusion.2
  297.3 0.9 select_multiply_fusion.1
  298.3 18.5 %all_gather.13 = f32[2,64,1536]{2,1,0:T(8,128)} all-gather(f32[2,64,384]{2,1,0:T(8,128)S(1)} %copy-done.6), channel_id=1, replica_groups=mesh['groups'=2,'seq'=4,'fsdp'=4] {'fsdp'}, dimensions={2}, use_global_device_ids=true | all-gather | bytes 983040 | tf_op jit(solution)/shard_map/all_gather | solution.py:108
  316.9 60.1 %while.16 = (s32[]{:T(128)}, f32[2,256,1536]{2,1,0:T(8,128)}, s32[]{:T(128)}, f32[17,64]{1,0:T(8,128)}, f32[64]{0:T(128)S(1)}, /*index=5*/f32[64,64]{1,0:T(8,128...) while((s32[]{:T(128)}, f32[2,256,1536]{2,1,0:T(8,128)}, ...), condition=%wide.region_1.2_spmd.clone, body=%wide.region_0.1_spmd.clone.sunk | while | flops 1934166400 | bytes 31061424 | solution.py:154
  317.2 1.2 fusion.92
  318.4 0.5 broadcast_multiply_fusion.3
  319.3 2.6 convolution_bitcast_fusion.6
  321.9 1.0 slice_bitcast_fusion.3
  322.8 2.6 convolution_bitcast_fusion.5
  325.5 1.9 select_subtract_fusion.2
  327.4 3.8 maximum_add_fusion.2
  331.5 1.2 fusion.92
  332.7 0.5 broadcast_multiply_fusion.3
  333.6 2.6 convolution_bitcast_fusion.6
  336.2 1.0 slice_bitcast_fusion.3
  337.1 2.6 convolution_bitcast_fusion.5
  339.8 1.9 select_subtract_fusion.2
  341.7 4.8 %maximum_add_fusion.2 = f32[2,256,1536]{2,1,0:T(8,128)} fusion(f32[2,128,1536]{2,1,0:T(8,128)} %get-tuple-element.484, f32[2,128,1536]{2,1,0:T(8,128)S(1)} %get-tuple-element.485, f32[2,256,1536]{2,1,0:T(8,128)} %get-tuple-element.502, pred[]{:T(512)S(6)} %compare.7), kind=kLoop, calls=%fused_computation.2.clone.1 | loop fusion | flops 2359296 | bytes 9437185 | tf_op jit(solution)/shard_map/while/body/eval_jaxpr/add | solution.py:143
  346.8 1.2 fusion.92
  348.0 0.5 broadcast_multiply_fusion.3
  348.4 0.4 fusion.93
  348.9 2.6 convolution_bitcast_fusion.6
  351.4 1.0 slice_bitcast_fusion.3
  352.4 2.6 convolution_bitcast_fusion.5
  355.0 1.9 select_subtract_fusion.2
  357.0 4.8 %maximum_add_fusion.2 = f32[2,256,1536]{2,1,0:T(8,128)} fusion(f32[2,128,1536]{2,1,0:T(8,128)} %get-tuple-element.484, f32[2,128,1536]{2,1,0:T(8,128)S(1)} %get-tuple-element.485, f32[2,256,1536]{2,1,0:T(8,128)} %get-tuple-element.502, pred[]{:T(512)S(6)} %compare.7), kind=kLoop, calls=%fused_computation.2.clone.1 | loop fusion | flops 2359296 | bytes 9437185 | tf_op jit(solution)/shard_map/while/body/eval_jaxpr/add | solution.py:143
  362.0 1.2 fusion.92
  363.2 0.5 broadcast_multiply_fusion.3
  363.7 0.4 fusion.93
  364.1 2.6 convolution_bitcast_fusion.6
  366.7 1.0 slice_bitcast_fusion.3
  367.7 2.6 convolution_bitcast_fusion.5
  370.3 1.9 select_subtract_fusion.2
  372.2 4.8 %maximum_add_fusion.2 = f32[2,256,1536]{2,1,0:T(8,128)} fusion(f32[2,128,1536]{2,1,0:T(8,128)} %get-tuple-element.484, f32[2,128,1536]{2,1,0:T(8,128)S(1)} %get-tuple-element.485, f32[2,256,1536]{2,1,0:T(8,128)} %get-tuple-element.502, pred[]{:T(512)S(6)} %compare.7), kind=kLoop, calls=%fused_computation.2.clone.1 | loop fusion | flops 2359296 | bytes 9437185 | tf_op jit(solution)/shard_map/while/body/eval_jaxpr/add | solution.py:143
  377.0 7.8 %fusion.32 = bf16[2,128,1536]{1,2,0:T(8,128)(2,1)S(1)} fusion(f32[2,128,4608]{1,2,0:T(8,128)} %copy-done.2, f32[2,256,1536]{2,1,0:T(8,128)} %get-tuple-element.539, bf16[2,128,1536]{1,2,0:T(8,128)(2,1)} %fusion.31, f32[1536]{0:T(1024)S(1)} %reshape.184, f32[128,128]{1,0:T(8,128)} %get-tuple-element.392, f32[128,128]{1,0:T(8,128)} %get-tuple-element.391), kind=kOutput, calls=%fused_computation.67 | convolution fusion | flops 1209958400 | bytes 6428672 | tf_op jit(solution)/shard_map/if,sfd->sid/dot_general | solution.py:155
  384.8 1.2 copy.37
  (85 shorter events, 2.6 us)
Async XLA Ops:
  6.5 249.1 %copy-start = (bf16[2,128,1536]{2,1,0:T(8,128)(2,1)S(1)}, bf16[2,128,1536]{2,1,0:T(8,128)(2,1)}, u32[]{:S(2)}) copy-start(bf16[2,128,1536]{2,1,0:T(8,128)(2,1)} %param.12) | copy-start | bytes 2359300
  6.5 0.8 copy-start.10
  6.5 249.1 %all-gather.4.cloned.1.call-start = ((), (), s32[]{:S(2)}) async-start(), calls=%async_computation | async-start | bytes 17694720 | tf_op jit(solution)/shard_map/all_gather | solution.py:90
  7.3 309.6 %all-gather.6.cloned.1.call-start = ((), (), s32[]{:S(2)}) async-start(), calls=%async_computation.1 | async-start | bytes 3932160 | tf_op jit(solution)/shard_map/all_gather | solution.py:146
  255.6 12.5 %copy-start.7 = (f32[3,4608]{1,0:T(4,128)S(1)}, f32[3,4608]{1,0:T(4,128)}, u32[]{:S(2)}) copy-start(f32[3,4608]{1,0:T(4,128)} %param.14) | copy-start | bytes 165892
  264.7 3.4 copy-start.3
  264.8 6.5 %collective-permute-start = (bf16[2,1,4608]{2,0,1:T(2,128)(2,1)S(1)}, bf16[2,1,4608]{2,0,1:T(2,128)(2,1)S(1)}, u32[]{:S(2)}, u32[]{:S(2)}) collective-permute-start(bf16[2,1,4608]{2,0,1:T(2,128)(2,1)S(1)} %copy.40), channel_id=1, source_target_pairs={{0,4},{4,8},{8,12},{1,5},{5,9},{9,13},{2,6},{6,10},{10,14},{3,7},{... | collective-permute-start | bytes 55304 | tf_op jit(solution)/shard_map/ppermute | solution.py:15
  266.8 6.5 %collective-permute-start.1 = (bf16[2,1,4608]{2,0,1:T(2,128)(2,1)S(1)}, bf16[2,1,4608]{2,0,1:T(2,128)(2,1)S(1)}, u32[]{:S(2)}, u32[]{:S(2)}) collective-permute-start(bf16[2,1,4608]{2,0,1:T(2,128)(2,1)S(1)} %copy.41), channel_id=1, source_target_pairs={{4,0},{8,4},{12,8},{5,1},{9,5},{13,9},{6,2},{10,6},{14,10},{7,3},{... | collective-permute-start | bytes 55304 | tf_op jit(solution)/shard_map/ppermute | solution.py:17
  281.6 2.1 copy-start.2
  283.7 1.1 copy-start.9
  283.7 14.6 %copy-start.6 = (f32[2,64,384]{2,1,0:T(8,128)S(1)}, f32[2,64,384]{2,1,0:T(8,128)}, u32[]{:S(2)}) copy-start(f32[2,64,384]{2,1,0:T(8,128)} %param.19) | copy-start | bytes 589828
  283.7 33.2 %copy-start.4 = (f32[64,64]{1,0:T(8,128)S(1)}, f32[64,64]{1,0:T(8,128)}, u32[]{:S(2)}) copy-start(f32[64,64]{1,0:T(8,128)} %param.17) | copy-start | bytes 49156
  283.7 33.2 %copy-start.8 = (f32[64]{0:T(128)S(1)}, f32[64]{0:T(128)}, u32[]{:S(2)}) copy-start(f32[64]{0:T(128)} %param.18) | copy-start | bytes 772
  283.7 33.2 %copy-start.11 = (f32[64]{0:T(128)S(1)}, f32[64]{0:T(128)}, u32[]{:S(2)}) copy-start(f32[64]{0:T(128)} %param.16) | copy-start | bytes 772
  322.8 2.6 copy-start.1
  327.4 3.8 copy-start.5
  337.1 2.6 copy-start.1
  341.7 4.8 %copy-start.5 = (f32[64,64]{1,0:T(8,128)S(1)}, f32[64,64]{1,0:T(8,128)}, u32[]{:S(2)}) copy-start(f32[64,64]{1,0:T(8,128)} %get-tuple-element.553) | copy-start | bytes 49156 | tf_op jit(solution)/shard_map/while
  352.4 2.6 copy-start.1
  357.0 4.8 %copy-start.5 = (f32[64,64]{1,0:T(8,128)S(1)}, f32[64,64]{1,0:T(8,128)}, u32[]{:S(2)}) copy-start(f32[64,64]{1,0:T(8,128)} %get-tuple-element.553) | copy-start | bytes 49156 | tf_op jit(solution)/shard_map/while
  367.7 2.6 copy-start.1
  372.2 4.8 %copy-start.5 = (f32[64,64]{1,0:T(8,128)S(1)}, f32[64,64]{1,0:T(8,128)}, u32[]{:S(2)}) copy-start(f32[64,64]{1,0:T(8,128)} %get-tuple-element.553) | copy-start | bytes 49156 | tf_op jit(solution)/shard_map/while
Sparse Core Ops, SparseCore 0:
  8.9 246.6 all-gather.3
  284.9 29.4 all-gather.5
where the time goes:
time: 394 us; the launch traced here: 393 us
  waiting for transfers between devices  249 us (63%)
  matrix products  45.8 us (12%)
  other arithmetic  36 us (9%)
  blocking collectives  30.4 us (8%)
  local copies, waits for them, and re-layouts  14.4 us (4%)
  between operations  13.6 us (3%)
    all_gather x1, waiting for transfers between devices, shards(): lax.all_gather(in_weight, 'fsdp', axis=1, tiled=True)  248 us
    all_gather x1, blocking collectives, shards(): lax.all_gather(response_out, 'fsdp', axis=2, tiled=True)  18.5 us
    add x4, other arithmetic, add_block(): return spectrum + packed_product(response[None], signal, block_len)  18.1 us
    all_gather x1, blocking collectives, shards(): lax.all_gather(skip_gain, 'fsdp', axis=0, tiled=True)  11.9 us
    dot_general x4, matrix products, add_block(): jnp.einsum('fc,scd->sfd', forward_half, block_rows.astype(jnp.float32), p...  10.4 us
    dot_general x4, matrix products, kernel_response(): jnp.dot(jnp.dot(forward, paired, precision=lax.Precision.HIGHEST), out_co...  10.3 us
    dot_general x1, matrix products, shards(): jnp.dot(flat_rows, lax.all_gather(in_weight, 'fsdp', axis=1, tiled=True),...  9.11 us
  transfers between devices with their start and end apart: 4, of which 1 were waited for; matrix products, arithmetic and copies ran while one was open for 2% of the time, Pallas kernels for 0%

commit v1 on v0

--- a/solution.py
+++ b/solution.py
@@ -84,13 +84,16 @@
     block_counts,
 ):
     seq_dev, block_len, width = tokens.shape
-    flat_rows = tokens.reshape(seq_dev * block_len, width)
-    projected = jnp.dot(
-        flat_rows,
-        lax.all_gather(in_weight, "fsdp", axis=1, tiled=True),
+    group_tokens = lax.all_gather(tokens, "fsdp", axis=0, tiled=True)
+    group_rows = group_tokens.shape[0]
+    local_cols = in_weight.shape[1]
+    partial = jnp.dot(
+        group_tokens.reshape(group_rows * block_len, width),
+        in_weight,
         preferred_element_type=jnp.float32,
     ).astype(jnp.bfloat16)
-    projected = projected.reshape(seq_dev, block_len, 3 * width)
+    partial = partial.reshape(group_rows, block_len, local_cols)
+    projected = lax.all_to_all(partial, "fsdp", 0, 2, tiled=True)
     padded = padded_2(projected, (("seq", 1),), 1)
     shorted = (
         short_weight[0] * padded[:, :-2]

time: 394 us -> 304 us (0.77)
  waiting for transfers between devices: 249 us -> 123 us
  local copies, waits for them, and re-layouts: 14.4 us -> 31.5 us
  other arithmetic: 36 us -> 42.7 us
  matrix products: 45.8 us -> 52.3 us
  starting transfers between devices: 3.29 us -> 7.85 us
    all_gather x1, waiting for transfers between devices: 248 us -> 67.9 us  [shards(): group_tokens = lax.all_gather(tokens, 'fsdp', axis=0, tiled=True)]
    all_to_all x0 -> x1, waiting for transfers between devices: none -> 54 us  [shards(): projected = lax.all_to_all(partial, 'fsdp', 0, 2, tiled=True)]
    slice x1 -> x2, local copies, waits for them, and re-layouts: 0.06 us -> 7.95 us  [padded_2(): lax.slice_in_dim(cells, cells.shape[dim] - width, cells.shape[dim], axis=...]
    all_to_all x0 -> x1, starting transfers between devices: none -> 4.64 us  [shards(): projected = lax.all_to_all(partial, 'fsdp', 0, 2, tiled=True)]
    all_to_all x0 -> x1, local copies, waits for them, and re-layouts: none -> 4.32 us  [shards(): projected = lax.all_to_all(partial, 'fsdp', 0, 2, tiled=True)]
  transfers between devices with their start and end apart: 4 -> 5, of which waited for: 1 -> 2; matrix products, arithmetic and copies ran while one was open for 2% -> 3% of each run, Pallas kernels for 0% -> 0%
where the time goes in v1:
time: 304 us; the launch traced here: 301 us
  waiting for transfers between devices  123 us (40%)
  matrix products  52.3 us (17%)
  other arithmetic  42.7 us (14%)
  local copies, waits for them, and re-layouts  31.5 us (10%)
  blocking collectives  30.6 us (10%)
  between operations  13.5 us (4%)
  starting transfers between devices  7.85 us (3%)
    all_gather x1, waiting for transfers between devices, shards(): group_tokens = lax.all_gather(tokens, 'fsdp', axis=0, tiled=True)  67.9 us
    all_to_all x1, waiting for transfers between devices, shards(): projected = lax.all_to_all(partial, 'fsdp', 0, 2, tiled=True)  54 us
    add x4, other arithmetic, add_block(): return spectrum + packed_product(response[None], signal, block_len)  19.9 us
    all_gather x1, blocking collectives, shards(): lax.all_gather(response_out, 'fsdp', axis=2, tiled=True)  18.7 us
    all_gather x1, blocking collectives, shards(): lax.all_gather(skip_gain, 'fsdp', axis=0, tiled=True)  11.9 us
    dot_general x4, matrix products, add_block(): jnp.einsum('fc,scd->sfd', forward_half, block_rows.astype(jnp.float32), p...  10.7 us
    dot_general x4, matrix products, kernel_response(): jnp.dot(jnp.dot(forward, paired, precision=lax.Precision.HIGHEST), out_co...  10.3 us
    sub x4, other arithmetic, packed_product(): prod_real = resp_real * sig_real - jnp.where(first_slot, 0.0, cross_term)  9.89 us
  transfers between devices with their start and end apart: 5, of which 2 were waited for; matrix products, arithmetic and copies ran while one was open for 3% of the time, Pallas kernels for 0%

profile of v1, /device:TPU:0, one launch (start us, length us, event | category | flops | bytes accessed | tf_op | source)
XLA Modules:
  0.0 301.4 jit_solution(2501134679842409714)
XLA Ops:
  7.3 67.9 %all-gather.4.cloned.1.call-done = bf16[8,128,1536]{2,1,0:T(8,128)(2,1)} async-done(((bf16[2,128,1536]{2,1,0:T(8,128)(2,1)}), bf16[8,128,1536]{2,1,0:T(8,128)(2,1)}) %all-gather.4.cloned.1.call-update) | async-done | bytes 3145744 | tf_op jit(solution)/shard_map/all_gather | solution.py:87
  75.2 7.6 %convolution_convert_fusion = bf16[1024,1152]{1,0:T(8,128)(2,1)} fusion(bf16[1024,1536]{1,0:T(8,128)(2,1)} %bitcast.65, bf16[1536,1152]{1,0:T(8,128)(2,1)S(1)} %copy-done), kind=kOutput, calls=%fused_computation.58 | convolution fusion | flops 3625058304 | bytes 9043968 | tf_op jit(solution)/shard_map/dot_general | solution.py:90
  82.7 4.6 %all-to-all-start = ((bf16[8,128,1152]{2,1,0:T(8,128)(2,1)}), bf16[8,128,1152]{2,1,0:T(8,128)(2,1)}, u32[]{:S(2)}, u32[]{:S(2)}) async-start(bf16[8,128,1152]{2,1,0:T(8,128)(2,1)} %bitcast.63), calls=%async_computation | async-start | bytes 4718592 | tf_op jit(solution)/shard_map/all_to_all | solution.py:96
  87.5 54.0 %all-to-all-done = bf16[8,128,1152]{2,1,0:T(8,128)(2,1)} async-done(((bf16[8,128,1152]{2,1,0:T(8,128)(2,1)}), bf16[8,128,1152]{2,1,0:T(8,128)(2,1)}, u32[]{:S(2)}, u32[]{:S(2)}) %all-to-all-start) | async-done | bytes 2359328 | tf_op jit(solution)/shard_map/all_to_all | solution.py:96
  141.5 4.3 %copy.20 = bf16[4,2,128,1152]{2,3,0,1:T(8,128)(2,1)} copy(bf16[4,2,128,1152]{3,2,1,0:T(8,128)(2,1)} %bitcast.2) | data formatting | bytes 4718592 | tf_op jit(solution)/shard_map/all_to_all | solution.py:96
  145.8 5.3 %fusion.56 = (bf16[2,1,4608]{1,2,0:T(8,128)(2,1)}, bf16[2,1,4608]{1,2,0:T(8,128)(2,1)}) fusion(bf16[2,128,4608]{1,2,0:T(8,128)(2,1)} %bitcast.60), kind=kLoop, calls=%fused_computation.111 | loop fusion | bytes 73728 | tf_op jit(solution)/shard_map/slice | solution.py:12
  151.1 2.7 copy.21
  153.8 1.9 collective-permute-start
  155.6 2.7 copy.23
  158.3 1.3 collective-permute-start.1
  159.6 1.8 slice_reduce_fusion.2
  161.4 2.6 copy.22
  164.0 2.6 copy.24
  166.7 7.7 %multiply_add_fusion = f32[2,128,4608]{1,2,0:T(8,128)S(1)} fusion(bf16[2,128,4608]{1,2,0:T(8,128)(2,1)} %bitcast.61, bf16[2,1,4608]{1,2,0:T(8,128)(2,1)} %copy.24, bf16[2,1,4608]{1,2,0:T(8,128)(2,1)} %copy.22, f32[4608]{0:T(1024)} %get-tuple-element.353, f32[4608]{0:T(1024)} %get-tuple-element.354, f32[4608]{0:T(1024)} %get-tuple-element.352), kind=kLoop, calls=%fused_computation.57 | loop fusion | flops 16515072 | bytes 7170048 | tf_op jit(solution)/shard_map/add | solution.py:99
  174.3 2.1 copy-done.3
  177.6 11.9 %all-gather = f32[4,1,384]{2,1,0:T(1,128)S(1)} all-gather(f32[1,1,384]{2,1,0:T(1,128)S(1)} %reshape.183), channel_id=1, replica_groups=mesh['groups'=2,'seq'=4,'fsdp'=4] {'fsdp'}, dimensions={0}, use_global_device_ids=true | all-gather | bytes 7680 | tf_op jit(solution)/shard_map/all_gather | solution.py:112
  192.4 18.7 %all_gather.13 = f32[2,64,1536]{2,1,0:T(8,128)} all-gather(f32[2,64,384]{2,1,0:T(8,128)} %param.19), channel_id=1, replica_groups=mesh['groups'=2,'seq'=4,'fsdp'=4] {'fsdp'}, dimensions={2}, use_global_device_ids=true | all-gather | bytes 983040 | tf_op jit(solution)/shard_map/all_gather | solution.py:111
  211.1 72.5 %while.16 = (s32[]{:T(128)}, f32[2,256,1536]{2,1,0:T(8,128)}, s32[]{:T(128)}, f32[17,64]{1,0:T(8,128)}, f32[64]{0:T(128)}, /*index=5*/f32[64,64]{1,0:T(8,128)}, ...) while((s32[]{:T(128)}, f32[2,256,1536]{2,1,0:T(8,128)}, ...), condition=%wide.region_1.2_spmd.clone, body=%wide.region_0.1_spmd.clone.sunk | while | flops 1934166400 | bytes 34141608 | solution.py:157
  212.6 1.2 broadcast_multiply_fusion.3
  213.9 1.3 fusion.93
  215.2 2.6 convolution_bitcast_fusion.6
  217.8 1.3 slice_bitcast_fusion.3
  219.1 2.7 convolution_bitcast_fusion.5
  221.8 2.5 select_subtract_fusion.2
  224.2 4.3 %maximum_add_fusion.2 = f32[2,256,1536]{2,1,0:T(8,128)} fusion(f32[2,128,1536]{2,1,0:T(8,128)} %get-tuple-element.484, f32[2,128,1536]{2,1,0:T(8,128)} %get-tuple-element.485, f32[2,256,1536]{2,1,0:T(8,128)} %get-tuple-element.502, pred[]{:T(512)S(6)} %compare.7), kind=kLoop, calls=%fused_computation.2.clone.1 | loop fusion | flops 2359296 | bytes 9437185 | tf_op jit(solution)/shard_map/while/body/eval_jaxpr/add | solution.py:146
  230.0 1.2 broadcast_multiply_fusion.3
  231.2 1.3 fusion.93
  232.6 2.6 convolution_bitcast_fusion.6
  235.2 1.3 slice_bitcast_fusion.3
  236.4 2.7 convolution_bitcast_fusion.5
  239.2 2.5 select_subtract_fusion.2
  241.6 5.2 %maximum_add_fusion.2 = f32[2,256,1536]{2,1,0:T(8,128)} fusion(f32[2,128,1536]{2,1,0:T(8,128)} %get-tuple-element.484, f32[2,128,1536]{2,1,0:T(8,128)} %get-tuple-element.485, f32[2,256,1536]{2,1,0:T(8,128)} %get-tuple-element.502, pred[]{:T(512)S(6)} %compare.7), kind=kLoop, calls=%fused_computation.2.clone.1 | loop fusion | flops 2359296 | bytes 9437185 | tf_op jit(solution)/shard_map/while/body/eval_jaxpr/add | solution.py:146
  248.4 1.2 broadcast_multiply_fusion.3
  249.6 1.3 fusion.93
  251.0 2.6 convolution_bitcast_fusion.6
  253.5 1.3 slice_bitcast_fusion.3
  254.8 2.7 convolution_bitcast_fusion.5
  257.5 2.5 select_subtract_fusion.2
  260.0 5.2 %maximum_add_fusion.2 = f32[2,256,1536]{2,1,0:T(8,128)} fusion(f32[2,128,1536]{2,1,0:T(8,128)} %get-tuple-element.484, f32[2,128,1536]{2,1,0:T(8,128)} %get-tuple-element.485, f32[2,256,1536]{2,1,0:T(8,128)} %get-tuple-element.502, pred[]{:T(512)S(6)} %compare.7), kind=kLoop, calls=%fused_computation.2.clone.1 | loop fusion | flops 2359296 | bytes 9437185 | tf_op jit(solution)/shard_map/while/body/eval_jaxpr/add | solution.py:146
  266.7 1.2 broadcast_multiply_fusion.3
  268.0 1.3 fusion.93
  269.3 2.6 convolution_bitcast_fusion.6
  271.9 1.3 slice_bitcast_fusion.3
  273.2 2.7 convolution_bitcast_fusion.5
  275.9 2.5 select_subtract_fusion.2
  278.3 5.2 %maximum_add_fusion.2 = f32[2,256,1536]{2,1,0:T(8,128)} fusion(f32[2,128,1536]{2,1,0:T(8,128)} %get-tuple-element.484, f32[2,128,1536]{2,1,0:T(8,128)} %get-tuple-element.485, f32[2,256,1536]{2,1,0:T(8,128)} %get-tuple-element.502, pred[]{:T(512)S(6)} %compare.7), kind=kLoop, calls=%fused_computation.2.clone.1 | loop fusion | flops 2359296 | bytes 9437185 | tf_op jit(solution)/shard_map/while/body/eval_jaxpr/add | solution.py:146
  283.6 8.8 %fusion.32 = bf16[2,128,1536]{1,2,0:T(8,128)(2,1)} fusion(f32[2,128,4608]{1,2,0:T(8,128)} %copy-done.3, f32[2,256,1536]{2,1,0:T(8,128)} %get-tuple-element.280, bf16[2,128,1536]{1,2,0:T(8,128)(2,1)} %fusion.31, f32[1536]{0:T(1024)S(1)} %reshape.184, f32[128,128]{1,0:T(8,128)} %get-tuple-element.392, f32[128,128]{1,0:T(8,128)} %get-tuple-element.391), kind=kOutput, calls=%fused_computation.67 | convolution fusion | flops 1209958400 | bytes 6428672 | tf_op jit(solution)/shard_map/if,sfd->sid/dot_general | solution.py:158
  292.3 2.3 copy.27
  (75 shorter events, 10.8 us)
Async XLA Ops:
  6.5 68.6 %copy-start = (bf16[1536,1152]{1,0:T(8,128)(2,1)S(1)}, bf16[1536,1152]{1,0:T(8,128)(2,1)}, u32[]{:S(2)}) copy-start(bf16[1536,1152]{1,0:T(8,128)(2,1)} %param.13) | copy-start | bytes 10616836
  6.5 68.6 %all-gather.4.cloned.1.call-start = ((), (), s32[]{:S(2)}) async-start(), calls=%async_computation.1 | async-start | bytes 3932160 | tf_op jit(solution)/shard_map/all_gather | solution.py:87
  82.7 4.7 %copy-start.5 = (s32[2,1]{0,1:T(1,128)S(1)}, s32[2,1]{0,1:T(1,128)}, u32[]{:S(2)}) copy-start(s32[2,1]{0,1:T(1,128)} %param.21) | copy-start | bytes 28
  82.7 58.8 %all-to-all-start = ((bf16[8,128,1152]{2,1,0:T(8,128)(2,1)}), bf16[8,128,1152]{2,1,0:T(8,128)(2,1)}, u32[]{:S(2)}, u32[]{:S(2)}) async-start(bf16[8,128,1152]{2,1,0:T(8,128)(2,1)} %bitcast.63), calls=%async_computation | async-start | bytes 4718592 | tf_op jit(solution)/shard_map/all_to_all | solution.py:96
  87.4 123.7 %all-gather.6.cloned.1.call-start = ((), (), s32[]{:S(2)}) async-start(), calls=%async_computation.2 | async-start | bytes 3932160 | tf_op jit(solution)/shard_map/all_gather | solution.py:149
  153.8 7.6 %collective-permute-start = (bf16[2,1,4608]{2,0,1:T(2,128)(2,1)}, bf16[2,1,4608]{2,0,1:T(2,128)(2,1)}, u32[]{:S(2)}, u32[]{:S(2)}) collective-permute-start(bf16[2,1,4608]{2,0,1:T(2,128)(2,1)} %copy.21), channel_id=1, source_target_pairs={{0,4},{4,8},{8,12},{1,5},{5,9},{9,13},{2,6},{6,10},{10,14},{3,7},{... | collective-permute-start | bytes 55304 | tf_op jit(solution)/shard_map/ppermute | solution.py:15
  158.3 5.7 %collective-permute-start.1 = (bf16[2,1,4608]{2,0,1:T(2,128)(2,1)}, bf16[2,1,4608]{2,0,1:T(2,128)(2,1)}, u32[]{:S(2)}, u32[]{:S(2)}) collective-permute-start(bf16[2,1,4608]{2,0,1:T(2,128)(2,1)} %copy.23), channel_id=1, source_target_pairs={{4,0},{8,4},{12,8},{5,1},{9,5},{13,9},{6,2},{10,6},{14,10},{7,3},{... | collective-permute-start | bytes 55304 | tf_op jit(solution)/shard_map/ppermute | solution.py:17
  174.3 2.1 copy-start.3
  176.4 1.1 copy-start.4
  219.1 2.7 copy-start.1
  219.1 2.7 copy-start.2
  236.4 2.7 copy-start.1
  236.4 2.7 copy-start.2
  254.8 2.7 copy-start.1
  254.8 2.7 copy-start.2
  273.2 2.7 copy-start.1
  273.2 2.7 copy-start.2
Sparse Core Ops, SparseCore 0:
  8.9 66.1 all-gather.3
  177.6 30.3 all-gather.5

commit v2 on v1

--- a/solution.py
+++ b/solution.py
@@ -107,55 +107,67 @@
         jnp.float32
     )
     carried = (key_part * value_part * valid_mask[:, :, None]).astype(jnp.bfloat16)
-    full_out, full_skip = (
-        lax.all_gather(response_out, "fsdp", axis=2, tiled=True),
-        lax.all_gather(skip_gain, "fsdp", axis=0, tiled=True),
+    local_ch = skip_gain.shape[0]
+    params = jnp.concatenate(
+        [response_out.reshape(2 * response_out.shape[1], local_ch), skip_gain[None, :]], axis=0
     )
-    stacked_out = full_out.reshape(2 * full_out.shape[1], width)
+    gathered = lax.all_gather(params, "fsdp", axis=0, tiled=False)
+    gathered = jnp.transpose(gathered, (1, 0, 2)).reshape(params.shape[0], width)
+    stacked_out = gathered[:-1]
+    full_skip = gathered[-1]
     seq_count = lax.axis_size("seq")
     position = lax.axis_index("seq")
     total_len = float(seq_count * block_len)
     forward = forward_table(block_len)
     forward_half = forward[:, :block_len]
+    half_hi = forward_half.astype(jnp.bfloat16)
+    half_lo = (forward_half - half_hi.astype(jnp.float32)).astype(jnp.bfloat16)
     inverse = inverse_table(block_len)
     circular = jnp.arange(2 * block_len, dtype=jnp.int32)
     wrapped = jnp.where(circular < block_len, circular, circular - 2 * block_len)
 
-    def kernel_response(offset, out_cols):
-        lag_values = offset + wrapped
+    piece = lax.all_gather(carried, "seq", axis=1, tiled=True)
+    block_total = piece.shape[1] // block_len
+
+    chunk = min(block_total, 4)
+
+    def chunk_spectrum(first, rows):
+        offsets = (position - first - jnp.arange(chunk, dtype=jnp.int32)) * block_len
+        lag_values = (offsets[:, None] + wrapped[None, :]).reshape(-1)
         basis_rows = filter_basis(
             lag_values, total_len, basis_in, basis_bias, basis_mid, basis_shift
         )
         ahead_mask = (lag_values >= 0).astype(jnp.float32)[:, None]
-        paired = jnp.concatenate([basis_rows * ahead_mask, basis_rows * (1.0 - ahead_mask)], axis=1)
-        return jnp.dot(
-            jnp.dot(forward, paired, precision=lax.Precision.HIGHEST),
-            out_cols,
-            precision=lax.Precision.HIGHEST,
+        paired = jnp.concatenate(
+            [basis_rows * ahead_mask, basis_rows * (1.0 - ahead_mask)], axis=1
         )
+        paired = paired.reshape(chunk, 2 * block_len, paired.shape[-1])
+        paired_spec = jnp.einsum("gf,bfk->bgk", forward, paired, precision=lax.Precision.HIGHEST)
+        response = jnp.einsum("bgk,kd->bgd", paired_spec, stacked_out, precision=lax.Precision.HIGH)
+        blocks = rows.reshape(seq_dev, chunk, block_len, width)
+        signal = jnp.einsum(
+            "fc,sbcd->sbfd", half_hi, blocks, preferred_element_type=jnp.float32
+        ) + jnp.einsum("fc,sbcd->sbfd", half_lo, blocks, preferred_element_type=jnp.float32)
+        total = packed_product(response[None, 0], signal[:, 0], block_len)
+        for index in range(1, chunk):
+            total = total + packed_product(response[None, index], signal[:, index], block_len)
+        return total
 
-    def add_block(spectrum, block_rows, start):
-        offset = position * block_len - start
-        response = kernel_response(offset, stacked_out)
-        signal = jnp.einsum(
-            "fc,scd->sfd",
-            forward_half,
-            block_rows.astype(jnp.float32),
-            precision=lax.Precision.HIGHEST,
+    if chunk == block_total:
+        spectrum = chunk_spectrum(0, piece)
+    else:
+
+        def one_chunk(chunk_index, carry):
+            rows = lax.dynamic_slice_in_dim(piece, chunk_index * chunk * block_len, chunk * block_len, 1)
+            return carry + chunk_spectrum(chunk_index * chunk, rows)
+
+        spectrum = lax.fori_loop(
+            0,
+            block_total // chunk,
+            one_chunk,
+            jnp.zeros((seq_dev, 2 * block_len, width), jnp.float32),
         )
-        return spectrum + packed_product(response[None], signal, block_len)
-
-    initial = jnp.zeros((seq_dev, 2 * block_len, width), jnp.float32)
-    piece = lax.all_gather(carried, "seq", axis=1, tiled=True)
-    piece_rows = piece.shape[1]
-    block_total = piece_rows // block_len
-
-    def one_block(block_index, carry):
-        block_rows = lax.dynamic_slice_in_dim(piece, block_index * block_len, block_len, 1)
-        return add_block(carry, block_rows, block_index * block_len)
-
-    spectrum = lax.fori_loop(0, block_total, one_block, initial)
-    conv = jnp.einsum("if,sfd->sid", inverse, spectrum, precision=lax.Precision.HIGHEST)
+    conv = jnp.einsum("if,sfd->sid", inverse, spectrum, precision=lax.Precision.HIGH)
     return (query_gate * (conv + full_skip * carried.astype(jnp.float32))).astype(jnp.bfloat16)
 
 

time: 304 us -> 244 us (0.80)
  other arithmetic: 42.7 us -> 14.8 us
  matrix products: 52.3 us -> 28.2 us
  blocking collectives: 30.6 us -> 18.9 us
  local copies, waits for them, and re-layouts: 31.5 us -> 37 us
    add x4 -> x0, other arithmetic: 19.9 us -> none  [add_block(): return spectrum + packed_product(response[None], signal, block_len)]
    dot_general x13 -> x5, matrix products: 35.1 us -> 16.7 us  [the longest x1 6.29 us: chunk_spectrum(): jnp.einsum('fc,sbcd->sbfd', half_lo, blocks, preferred_element_type=jnp.f...]
    all_gather x2 -> x1, blocking collectives: 30.6 us -> 18.9 us  [shards(): gathered = lax.all_gather(params, 'fsdp', axis=0, tiled=False)]
    squeeze x0 -> x1, local copies, waits for them, and re-layouts: none -> 8.56 us  [chunk_spectrum(): signal[:, index]]
    sub x4 -> x2, other arithmetic: 9.89 us -> 5.04 us  [packed_product(): prod_real = resp_real * sig_real - jnp.where(first_slot, 0.0, cross_term)]
    dot_general x4 -> x1, matrix products: 4.95 us -> 1.54 us  [filter_basis(): jnp.dot(hidden, basis_mid, precision=lax.Precision.HIGHEST) + basis_shift]
    all_gather x0 -> x1, local copies, waits for them, and re-layouts: none -> 3.18 us  [shards(): piece = lax.all_gather(carried, 'seq', axis=1, tiled=True)]
  transfers between devices with their start and end apart: 5 -> 5, of which waited for: 2 -> 2; matrix products, arithmetic and copies ran while one was open for 3% -> 7% of each run, Pallas kernels for 0% -> 0%
where the time goes in v2:
time: 244 us; the launch traced here: 243 us
  waiting for transfers between devices  122 us (50%)
  local copies, waits for them, and re-layouts  37 us (15%)
  matrix products  28.2 us (12%)
  blocking collectives  18.9 us (8%)
  other arithmetic  14.8 us (6%)
  between operations  13.8 us (6%)
  starting transfers between devices  8.13 us (3%)
    all_gather x1, waiting for transfers between devices, shards(): group_tokens = lax.all_gather(tokens, 'fsdp', axis=0, tiled=True)  67.9 us
    all_to_all x1, waiting for transfers between devices, shards(): projected = lax.all_to_all(partial, 'fsdp', 0, 2, tiled=True)  53.7 us
    all_gather x1, blocking collectives, shards(): gathered = lax.all_gather(params, 'fsdp', axis=0, tiled=False)  18.9 us
    squeeze x1, local copies, waits for them, and re-layouts, chunk_spectrum(): signal[:, index]  8.56 us
    dot_general x1, matrix products, shards(): jnp.dot(group_tokens.reshape(group_rows * block_len, width), in_weight, p...  7.53 us
    dot_general x1, matrix products, chunk_spectrum(): jnp.einsum('fc,sbcd->sbfd', half_lo, blocks, preferred_element_type=jnp.f...  6.29 us
    add x1, other arithmetic, shards(): short_weight[0] * padded[:, :-2] + short_weight[1] * padded[:, 1:-1]  6.29 us
    dot_general x1, matrix products, shards(): jnp.einsum('if,sfd->sid', inverse, spectrum, precision=lax.Precision.HIGH)  5.28 us
  transfers between devices with their start and end apart: 5, of which 2 were waited for; matrix products, arithmetic and copies ran while one was open for 7% of the time, Pallas kernels for 0%

profile of v2, /device:TPU:0, one launch (start us, length us, event | category | flops | bytes accessed | tf_op | source)
XLA Modules:
  0.0 243.3 jit_solution(17354887653073094636)
XLA Ops:
  6.5 0.7 all-gather.5.cloned.1.call-update
  7.3 67.9 %all-gather.5.cloned.1.call-done = bf16[8,128,1536]{2,1,0:T(8,128)(2,1)} async-done(((bf16[2,128,1536]{2,1,0:T(8,128)(2,1)}), bf16[8,128,1536]{2,1,0:T(8,128)(2,1)}) %all-gather.5.cloned.1.call-update) | async-done | bytes 3145744 | tf_op jit(solution)/shard_map/all_gather | solution.py:87
  75.2 7.5 %convolution_convert_fusion = bf16[1024,1152]{1,0:T(8,128)(2,1)} fusion(bf16[1024,1536]{1,0:T(8,128)(2,1)} %bitcast.106, bf16[1536,1152]{1,0:T(8,128)(2,1)S(1)} %copy-done), kind=kOutput, calls=%fused_computation.2 | convolution fusion | flops 3625058304 | bytes 9043968 | tf_op jit(solution)/shard_map/dot_general | solution.py:90
  82.7 3.8 %all-to-all-start = ((bf16[8,128,1152]{2,1,0:T(8,128)(2,1)}), bf16[8,128,1152]{2,1,0:T(8,128)(2,1)S(1)}, u32[]{:S(2)}, u32[]{:S(2)}) async-start(bf16[8,128,1152]{2,1,0:T(8,128)(2,1)} %bitcast.99), calls=%async_computation | async-start | bytes 4718592 | tf_op jit(solution)/shard_map/all_to_all | solution.py:96
  86.5 0.1 slice_reduce_fusion.2
  86.7 0.1 compare_convert_fusion
  86.8 53.7 %all-to-all-done = bf16[8,128,1152]{2,1,0:T(8,128)(2,1)S(1)} async-done(((bf16[8,128,1152]{2,1,0:T(8,128)(2,1)}), bf16[8,128,1152]{2,1,0:T(8,128)(2,1)S(1)}, u32[]{:S(2)}, u32[]{:S(2)}) %all-to-all-start) | async-done | bytes 2359328 | tf_op jit(solution)/shard_map/all_to_all | solution.py:96
  140.5 1.4 copy-done.4
  141.9 3.0 %copy.19 = bf16[4,2,128,1152]{2,3,0,1:T(8,128)(2,1)S(1)} copy(bf16[4,2,128,1152]{3,2,1,0:T(8,128)(2,1)} %bitcast.96) | data formatting | bytes 4718592 | tf_op jit(solution)/shard_map/all_to_all | solution.py:96
  145.0 2.9 %fusion.85 = (bf16[2,1,4608]{1,2,0:T(8,128)(2,1)}, bf16[2,1,4608]{1,2,0:T(8,128)(2,1)}) fusion(bf16[2,128,4608]{1,2,0:T(8,128)(2,1)S(1)} %bitcast.92), kind=kLoop, calls=%fused_computation.153 | loop fusion | bytes 73728 | tf_op jit(solution)/shard_map/slice | solution.py:12
  147.9 2.1 copy.22
  150.0 1.3 collective-permute-start.1
  151.3 2.1 copy.20
  153.4 3.0 %collective-permute-start = (bf16[2,1,4608]{2,0,1:T(2,128)(2,1)S(1)}, bf16[2,1,4608]{2,0,1:T(2,128)(2,1)S(1)}, u32[]{:S(2)}, u32[]{:S(2)}) collective-permute-start(bf16[2,1,4608]{2,0,1:T(2,128)(2,1)S(1)} %copy.20), channel_id=1, source_target_pairs={{0,4},{4,8},{8,12},{1,5},{5,9},{9,13},{2,6},{6,10},{10,14},{3,7},{... | collective-permute-start | bytes 55304 | tf_op jit(solution)/shard_map/ppermute | solution.py:15
  156.5 2.0 copy.23
  158.5 2.0 copy.21
  160.4 6.3 %multiply_add_fusion = f32[2,128,4608]{1,2,0:T(8,128)S(1)} fusion(bf16[2,128,4608]{1,2,0:T(8,128)(2,1)S(1)} %bitcast.93, bf16[2,1,4608]{1,2,0:T(8,128)(2,1)} %copy.23, bf16[2,1,4608]{1,2,0:T(8,128)(2,1)} %copy.21, f32[4608]{0:T(1024)S(1)} %get-tuple-element.6, f32[4608]{0:T(1024)S(1)} %get-tuple-element.7, f32[4608]{0:T(1024)S(1)} %get-tuple-element.5), kind=kLoop, calls=%fused_computation.1 | loop fusion | flops 16515072 | bytes 7170048 | tf_op jit(solution)/shard_map/add | solution.py:99
  166.7 2.1 copy-done.2
  168.8 1.0 fusion.22
  169.9 0.1 convert_bitcast_fusion
  170.0 0.1 fusion.68
  170.1 0.1 fusion.71
  170.2 18.9 %all-gather.1 = f32[4,129,384]{2,1,0:T(8,128)S(1)} all-gather(f32[1,129,384]{2,1,0:T(8,128)S(1)} %maximum_bitcast_fusion), channel_id=2, replica_groups=mesh['groups'=2,'seq'=4,'fsdp'=4] {'fsdp'}, dimensions={0}, use_global_device_ids=true | all-gather | bytes 990720 | tf_op jit(solution)/shard_map/all_gather | solution.py:114
  189.2 0.5 copy.24
  189.7 0.3 reshape.231
  190.2 0.6 fusion.65
  190.8 2.5 %fusion.26 = f32[1024,64]{1,0:T(8,128)S(1)} fusion(f32[17,64]{1,0:T(8,128)S(1)} %copy-done.17, f32[64]{0:T(128)S(1)} %copy-done.20, f32[1024,8]{0,1:T(8,128)S(1)} %get-tuple-element.33, f32[1024,8]{0,1:T(8,128)S(1)} %get-tuple-element.32, f32[1024,1]{0,1:T(1,128)S(1)} %bitcast.104), kind=kOutput, calls=%fused_computation.45 | convolution fusion | flops 13469696 | bytes 336384 | tf_op jit(solution)/shard_map/dot_general | solution.py:36
  193.3 1.5 broadcast_multiply_fusion.1
  194.9 0.9 select_multiply_fusion.1
  195.8 0.5 negate_select_fusion.2
  196.4 0.7 convolution_bitcast_fusion
  197.1 2.7 %fusion.86 = f32[4,256,1536]{2,1,0:T(8,128)S(1)} fusion(f32[4,256,128]{2,1,0:T(8,128)S(1)} %convolution_bitcast_fusion, f32[128,1536,1]{1,0,2:T(8,128)S(1)} %reshape.231), kind=kOutput, calls=%fused_computation.154 | convolution fusion | flops 1207959552 | bytes 7602176 | tf_op jit(solution)/shard_map/bgk,kd->bgd/dot_general | solution.py:146
  199.7 2.7 %slice_bitcast_fusion.5 = (f32[128,1536]{1,0:T(8,128)}, f32[128,1536]{1,0:T(8,128)}, f32[128,1536]{1,0:T(8,128)}, f32[128,1536]{1,0:T(8,128)}, f32[128,1536]{1,0...) fusion(f32[4,256,1536]{2,1,0:T(8,128)S(1)} %fusion.86), kind=kLoop, calls=%fused_computation.49 | loop fusion | bytes 12582912 | tf_op jit(solution)/shard_map/mul | solution.py:69
  202.5 3.2 %copy.25 = bf16[2,512,1536]{2,1,0:T(8,128)(2,1)S(1)} copy(bf16[2,512,1536]{1,2,0:T(8,128)(2,1)} %all-gather.7.cloned.1.call-done) | data formatting | bytes 6291456 | tf_op jit(solution)/shard_map/all_gather | solution.py:129
  205.7 1.8 fusion.51
  207.4 6.3 %add_bitcast_fusion = f32[2,4,256,1536]{3,2,1,0:T(8,128)} fusion(f32[2,4,1536,256]{2,3,1,0:T(8,128)S(1)} %fusion.51, bf16[2,4,128,1536]{3,2,1,0:T(8,128)(2,1)S(1)} %bitcast.95, f32[128,256]{1,0:T(8,128)S(1)} %get-tuple-element.41, f32[128,256]{1,0:T(8,128)S(1)} %get-tuple-element.40), kind=kOutput, calls=%fused_computation | convolution fusion | flops 808615936 | bytes 28573696 | tf_op jit(solution)/shard_map/fc,sbcd->sbfd/dot_general | solution.py:150
  213.7 8.6 %slice_bitcast_fusion = (f32[2,256,1536]{2,1,0:T(8,128)S(1)}, f32[2,256,1536]{2,1,0:T(8,128)S(1)}, f32[2,256,1536]{2,1,0:T(8,128)}, f32[2,256,1536]{2,1,0:T(8,128)}) fusion(f32[2,4,256,1536]{3,2,1,0:T(8,128)} %add_bitcast_fusion), kind=kLoop, calls=%fused_computation.3 | loop fusion | bytes 25165824 | tf_op jit(solution)/shard_map/squeeze | solution.py:153
  222.3 3.1 %select_subtract_fusion.3 = (f32[2,128,1536]{2,1,0:T(8,128)S(1)}, f32[2,128,1536]{2,1,0:T(8,128)S(1)}) fusion(f32[2,256,1536]{2,1,0:T(8,128)} %get-tuple-element.10, f32[128,1536]{1,0:T(8,128)} %get-tuple-element.18, f32[128,1536]{1,0:T(8,128)} %get-tuple-element.19, pred[128]{0:T(512)(128)(4,1)S(1)} %iota_compare_fusion), kind=kLoop, calls=%fused_computation.38 | loop fusion | flops 3145728 | bytes 7864448 | tf_op jit(solution)/shard_map/sub | solution.py:69
  225.5 0.1 copy-done.3
  225.6 0.2 copy-done.6
  225.8 0.2 copy-done.7
  226.0 0.2 copy-done.8
  226.3 0.2 copy-done.9
  226.5 0.2 copy-done.10
  226.7 0.2 copy-done.11
  226.9 1.9 select_subtract_fusion
  228.9 5.3 %fusion.23 = bf16[2,128,1536]{1,2,0:T(8,128)(2,1)} fusion(f32[2,128,4608]{1,2,0:T(8,128)} %copy-done.2, f32[2,128,1536]{2,1,0:T(8,128)S(1)} %get-tuple-element.27, f32[2,128,1536]{2,1,0:T(8,128)S(1)} %get-tuple-element.26, f32[2,128,1536]{2,1,0:T(8,128)S(1)} %get-tuple-element.36, f32[2,128,1536]{2,1,0:T(8,128)S(1)} %get-tuple-element.37, ...), kind=kOutput, calls=%fused_computation.30 | convolution fusion | flops 611483648 | bytes 15865856 | tf_op jit(solution)/shard_map/if,sfd->sid/dot_general | solution.py:170
  234.2 2.3 copy.30
  (58 shorter events, 0.4 us)
Async XLA Ops:
  6.5 68.6 %copy-start = (bf16[1536,1152]{1,0:T(8,128)(2,1)S(1)}, bf16[1536,1152]{1,0:T(8,128)(2,1)}, u32[]{:S(2)}) copy-start(bf16[1536,1152]{1,0:T(8,128)(2,1)} %param.11) | copy-start | bytes 10616836
  6.5 68.6 %all-gather.5.cloned.1.call-start = ((), (), s32[]{:S(2)}) async-start(), calls=%async_computation.1 | async-start | bytes 3932160 | tf_op jit(solution)/shard_map/all_gather | solution.py:87
  82.7 3.8 %copy-start.15 = (f32[3,4608]{1,0:T(4,128)S(1)}, f32[3,4608]{1,0:T(4,128)}, u32[]{:S(2)}) copy-start(f32[3,4608]{1,0:T(4,128)} %param.12) | copy-start | bytes 165892
  82.7 4.0 %copy-start.21 = (s32[2,1]{0,1:T(1,128)S(1)}, s32[2,1]{0,1:T(1,128)}, u32[]{:S(2)}) copy-start(s32[2,1]{0,1:T(1,128)} %param.19) | copy-start | bytes 28
  82.7 57.8 %all-to-all-start = ((bf16[8,128,1152]{2,1,0:T(8,128)(2,1)}), bf16[8,128,1152]{2,1,0:T(8,128)(2,1)S(1)}, u32[]{:S(2)}, u32[]{:S(2)}) async-start(bf16[8,128,1152]{2,1,0:T(8,128)(2,1)} %bitcast.99), calls=%async_computation | async-start | bytes 4718592 | tf_op jit(solution)/shard_map/all_to_all | solution.py:96
  86.5 116.0 %all-gather.7.cloned.1.call-start = ((), (), s32[]{:S(2)}) async-start(), calls=%async_computation.2 | async-start | bytes 3932160 | tf_op jit(solution)/shard_map/all_gather | solution.py:129
  140.5 1.4 copy-start.4
  150.0 6.5 %collective-permute-start.1 = (bf16[2,1,4608]{2,0,1:T(2,128)(2,1)S(1)}, bf16[2,1,4608]{2,0,1:T(2,128)(2,1)S(1)}, u32[]{:S(2)}, u32[]{:S(2)}) collective-permute-start(bf16[2,1,4608]{2,0,1:T(2,128)(2,1)S(1)} %copy.22), channel_id=1, source_target_pairs={{4,0},{8,4},{12,8},{5,1},{9,5},{13,9},{6,2},{10,6},{14,10},{7,3},{... | collective-permute-start | bytes 55304 | tf_op jit(solution)/shard_map/ppermute | solution.py:17
  153.4 5.0 %collective-permute-start = (bf16[2,1,4608]{2,0,1:T(2,128)(2,1)S(1)}, bf16[2,1,4608]{2,0,1:T(2,128)(2,1)S(1)}, u32[]{:S(2)}, u32[]{:S(2)}) collective-permute-start(bf16[2,1,4608]{2,0,1:T(2,128)(2,1)S(1)} %copy.20), channel_id=1, source_target_pairs={{0,4},{4,8},{8,12},{1,5},{5,9},{9,13},{2,6},{6,10},{10,14},{3,7},{... | collective-permute-start | bytes 55304 | tf_op jit(solution)/shard_map/ppermute | solution.py:15
  166.7 2.1 copy-start.2
  168.8 1.3 copy-start.18
  168.8 1.3 copy-start.14
  189.1 1.6 copy-start.17
  189.1 1.6 copy-start.20
  189.1 4.1 %copy-start.16 = (f32[64,64]{1,0:T(8,128)S(1)}, f32[64,64]{1,0:T(8,128)}, u32[]{:S(2)}) copy-start(f32[64,64]{1,0:T(8,128)} %param.15) | copy-start | bytes 49156
  189.2 4.1 %copy-start.19 = (f32[64]{0:T(128)S(1)}, f32[64]{0:T(128)}, u32[]{:S(2)}) copy-start(f32[64]{0:T(128)} %param.16) | copy-start | bytes 772
  222.3 3.3 %copy-start.3 = (f32[2,256,1536]{2,1,0:T(8,128)S(1)}, f32[2,256,1536]{2,1,0:T(8,128)}, u32[]{:S(2)}) copy-start(f32[2,256,1536]{2,1,0:T(8,128)} %get-tuple-element.11) | copy-start | bytes 9437188
  222.3 3.5 %copy-start.6 = (f32[128,1536]{1,0:T(8,128)S(1)}, f32[128,1536]{1,0:T(8,128)}, u32[]{:S(2)}) copy-start(f32[128,1536]{1,0:T(8,128)} %get-tuple-element.12) | copy-start | bytes 2359300
  222.3 3.7 %copy-start.7 = (f32[128,1536]{1,0:T(8,128)S(1)}, f32[128,1536]{1,0:T(8,128)}, u32[]{:S(2)}) copy-start(f32[128,1536]{1,0:T(8,128)} %get-tuple-element.13) | copy-start | bytes 2359300
  222.3 4.0 %copy-start.8 = (f32[128,1536]{1,0:T(8,128)S(1)}, f32[128,1536]{1,0:T(8,128)}, u32[]{:S(2)}) copy-start(f32[128,1536]{1,0:T(8,128)} %get-tuple-element.14) | copy-start | bytes 2359300
  222.3 4.2 %copy-start.9 = (f32[128,1536]{1,0:T(8,128)S(1)}, f32[128,1536]{1,0:T(8,128)}, u32[]{:S(2)}) copy-start(f32[128,1536]{1,0:T(8,128)} %get-tuple-element.15) | copy-start | bytes 2359300
  222.3 4.4 %copy-start.10 = (f32[128,1536]{1,0:T(8,128)S(1)}, f32[128,1536]{1,0:T(8,128)}, u32[]{:S(2)}) copy-start(f32[128,1536]{1,0:T(8,128)} %get-tuple-element.16) | copy-start | bytes 2359300
  222.3 4.6 %copy-start.11 = (f32[128,1536]{1,0:T(8,128)S(1)}, f32[128,1536]{1,0:T(8,128)}, u32[]{:S(2)}) copy-start(f32[128,1536]{1,0:T(8,128)} %get-tuple-element.17) | copy-start | bytes 2359300
  226.9 1.9 copy-start.5
  226.9 1.9 copy-start.12
  226.9 1.9 copy-start.13
  228.9 7.6 %copy-start.1 = (bf16[1536,1152]{1,0:T(8,128)(2,1)S(1)}, bf16[1536,1152]{1,0:T(8,128)(2,1)}, u32[]{:S(2)}) copy-start(bf16[1536,1152]{1,0:T(8,128)(2,1)} %param.11) | copy-start | bytes 10616836
Sparse Core Ops, SparseCore 0:
  8.9 66.1 all-gather.4
  170.0 28.6 all-gather.6

commit v3 on v2

--- a/solution.py
+++ b/solution.py
@@ -84,7 +84,59 @@
     block_counts,
 ):
     seq_dev, block_len, width = tokens.shape
+    local_ch = skip_gain.shape[0]
+    params = jnp.concatenate(
+        [response_out.reshape(2 * response_out.shape[1], local_ch), skip_gain[None, :]], axis=0
+    )
+    gathered = lax.all_gather(params, "fsdp", axis=0, tiled=False)
+    gathered = jnp.transpose(gathered, (1, 0, 2)).reshape(params.shape[0], width)
+    stacked_out = gathered[:-1]
+    full_skip = gathered[-1]
+    seq_count = lax.axis_size("seq")
+    position = lax.axis_index("seq")
+    total_len = float(seq_count * block_len)
+    forward = forward_table(block_len)
+    forward_half = forward[:, :block_len]
+    half_hi = forward_half.astype(jnp.bfloat16)
+    half_lo = (forward_half - half_hi.astype(jnp.float32)).astype(jnp.bfloat16)
+    inverse = inverse_table(block_len)
+    circular = jnp.arange(2 * block_len, dtype=jnp.int32)
+    wrapped = jnp.where(circular < block_len, circular, circular - 2 * block_len)
+
+    block_total = seq_count
+    chunk = min(block_total, 4)
+
+    def chunk_response(first):
+        offsets = (position - first - jnp.arange(chunk, dtype=jnp.int32)) * block_len
+        lag_values = (offsets[:, None] + wrapped[None, :]).reshape(-1)
+        basis_rows = filter_basis(
+            lag_values, total_len, basis_in, basis_bias, basis_mid, basis_shift
+        )
+        ahead_mask = (lag_values >= 0).astype(jnp.float32)[:, None]
+        paired = jnp.concatenate(
+            [basis_rows * ahead_mask, basis_rows * (1.0 - ahead_mask)], axis=1
+        )
+        paired = paired.reshape(chunk, 2 * block_len, paired.shape[-1])
+        paired_spec = jnp.einsum("gf,bfk->bgk", forward, paired, precision=lax.Precision.HIGHEST)
+        return jnp.einsum("bgk,kd->bgd", paired_spec, stacked_out, precision=lax.Precision.HIGH)
+
+    def chunk_apply(response, rows):
+        blocks = rows.reshape(seq_dev, chunk, block_len, width)
+        signal = jnp.einsum(
+            "fc,sbcd->sbfd", half_hi, blocks, preferred_element_type=jnp.float32
+        ) + jnp.einsum("fc,sbcd->sbfd", half_lo, blocks, preferred_element_type=jnp.float32)
+        total = packed_product(response[None, 0], signal[:, 0], block_len)
+        for index in range(1, chunk):
+            total = total + packed_product(response[None, index], signal[:, index], block_len)
+        return total
+
     group_tokens = lax.all_gather(tokens, "fsdp", axis=0, tiled=True)
+    single = chunk == block_total
+    if single:
+        early_response = chunk_response(0)
+        group_tokens, early_response, full_skip = lax.optimization_barrier(
+            (group_tokens, early_response, full_skip)
+        )
     group_rows = group_tokens.shape[0]
     local_cols = in_weight.shape[1]
     partial = jnp.dot(
@@ -107,59 +159,15 @@
         jnp.float32
     )
     carried = (key_part * value_part * valid_mask[:, :, None]).astype(jnp.bfloat16)
-    local_ch = skip_gain.shape[0]
-    params = jnp.concatenate(
-        [response_out.reshape(2 * response_out.shape[1], local_ch), skip_gain[None, :]], axis=0
-    )
-    gathered = lax.all_gather(params, "fsdp", axis=0, tiled=False)
-    gathered = jnp.transpose(gathered, (1, 0, 2)).reshape(params.shape[0], width)
-    stacked_out = gathered[:-1]
-    full_skip = gathered[-1]
-    seq_count = lax.axis_size("seq")
-    position = lax.axis_index("seq")
-    total_len = float(seq_count * block_len)
-    forward = forward_table(block_len)
-    forward_half = forward[:, :block_len]
-    half_hi = forward_half.astype(jnp.bfloat16)
-    half_lo = (forward_half - half_hi.astype(jnp.float32)).astype(jnp.bfloat16)
-    inverse = inverse_table(block_len)
-    circular = jnp.arange(2 * block_len, dtype=jnp.int32)
-    wrapped = jnp.where(circular < block_len, circular, circular - 2 * block_len)
-
     piece = lax.all_gather(carried, "seq", axis=1, tiled=True)
-    block_total = piece.shape[1] // block_len
-
-    chunk = min(block_total, 4)
-
-    def chunk_spectrum(first, rows):
-        offsets = (position - first - jnp.arange(chunk, dtype=jnp.int32)) * block_len
-        lag_values = (offsets[:, None] + wrapped[None, :]).reshape(-1)
-        basis_rows = filter_basis(
-            lag_values, total_len, basis_in, basis_bias, basis_mid, basis_shift
-        )
-        ahead_mask = (lag_values >= 0).astype(jnp.float32)[:, None]
-        paired = jnp.concatenate(
-            [basis_rows * ahead_mask, basis_rows * (1.0 - ahead_mask)], axis=1
-        )
-        paired = paired.reshape(chunk, 2 * block_len, paired.shape[-1])
-        paired_spec = jnp.einsum("gf,bfk->bgk", forward, paired, precision=lax.Precision.HIGHEST)
-        response = jnp.einsum("bgk,kd->bgd", paired_spec, stacked_out, precision=lax.Precision.HIGH)
-        blocks = rows.reshape(seq_dev, chunk, block_len, width)
-        signal = jnp.einsum(
-            "fc,sbcd->sbfd", half_hi, blocks, preferred_element_type=jnp.float32
-        ) + jnp.einsum("fc,sbcd->sbfd", half_lo, blocks, preferred_element_type=jnp.float32)
-        total = packed_product(response[None, 0], signal[:, 0], block_len)
-        for index in range(1, chunk):
-            total = total + packed_product(response[None, index], signal[:, index], block_len)
-        return total
-
-    if chunk == block_total:
-        spectrum = chunk_spectrum(0, piece)
+
+    if single:
+        spectrum = chunk_apply(early_response, piece)
     else:
 
         def one_chunk(chunk_index, carry):
             rows = lax.dynamic_slice_in_dim(piece, chunk_index * chunk * block_len, chunk * block_len, 1)
-            return carry + chunk_spectrum(chunk_index * chunk, rows)
+            return carry + chunk_apply(chunk_response(chunk_index * chunk), rows)
 
         spectrum = lax.fori_loop(
             0,

time: 244 us -> 248 us (1.016)
  waiting for transfers between devices: 122 us -> 102 us
  local copies, waits for them, and re-layouts: 37 us -> 47.8 us
  blocking collectives: 18.9 us -> 28.7 us
  matrix products: 28.2 us -> 31.6 us
    all_gather x1, waiting for transfers between devices: 67.9 us -> 22.3 us  [shards(): group_tokens = lax.all_gather(tokens, 'fsdp', axis=0, tiled=True)]
    all_gather x1, waiting for transfers between devices: 0.01 us -> 23.3 us  [shards(): piece = lax.all_gather(carried, 'seq', axis=1, tiled=True)]
    all_gather x1, blocking collectives: 18.9 us -> 28.7 us  [shards(): gathered = lax.all_gather(params, 'fsdp', axis=0, tiled=False)]
    slice x3, local copies, waits for them, and re-layouts: 0.88 us -> 3.78 us  [shards(): stacked_out = gathered[:-1]]
    mul x1, local copies, waits for them, and re-layouts: 2.74 us -> 5.53 us  [packed_product(): prod_real = resp_real * sig_real - jnp.where(first_slot, 0.0, cross_term)]
    unnamed x47 -> x51, local copies, waits for them, and re-layouts: 5.05 us -> 7.28 us
    squeeze x1 -> x2, local copies, waits for them, and re-layouts: 8.56 us -> 9.25 us  [the longest x1 8.55 us: chunk_apply(): signal[:, index]]
  transfers between devices with their start and end apart: 5 -> 5, of which waited for: 2 -> 4; matrix products, arithmetic and copies ran while one was open for 7% -> 13% of each run, Pallas kernels for 0% -> 0%
where the time goes in v3:
time: 248 us; the launch traced here: 247 us
  waiting for transfers between devices  102 us (41%)
  local copies, waits for them, and re-layouts  47.8 us (19%)
  matrix products  31.6 us (13%)
  blocking collectives  28.7 us (12%)
  other arithmetic  16.5 us (7%)
  between operations  13.8 us (6%)
  starting transfers between devices  6.58 us (3%)
    all_to_all x1, waiting for transfers between devices, shards(): projected = lax.all_to_all(partial, 'fsdp', 0, 2, tiled=True)  54 us
    all_gather x1, blocking collectives, shards(): gathered = lax.all_gather(params, 'fsdp', axis=0, tiled=False)  28.7 us
    all_gather x1, waiting for transfers between devices, shards(): piece = lax.all_gather(carried, 'seq', axis=1, tiled=True)  23.3 us
    all_gather x1, waiting for transfers between devices, shards(): group_tokens = lax.all_gather(tokens, 'fsdp', axis=0, tiled=True)  22.3 us
    squeeze x1, local copies, waits for them, and re-layouts, chunk_apply(): signal[:, index]  8.55 us
    dot_general x1, matrix products, shards(): jnp.dot(group_tokens.reshape(group_rows * block_len, width), in_weight, p...  7.5 us
    unnamed x51, local copies, waits for them, and re-layouts  7.28 us
    dot_general x1, matrix products, chunk_apply(): jnp.einsum('fc,sbcd->sbfd', half_lo, blocks, preferred_element_type=jnp.f...  6.3 us
  transfers between devices with their start and end apart: 5, of which 4 were waited for; matrix products, arithmetic and copies ran while one was open for 13% of the time, Pallas kernels for 0%

profile of v3, /device:TPU:0, one launch (start us, length us, event | category | flops | bytes accessed | tf_op | source)
XLA Modules:
  0.0 246.6 jit_solution(16606559991859919696)
XLA Ops:
  6.5 0.7 all-gather.5.cloned.1.call-update
  7.4 0.6 copy.40
  8.1 0.7 broadcast_in_dim.126
  8.8 0.9 maximum_bitcast_fusion
  9.7 28.7 %all-gather.1 = f32[4,129,384]{2,1,0:T(8,128)S(1)} all-gather(f32[1,129,384]{2,1,0:T(8,128)S(1)} %maximum_bitcast_fusion), channel_id=2, replica_groups=mesh['groups'=2,'seq'=4,'fsdp'=4] {'fsdp'}, dimensions={0}, use_global_device_ids=true | all-gather | bytes 990720 | tf_op jit(solution)/shard_map/all_gather | solution.py:91
  38.5 0.9 copy-done.6
  39.4 1.4 copy.19
  40.8 2.3 reshape.231
  43.2 1.4 slice_reduce_fusion.3
  44.6 0.7 squeeze.15
  45.4 1.3 fusion.65
  46.6 3.2 %fusion.26 = f32[1024,64]{1,0:T(8,128)S(1)} fusion(f32[17,64]{1,0:T(8,128)} %param.13, f32[64]{0:T(128)} %param.14, f32[1024,8]{0,1:T(8,128)S(1)} %get-tuple-element.39, f32[1024,8]{0,1:T(8,128)S(1)} %get-tuple-element.38, f32[1024,1]{0,1:T(1,128)S(1)} %bitcast.104), kind=kOutput, calls=%fused_computation.45 | convolution fusion | flops 13469696 | bytes 336384 | tf_op jit(solution)/shard_map/dot_general | solution.py:36
  49.9 2.3 broadcast_multiply_fusion.1
  52.2 0.5 negate_select_fusion.2
  52.8 0.6 copy-done.14
  53.5 0.6 convolution_bitcast_fusion
  54.2 4.6 %fusion.86 = f32[4,256,1536]{2,1,0:T(8,128)} fusion(f32[4,256,128]{2,1,0:T(8,128)S(1)} %convolution_bitcast_fusion, f32[128,1536,1]{1,0,2:T(8,128)S(1)} %copy-done.13), kind=kOutput, calls=%fused_computation.154 | convolution fusion | flops 1207959552 | bytes 7602176 | tf_op jit(solution)/shard_map/bgk,kd->bgd/dot_general | solution.py:121
  58.8 22.3 %all-gather.5.cloned.1.call-done = bf16[8,128,1536]{2,1,0:T(8,128)(2,1)} async-done(((bf16[2,128,1536]{2,1,0:T(8,128)(2,1)}), bf16[8,128,1536]{2,1,0:T(8,128)(2,1)}) %all-gather.5.cloned.1.call-update) | async-done | bytes 3145744 | tf_op jit(solution)/shard_map/all_gather | solution.py:133
  81.1 7.5 %convolution_convert_fusion = bf16[1024,1152]{1,0:T(8,128)(2,1)} fusion(bf16[1024,1536]{1,0:T(8,128)(2,1)} %bitcast.106, bf16[1536,1152]{1,0:T(8,128)(2,1)S(1)} %copy-done), kind=kOutput, calls=%fused_computation.2 | convolution fusion | flops 3625058304 | bytes 9043968 | tf_op jit(solution)/shard_map/dot_general | solution.py:142
  88.6 3.8 %all-to-all-start = ((bf16[8,128,1152]{2,1,0:T(8,128)(2,1)}), bf16[8,128,1152]{2,1,0:T(8,128)(2,1)S(1)}, u32[]{:S(2)}, u32[]{:S(2)}) async-start(bf16[8,128,1152]{2,1,0:T(8,128)(2,1)} %bitcast.99), calls=%async_computation | async-start | bytes 4718592 | tf_op jit(solution)/shard_map/all_to_all | solution.py:148
  92.6 54.0 %all-to-all-done = bf16[8,128,1152]{2,1,0:T(8,128)(2,1)S(1)} async-done(((bf16[8,128,1152]{2,1,0:T(8,128)(2,1)}), bf16[8,128,1152]{2,1,0:T(8,128)(2,1)S(1)}, u32[]{:S(2)}, u32[]{:S(2)}) %all-to-all-start) | async-done | bytes 2359328 | tf_op jit(solution)/shard_map/all_to_all | solution.py:148
  146.6 1.5 copy-done.4
  148.1 3.0 %copy.20 = bf16[4,2,128,1152]{2,3,0,1:T(8,128)(2,1)S(1)} copy(bf16[4,2,128,1152]{3,2,1,0:T(8,128)(2,1)} %bitcast.96) | data formatting | bytes 4718592 | tf_op jit(solution)/shard_map/all_to_all | solution.py:148
  151.1 3.0 %fusion.85 = (bf16[2,1,4608]{1,2,0:T(8,128)(2,1)}, bf16[2,1,4608]{1,2,0:T(8,128)(2,1)}) fusion(bf16[2,128,4608]{1,2,0:T(8,128)(2,1)S(1)} %bitcast.92), kind=kLoop, calls=%fused_computation.153 | loop fusion | bytes 73728 | tf_op jit(solution)/shard_map/slice | solution.py:12
  154.2 2.1 copy.21
  156.3 1.3 collective-permute-start
  157.6 2.1 copy.23
  159.7 1.3 collective-permute-start.1
  161.2 2.0 copy.22
  163.2 1.4 collective-permute-done.1
  164.5 2.0 copy.24
  166.5 6.3 %multiply_add_fusion = f32[2,128,4608]{1,2,0:T(8,128)S(1)} fusion(bf16[2,128,4608]{1,2,0:T(8,128)(2,1)S(1)} %bitcast.93, bf16[2,1,4608]{1,2,0:T(8,128)(2,1)} %copy.24, bf16[2,1,4608]{1,2,0:T(8,128)(2,1)} %copy.22, f32[4608]{0:T(1024)S(1)} %get-tuple-element.12, f32[4608]{0:T(1024)S(1)} %get-tuple-element.13, f32[4608]{0:T(1024)S(1)} %get-tuple-element.11), kind=kLoop, calls=%fused_computation.1 | loop fusion | flops 16515072 | bytes 7170048 | tf_op jit(solution)/shard_map/add | solution.py:151
  172.8 2.1 copy-done.2
  174.9 1.0 fusion.22
  176.0 0.9 select_multiply_fusion.1
  176.9 5.5 %slice_bitcast_fusion.5 = (f32[128,1536]{1,0:T(8,128)}, f32[128,1536]{1,0:T(8,128)}, f32[128,1536]{1,0:T(8,128)}, f32[128,1536]{1,0:T(8,128)}, f32[128,1536]{1,0...) fusion(f32[4,256,1536]{2,1,0:T(8,128)} %fusion.86), kind=kLoop, calls=%fused_computation.49 | loop fusion | bytes 12582912 | tf_op jit(solution)/shard_map/mul | solution.py:69
  182.5 23.3 %all-gather.7.cloned.1.call-done = bf16[2,512,1536]{1,2,0:T(8,128)(2,1)} async-done(((bf16[2,128,1536]{1,2,0:T(8,128)(2,1)}), bf16[2,512,1536]{1,2,0:T(8,128)(2,1)}) %all-gather.7.cloned.1.call-update) | async-done | bytes 3145744 | tf_op jit(solution)/shard_map/all_gather | solution.py:162
  205.8 3.2 %copy.25 = bf16[2,512,1536]{2,1,0:T(8,128)(2,1)S(1)} copy(bf16[2,512,1536]{1,2,0:T(8,128)(2,1)} %all-gather.7.cloned.1.call-done) | data formatting | bytes 6291456 | tf_op jit(solution)/shard_map/all_gather | solution.py:162
  209.0 1.8 fusion.51
  210.8 6.3 %add_bitcast_fusion = f32[2,4,256,1536]{3,2,1,0:T(8,128)} fusion(f32[2,4,1536,256]{2,3,1,0:T(8,128)S(1)} %fusion.51, bf16[2,4,128,1536]{3,2,1,0:T(8,128)(2,1)S(1)} %bitcast.95, f32[128,256]{1,0:T(8,128)S(1)} %copy-done.17, f32[128,256]{1,0:T(8,128)S(1)} %copy-done.15), kind=kOutput, calls=%fused_computation | convolution fusion | flops 808615936 | bytes 28573696 | tf_op jit(solution)/shard_map/fc,sbcd->sbfd/dot_general | solution.py:127
  217.1 8.5 %slice_bitcast_fusion = (f32[2,256,1536]{2,1,0:T(8,128)S(1)}, f32[2,256,1536]{2,1,0:T(8,128)S(1)}, f32[2,256,1536]{2,1,0:T(8,128)}, f32[2,256,1536]{2,1,0:T(8,128)}) fusion(f32[2,4,256,1536]{3,2,1,0:T(8,128)} %add_bitcast_fusion), kind=kLoop, calls=%fused_computation.3 | loop fusion | bytes 25165824 | tf_op jit(solution)/shard_map/squeeze | solution.py:130
  225.7 3.1 %select_subtract_fusion.3 = (f32[2,128,1536]{2,1,0:T(8,128)S(1)}, f32[2,128,1536]{2,1,0:T(8,128)S(1)}) fusion(f32[2,256,1536]{2,1,0:T(8,128)} %get-tuple-element.16, f32[128,1536]{1,0:T(8,128)} %get-tuple-element.24, f32[128,1536]{1,0:T(8,128)} %get-tuple-element.25, pred[128]{0:T(512)(128)(4,1)S(1)} %copy-done.22), kind=kLoop, calls=%fused_computation.38 | loop fusion | flops 3145728 | bytes 7864448 | tf_op jit(solution)/shard_map/sub | solution.py:69
  229.1 0.2 copy-done.8
  229.3 0.2 copy-done.9
  229.6 0.2 copy-done.10
  230.3 1.9 select_subtract_fusion
  232.2 5.3 %fusion.23 = bf16[2,128,1536]{1,2,0:T(8,128)(2,1)} fusion(f32[2,128,4608]{1,2,0:T(8,128)} %copy-done.2, f32[2,128,1536]{2,1,0:T(8,128)S(1)} %get-tuple-element.33, f32[2,128,1536]{2,1,0:T(8,128)S(1)} %get-tuple-element.32, f32[2,128,1536]{2,1,0:T(8,128)S(1)} %get-tuple-element.42, f32[2,128,1536]{2,1,0:T(8,128)S(1)} %get-tuple-element.43, ...), kind=kOutput, calls=%fused_computation.30 | convolution fusion | flops 611483648 | bytes 15865856 | tf_op jit(solution)/shard_map/if,sfd->sid/dot_general | solution.py:178
  237.5 2.3 copy.30
  (62 shorter events, 1.7 us)
Async XLA Ops:
  6.5 74.5 %copy-start = (bf16[1536,1152]{1,0:T(8,128)(2,1)S(1)}, bf16[1536,1152]{1,0:T(8,128)(2,1)}, u32[]{:S(2)}) copy-start(bf16[1536,1152]{1,0:T(8,128)(2,1)} %param.11) | copy-start | bytes 10616836
  6.5 74.5 %all-gather.5.cloned.1.call-start = ((), (), s32[]{:S(2)}) async-start(), calls=%async_computation.1 | async-start | bytes 3932160 | tf_op jit(solution)/shard_map/all_gather | solution.py:133
  38.5 0.9 copy-start.6
  45.3 8.9 %copy-start.13 = (f32[128,1536,1]{1,0,2:T(8,128)S(1)}, f32[128,1536,1]{1,0,2:T(8,128)}, u32[]{:S(2)}) copy-start(f32[128,1536,1]{1,0,2:T(8,128)} %reshape.231) | copy-start | bytes 2359300
  45.3 7.5 %copy-start.21 = (pred[128]{0:T(512)(128)(4,1)}, pred[128]{0:T(512)(128)(4,1)S(1)}, u32[]{:S(2)}) copy-start(pred[128]{0:T(512)(128)(4,1)S(1)} %iota_compare_fusion) | copy-start | bytes 388
  52.8 0.7 copy-start.14
  52.8 0.7 copy-start.16
  88.6 4.0 %copy-start.23 = (s32[2,1]{0,1:T(1,128)S(1)}, s32[2,1]{0,1:T(1,128)}, u32[]{:S(2)}) copy-start(s32[2,1]{0,1:T(1,128)} %param.19) | copy-start | bytes 28
  88.6 58.1 %all-to-all-start = ((bf16[8,128,1152]{2,1,0:T(8,128)(2,1)}), bf16[8,128,1152]{2,1,0:T(8,128)(2,1)S(1)}, u32[]{:S(2)}, u32[]{:S(2)}) async-start(bf16[8,128,1152]{2,1,0:T(8,128)(2,1)} %bitcast.99), calls=%async_computation | async-start | bytes 4718592 | tf_op jit(solution)/shard_map/all_to_all | solution.py:148
  92.4 113.4 %all-gather.7.cloned.1.call-start = ((), (), s32[]{:S(2)}) async-start(), calls=%async_computation.2 | async-start | bytes 3932160 | tf_op jit(solution)/shard_map/all_gather | solution.py:162
  146.6 1.5 copy-start.4
  154.2 6.9 %copy-start.20 = (f32[3,4608]{1,0:T(4,128)S(1)}, f32[3,4608]{1,0:T(4,128)}, u32[]{:S(2)}) copy-start(f32[3,4608]{1,0:T(4,128)} %param.12) | copy-start | bytes 165892
  156.3 4.9 %collective-permute-start = (bf16[2,1,4608]{2,0,1:T(2,128)(2,1)S(1)}, bf16[2,1,4608]{2,0,1:T(2,128)(2,1)S(1)}, u32[]{:S(2)}, u32[]{:S(2)}) collective-permute-start(bf16[2,1,4608]{2,0,1:T(2,128)(2,1)S(1)} %copy.21), channel_id=1, source_target_pairs={{0,4},{4,8},{8,12},{1,5},{5,9},{9,13},{2,6},{6,10},{10,14},{3,7},{... | collective-permute-start | bytes 55304 | tf_op jit(solution)/shard_map/ppermute | solution.py:15
  159.7 4.8 %collective-permute-start.1 = (bf16[2,1,4608]{2,0,1:T(2,128)(2,1)S(1)}, bf16[2,1,4608]{2,0,1:T(2,128)(2,1)S(1)}, u32[]{:S(2)}, u32[]{:S(2)}) collective-permute-start(bf16[2,1,4608]{2,0,1:T(2,128)(2,1)S(1)} %copy.23), channel_id=1, source_target_pairs={{4,0},{8,4},{12,8},{5,1},{9,5},{13,9},{6,2},{10,6},{14,10},{7,3},{... | collective-permute-start | bytes 55304 | tf_op jit(solution)/shard_map/ppermute | solution.py:17
  172.8 2.1 copy-start.2
  174.9 1.1 copy-start.22
  182.5 26.5 %copy-start.15 = (f32[128,256]{1,0:T(8,128)S(1)}, f32[128,256]{1,0:T(8,128)}, u32[]{:S(2)}) copy-start(f32[128,256]{1,0:T(8,128)} %copy-done.14) | copy-start | bytes 393220
  182.5 26.5 %copy-start.17 = (f32[128,256]{1,0:T(8,128)S(1)}, f32[128,256]{1,0:T(8,128)}, u32[]{:S(2)}) copy-start(f32[128,256]{1,0:T(8,128)} %copy-done.16) | copy-start | bytes 393220
  225.6 3.3 %copy-start.3 = (f32[2,256,1536]{2,1,0:T(8,128)S(1)}, f32[2,256,1536]{2,1,0:T(8,128)}, u32[]{:S(2)}) copy-start(f32[2,256,1536]{2,1,0:T(8,128)} %get-tuple-element.17) | copy-start | bytes 9437188
  225.6 3.5 %copy-start.7 = (f32[128,1536]{1,0:T(8,128)S(1)}, f32[128,1536]{1,0:T(8,128)}, u32[]{:S(2)}) copy-start(f32[128,1536]{1,0:T(8,128)} %get-tuple-element.18) | copy-start | bytes 2359300
  225.6 3.7 %copy-start.8 = (f32[128,1536]{1,0:T(8,128)S(1)}, f32[128,1536]{1,0:T(8,128)}, u32[]{:S(2)}) copy-start(f32[128,1536]{1,0:T(8,128)} %get-tuple-element.19) | copy-start | bytes 2359300
  225.6 4.0 %copy-start.9 = (f32[128,1536]{1,0:T(8,128)S(1)}, f32[128,1536]{1,0:T(8,128)}, u32[]{:S(2)}) copy-start(f32[128,1536]{1,0:T(8,128)} %get-tuple-element.20) | copy-start | bytes 2359300
  225.6 4.2 %copy-start.10 = (f32[128,1536]{1,0:T(8,128)S(1)}, f32[128,1536]{1,0:T(8,128)}, u32[]{:S(2)}) copy-start(f32[128,1536]{1,0:T(8,128)} %get-tuple-element.21) | copy-start | bytes 2359300
  225.6 4.4 %copy-start.11 = (f32[128,1536]{1,0:T(8,128)S(1)}, f32[128,1536]{1,0:T(8,128)}, u32[]{:S(2)}) copy-start(f32[128,1536]{1,0:T(8,128)} %get-tuple-element.22) | copy-start | bytes 2359300
  225.6 4.6 %copy-start.12 = (f32[128,1536]{1,0:T(8,128)S(1)}, f32[128,1536]{1,0:T(8,128)}, u32[]{:S(2)}) copy-start(f32[128,1536]{1,0:T(8,128)} %get-tuple-element.23) | copy-start | bytes 2359300
  230.3 1.9 copy-start.5
  230.3 1.9 copy-start.18
  230.3 1.9 copy-start.19
  232.2 7.6 %copy-start.1 = (bf16[1536,1152]{1,0:T(8,128)(2,1)S(1)}, bf16[1536,1152]{1,0:T(8,128)(2,1)}, u32[]{:S(2)}) copy-start(bf16[1536,1152]{1,0:T(8,128)(2,1)} %param.11) | copy-start | bytes 10616836
Sparse Core Ops, SparseCore 0:
  8.9 72.0 all-gather.4
  176.1 29.6 all-gather.6

commit v4 on v3

--- a/solution.py
+++ b/solution.py
@@ -121,7 +121,7 @@
         return jnp.einsum("bgk,kd->bgd", paired_spec, stacked_out, precision=lax.Precision.HIGH)
 
     def chunk_apply(response, rows):
-        blocks = rows.reshape(seq_dev, chunk, block_len, width)
+        blocks = rows.reshape(rows.shape[0], chunk, block_len, width)
         signal = jnp.einsum(
             "fc,sbcd->sbfd", half_hi, blocks, preferred_element_type=jnp.float32
         ) + jnp.einsum("fc,sbcd->sbfd", half_lo, blocks, preferred_element_type=jnp.float32)
@@ -130,53 +130,62 @@
             total = total + packed_product(response[None, index], signal[:, index], block_len)
         return total
 
-    group_tokens = lax.all_gather(tokens, "fsdp", axis=0, tiled=True)
     single = chunk == block_total
     if single:
         early_response = chunk_response(0)
-        group_tokens, early_response, full_skip = lax.optimization_barrier(
-            (group_tokens, early_response, full_skip)
-        )
-    group_rows = group_tokens.shape[0]
     local_cols = in_weight.shape[1]
-    partial = jnp.dot(
-        group_tokens.reshape(group_rows * block_len, width),
-        in_weight,
-        preferred_element_type=jnp.float32,
-    ).astype(jnp.bfloat16)
-    partial = partial.reshape(group_rows, block_len, local_cols)
-    projected = lax.all_to_all(partial, "fsdp", 0, 2, tiled=True)
-    padded = padded_2(projected, (("seq", 1),), 1)
-    shorted = (
-        short_weight[0] * padded[:, :-2]
-        + short_weight[1] * padded[:, 1:-1]
-        + short_weight[2] * padded[:, 2:]
-    )
-    query_gate = shorted[:, :, :width]
-    key_part = shorted[:, :, width : 2 * width]
-    value_part = shorted[:, :, 2 * width :]
-    valid_mask = (jnp.arange(block_len, dtype=jnp.int32)[None, :] < block_counts).astype(
-        jnp.float32
-    )
-    carried = (key_part * value_part * valid_mask[:, :, None]).astype(jnp.bfloat16)
-    piece = lax.all_gather(carried, "seq", axis=1, tiled=True)
-
-    if single:
-        spectrum = chunk_apply(early_response, piece)
-    else:
-
-        def one_chunk(chunk_index, carry):
-            rows = lax.dynamic_slice_in_dim(piece, chunk_index * chunk * block_len, chunk * block_len, 1)
-            return carry + chunk_apply(chunk_response(chunk_index * chunk), rows)
-
-        spectrum = lax.fori_loop(
-            0,
-            block_total // chunk,
-            one_chunk,
-            jnp.zeros((seq_dev, 2 * block_len, width), jnp.float32),
-        )
-    conv = jnp.einsum("if,sfd->sid", inverse, spectrum, precision=lax.Precision.HIGH)
-    return (query_gate * (conv + full_skip * carried.astype(jnp.float32))).astype(jnp.bfloat16)
+    outputs = []
+    for table in range(seq_dev):
+        table_tokens = lax.all_gather(tokens[table : table + 1], "fsdp", axis=0, tiled=True)
+        if single and table == 0:
+            table_tokens, early_response, full_skip = lax.optimization_barrier(
+                (table_tokens, early_response, full_skip)
+            )
+        group_rows = table_tokens.shape[0]
+        partial = jnp.dot(
+            table_tokens.reshape(group_rows * block_len, width),
+            in_weight,
+            preferred_element_type=jnp.float32,
+        ).astype(jnp.bfloat16)
+        partial = partial.reshape(group_rows, block_len, local_cols)
+        projected = lax.all_to_all(partial, "fsdp", 0, 2, tiled=True)
+        padded = padded_2(projected, (("seq", 1),), 1)
+        shorted = (
+            short_weight[0] * padded[:, :-2]
+            + short_weight[1] * padded[:, 1:-1]
+            + short_weight[2] * padded[:, 2:]
+        )
+        query_gate = shorted[:, :, :width]
+        key_part = shorted[:, :, width : 2 * width]
+        value_part = shorted[:, :, 2 * width :]
+        valid_mask = (
+            jnp.arange(block_len, dtype=jnp.int32)[None, :] < block_counts[table : table + 1]
+        ).astype(jnp.float32)
+        carried = (key_part * value_part * valid_mask[:, :, None]).astype(jnp.bfloat16)
+        piece = lax.all_gather(carried, "seq", axis=1, tiled=True)
+        rows_dev = carried.shape[0]
+
+        if single:
+            spectrum = chunk_apply(early_response, piece)
+        else:
+
+            def one_chunk(chunk_index, carry):
+                rows = lax.dynamic_slice_in_dim(
+                    piece, chunk_index * chunk * block_len, chunk * block_len, 1
+                )
+                return carry + chunk_apply(chunk_response(chunk_index * chunk), rows)
+
+            spectrum = lax.fori_loop(
+                0,
+                block_total // chunk,
+                one_chunk,
+                jnp.zeros((rows_dev, 2 * block_len, width), jnp.float32),
+            )
+        conv = jnp.einsum("if,sfd->sid", inverse, spectrum, precision=lax.Precision.HIGH)
+        outputs.append(
+            (query_gate * (conv + full_skip * carried.astype(jnp.float32))).astype(jnp.bfloat16)
+        )
+    return jnp.concatenate(outputs, axis=0)
 
 
 def solution(mesh):

time: 248 us -> 254 us (1.024)
  starting transfers between devices: 6.58 us -> 16 us
  waiting for transfers between devices: 102 us -> 95.5 us
  other arithmetic: 16.5 us -> 20.8 us
  local copies, waits for them, and re-layouts: 47.8 us -> 44.4 us
  blocking collectives: 28.7 us -> 32 us
    all_to_all x1 -> x2, waiting for transfers between devices: 54 us -> 17 us  [shards(): projected = lax.all_to_all(partial, 'fsdp', 0, 2, tiled=True)]
    all_gather x1 -> x2, waiting for transfers between devices: 22.3 us -> 43.5 us  [shards(): lax.all_gather(tokens[table:table + 1], 'fsdp', axis=0, tiled=True)]
    all_gather x1 -> x2, waiting for transfers between devices: 23.3 us -> 34.2 us  [shards(): piece = lax.all_gather(carried, 'seq', axis=1, tiled=True)]
    squeeze x1 -> x2, local copies, waits for them, and re-layouts: 8.55 us -> 2.73 us  [chunk_apply(): signal[:, index]]
    mul x1 -> x0, local copies, waits for them, and re-layouts: 5.53 us -> none  [packed_product(): prod_real = resp_real * sig_real - jnp.where(first_slot, 0.0, cross_term)]
    all_to_all x1 -> x2, starting transfers between devices: 3.82 us -> 9.34 us  [shards(): projected = lax.all_to_all(partial, 'fsdp', 0, 2, tiled=True)]
    sub x2 -> x0, other arithmetic: 5.04 us -> none  [packed_product(): prod_real = resp_real * sig_real - jnp.where(first_slot, 0.0, cross_term)]
    dot_general x1 -> x2, matrix products: 6.3 us -> 1.97 us  [chunk_apply(): jnp.einsum('fc,sbcd->sbfd', half_lo, blocks, preferred_element_type=jnp.f...]
  transfers between devices with their start and end apart: 5 -> 10, of which waited for: 4 -> 4; matrix products, arithmetic and copies ran while one was open for 13% -> 24% of each run, Pallas kernels for 0% -> 0%
where the time goes in v4:
time: 254 us; the launch traced here: 253 us
  waiting for transfers between devices  95.5 us (38%)
  local copies, waits for them, and re-layouts  44.4 us (17%)
  blocking collectives  32 us (13%)
  matrix products  30.4 us (12%)
  other arithmetic  20.8 us (8%)
  starting transfers between devices  16 us (6%)
  between operations  13.5 us (5%)
    all_gather x2, waiting for transfers between devices, shards(): lax.all_gather(tokens[table:table + 1], 'fsdp', axis=0, tiled=True)  43.5 us
    all_gather x2, waiting for transfers between devices, shards(): piece = lax.all_gather(carried, 'seq', axis=1, tiled=True)  34.2 us
    all_gather x1, blocking collectives, shards(): gathered = lax.all_gather(params, 'fsdp', axis=0, tiled=False)  32 us
    all_to_all x2, waiting for transfers between devices, shards(): projected = lax.all_to_all(partial, 'fsdp', 0, 2, tiled=True)  17 us
    all_to_all x2, starting transfers between devices, shards(): projected = lax.all_to_all(partial, 'fsdp', 0, 2, tiled=True)  9.34 us
    dot_general x2, matrix products, shards(): jnp.dot(table_tokens.reshape(group_rows * block_len, width), in_weight, p...  9.29 us
    slice x4, local copies, waits for them, and re-layouts, padded_2(): lax.slice_in_dim(cells, cells.shape[dim] - width, cells.shape[dim], axis=...  7.55 us
    add x1, other arithmetic, shards(): short_weight[0] * padded[:, :-2] + short_weight[1] * padded[:, 1:-1]  7.37 us
  transfers between devices with their start and end apart: 10, of which 4 were waited for; matrix products, arithmetic and copies ran while one was open for 24% of the time, Pallas kernels for 0%

profile of v4, /device:TPU:0, one launch (start us, length us, event | category | flops | bytes accessed | tf_op | source)
XLA Modules:
  0.0 252.6 jit_solution(14721569818488681049)
XLA Ops:
  6.5 2.2 fusion.97
  11.5 0.9 maximum_bitcast_fusion
  12.4 32.0 %all-gather.1 = f32[4,129,384]{2,1,0:T(8,128)S(1)} all-gather(f32[1,129,384]{2,1,0:T(8,128)S(1)} %maximum_bitcast_fusion), channel_id=2, replica_groups=mesh['groups'=2,'seq'=4,'fsdp'=4] {'fsdp'}, dimensions={0}, use_global_device_ids=true | all-gather | bytes 990720 | tf_op jit(solution)/shard_map/all_gather | solution.py:91
  46.8 1.4 copy.18
  48.2 2.3 reshape.436
  51.3 1.2 fusion.78
  52.5 3.5 %fusion.34 = f32[1024,64]{1,0:T(8,128)S(1)} fusion(f32[17,64]{1,0:T(8,128)} %param.13, f32[64]{0:T(128)} %param.14, f32[1024,8]{0,1:T(8,128)S(1)} %get-tuple-element.57, f32[1024,8]{0,1:T(8,128)S(1)} %get-tuple-element.56, f32[1024,1]{0,1:T(1,128)} %bitcast.157), kind=kOutput, calls=%fused_computation.52 | convolution fusion | flops 13469696 | bytes 336384 | tf_op jit(solution)/shard_map/dot_general | solution.py:36
  56.0 2.3 broadcast_multiply_fusion.1
  60.3 4.6 %fusion.99 = f32[4,256,1536]{2,1,0:T(8,128)} fusion(f32[4,256,128]{2,1,0:T(8,128)S(1)} %convolution_bitcast_fusion.2, f32[128,1536,1]{1,0,2:T(8,128)S(1)} %copy-done.9), kind=kOutput, calls=%fused_computation.191 | convolution fusion | flops 1207959552 | bytes 7602176 | tf_op jit(solution)/shard_map/bgk,kd->bgd/dot_general | solution.py:121
  64.9 4.7 %convolution_convert_fusion.1 = bf16[512,1152]{1,0:T(8,128)(2,1)} fusion(bf16[512,1536]{1,0:T(8,128)(2,1)} %bitcast.159, bf16[1536,1152]{1,0:T(8,128)(2,1)S(1)} %copy-done), kind=kOutput, calls=%fused_computation.3 | convolution fusion | flops 1812529152 | bytes 6291456 | tf_op jit(solution)/shard_map/dot_general | solution.py:145
  69.6 5.7 %all-to-all-start = ((bf16[4,128,1152]{2,1,0:T(8,128)(2,1)}), bf16[4,128,1152]{2,1,0:T(8,128)(2,1)}, u32[]{:S(2)}, u32[]{:S(2)}) async-start(bf16[4,128,1152]{2,1,0:T(8,128)(2,1)} %bitcast.152), calls=%async_computation | async-start | bytes 2359296 | tf_op jit(solution)/shard_map/all_to_all | solution.py:151
  75.2 43.5 %all-gather.11.cloned.1.call-done = bf16[4,128,1536]{2,1,0:T(8,128)(2,1)} async-done(((bf16[1,128,1536]{2,1,0:T(8,128)(2,1)}), bf16[4,128,1536]{2,1,0:T(8,128)(2,1)}) %all-gather.11.cloned.1.call-update) | async-done | bytes 1572880 | tf_op jit(solution)/shard_map/all_gather | solution.py:139
  118.7 4.6 %convolution_convert_fusion = bf16[512,1152]{1,0:T(8,128)(2,1)} fusion(bf16[512,1536]{1,0:T(8,128)(2,1)} %bitcast.160, bf16[1536,1152]{1,0:T(8,128)(2,1)S(1)} %copy-done), kind=kOutput, calls=%fused_computation.2 | convolution fusion | flops 1812529152 | bytes 6291456 | tf_op jit(solution)/shard_map/dot_general | solution.py:145
  123.4 2.4 copy.25
  125.7 3.7 %all-to-all-start.1 = ((bf16[4,128,1152]{1,2,0:T(8,128)(2,1)}), bf16[4,128,1152]{1,2,0:T(8,128)(2,1)S(1)}, u32[]{:S(2)}, u32[]{:S(2)}) async-start(bf16[4,128,1152]{1,2,0:T(8,128)(2,1)} %copy.25), calls=%async_computation.1 | async-start | bytes 2359296 | tf_op jit(solution)/shard_map/all_to_all | solution.py:151
  131.0 1.7 copy.19
  132.7 1.5 fusion.95
  134.3 2.3 copy.20
  136.5 1.9 collective-permute-start
  138.4 1.0 copy.22
  139.5 1.3 collective-permute-start.1
  140.7 17.0 %all-to-all-done.1 = bf16[4,128,1152]{1,2,0:T(8,128)(2,1)S(1)} async-done(((bf16[4,128,1152]{1,2,0:T(8,128)(2,1)}), bf16[4,128,1152]{1,2,0:T(8,128)(2,1)S(1)}, u32[]{:S(2)}, u32[]{:S(2)}) %all-to-all-start.1) | async-done | bytes 1179680 | tf_op jit(solution)/shard_map/all_to_all | solution.py:151
  157.7 1.4 fusion.96
  159.2 2.3 copy.26
  161.5 1.9 collective-permute-start.2
  163.4 1.0 copy.28
  164.4 1.3 collective-permute-start.3
  166.3 1.3 copy.21
  167.6 2.2 copy.23
  169.8 2.2 copy.27
  172.0 2.2 copy.29
  174.2 7.4 %multiply_add_fusion.1 = (f32[1,128,4608]{1,2,0:T(8,128)}, f32[1,128,4608]{1,2,0:T(8,128)S(1)}) fusion(bf16[1,128,4608]{1,2,0:T(8,128)(2,1)S(1)} %bitcast.144, bf16[1,1,4608]{1,2,0:T(8,128)(2,1)} %copy.23, bf16[1,1,4608]{1,2,0:T(8,128)(2,1)S(1)} %copy.21, f32[4608]{0:T(1024)} %get-tuple-element.12, f32[4608]{0:T(1024)} %get-tuple-element.13, ...), kind=kLoop, calls=%fused_computation.13 | loop fusion | flops 16515072 | bytes 7170048 | tf_op jit(solution)/shard_map/add | solution.py:154
  181.6 1.4 copy-done.2
  183.0 0.9 fusion.37
  185.6 0.9 select_multiply_fusion.1
  186.5 18.9 %all-gather.13.cloned.1.call-done = bf16[1,512,1536]{1,2,0:T(8,128)(2,1)} async-done(((bf16[1,128,1536]{1,2,0:T(8,128)(2,1)}), bf16[1,512,1536]{1,2,0:T(8,128)(2,1)}) %all-gather.13.cloned.1.call-update) | async-done | bytes 1572880 | tf_op jit(solution)/shard_map/all_gather | solution.py:165
  205.4 1.7 copy.34
  207.1 1.0 fusion.62
  208.1 1.0 add_bitcast_fusion
  209.1 2.3 slice_bitcast_fusion
  211.4 15.3 %all-gather.9.cloned.1.call-done = bf16[1,512,1536]{1,2,0:T(8,128)(2,1)} async-done(((bf16[1,128,1536]{1,2,0:T(8,128)(2,1)}), bf16[1,512,1536]{1,2,0:T(8,128)(2,1)}) %all-gather.9.cloned.1.call-update) | async-done | bytes 1572880 | tf_op jit(solution)/shard_map/all_gather | solution.py:165
  226.7 1.7 copy.24
  228.4 1.0 fusion.60
  229.4 1.0 add_bitcast_fusion.1
  236.6 3.0 %fusion.5 = bf16[1,128,1536]{1,2,0:T(8,128)(2,1)S(1)} fusion(f32[128,1536]{1,0:T(8,128)S(1)} %get-tuple-element.21, f32[128,1536]{1,0:T(8,128)S(1)} %get-tuple-element.20, f32[128,1536]{1,0:T(8,128)S(1)} %get-tuple-element.19, f32[128,1536]{1,0:T(8,128)S(1)} %get-tuple-element.18, f32[128,1536]{1,0:T(8,128)S(1)} %get-tuple-element.17, ...), kind=kOutput, calls=%fused_computation.11 | convolution fusion | flops 305758208 | bytes 8001536 | tf_op jit(solution)/shard_map/if,sfd->sid/dot_general | solution.py:184
  239.6 3.1 %fusion.4 = bf16[1,128,1536]{1,2,0:T(8,128)(2,1)S(1)} fusion(f32[128,1536]{1,0:T(8,128)S(1)} %get-tuple-element.30, f32[128,1536]{1,0:T(8,128)S(1)} %get-tuple-element.31, f32[128,1536]{1,0:T(8,128)S(1)} %get-tuple-element.32, f32[128,1536]{1,0:T(8,128)S(1)} %get-tuple-element.33, f32[128,1536]{1,0:T(8,128)S(1)} %get-tuple-element.34, ...), kind=kOutput, calls=%fused_computation.10 | convolution fusion | flops 305758208 | bytes 8001536 | tf_op jit(solution)/shard_map/if,sfd->sid/dot_general | solution.py:184
  242.8 1.0 pad_maximum_fusion.4
  243.7 2.3 copy.32
  (90 shorter events, 17.8 us)
Async XLA Ops:
  6.5 58.4 %copy-start = (bf16[1536,1152]{1,0:T(8,128)(2,1)S(1)}, bf16[1536,1152]{1,0:T(8,128)(2,1)}, u32[]{:S(2)}) copy-start(bf16[1536,1152]{1,0:T(8,128)(2,1)} %param.11) | copy-start | bytes 10616836
  6.5 4.9 %copy-start.17 = (f32[384]{0:T(512)S(1)}, f32[384]{0:T(512)}, u32[]{:S(2)}) copy-start(f32[384]{0:T(512)} %param.18) | copy-start | bytes 4612
  6.5 58.4 %all-gather.7.cloned.1.call-start = ((), (), s32[]{:S(2)}) async-start(), calls=%async_computation.2 | async-start | bytes 1966080 | tf_op jit(solution)/shard_map/all_gather | solution.py:139
  8.8 110.0 %all-gather.11.cloned.1.call-start = ((), (), s32[]{:S(2)}) async-start(), calls=%async_computation.4 | async-start | bytes 1966080 | tf_op jit(solution)/shard_map/all_gather | solution.py:139
  51.3 7.1 %copy-start.19 = (f32[256]{0:T(256)S(1)}, f32[256]{0:T(256)}, u32[]{:S(2)}) copy-start(f32[256]{0:T(256)} %fusion.85) | copy-start | bytes 3076
  58.3 2.0 copy-start.9
  58.9 0.7 copy-start.10
  58.9 0.7 copy-start.12
  69.6 56.2 %all-to-all-start = ((bf16[4,128,1152]{2,1,0:T(8,128)(2,1)}), bf16[4,128,1152]{2,1,0:T(8,128)(2,1)}, u32[]{:S(2)}, u32[]{:S(2)}) async-start(bf16[4,128,1152]{2,1,0:T(8,128)(2,1)} %bitcast.152), calls=%async_computation | async-start | bytes 2359296 | tf_op jit(solution)/shard_map/all_to_all | solution.py:151
  125.7 3.9 %copy-start.18 = (s32[2,1]{0,1:T(1,128)S(1)}, s32[2,1]{0,1:T(1,128)}, u32[]{:S(2)}) copy-start(s32[2,1]{0,1:T(1,128)} %param.19) | copy-start | bytes 28
  125.7 4.6 %copy-start.16 = (f32[3,4608]{1,0:T(4,128)S(1)}, f32[3,4608]{1,0:T(4,128)}, u32[]{:S(2)}) copy-start(f32[3,4608]{1,0:T(4,128)} %param.12) | copy-start | bytes 165892
  125.7 32.0 %all-to-all-start.1 = ((bf16[4,128,1152]{1,2,0:T(8,128)(2,1)}), bf16[4,128,1152]{1,2,0:T(8,128)(2,1)S(1)}, u32[]{:S(2)}, u32[]{:S(2)}) async-start(bf16[4,128,1152]{1,2,0:T(8,128)(2,1)} %copy.25), calls=%async_computation.1 | async-start | bytes 2359296 | tf_op jit(solution)/shard_map/all_to_all | solution.py:151
  129.4 76.0 %all-gather.13.cloned.1.call-start = ((), (), s32[]{:S(2)}) async-start(), calls=%async_computation.5 | async-start | bytes 1966080 | tf_op jit(solution)/shard_map/all_gather | solution.py:165
  136.5 29.8 %collective-permute-start = (bf16[1,1,4608]{2,1,0:T(2,128)(2,1)}, bf16[1,1,4608]{2,1,0:T(2,128)(2,1)}, u32[]{:S(2)}, u32[]{:S(2)}) collective-permute-start(bf16[1,1,4608]{2,1,0:T(2,128)(2,1)} %copy.20), channel_id=1, source_target_pairs={{0,4},{4,8},{8,12},{1,5},{5,9},{9,13},{2,6},{6,10},{10,14},{3,7},{... | collective-permute-start | bytes 27656 | tf_op jit(solution)/shard_map/ppermute | solution.py:15
  139.5 28.1 %collective-permute-start.1 = (bf16[1,1,4608]{2,1,0:T(2,128)(2,1)}, bf16[1,1,4608]{2,1,0:T(2,128)(2,1)}, u32[]{:S(2)}, u32[]{:S(2)}) collective-permute-start(bf16[1,1,4608]{2,1,0:T(2,128)(2,1)} %copy.22), channel_id=1, source_target_pairs={{4,0},{8,4},{12,8},{5,1},{9,5},{13,9},{6,2},{10,6},{14,10},{7,3},{... | collective-permute-start | bytes 27656 | tf_op jit(solution)/shard_map/ppermute | solution.py:17
  161.5 8.3 %collective-permute-start.2 = (bf16[1,1,4608]{2,1,0:T(2,128)(2,1)}, bf16[1,1,4608]{2,1,0:T(2,128)(2,1)}, u32[]{:S(2)}, u32[]{:S(2)}) collective-permute-start(bf16[1,1,4608]{2,1,0:T(2,128)(2,1)} %copy.26), channel_id=1, source_target_pairs={{0,4},{4,8},{8,12},{1,5},{5,9},{9,13},{2,6},{6,10},{10,14},{3,7},{... | collective-permute-start | bytes 27656 | tf_op jit(solution)/shard_map/ppermute | solution.py:15
  164.4 7.6 %collective-permute-start.3 = (bf16[1,1,4608]{2,1,0:T(2,128)(2,1)}, bf16[1,1,4608]{2,1,0:T(2,128)(2,1)}, u32[]{:S(2)}, u32[]{:S(2)}) collective-permute-start(bf16[1,1,4608]{2,1,0:T(2,128)(2,1)} %copy.28), channel_id=1, source_target_pairs={{4,0},{8,4},{12,8},{5,1},{9,5},{13,9},{6,2},{10,6},{14,10},{7,3},{... | collective-permute-start | bytes 27656 | tf_op jit(solution)/shard_map/ppermute | solution.py:17
  181.6 1.4 copy-start.2
  181.6 3.0 %copy-start.3 = (f32[1,128,4608]{1,2,0:T(8,128)S(1)}, f32[1,128,4608]{1,2,0:T(8,128)}, u32[]{:S(2)}) copy-start(f32[1,128,4608]{1,2,0:T(8,128)} %get-tuple-element.54) | copy-start | bytes 7077892
  183.9 1.7 copy-start.11
  183.9 1.7 copy-start.13
  183.9 42.8 %all-gather.9.cloned.1.call-start = ((), (), s32[]{:S(2)}) async-start(), calls=%async_computation.3 | async-start | bytes 1966080 | tf_op jit(solution)/shard_map/all_gather | solution.py:165
  228.4 2.4 slice-start
  229.4 2.1 slice-start.1
  230.4 1.6 copy-start.6
  231.9 1.4 copy-start.5
  233.3 1.4 copy-start.4
  235.6 1.0 copy-start.8
  235.6 1.0 copy-start.14
  235.6 1.0 copy-start.15
  236.6 3.0 %copy-start.7 = (bf16[1,128,1536]{1,2,0:T(8,128)(2,1)S(1)}, bf16[1,128,1536]{1,2,0:T(8,128)(2,1)}, u32[]{:S(2)}) copy-start(bf16[1,128,1536]{1,2,0:T(8,128)(2,1)} %fusion.37) | copy-start | bytes 1179652
  239.6 6.4 %copy-start.1 = (bf16[1536,1152]{1,0:T(8,128)(2,1)S(1)}, bf16[1536,1152]{1,0:T(8,128)(2,1)}, u32[]{:S(2)}) copy-start(bf16[1536,1152]{1,0:T(8,128)(2,1)} %param.11) | copy-start | bytes 10616836
Sparse Core Ops, SparseCore 0:
  8.9 49.1 all-gather.6
  59.7 58.9 all-gather.10
  184.0 21.3 all-gather.12
  206.8 19.8 all-gather.8

commit v5 on v2

--- a/solution.py
+++ b/solution.py
@@ -2,6 +2,8 @@
 import jax.numpy as jnp
 from jax import lax
 from jax.sharding import PartitionSpec as P
+from jax.experimental import pallas as pl
+from jax.experimental.pallas import tpu as pltpu
 
 
 def padded_2(cells, sides, width):
@@ -69,6 +71,78 @@
     prod_real = resp_real * sig_real - jnp.where(first_slot, 0.0, cross_term)
     prod_imag = jnp.where(first_slot, cross_term, resp_real * sig_imag + resp_imag * sig_real)
     return jnp.concatenate([prod_real, prod_imag], axis=-2)
+
+
+def split_bf16(values):
+    high = values.astype(jnp.bfloat16)
+    return high, (values - high.astype(jnp.float32)).astype(jnp.bfloat16)
+
+
+def conv_kernel(
+    piece_ref, resp_ref, query_ref, carried_ref, skip_ref,
+    fwd_hi_ref, fwd_lo_ref, inv_hi_ref, inv_lo_ref, out_ref,
+):
+    tables, rows, lanes = carried_ref.shape
+    block_total = resp_ref.shape[0]
+    first = lax.broadcasted_iota(jnp.int32, (rows, lanes), 0) == 0
+    fwd_hi = fwd_hi_ref[...]
+    fwd_lo = fwd_lo_ref[...]
+
+    def dot(a, b):
+        return jnp.dot(a, b, preferred_element_type=jnp.float32)
+
+    for table in range(tables):
+
+        def one_block(block, acc):
+            acc_real, acc_imag = acc
+            block_rows = piece_ref[table, pl.ds(pl.multiple_of(block * rows, rows), rows), :]
+            signal = dot(fwd_hi, block_rows) + dot(fwd_lo, block_rows)
+            response = resp_ref[block]
+            resp_real = response[:rows]
+            resp_imag = response[rows:]
+            sig_real = signal[:rows]
+            sig_imag = signal[rows:]
+            cross = resp_imag * sig_imag
+            acc_real = acc_real + (resp_real * sig_real - jnp.where(first, 0.0, cross))
+            acc_imag = acc_imag + jnp.where(first, cross, resp_real * sig_imag + resp_imag * sig_real)
+            return acc_real, acc_imag
+
+        zeros = jnp.zeros((rows, lanes), jnp.float32)
+        acc_real, acc_imag = lax.fori_loop(0, block_total, one_block, (zeros, zeros))
+        spectrum = jnp.concatenate([acc_real, acc_imag], axis=0)
+        spec_hi, spec_lo = split_bf16(spectrum)
+        inv_hi = inv_hi_ref[...]
+        conv = dot(inv_hi, spec_hi) + dot(inv_hi, spec_lo) + dot(inv_lo_ref[...], spec_hi)
+        gated = query_ref[table] * (conv + skip_ref[...] * carried_ref[table].astype(jnp.float32))
+        out_ref[table] = gated.astype(out_ref.dtype)
+
+
+def fused_conv(piece, response, query_gate, carried, skip, fwd_half, inverse):
+    tables, rows, width = carried.shape
+    block_total = response.shape[0]
+    lanes = 256 if width % 256 == 0 else width
+    fwd_hi, fwd_lo = split_bf16(fwd_half)
+    inv_hi, inv_lo = split_bf16(inverse)
+    tile3 = lambda i: (0, 0, i)
+    whole2 = lambda i: (0, 0)
+    return pl.pallas_call(
+        conv_kernel,
+        grid=(width // lanes,),
+        in_specs=[
+            pl.BlockSpec((tables, piece.shape[1], lanes), tile3),
+            pl.BlockSpec((block_total, 2 * rows, lanes), tile3),
+            pl.BlockSpec((tables, rows, lanes), tile3),
+            pl.BlockSpec((tables, rows, lanes), tile3),
+            pl.BlockSpec((1, lanes), lambda i: (0, i)),
+            pl.BlockSpec(fwd_hi.shape, whole2),
+            pl.BlockSpec(fwd_lo.shape, whole2),
+            pl.BlockSpec(inv_hi.shape, whole2),
+            pl.BlockSpec(inv_lo.shape, whole2),
+        ],
+        out_specs=pl.BlockSpec((tables, rows, lanes), tile3),
+        out_shape=jax.ShapeDtypeStruct((tables, rows, width), jnp.bfloat16),
+        compiler_params=pltpu.CompilerParams(vmem_limit_bytes=48 * 1024 * 1024),
+    )(piece, response, query_gate, carried, skip.reshape(1, width), fwd_hi, fwd_lo, inv_hi, inv_lo)
 
 
 def shards(
@@ -129,46 +203,15 @@
     piece = lax.all_gather(carried, "seq", axis=1, tiled=True)
     block_total = piece.shape[1] // block_len
 
-    chunk = min(block_total, 4)
-
-    def chunk_spectrum(first, rows):
-        offsets = (position - first - jnp.arange(chunk, dtype=jnp.int32)) * block_len
-        lag_values = (offsets[:, None] + wrapped[None, :]).reshape(-1)
-        basis_rows = filter_basis(
-            lag_values, total_len, basis_in, basis_bias, basis_mid, basis_shift
-        )
-        ahead_mask = (lag_values >= 0).astype(jnp.float32)[:, None]
-        paired = jnp.concatenate(
-            [basis_rows * ahead_mask, basis_rows * (1.0 - ahead_mask)], axis=1
-        )
-        paired = paired.reshape(chunk, 2 * block_len, paired.shape[-1])
-        paired_spec = jnp.einsum("gf,bfk->bgk", forward, paired, precision=lax.Precision.HIGHEST)
-        response = jnp.einsum("bgk,kd->bgd", paired_spec, stacked_out, precision=lax.Precision.HIGH)
-        blocks = rows.reshape(seq_dev, chunk, block_len, width)
-        signal = jnp.einsum(
-            "fc,sbcd->sbfd", half_hi, blocks, preferred_element_type=jnp.float32
-        ) + jnp.einsum("fc,sbcd->sbfd", half_lo, blocks, preferred_element_type=jnp.float32)
-        total = packed_product(response[None, 0], signal[:, 0], block_len)
-        for index in range(1, chunk):
-            total = total + packed_product(response[None, index], signal[:, index], block_len)
-        return total
-
-    if chunk == block_total:
-        spectrum = chunk_spectrum(0, piece)
-    else:
-
-        def one_chunk(chunk_index, carry):
-            rows = lax.dynamic_slice_in_dim(piece, chunk_index * chunk * block_len, chunk * block_len, 1)
-            return carry + chunk_spectrum(chunk_index * chunk, rows)
-
-        spectrum = lax.fori_loop(
-            0,
-            block_total // chunk,
-            one_chunk,
-            jnp.zeros((seq_dev, 2 * block_len, width), jnp.float32),
-        )
-    conv = jnp.einsum("if,sfd->sid", inverse, spectrum, precision=lax.Precision.HIGH)
-    return (query_gate * (conv + full_skip * carried.astype(jnp.float32))).astype(jnp.bfloat16)
+    offsets = (position - jnp.arange(block_total, dtype=jnp.int32)) * block_len
+    lag_values = (offsets[:, None] + wrapped[None, :]).reshape(-1)
+    basis_rows = filter_basis(lag_values, total_len, basis_in, basis_bias, basis_mid, basis_shift)
+    ahead_mask = (lag_values >= 0).astype(jnp.float32)[:, None]
+    paired = jnp.concatenate([basis_rows * ahead_mask, basis_rows * (1.0 - ahead_mask)], axis=1)
+    paired = paired.reshape(block_total, 2 * block_len, paired.shape[-1])
+    paired_spec = jnp.einsum("gf,bfk->bgk", forward, paired, precision=lax.Precision.HIGHEST)
+    response = jnp.einsum("bgk,kd->bgd", paired_spec, stacked_out, precision=lax.Precision.HIGH)
+    return fused_conv(piece, response, query_gate, carried, full_skip, forward_half, inverse)
 
 
 def solution(mesh):

time: 244 us -> 225 us (0.922)
  local copies, waits for them, and re-layouts: 37 us -> 16.4 us
  Pallas kernels: 0 us -> 16.6 us
  matrix products: 28.2 us -> 16.9 us
  other arithmetic: 14.8 us -> 8.98 us
  waiting for transfers between devices: 122 us -> 126 us
    pallas_call x0 -> x1, Pallas kernels: none -> 16.6 us  [fused_conv(): pl.pallas_call(conv_kernel, grid=(width // lanes,), in_specs=[pl.BlockSpe...]
    dot_general x5 -> x2, matrix products: 16.7 us -> 5.33 us  [the longest x1 4.71 us: shards(): jnp.einsum('bgk,kd->bgd', paired_spec, stacked_out, precision=lax.Precisi...]
    squeeze x1 -> x0, local copies, waits for them, and re-layouts: 8.56 us -> none  [chunk_spectrum(): signal[:, index]]
    sub x3 -> x1, other arithmetic: 5.05 us -> 0.01 us  [shards(): 1.0 - ahead_mask]
    slice x2 -> x1, local copies, waits for them, and re-layouts: 5.05 us -> 0.06 us  [padded_2(): lax.slice_in_dim(cells, cells.shape[dim] - width, cells.shape[dim], axis=...]
    slice x3, local copies, waits for them, and re-layouts: 0.88 us -> 5.83 us  [shards(): stacked_out = gathered[:-1]]
    add x1, other arithmetic: 6.29 us -> 1.93 us  [shards(): short_weight[0] * padded[:, :-2] + short_weight[1] * padded[:, 1:-1]]
    ppermute x2 -> x0, local copies, waits for them, and re-layouts: 3.94 us -> none  [the longest x1 1.98 us: padded_2(): lax.ppermute(tail, axis, [(i, (i + 1) % count) for i in range(ends)])]
  transfers between devices with their start and end apart: 5 -> 5, of which waited for: 2 -> 3; matrix products, arithmetic and copies ran while one was open for 7% -> 9% of each run, Pallas kernels for 0% -> 0%
where the time goes in v5:
time: 225 us; the launch traced here: 224 us
  waiting for transfers between devices  126 us (56%)
  blocking collectives  18.3 us (8%)
  matrix products  16.9 us (8%)
  Pallas kernels  16.6 us (7%)
  local copies, waits for them, and re-layouts  16.4 us (7%)
  between operations  13.6 us (6%)
  other arithmetic  8.98 us (4%)
  starting transfers between devices  7.25 us (3%)
    all_gather x1, waiting for transfers between devices, shards(): group_tokens = lax.all_gather(tokens, 'fsdp', axis=0, tiled=True)  67.9 us
    all_to_all x1, waiting for transfers between devices, shards(): projected = lax.all_to_all(partial, 'fsdp', 0, 2, tiled=True)  54 us
    all_gather x1, blocking collectives, shards(): gathered = lax.all_gather(params, 'fsdp', axis=0, tiled=False)  18.3 us
    pallas_call x1, Pallas kernels, fused_conv(): pl.pallas_call(conv_kernel, grid=(width // lanes,), in_specs=[pl.BlockSpe...  16.6 us
    unnamed x27, local copies, waits for them, and re-layouts  8.42 us
    dot_general x1, matrix products, shards(): jnp.dot(group_tokens.reshape(group_rows * block_len, width), in_weight, p...  7.56 us
    slice x3, local copies, waits for them, and re-layouts, shards(): stacked_out = gathered[:-1]  5.83 us
    dot_general x1, matrix products, shards(): jnp.einsum('bgk,kd->bgd', paired_spec, stacked_out, precision=lax.Precisi...  4.71 us
  transfers between devices with their start and end apart: 5, of which 3 were waited for; matrix products, arithmetic and copies ran while one was open for 9% of the time, Pallas kernels for 0%

profile of v5, /device:TPU:0, one launch (start us, length us, event | category | flops | bytes accessed | tf_op | source)
XLA Modules:
  0.0 224.0 jit_solution(2233752900119789724)
XLA Ops:
  6.5 0.0 all-gather.5.cloned.1.call-start
  6.5 0.7 all-gather.5.cloned.1.call-update
  7.3 67.9 %all-gather.5.cloned.1.call-done = bf16[8,128,1536]{2,1,0:T(8,128)(2,1)} async-done(((bf16[2,128,1536]{2,1,0:T(8,128)(2,1)}), bf16[8,128,1536]{2,1,0:T(8,128)(2,1)}) %all-gather.5.cloned.1.call-update) | async-done | bytes 3145744 | tf_op jit(solution)/shard_map/all_gather | solution.py:161
  75.2 0.0 copy-done
  75.2 7.6 %convolution_convert_fusion = bf16[1024,1152]{1,0:T(8,128)(2,1)} fusion(bf16[1024,1536]{1,0:T(8,128)(2,1)} %bitcast.52, bf16[1536,1152]{1,0:T(8,128)(2,1)S(1)} %copy-done), kind=kOutput, calls=%fused_computation.1 | convolution fusion | flops 3625058304 | bytes 9043968 | tf_op jit(solution)/shard_map/dot_general | solution.py:164
  82.7 4.6 %all-to-all-start = ((bf16[8,128,1152]{2,1,0:T(8,128)(2,1)}), bf16[8,128,1152]{2,1,0:T(8,128)(2,1)}, u32[]{:S(2)}, u32[]{:S(2)}) async-start(bf16[8,128,1152]{2,1,0:T(8,128)(2,1)} %bitcast.45), calls=%async_computation | async-start | bytes 4718592 | tf_op jit(solution)/shard_map/all_to_all | solution.py:170
  87.4 0.0 all-gather.7.cloned.1.call-start
  87.4 0.1 compare_convert_fusion
  87.5 54.0 %all-to-all-done = bf16[8,128,1152]{2,1,0:T(8,128)(2,1)} async-done(((bf16[8,128,1152]{2,1,0:T(8,128)(2,1)}), bf16[8,128,1152]{2,1,0:T(8,128)(2,1)}, u32[]{:S(2)}, u32[]{:S(2)}) %all-to-all-start) | async-done | bytes 2359328 | tf_op jit(solution)/shard_map/all_to_all | solution.py:170
  141.5 1.9 copy.20
  143.4 0.1 fusion.52
  143.5 1.3 collective-permute-start
  144.8 1.3 collective-permute-start.1
  146.1 0.1 slice_reduce_fusion.2
  146.2 0.0 collective-permute-done
  146.3 3.3 %collective-permute-done.1 = bf16[2,1,4608]{2,1,0:T(2,128)(2,1)S(1)} collective-permute-done((bf16[2,1,4608]{2,1,0:T(2,128)(2,1)S(1)}, bf16[2,1,4608]{2,1,0:T(2,128)(2,1)S(1)}, u32[]{:S(2)}, u32[]{:S(2)}) %collective-permute-start.1) | collective-permute-done | bytes 18464 | tf_op jit(solution)/shard_map/ppermute | solution.py:19
  149.6 1.9 multiply_add_fusion
  151.5 0.0 copy-start.10
  151.5 1.7 fusion.51
  153.3 0.0 all-gather.7.cloned.1.call-update
  153.3 0.9 maximum_bitcast_fusion
  154.3 18.3 %all-gather.1 = f32[4,129,384]{2,1,0:T(8,128)S(1)} all-gather(f32[1,129,384]{2,1,0:T(8,128)S(1)} %maximum_bitcast_fusion), channel_id=2, replica_groups=mesh['groups'=2,'seq'=4,'fsdp'=4] {'fsdp'}, dimensions={0}, use_global_device_ids=true | all-gather | bytes 990720 | tf_op jit(solution)/shard_map/all_gather | solution.py:188
  172.6 0.9 slice.66
  173.5 0.1 convert_bitcast_fusion
  173.6 0.1 fusion.36
  173.7 0.6 copy.22
  174.3 0.1 fusion.39
  174.4 2.5 %copy.16 = f32[128,4,384]{2,1,0:T(4,128)} copy(f32[128,4,384]{2,0,1:T(8,128)} %slice.66) | data formatting | bytes 1572864 | tf_op jit(solution)/shard_map/slice | solution.py:190
  176.9 2.3 %reshape.225 = f32[128,1536,1]{1,0,2:T(8,128)} reshape(f32[128,4,384]{2,1,0:T(4,128)} %copy.16) | data formatting | bytes 1572864 | tf_op jit(solution)/shard_map/slice | solution.py:190
  179.3 0.3 select_multiply_fusion.1
  179.6 0.6 subtract_convert_fusion.inv_lo_ref
  180.2 0.6 fusion.15.inv_hi_ref
  180.9 0.5 negate_select_fusion.2
  181.4 0.7 subtract_convert_fusion.1
  182.1 1.2 fusion.34
  183.3 2.0 fusion.3
  185.3 2.0 broadcast_multiply_fusion.1
  187.4 0.6 convolution_bitcast_fusion
  188.0 0.0 copy-done.8
  188.0 4.7 %fusion.53.resp_ref = f32[4,256,1536]{2,1,0:T(8,128)} fusion(f32[4,256,128]{1,2,0:T(8,128)S(1)} %convolution_bitcast_fusion, f32[128,1536,1]{1,0,2:T(8,128)S(1)} %copy-done.8), kind=kOutput, calls=%fused_computation.103 | convolution fusion | flops 1207959552 | bytes 7602176 | tf_op jit(solution)/shard_map/bgk,kd->bgd/dot_general | solution.py:213
  192.7 1.1 copy-done.1
  193.9 1.4 copy-done.2
  195.3 1.9 copy-done.3
  197.2 0.8 copy-done.4
  198.0 0.8 copy-done.5
  198.9 0.8 copy-done.6
  199.7 0.8 copy-done.7
  200.5 16.6 %shard_map.103 = bf16[2,128,1536]{2,1,0:T(8,128)(2,1)} custom-call(bf16[2,512,1536]{2,1,0:T(8,128)(2,1)S(1)} %copy-done.3, f32[4,256,1536]{2,1,0:T(8,128)} %fusion.53.resp_ref, f32[2,128,1536]{2,1,0:T(8,128)S(1)} %copy-done.2, bf16[2,128,1536]{2,1,0:T(8,128)(2,1)S(1)} %copy-done.1, f32[1,1536]{1,0:T(1,128)S(1)} %bitcast.40, bf16[256,128]{1,0:T(8,128)(2,1)S(1)} %copy-done.7, ...), custom_call_target="tpu_custom_call" | custom-call | tf_op jit(solution)/shard_map/pallas_call | solution.py:128
  (28 shorter events, 0.2 us)
Async XLA Ops:
  6.5 68.6 %copy-start = (bf16[1536,1152]{1,0:T(8,128)(2,1)S(1)}, bf16[1536,1152]{1,0:T(8,128)(2,1)}, u32[]{:S(2)}) copy-start(bf16[1536,1152]{1,0:T(8,128)(2,1)} %param.11) | copy-start | bytes 10616836
  6.5 68.6 %all-gather.5.cloned.1.call-start = ((), (), s32[]{:S(2)}) async-start(), calls=%async_computation.1 | async-start | bytes 3932160 | tf_op jit(solution)/shard_map/all_gather | solution.py:161
  82.7 4.7 %copy-start.11 = (s32[2,1]{0,1:T(1,128)S(1)}, s32[2,1]{0,1:T(1,128)}, u32[]{:S(2)}) copy-start(s32[2,1]{0,1:T(1,128)} %param.19) | copy-start | bytes 28
  82.7 58.7 %all-to-all-start = ((bf16[8,128,1152]{2,1,0:T(8,128)(2,1)}), bf16[8,128,1152]{2,1,0:T(8,128)(2,1)}, u32[]{:S(2)}, u32[]{:S(2)}) async-start(bf16[8,128,1152]{2,1,0:T(8,128)(2,1)} %bitcast.45), calls=%async_computation | async-start | bytes 4718592 | tf_op jit(solution)/shard_map/all_to_all | solution.py:170
  87.4 105.4 %all-gather.7.cloned.1.call-start = ((), (), s32[]{:S(2)}) async-start(), calls=%async_computation.2 | async-start | bytes 3932160 | tf_op jit(solution)/shard_map/all_gather | solution.py:203
  141.5 4.6 %copy-start.9 = (f32[3,4608]{1,0:T(4,128)S(1)}, f32[3,4608]{1,0:T(4,128)}, u32[]{:S(2)}) copy-start(f32[3,4608]{1,0:T(4,128)} %param.12) | copy-start | bytes 165892
  143.5 2.8 %collective-permute-start = (bf16[2,1,4608]{2,1,0:T(2,128)(2,1)S(1)}, bf16[2,1,4608]{2,1,0:T(2,128)(2,1)S(1)}, u32[]{:S(2)}, u32[]{:S(2)}) collective-permute-start(bf16[2,1,4608]{2,1,0:T(2,128)(2,1)S(1)} %get-tuple-element.12), channel_id=1, source_target_pairs={{0,4},{4,8},{8,12},{1,5},{5,9},{9,13},{2,6},{6,10},{10,14},{3,7},{... | collective-permute-start | bytes 55304 | tf_op jit(solution)/shard_map/ppermute | solution.py:17
  144.8 4.8 %collective-permute-start.1 = (bf16[2,1,4608]{2,1,0:T(2,128)(2,1)S(1)}, bf16[2,1,4608]{2,1,0:T(2,128)(2,1)S(1)}, u32[]{:S(2)}, u32[]{:S(2)}) collective-permute-start(bf16[2,1,4608]{2,1,0:T(2,128)(2,1)S(1)} %get-tuple-element.13), channel_id=1, source_target_pairs={{4,0},{8,4},{12,8},{5,1},{9,5},{13,9},{6,2},{10,6},{14,10},{7,3},{... | collective-permute-start | bytes 55304 | tf_op jit(solution)/shard_map/ppermute | solution.py:19
  151.5 1.8 copy-start.10
  179.2 8.8 %copy-start.8 = (f32[128,1536,1]{1,0,2:T(8,128)S(1)}, f32[128,1536,1]{1,0,2:T(8,128)}, u32[]{:S(2)}) copy-start(f32[128,1536,1]{1,0,2:T(8,128)} %reshape.225) | copy-start | bytes 2359300
  192.7 1.1 copy-start.1
  193.9 1.4 copy-start.2
  195.3 1.9 copy-start.3
  197.2 0.8 copy-start.4
  198.0 0.8 copy-start.5
  198.9 0.8 copy-start.6
  199.7 0.8 copy-start.7
Sparse Core Ops, SparseCore 0:
  8.9 66.1 all-gather.4
  153.4 28.9 all-gather.6

commit v6 on v5

--- a/solution.py
+++ b/solution.py
@@ -23,6 +23,20 @@
     return cells
 
 
+def gather_by_permutes(values, axis):
+    count = lax.axis_size(axis)
+    own = lax.axis_index(axis)
+    received = [values]
+    for shift in range(1, count):
+        received.append(
+            lax.ppermute(values, axis, [(i, (i + shift) % count) for i in range(count)])
+        )
+    stacked = jnp.stack(received)
+    sources = (own - jnp.arange(count, dtype=jnp.int32)) % count
+    order = jnp.argsort(sources)
+    return jnp.take(stacked, order, axis=0)
+
+
 def filter_basis(lag_values, total_len, basis_in, basis_bias, basis_mid, basis_shift):
     band_count = (basis_in.shape[0] - 1) // 2
     distance = jnp.abs(lag_values)
@@ -79,11 +93,23 @@
 
 
 def conv_kernel(
-    piece_ref, resp_ref, query_ref, carried_ref, skip_ref,
-    fwd_hi_ref, fwd_lo_ref, inv_hi_ref, inv_lo_ref, out_ref,
+    piece_ref, basis_hi_ref, basis_lo_ref, out_cols_ref, query_ref, carried_ref, skip_ref,
+    fwd_hi_ref, fwd_lo_ref, inv_hi_ref, inv_lo_ref, out_ref, resp_ref,
 ):
     tables, rows, lanes = carried_ref.shape
     block_total = resp_ref.shape[0]
+    cols_hi, cols_lo = split_bf16(out_cols_ref[...])
+
+    def fill(block, carry):
+        basis_hi = basis_hi_ref[block]
+        resp_ref[block] = (
+            jnp.dot(basis_hi, cols_hi, preferred_element_type=jnp.float32)
+            + jnp.dot(basis_hi, cols_lo, preferred_element_type=jnp.float32)
+            + jnp.dot(basis_lo_ref[block], cols_hi, preferred_element_type=jnp.float32)
+        )
+        return carry
+
+    lax.fori_loop(0, block_total, fill, 0)
     first = lax.broadcasted_iota(jnp.int32, (rows, lanes), 0) == 0
     fwd_hi = fwd_hi_ref[...]
     fwd_lo = fwd_lo_ref[...]
@@ -117,9 +143,10 @@
         out_ref[table] = gated.astype(out_ref.dtype)
 
 
-def fused_conv(piece, response, query_gate, carried, skip, fwd_half, inverse):
+def fused_conv(piece, basis_spec, out_cols, query_gate, carried, skip, fwd_half, inverse):
     tables, rows, width = carried.shape
-    block_total = response.shape[0]
+    block_total = basis_spec.shape[0]
+    basis_hi, basis_lo = split_bf16(basis_spec)
     lanes = 256 if width % 256 == 0 else width
     fwd_hi, fwd_lo = split_bf16(fwd_half)
     inv_hi, inv_lo = split_bf16(inverse)
@@ -130,7 +157,9 @@
         grid=(width // lanes,),
         in_specs=[
             pl.BlockSpec((tables, piece.shape[1], lanes), tile3),
-            pl.BlockSpec((block_total, 2 * rows, lanes), tile3),
+            pl.BlockSpec(basis_hi.shape, lambda i: (0, 0, 0)),
+            pl.BlockSpec(basis_lo.shape, lambda i: (0, 0, 0)),
+            pl.BlockSpec((out_cols.shape[0], lanes), lambda i: (0, i)),
             pl.BlockSpec((tables, rows, lanes), tile3),
             pl.BlockSpec((tables, rows, lanes), tile3),
             pl.BlockSpec((1, lanes), lambda i: (0, i)),
@@ -141,8 +170,9 @@
         ],
         out_specs=pl.BlockSpec((tables, rows, lanes), tile3),
         out_shape=jax.ShapeDtypeStruct((tables, rows, width), jnp.bfloat16),
+        scratch_shapes=[pltpu.VMEM((block_total, 2 * rows, lanes), jnp.float32)],
         compiler_params=pltpu.CompilerParams(vmem_limit_bytes=48 * 1024 * 1024),
-    )(piece, response, query_gate, carried, skip.reshape(1, width), fwd_hi, fwd_lo, inv_hi, inv_lo)
+    )(piece, basis_hi, basis_lo, out_cols, query_gate, carried, skip.reshape(1, width), fwd_hi, fwd_lo, inv_hi, inv_lo)
 
 
 def shards(
@@ -158,7 +188,33 @@
     block_counts,
 ):
     seq_dev, block_len, width = tokens.shape
+    local_ch = skip_gain.shape[0]
+    params = jnp.concatenate(
+        [response_out.reshape(2 * response_out.shape[1], local_ch), skip_gain[None, :]], axis=0
+    )
+    gathered = gather_by_permutes(params, "fsdp")
+    gathered = jnp.transpose(gathered, (1, 0, 2)).reshape(params.shape[0], width)
+    stacked_out = gathered[:-1]
+    full_skip = gathered[-1]
+    seq_count = lax.axis_size("seq")
+    position = lax.axis_index("seq")
+    total_len = float(seq_count * block_len)
+    forward = forward_table(block_len)
+    forward_half = forward[:, :block_len]
+    inverse = inverse_table(block_len)
+    circular = jnp.arange(2 * block_len, dtype=jnp.int32)
+    wrapped = jnp.where(circular < block_len, circular, circular - 2 * block_len)
+
+    block_total = seq_count
+    offsets = (position - jnp.arange(block_total, dtype=jnp.int32)) * block_len
+    lag_values = (offsets[:, None] + wrapped[None, :]).reshape(-1)
+    basis_rows = filter_basis(lag_values, total_len, basis_in, basis_bias, basis_mid, basis_shift)
+    ahead_mask = (lag_values >= 0).astype(jnp.float32)[:, None]
+    paired = jnp.concatenate([basis_rows * ahead_mask, basis_rows * (1.0 - ahead_mask)], axis=1)
+    paired = paired.reshape(block_total, 2 * block_len, paired.shape[-1])
+    basis_spec = jnp.einsum("gf,bfk->bgk", forward, paired, precision=lax.Precision.HIGHEST)
     group_tokens = lax.all_gather(tokens, "fsdp", axis=0, tiled=True)
+    group_tokens, basis_spec = lax.optimization_barrier((group_tokens, basis_spec))
     group_rows = group_tokens.shape[0]
     local_cols = in_weight.shape[1]
     partial = jnp.dot(
@@ -181,37 +237,9 @@
         jnp.float32
     )
     carried = (key_part * value_part * valid_mask[:, :, None]).astype(jnp.bfloat16)
-    local_ch = skip_gain.shape[0]
-    params = jnp.concatenate(
-        [response_out.reshape(2 * response_out.shape[1], local_ch), skip_gain[None, :]], axis=0
-    )
-    gathered = lax.all_gather(params, "fsdp", axis=0, tiled=False)
-    gathered = jnp.transpose(gathered, (1, 0, 2)).reshape(params.shape[0], width)
-    stacked_out = gathered[:-1]
-    full_skip = gathered[-1]
-    seq_count = lax.axis_size("seq")
-    position = lax.axis_index("seq")
-    total_len = float(seq_count * block_len)
-    forward = forward_table(block_len)
-    forward_half = forward[:, :block_len]
-    half_hi = forward_half.astype(jnp.bfloat16)
-    half_lo = (forward_half - half_hi.astype(jnp.float32)).astype(jnp.bfloat16)
-    inverse = inverse_table(block_len)
-    circular = jnp.arange(2 * block_len, dtype=jnp.int32)
-    wrapped = jnp.where(circular < block_len, circular, circular - 2 * block_len)
-
     piece = lax.all_gather(carried, "seq", axis=1, tiled=True)
-    block_total = piece.shape[1] // block_len
-
-    offsets = (position - jnp.arange(block_total, dtype=jnp.int32)) * block_len
-    lag_values = (offsets[:, None] + wrapped[None, :]).reshape(-1)
-    basis_rows = filter_basis(lag_values, total_len, basis_in, basis_bias, basis_mid, basis_shift)
-    ahead_mask = (lag_values >= 0).astype(jnp.float32)[:, None]
-    paired = jnp.concatenate([basis_rows * ahead_mask, basis_rows * (1.0 - ahead_mask)], axis=1)
-    paired = paired.reshape(block_total, 2 * block_len, paired.shape[-1])
-    paired_spec = jnp.einsum("gf,bfk->bgk", forward, paired, precision=lax.Precision.HIGHEST)
-    response = jnp.einsum("bgk,kd->bgd", paired_spec, stacked_out, precision=lax.Precision.HIGH)
-    return fused_conv(piece, response, query_gate, carried, full_skip, forward_half, inverse)
+
+    return fused_conv(piece, basis_spec, stacked_out, query_gate, carried, full_skip, forward_half, inverse)
 
 
 def solution(mesh):

time: 225 us -> 221 us (0.982)
  blocking collectives: 18.3 us -> 0 us
  other arithmetic: 8.98 us -> 15.3 us
  Pallas kernels: 16.6 us -> 22.2 us
  waiting for transfers between devices: 126 us -> 131 us
  matrix products: 16.9 us -> 13 us
    all_gather x1 -> x0, blocking collectives: 18.3 us -> none  [shards(): gathered = lax.all_gather(params, 'fsdp', axis=0, tiled=False)]
    ppermute x0 -> x3, waiting for transfers between devices: none -> 9.27 us  [gather_by_permutes(): lax.ppermute(values, axis, [(i, (i + shift) % count) for i in range(count)])]
    all_gather x1, waiting for transfers between devices: 67.9 us -> 60.2 us  [shards(): group_tokens = lax.all_gather(tokens, 'fsdp', axis=0, tiled=True)]
    pallas_call x1, Pallas kernels: 16.6 us -> 22.2 us  [fused_conv(): pl.pallas_call(conv_kernel, grid=(width // lanes,), in_specs=[pl.BlockSpe...]
    slice x3 -> x1, local copies, waits for them, and re-layouts: 5.83 us -> 0.98 us  [shards(): stacked_out = gathered[:-1]]
    dot_general x1 -> x0, matrix products: 4.71 us -> none  [shards(): jnp.einsum('bgk,kd->bgd', paired_spec, stacked_out, precision=lax.Precisi...]
    another operation x0 -> x2, other arithmetic: none -> 3.97 us  [gather_by_permutes(): stacked = jnp.stack(received)]
    all_gather x1, waiting for transfers between devices: 0.01 us -> 3.89 us  [shards(): piece = lax.all_gather(carried, 'seq', axis=1, tiled=True)]
  transfers between devices with their start and end apart: 5 -> 8, of which waited for: 3 -> 6; matrix products, arithmetic and copies ran while one was open for 9% -> 10% of each run, Pallas kernels for 0% -> 0%
where the time goes in v6:
time: 221 us; the launch traced here: 220 us
  waiting for transfers between devices  131 us (59%)
  Pallas kernels  22.2 us (10%)
  local copies, waits for them, and re-layouts  15.5 us (7%)
  other arithmetic  15.3 us (7%)
  between operations  13.6 us (6%)
  matrix products  13 us (6%)
  starting transfers between devices  9.3 us (4%)
    all_gather x1, waiting for transfers between devices, shards(): group_tokens = lax.all_gather(tokens, 'fsdp', axis=0, tiled=True)  60.2 us
    all_to_all x1, waiting for transfers between devices, shards(): projected = lax.all_to_all(partial, 'fsdp', 0, 2, tiled=True)  54 us
    pallas_call x1, Pallas kernels, fused_conv(): pl.pallas_call(conv_kernel, grid=(width // lanes,), in_specs=[pl.BlockSpe...  22.2 us
    unnamed x36, local copies, waits for them, and re-layouts  9.71 us
    ppermute x3, waiting for transfers between devices, gather_by_permutes(): lax.ppermute(values, axis, [(i, (i + shift) % count) for i in range(count)])  9.27 us
    dot_general x1, matrix products, shards(): jnp.dot(group_tokens.reshape(group_rows * block_len, width), in_weight, p...  7.54 us
    all_to_all x1, starting transfers between devices, shards(): projected = lax.all_to_all(partial, 'fsdp', 0, 2, tiled=True)  4.64 us
  transfers between devices with their start and end apart: 8, of which 6 were waited for; matrix products, arithmetic and copies ran while one was open for 10% of the time, Pallas kernels for 0%

profile of v6, /device:TPU:0, one launch (start us, length us, event | category | flops | bytes accessed | tf_op | source)
XLA Modules:
  0.0 220.4 jit_solution(13030045302592822506)
XLA Ops:
  6.5 0.7 all-gather.3.cloned.1.call-update
  7.3 0.1 fusion.36
  7.4 0.1 fusion.39
  7.5 0.1 convert_bitcast_fusion
  7.6 0.6 fusion.34
  8.2 2.0 fusion.3
  10.1 2.0 broadcast_multiply_fusion.1
  12.2 0.5 negate_select_fusion.2
  12.8 0.6 copy-done.11
  13.5 1.5 convolution_bitcast_fusion
  14.9 60.2 %all-gather.3.cloned.1.call-done = bf16[8,128,1536]{2,1,0:T(8,128)(2,1)} async-done(((bf16[2,128,1536]{2,1,0:T(8,128)(2,1)}), bf16[8,128,1536]{2,1,0:T(8,128)(2,1)}) %all-gather.3.cloned.1.call-update) | async-done | bytes 3145744 | tf_op jit(solution)/shard_map/all_gather | solution.py:216
  75.2 7.5 %convolution_convert_fusion = bf16[1024,1152]{1,0:T(8,128)(2,1)} fusion(bf16[1024,1536]{1,0:T(8,128)(2,1)} %bitcast.56, bf16[1536,1152]{1,0:T(8,128)(2,1)S(1)} %copy-done), kind=kOutput, calls=%fused_computation.2 | convolution fusion | flops 3625058304 | bytes 9043968 | tf_op jit(solution)/shard_map/dot_general | solution.py:220
  82.7 4.6 %all-to-all-start = ((bf16[8,128,1152]{2,1,0:T(8,128)(2,1)}), bf16[8,128,1152]{2,1,0:T(8,128)(2,1)}, u32[]{:S(2)}, u32[]{:S(2)}) async-start(bf16[8,128,1152]{2,1,0:T(8,128)(2,1)} %bitcast.49), calls=%async_computation | async-start | bytes 4718592 | tf_op jit(solution)/shard_map/all_to_all | solution.py:226
  87.4 0.1 compare_convert_fusion
  87.5 54.0 %all-to-all-done = bf16[8,128,1152]{2,1,0:T(8,128)(2,1)} async-done(((bf16[8,128,1152]{2,1,0:T(8,128)(2,1)}), bf16[8,128,1152]{2,1,0:T(8,128)(2,1)}, u32[]{:S(2)}, u32[]{:S(2)}) %all-to-all-start) | async-done | bytes 2359328 | tf_op jit(solution)/shard_map/all_to_all | solution.py:226
  141.5 1.9 copy.25
  143.5 1.3 collective-permute-start
  144.8 1.3 collective-permute-start.1
  146.1 0.1 slice_reduce_fusion.2
  146.3 3.3 %collective-permute-done.1 = bf16[2,1,4608]{2,1,0:T(2,128)(2,1)S(1)} collective-permute-done((bf16[2,1,4608]{2,1,0:T(2,128)(2,1)S(1)}, bf16[2,1,4608]{2,1,0:T(2,128)(2,1)S(1)}, u32[]{:S(2)}, u32[]{:S(2)}) %collective-permute-start.1) | collective-permute-done | bytes 18464 | tf_op jit(solution)/shard_map/ppermute | solution.py:19
  149.6 1.9 multiply_add_fusion
  151.5 1.7 fusion.53
  153.3 1.7 fusion.51
  155.1 1.5 collective-permute-start.4
  156.5 0.6 collective-permute-start.2
  157.1 0.8 sort.17
  157.9 0.3 select_multiply_fusion.1
  158.2 0.6 fusion.15.inv_hi_ref
  158.9 0.6 subtract_convert_fusion.1.inv_lo_ref
  159.5 1.6 subtract_convert_fusion.2
  161.1 7.7 %collective-permute-done.3 = f32[129,384]{1,0:T(8,128)} collective-permute-done((f32[129,384]{1,0:T(8,128)}, f32[129,384]{1,0:T(8,128)}, u32[]{:S(2)}, u32[]{:S(2)}) %collective-permute-start.3) | collective-permute-done | bytes 198176 | tf_op jit(solution)/shard_map/ppermute | solution.py:32
  168.8 1.6 collective-permute-done.2
  170.4 2.2 %pad_maximum_fusion.2 = f32[4,129,384]{2,1,0:T(8,128)} fusion(f32[1,129,384]{2,1,0:T(8,128)} %bitcast.11, f32[1,129,384]{2,1,0:T(8,128)} %bitcast.10, f32[1,129,384]{2,1,0:T(8,128)} %bitcast.9, f32[1,129,384]{2,1,0:T(8,128)} %get-tuple-element.24), kind=kLoop, calls=%fused_computation.13 | loop fusion | flops 594432 | bytes 1585152 | tf_op jit(solution)/shard_map/stack | solution.py:34
  172.6 2.7 %gather_fusion = f32[4,129,384]{2,1,0:T(8,128)} fusion(f32[4,129,384]{2,1,0:T(8,128)} %pad_maximum_fusion.2, s32[1024]{0:T(1024)S(1)} %pad_clamp_fusion), kind=kCustom, calls=%fused_computation | custom fusion | bytes 1585168 | tf_op jit(solution)/shard_map/jit(_take)/gather | solution.py:37
  175.3 1.3 select_bitcast_fusion
  176.7 1.0 copy.26
  177.7 0.9 subtract_convert_fusion
  178.6 3.9 %all-gather.5.cloned.1.call-done.piece_ref = bf16[2,512,1536]{2,1,0:T(8,128)(2,1)} async-done(((bf16[2,128,1536]{2,1,0:T(8,128)(2,1)}), bf16[2,512,1536]{2,1,0:T(8,128)(2,1)}) %all-gather.5.cloned.1.call-update) | async-done | bytes 3145744 | tf_op jit(solution)/shard_map/all_gather | solution.py:240
  182.4 1.1 copy-done.1
  183.6 1.4 copy-done.2
  185.0 1.1 copy-done.3
  186.1 0.9 copy-done.4
  187.1 0.9 copy-done.5
  188.0 0.8 copy-done.6
  188.9 0.8 copy-done.7
  189.7 0.8 copy-done.8
  190.5 0.8 copy-done.9
  191.4 22.2 %shard_map.103 = bf16[2,128,1536]{2,1,0:T(8,128)(2,1)} custom-call(bf16[2,512,1536]{2,1,0:T(8,128)(2,1)} %all-gather.5.cloned.1.call-done.piece_ref, bf16[4,256,128]{2,1,0:T(8,128)(2,1)S(1)} %copy-done.5, bf16[4,256,128]{2,1,0:T(8,128)(2,1)S(1)} %copy-done.4, f32[128,1536]{1,0:T(8,128)S(1)} %bitcast.45, f32[2,128,1536]{2,1,0:T(8,128)S(1)} %copy-done.2, ...), custom_call_target="tpu_custom_call" | custom-call | tf_op jit(solution)/shard_map/pallas_call | solution.py:155
  (49 shorter events, 0.4 us)
Async XLA Ops:
  6.5 68.6 %copy-start = (bf16[1536,1152]{1,0:T(8,128)(2,1)S(1)}, bf16[1536,1152]{1,0:T(8,128)(2,1)}, u32[]{:S(2)}) copy-start(bf16[1536,1152]{1,0:T(8,128)(2,1)} %param.11) | copy-start | bytes 10616836
  6.5 68.6 %all-gather.3.cloned.1.call-start = ((), (), s32[]{:S(2)}) async-start(), calls=%async_computation.1 | async-start | bytes 3932160 | tf_op jit(solution)/shard_map/all_gather | solution.py:216
  12.8 0.6 copy-start.11
  12.8 0.7 copy-start.12
  82.7 4.7 %copy-start.15 = (s32[2,1]{0,1:T(1,128)S(1)}, s32[2,1]{0,1:T(1,128)}, u32[]{:S(2)}) copy-start(s32[2,1]{0,1:T(1,128)} %param.19) | copy-start | bytes 28
  82.7 58.8 %all-to-all-start = ((bf16[8,128,1152]{2,1,0:T(8,128)(2,1)}), bf16[8,128,1152]{2,1,0:T(8,128)(2,1)}, u32[]{:S(2)}, u32[]{:S(2)}) async-start(bf16[8,128,1152]{2,1,0:T(8,128)(2,1)} %bitcast.49), calls=%async_computation | async-start | bytes 4718592 | tf_op jit(solution)/shard_map/all_to_all | solution.py:226
  87.4 95.1 %all-gather.5.cloned.1.call-start = ((), (), s32[]{:S(2)}) async-start(), calls=%async_computation.2 | async-start | bytes 3932160 | tf_op jit(solution)/shard_map/all_gather | solution.py:240
  141.5 4.6 %copy-start.13 = (f32[3,4608]{1,0:T(4,128)S(1)}, f32[3,4608]{1,0:T(4,128)}, u32[]{:S(2)}) copy-start(f32[3,4608]{1,0:T(4,128)} %param.12) | copy-start | bytes 165892
  143.5 2.8 %collective-permute-start = (bf16[2,1,4608]{2,1,0:T(2,128)(2,1)S(1)}, bf16[2,1,4608]{2,1,0:T(2,128)(2,1)S(1)}, u32[]{:S(2)}, u32[]{:S(2)}) collective-permute-start(bf16[2,1,4608]{2,1,0:T(2,128)(2,1)S(1)} %get-tuple-element.20), channel_id=1, source_target_pairs={{0,4},{4,8},{8,12},{1,5},{5,9},{9,13},{2,6},{6,10},{10,14},{3,7},{... | collective-permute-start | bytes 55304 | tf_op jit(solution)/shard_map/ppermute | solution.py:17
  144.8 4.8 %collective-permute-start.1 = (bf16[2,1,4608]{2,1,0:T(2,128)(2,1)S(1)}, bf16[2,1,4608]{2,1,0:T(2,128)(2,1)S(1)}, u32[]{:S(2)}, u32[]{:S(2)}) collective-permute-start(bf16[2,1,4608]{2,1,0:T(2,128)(2,1)S(1)} %get-tuple-element.21), channel_id=1, source_target_pairs={{4,0},{8,4},{12,8},{5,1},{9,5},{13,9},{6,2},{10,6},{14,10},{7,3},{... | collective-permute-start | bytes 55304 | tf_op jit(solution)/shard_map/ppermute | solution.py:19
  151.5 1.8 copy-start.14
  155.1 13.7 %collective-permute-start.3 = (f32[129,384]{1,0:T(8,128)}, f32[129,384]{1,0:T(8,128)}, u32[]{:S(2)}, u32[]{:S(2)}) collective-permute-start(f32[129,384]{1,0:T(8,128)} %get-tuple-element.25), channel_id=1, source_target_pairs={{0,2},{1,3},{2,0},{3,1},{4,6},{5,7},{6,4},{7,5},{8,10},{9,11},{10,... | collective-permute-start | bytes 594440 | tf_op jit(solution)/shard_map/ppermute | solution.py:32
  155.1 13.7 %collective-permute-start.4 = (f32[129,384]{1,0:T(8,128)}, f32[129,384]{1,0:T(8,128)}, u32[]{:S(2)}, u32[]{:S(2)}) collective-permute-start(f32[129,384]{1,0:T(8,128)} %get-tuple-element.25), channel_id=1, source_target_pairs={{0,3},{1,0},{2,1},{3,2},{4,7},{5,4},{6,5},{7,6},{8,11},{9,8},{10,9... | collective-permute-start | bytes 594440 | tf_op jit(solution)/shard_map/ppermute | solution.py:32
  156.5 13.9 %collective-permute-start.2 = (f32[129,384]{1,0:T(8,128)}, f32[129,384]{1,0:T(8,128)}, u32[]{:S(2)}, u32[]{:S(2)}) collective-permute-start(f32[129,384]{1,0:T(8,128)} %get-tuple-element.25), channel_id=1, source_target_pairs={{0,1},{1,2},{2,3},{3,0},{4,5},{5,6},{6,7},{7,4},{8,9},{9,10},{10,1... | collective-permute-start | bytes 594440 | tf_op jit(solution)/shard_map/ppermute | solution.py:32
  175.3 2.4 %copy-start.10 = (f32[4,256,128]{2,1,0:T(8,128)S(1)}, f32[4,256,128]{2,1,0:T(8,128)}, u32[]{:S(2)}) copy-start(f32[4,256,128]{2,1,0:T(8,128)} %convolution_bitcast_fusion) | copy-start | bytes 1572868
  182.4 1.1 copy-start.1
  183.6 1.4 copy-start.2
  185.0 1.1 copy-start.3
  186.1 0.9 copy-start.4
  187.1 0.9 copy-start.5
  188.0 0.8 copy-start.6
  188.9 0.8 copy-start.7
  189.7 0.8 copy-start.8
  190.5 0.8 copy-start.9
Sparse Core Ops, SparseCore 0:
  8.9 66.1 all-gather.2
  153.4 28.9 all-gather.4

commit v7 on v6

--- a/solution.py
+++ b/solution.py
@@ -1,4 +1,6 @@
 import jax
+import ml_dtypes
+import numpy as np
 import jax.numpy as jnp
 from jax import lax
 from jax.sharding import PartitionSpec as P
@@ -92,27 +94,52 @@
     return high, (values - high.astype(jnp.float32)).astype(jnp.bfloat16)
 
 
+def split_table(values):
+    high = values.astype(ml_dtypes.bfloat16)
+    low = (values - high.astype(np.float64)).astype(ml_dtypes.bfloat16)
+    return np.stack([high, low])
+
+
+def dft_tables(block_len):
+    period = 2 * block_len
+    frequency = np.arange(block_len)[:, None]
+    samples = np.arange(block_len)[None, :]
+    phases = 2.0 * np.pi / period * (frequency * samples % period)
+    alternate = (1 - 2 * (samples % 2)).astype(np.float64)
+    real_rows = np.cos(phases)
+    imag_rows = np.where(frequency == 0, alternate, -np.sin(phases))
+    forward = np.concatenate([real_rows, imag_rows], axis=0)
+    places = np.arange(block_len)[:, None]
+    freq = np.arange(block_len)[None, :]
+    phases = 2.0 * np.pi / period * (places * freq % period)
+    alt = (1 - 2 * (places % 2)).astype(np.float64)
+    real_cols = np.where(freq == 0, 1.0, 2.0 * np.cos(phases)) / period
+    imag_cols = np.where(freq == 0, alt, -2.0 * np.sin(phases)) / period
+    inverse = np.concatenate([np.broadcast_to(real_cols, (block_len, block_len)), imag_cols], axis=1)
+    return split_table(forward), split_table(inverse)
+
+
 def conv_kernel(
-    piece_ref, basis_hi_ref, basis_lo_ref, out_cols_ref, query_ref, carried_ref, skip_ref,
-    fwd_hi_ref, fwd_lo_ref, inv_hi_ref, inv_lo_ref, out_ref, resp_ref,
+    piece_ref, basis_ref, out_cols_ref, query_ref, carried_ref, skip_ref, fwd_ref, inv_ref,
+    out_ref, resp_ref,
 ):
     tables, rows, lanes = carried_ref.shape
     block_total = resp_ref.shape[0]
     cols_hi, cols_lo = split_bf16(out_cols_ref[...])
 
     def fill(block, carry):
-        basis_hi = basis_hi_ref[block]
+        basis_hi = basis_ref[0, block]
         resp_ref[block] = (
             jnp.dot(basis_hi, cols_hi, preferred_element_type=jnp.float32)
             + jnp.dot(basis_hi, cols_lo, preferred_element_type=jnp.float32)
-            + jnp.dot(basis_lo_ref[block], cols_hi, preferred_element_type=jnp.float32)
+            + jnp.dot(basis_ref[1, block], cols_hi, preferred_element_type=jnp.float32)
         )
         return carry
 
     lax.fori_loop(0, block_total, fill, 0)
     first = lax.broadcasted_iota(jnp.int32, (rows, lanes), 0) == 0
-    fwd_hi = fwd_hi_ref[...]
-    fwd_lo = fwd_lo_ref[...]
+    fwd_hi = fwd_ref[0]
+    fwd_lo = fwd_ref[1]
 
     def dot(a, b):
         return jnp.dot(a, b, preferred_element_type=jnp.float32)
@@ -137,42 +164,37 @@
         acc_real, acc_imag = lax.fori_loop(0, block_total, one_block, (zeros, zeros))
         spectrum = jnp.concatenate([acc_real, acc_imag], axis=0)
         spec_hi, spec_lo = split_bf16(spectrum)
-        inv_hi = inv_hi_ref[...]
-        conv = dot(inv_hi, spec_hi) + dot(inv_hi, spec_lo) + dot(inv_lo_ref[...], spec_hi)
+        inv_hi = inv_ref[0]
+        conv = dot(inv_hi, spec_hi) + dot(inv_hi, spec_lo) + dot(inv_ref[1], spec_hi)
         gated = query_ref[table] * (conv + skip_ref[...] * carried_ref[table].astype(jnp.float32))
         out_ref[table] = gated.astype(out_ref.dtype)
 
 
-def fused_conv(piece, basis_spec, out_cols, query_gate, carried, skip, fwd_half, inverse):
+def fused_conv(piece, basis_spec, out_cols, query_gate, carried, skip):
     tables, rows, width = carried.shape
     block_total = basis_spec.shape[0]
-    basis_hi, basis_lo = split_bf16(basis_spec)
+    basis = jnp.stack(split_bf16(basis_spec))
+    fwd, inv = dft_tables(rows)
     lanes = 256 if width % 256 == 0 else width
-    fwd_hi, fwd_lo = split_bf16(fwd_half)
-    inv_hi, inv_lo = split_bf16(inverse)
     tile3 = lambda i: (0, 0, i)
-    whole2 = lambda i: (0, 0)
     return pl.pallas_call(
         conv_kernel,
         grid=(width // lanes,),
         in_specs=[
             pl.BlockSpec((tables, piece.shape[1], lanes), tile3),
-            pl.BlockSpec(basis_hi.shape, lambda i: (0, 0, 0)),
-            pl.BlockSpec(basis_lo.shape, lambda i: (0, 0, 0)),
+            pl.BlockSpec(basis.shape, lambda i: (0, 0, 0, 0)),
             pl.BlockSpec((out_cols.shape[0], lanes), lambda i: (0, i)),
             pl.BlockSpec((tables, rows, lanes), tile3),
             pl.BlockSpec((tables, rows, lanes), tile3),
             pl.BlockSpec((1, lanes), lambda i: (0, i)),
-            pl.BlockSpec(fwd_hi.shape, whole2),
-            pl.BlockSpec(fwd_lo.shape, whole2),
-            pl.BlockSpec(inv_hi.shape, whole2),
-            pl.BlockSpec(inv_lo.shape, whole2),
+            pl.BlockSpec(fwd.shape, lambda i: (0, 0, 0)),
+            pl.BlockSpec(inv.shape, lambda i: (0, 0, 0)),
         ],
         out_specs=pl.BlockSpec((tables, rows, lanes), tile3),
         out_shape=jax.ShapeDtypeStruct((tables, rows, width), jnp.bfloat16),
         scratch_shapes=[pltpu.VMEM((block_total, 2 * rows, lanes), jnp.float32)],
         compiler_params=pltpu.CompilerParams(vmem_limit_bytes=48 * 1024 * 1024),
-    )(piece, basis_hi, basis_lo, out_cols, query_gate, carried, skip.reshape(1, width), fwd_hi, fwd_lo, inv_hi, inv_lo)
+    )(piece, basis, out_cols, query_gate, carried, skip.reshape(1, width), jnp.asarray(fwd), jnp.asarray(inv))
 
 
 def shards(
@@ -214,7 +236,9 @@
     paired = paired.reshape(block_total, 2 * block_len, paired.shape[-1])
     basis_spec = jnp.einsum("gf,bfk->bgk", forward, paired, precision=lax.Precision.HIGHEST)
     group_tokens = lax.all_gather(tokens, "fsdp", axis=0, tiled=True)
-    group_tokens, basis_spec = lax.optimization_barrier((group_tokens, basis_spec))
+    group_tokens, basis_spec, stacked_out, full_skip = lax.optimization_barrier(
+        (group_tokens, basis_spec, stacked_out, full_skip)
+    )
     group_rows = group_tokens.shape[0]
     local_cols = in_weight.shape[1]
     partial = jnp.dot(
@@ -239,7 +263,7 @@
     carried = (key_part * value_part * valid_mask[:, :, None]).astype(jnp.bfloat16)
     piece = lax.all_gather(carried, "seq", axis=1, tiled=True)
 
-    return fused_conv(piece, basis_spec, stacked_out, query_gate, carried, full_skip, forward_half, inverse)
+    return fused_conv(piece, basis_spec, stacked_out, query_gate, carried, full_skip)
 
 
 def solution(mesh):

time: 221 us -> 228 us (1.032)
  starting transfers between devices: 9.3 us -> 15.3 us
  waiting for transfers between devices: 131 us -> 134 us
    all_gather x1, waiting for transfers between devices: 3.89 us -> 27 us  [shards(): piece = lax.all_gather(carried, 'seq', axis=1, tiled=True)]
    all_gather x1, waiting for transfers between devices: 60.2 us -> 39.2 us  [shards(): group_tokens = lax.all_gather(tokens, 'fsdp', axis=0, tiled=True)]
    ppermute x3, starting transfers between devices: 2.03 us -> 7.86 us  [gather_by_permutes(): lax.ppermute(values, axis, [(i, (i + shift) % count) for i in range(count)])]
    convert_element_type x5 -> x0, other arithmetic: 3.77 us -> none  [the longest x3 3.13 us: split_bf16(): return (high, (values - high.astype(jnp.float32)).astype(jnp.bfloat16))]
    unnamed x36 -> x28, local copies, waits for them, and re-layouts: 9.71 us -> 7.07 us
  transfers between devices with their start and end apart: 8 -> 8, of which waited for: 6 -> 5; matrix products, arithmetic and copies ran while one was open for 10% -> 10% of each run, Pallas kernels for 0% -> 0%
where the time goes in v7:
time: 228 us; the launch traced here: 227 us
  waiting for transfers between devices  134 us (59%)
  Pallas kernels  22.2 us (10%)
  starting transfers between devices  15.3 us (7%)
  local copies, waits for them, and re-layouts  14.4 us (6%)
  other arithmetic  14.4 us (6%)
  between operations  13.6 us (6%)
  matrix products  13 us (6%)
    all_to_all x1, waiting for transfers between devices, shards(): projected = lax.all_to_all(partial, 'fsdp', 0, 2, tiled=True)  54.1 us
    all_gather x1, waiting for transfers between devices, shards(): group_tokens = lax.all_gather(tokens, 'fsdp', axis=0, tiled=True)  39.2 us
    all_gather x1, waiting for transfers between devices, shards(): piece = lax.all_gather(carried, 'seq', axis=1, tiled=True)  27 us
    pallas_call x1, Pallas kernels, fused_conv(): pl.pallas_call(conv_kernel, grid=(width // lanes,), in_specs=[pl.BlockSpe...  22.2 us
    ppermute x3, waiting for transfers between devices, gather_by_permutes(): lax.ppermute(values, axis, [(i, (i + shift) % count) for i in range(count)])  9.83 us
    ppermute x3, starting transfers between devices, gather_by_permutes(): lax.ppermute(values, axis, [(i, (i + shift) % count) for i in range(count)])  7.86 us
    dot_general x1, matrix products, shards(): jnp.dot(group_tokens.reshape(group_rows * block_len, width), in_weight, p...  7.57 us
    unnamed x28, local copies, waits for them, and re-layouts  7.07 us
  transfers between devices with their start and end apart: 8, of which 5 were waited for; matrix products, arithmetic and copies ran while one was open for 10% of the time, Pallas kernels for 0%

profile of v7, /device:TPU:0, one launch (start us, length us, event | category | flops | bytes accessed | tf_op | source)
XLA Modules:
  0.0 227.2 jit_solution(14293830171316354772)
XLA Ops:
  6.5 0.7 all-gather.3.cloned.1.call-update
  7.3 1.0 broadcast_in_dim.51
  8.3 1.7 fusion.40
  10.0 4.0 %collective-permute-start.1 = (f32[129,384]{1,0:T(8,128)}, f32[129,384]{1,0:T(8,128)}, u32[]{:S(2)}, u32[]{:S(2)}) collective-permute-start(f32[129,384]{1,0:T(8,128)} %get-tuple-element.27), channel_id=1, source_target_pairs={{0,2},{1,3},{2,0},{3,1},{4,6},{5,7},{6,4},{7,5},{8,10},{9,11},{10,... | collective-permute-start | bytes 594440 | tf_op jit(solution)/shard_map/ppermute | solution.py:34
  14.0 1.6 collective-permute-start
  15.6 2.2 collective-permute-start.2
  17.9 0.1 convert_bitcast_fusion.1
  17.9 0.1 fusion.28
  18.0 0.1 fusion.31
  18.1 0.6 and_select_fusion
  18.7 0.5 iota.59
  19.2 1.5 sort.17
  20.7 0.5 copy-done.10
  21.2 0.6 fusion.27
  21.8 2.0 fusion.3
  23.8 2.0 broadcast_multiply_fusion.1
  25.8 0.5 negate_select_fusion.2
  26.4 1.4 convolution_bitcast_fusion
  27.8 9.8 %collective-permute-done.1 = f32[129,384]{1,0:T(8,128)} collective-permute-done((f32[129,384]{1,0:T(8,128)}, f32[129,384]{1,0:T(8,128)}, u32[]{:S(2)}, u32[]{:S(2)}) %collective-permute-start.1) | collective-permute-done | bytes 198176 | tf_op jit(solution)/shard_map/ppermute | solution.py:34
  37.7 2.1 pad_maximum_fusion.2
  39.8 2.7 %gather_fusion = f32[4,129,384]{2,1,0:T(8,128)} fusion(f32[4,129,384]{2,1,0:T(8,128)} %pad_maximum_fusion.2, s32[1024]{0:T(1024)S(1)} %pad_clamp_fusion), kind=kCustom, calls=%fused_computation | custom fusion | bytes 1585168 | tf_op jit(solution)/shard_map/jit(_take)/gather | solution.py:39
  42.5 1.3 select_bitcast_fusion
  43.7 0.1 slice_bitcast_fusion
  43.8 1.0 copy.27
  44.8 39.2 %all-gather.3.cloned.1.call-done = bf16[8,128,1536]{2,1,0:T(8,128)(2,1)} async-done(((bf16[2,128,1536]{2,1,0:T(8,128)(2,1)}), bf16[8,128,1536]{2,1,0:T(8,128)(2,1)}) %all-gather.3.cloned.1.call-update) | async-done | bytes 3145744 | tf_op jit(solution)/shard_map/all_gather | solution.py:238
  84.0 7.6 %convolution_convert_fusion = bf16[1024,1152]{1,0:T(8,128)(2,1)} fusion(bf16[1024,1536]{1,0:T(8,128)(2,1)} %bitcast.58, bf16[1536,1152]{1,0:T(8,128)(2,1)S(1)} %copy-done), kind=kOutput, calls=%fused_computation.2 | convolution fusion | flops 3625058304 | bytes 9043968 | tf_op jit(solution)/shard_map/dot_general | solution.py:244
  91.6 4.9 %all-to-all-start = ((bf16[8,128,1152]{2,1,0:T(8,128)(2,1)}), bf16[8,128,1152]{2,1,0:T(8,128)(2,1)}, u32[]{:S(2)}, u32[]{:S(2)}) async-start(bf16[8,128,1152]{2,1,0:T(8,128)(2,1)} %bitcast.51), calls=%async_computation | async-start | bytes 4718592 | tf_op jit(solution)/shard_map/all_to_all | solution.py:250
  96.4 0.1 compare_convert_fusion
  96.5 54.1 %all-to-all-done = bf16[8,128,1152]{2,1,0:T(8,128)(2,1)} async-done(((bf16[8,128,1152]{2,1,0:T(8,128)(2,1)}), bf16[8,128,1152]{2,1,0:T(8,128)(2,1)}, u32[]{:S(2)}, u32[]{:S(2)}) %all-to-all-start) | async-done | bytes 2359328 | tf_op jit(solution)/shard_map/all_to_all | solution.py:250
  150.6 1.9 copy.28
  152.5 0.1 fusion.42
  152.6 1.3 collective-permute-start.3
  153.9 1.3 collective-permute-start.4
  155.2 0.1 slice_reduce_fusion.2
  155.4 3.4 %collective-permute-done.4 = bf16[2,1,4608]{2,1,0:T(2,128)(2,1)S(1)} collective-permute-done((bf16[2,1,4608]{2,1,0:T(2,128)(2,1)S(1)}, bf16[2,1,4608]{2,1,0:T(2,128)(2,1)S(1)}, u32[]{:S(2)}, u32[]{:S(2)}) %collective-permute-start.4) | collective-permute-done | bytes 18464 | tf_op jit(solution)/shard_map/ppermute | solution.py:21
  158.8 1.9 multiply_add_fusion
  160.7 1.7 fusion.41
  162.4 0.0 all-gather.5.cloned.1.call-update
  162.5 1.3 convert_bitcast_fusion
  163.8 0.8 pad_maximum_fusion.4.basis_ref
  164.6 27.0 %all-gather.5.cloned.1.call-done.piece_ref = bf16[2,512,1536]{2,1,0:T(8,128)(2,1)} async-done(((bf16[2,128,1536]{2,1,0:T(8,128)(2,1)}), bf16[2,512,1536]{2,1,0:T(8,128)(2,1)}) %all-gather.5.cloned.1.call-update) | async-done | bytes 3145744 | tf_op jit(solution)/shard_map/all_gather | solution.py:264
  191.6 1.1 copy-done.1
  192.8 1.4 copy-done.2
  194.2 1.1 copy-done.3
  195.3 1.0 copy-done.4
  196.4 0.9 copy-done.5
  197.3 0.9 copy-done.6
  198.2 22.2 %shard_map.121 = bf16[2,128,1536]{2,1,0:T(8,128)(2,1)} custom-call(bf16[2,512,1536]{2,1,0:T(8,128)(2,1)} %all-gather.5.cloned.1.call-done.piece_ref, bf16[2,4,256,128]{3,2,1,0:T(8,128)(2,1)S(1)} %copy-done.4, f32[128,1536]{1,0:T(8,128)S(1)} %bitcast.48, f32[2,128,1536]{2,1,0:T(8,128)S(1)} %copy-done.2, bf16[2,128,1536]{2,1,0:T(8,128)(2,1)S(1)} %copy-done.1, ...), custom_call_target="tpu_custom_call" | custom-call | tf_op jit(solution)/shard_map/pallas_call | solution.py:180
  (39 shorter events, 0.2 us)
Async XLA Ops:
  6.5 77.5 %copy-start = (bf16[1536,1152]{1,0:T(8,128)(2,1)S(1)}, bf16[1536,1152]{1,0:T(8,128)(2,1)}, u32[]{:S(2)}) copy-start(bf16[1536,1152]{1,0:T(8,128)(2,1)} %param.13) | copy-start | bytes 10616836
  6.5 77.4 %all-gather.3.cloned.1.call-start = ((), (), s32[]{:S(2)}) async-start(), calls=%async_computation.1 | async-start | bytes 3932160 | tf_op jit(solution)/shard_map/all_gather | solution.py:238
  10.0 27.7 %collective-permute-start.1 = (f32[129,384]{1,0:T(8,128)}, f32[129,384]{1,0:T(8,128)}, u32[]{:S(2)}, u32[]{:S(2)}) collective-permute-start(f32[129,384]{1,0:T(8,128)} %get-tuple-element.27), channel_id=1, source_target_pairs={{0,2},{1,3},{2,0},{3,1},{4,6},{5,7},{6,4},{7,5},{8,10},{9,11},{10,... | collective-permute-start | bytes 594440 | tf_op jit(solution)/shard_map/ppermute | solution.py:34
  14.0 23.7 %collective-permute-start = (f32[129,384]{1,0:T(8,128)}, f32[129,384]{1,0:T(8,128)}, u32[]{:S(2)}, u32[]{:S(2)}) collective-permute-start(f32[129,384]{1,0:T(8,128)} %get-tuple-element.27), channel_id=1, source_target_pairs={{0,1},{1,2},{2,3},{3,0},{4,5},{5,6},{6,7},{7,4},{8,9},{9,10},{10,1... | collective-permute-start | bytes 594440 | tf_op jit(solution)/shard_map/ppermute | solution.py:34
  15.6 22.1 %collective-permute-start.2 = (f32[129,384]{1,0:T(8,128)}, f32[129,384]{1,0:T(8,128)}, u32[]{:S(2)}, u32[]{:S(2)}) collective-permute-start(f32[129,384]{1,0:T(8,128)} %get-tuple-element.27), channel_id=1, source_target_pairs={{0,3},{1,0},{2,1},{3,2},{4,7},{5,4},{6,5},{7,6},{8,11},{9,8},{10,9... | collective-permute-start | bytes 594440 | tf_op jit(solution)/shard_map/ppermute | solution.py:34
  20.7 0.5 copy-start.10
  20.7 17.0 %copy-start.7 = (f32[1,129,384]{2,1,0:T(8,128)S(1)}, f32[1,129,384]{2,1,0:T(8,128)}, u32[]{:S(2)}) copy-start(f32[1,129,384]{2,1,0:T(8,128)} %get-tuple-element.26) | copy-start | bytes 594436
  21.2 6.6 %copy-start.11 = (s32[4]{0:T(128)S(1)}, s32[4]{0:T(128)}, u32[]{:S(2)}) copy-start(s32[4]{0:T(128)} %copy-done.10) | copy-start | bytes 52
  91.6 4.9 %copy-start.9 = (s32[2,1]{0,1:T(1,128)S(1)}, s32[2,1]{0,1:T(1,128)}, u32[]{:S(2)}) copy-start(s32[2,1]{0,1:T(1,128)} %param.21) | copy-start | bytes 28
  91.6 59.0 %all-to-all-start = ((bf16[8,128,1152]{2,1,0:T(8,128)(2,1)}), bf16[8,128,1152]{2,1,0:T(8,128)(2,1)}, u32[]{:S(2)}, u32[]{:S(2)}) async-start(bf16[8,128,1152]{2,1,0:T(8,128)(2,1)} %bitcast.51), calls=%async_computation | async-start | bytes 4718592 | tf_op jit(solution)/shard_map/all_to_all | solution.py:250
  96.4 95.2 %all-gather.5.cloned.1.call-start = ((), (), s32[]{:S(2)}) async-start(), calls=%async_computation.2 | async-start | bytes 3932160 | tf_op jit(solution)/shard_map/all_gather | solution.py:264
  150.6 4.6 %copy-start.8 = (f32[3,4608]{1,0:T(4,128)S(1)}, f32[3,4608]{1,0:T(4,128)}, u32[]{:S(2)}) copy-start(f32[3,4608]{1,0:T(4,128)} %param.14) | copy-start | bytes 165892
  152.6 2.8 %collective-permute-start.3 = (bf16[2,1,4608]{2,1,0:T(2,128)(2,1)S(1)}, bf16[2,1,4608]{2,1,0:T(2,128)(2,1)S(1)}, u32[]{:S(2)}, u32[]{:S(2)}) collective-permute-start(bf16[2,1,4608]{2,1,0:T(2,128)(2,1)S(1)} %get-tuple-element.20), channel_id=1, source_target_pairs={{0,4},{4,8},{8,12},{1,5},{5,9},{9,13},{2,6},{6,10},{10,14},{3,7},{... | collective-permute-start | bytes 55304 | tf_op jit(solution)/shard_map/ppermute | solution.py:19
  153.9 4.9 %collective-permute-start.4 = (bf16[2,1,4608]{2,1,0:T(2,128)(2,1)S(1)}, bf16[2,1,4608]{2,1,0:T(2,128)(2,1)S(1)}, u32[]{:S(2)}, u32[]{:S(2)}) collective-permute-start(bf16[2,1,4608]{2,1,0:T(2,128)(2,1)S(1)} %get-tuple-element.21), channel_id=1, source_target_pairs={{4,0},{8,4},{12,8},{5,1},{9,5},{13,9},{6,2},{10,6},{14,10},{7,3},{... | collective-permute-start | bytes 55304 | tf_op jit(solution)/shard_map/ppermute | solution.py:21
  191.6 1.1 copy-start.1
  192.8 1.4 copy-start.2
  194.2 1.1 copy-start.3
  195.3 1.0 copy-start.4
  196.4 0.9 copy-start.5
  197.3 0.9 copy-start.6
Sparse Core Ops, SparseCore 0:
  8.9 75.0 all-gather.2
  162.6 29.0 all-gather.4

commit v8 on v7

--- a/solution.py
+++ b/solution.py
@@ -236,9 +236,7 @@
     paired = paired.reshape(block_total, 2 * block_len, paired.shape[-1])
     basis_spec = jnp.einsum("gf,bfk->bgk", forward, paired, precision=lax.Precision.HIGHEST)
     group_tokens = lax.all_gather(tokens, "fsdp", axis=0, tiled=True)
-    group_tokens, basis_spec, stacked_out, full_skip = lax.optimization_barrier(
-        (group_tokens, basis_spec, stacked_out, full_skip)
-    )
+    group_tokens, basis_spec = lax.optimization_barrier((group_tokens, basis_spec))
     group_rows = group_tokens.shape[0]
     local_cols = in_weight.shape[1]
     partial = jnp.dot(

time: 228 us -> 220 us (0.965)
  starting transfers between devices: 15.3 us -> 11.1 us
    all_gather x1, waiting for transfers between devices: 27 us -> 1.88 us  [shards(): piece = lax.all_gather(carried, 'seq', axis=1, tiled=True)]
    all_gather x1, waiting for transfers between devices: 39.2 us -> 61 us  [shards(): group_tokens = lax.all_gather(tokens, 'fsdp', axis=0, tiled=True)]
    ppermute x3, starting transfers between devices: 7.86 us -> 3.83 us  [gather_by_permutes(): lax.ppermute(values, axis, [(i, (i + shift) % count) for i in range(count)])]
    ppermute x3, waiting for transfers between devices: 9.83 us -> 12.6 us  [gather_by_permutes(): lax.ppermute(values, axis, [(i, (i + shift) % count) for i in range(count)])]
    unnamed x28 -> x26, local copies, waits for them, and re-layouts: 7.07 us -> 6.62 us
  transfers between devices with their start and end apart: 8 -> 8, of which waited for: 5 -> 6; matrix products, arithmetic and copies ran while one was open for 10% -> 8% of each run, Pallas kernels for 0% -> 0%
where the time goes in v8:
time: 220 us; the launch traced here: 218 us
  waiting for transfers between devices  133 us (60%)
  Pallas kernels  22.2 us (10%)
  between operations  13.6 us (6%)
  matrix products  13 us (6%)
  local copies, waits for them, and re-layouts  12.5 us (6%)
  other arithmetic  12.2 us (6%)
  starting transfers between devices  11.1 us (5%)
    all_gather x1, waiting for transfers between devices, shards(): group_tokens = lax.all_gather(tokens, 'fsdp', axis=0, tiled=True)  61 us
    all_to_all x1, waiting for transfers between devices, shards(): projected = lax.all_to_all(partial, 'fsdp', 0, 2, tiled=True)  54 us
    pallas_call x1, Pallas kernels, fused_conv(): pl.pallas_call(conv_kernel, grid=(width // lanes,), in_specs=[pl.BlockSpe...  22.2 us
    ppermute x3, waiting for transfers between devices, gather_by_permutes(): lax.ppermute(values, axis, [(i, (i + shift) % count) for i in range(count)])  12.6 us
    dot_general x1, matrix products, shards(): jnp.dot(group_tokens.reshape(group_rows * block_len, width), in_weight, p...  7.52 us
    unnamed x26, local copies, waits for them, and re-layouts  6.62 us
    all_to_all x1, starting transfers between devices, shards(): projected = lax.all_to_all(partial, 'fsdp', 0, 2, tiled=True)  4.62 us
  transfers between devices with their start and end apart: 8, of which 6 were waited for; matrix products, arithmetic and copies ran while one was open for 8% of the time, Pallas kernels for 0%

profile of v8, /device:TPU:0, one launch (start us, length us, event | category | flops | bytes accessed | tf_op | source)
XLA Modules:
  0.0 218.0 jit_solution(1102113398297986963)
XLA Ops:
  6.5 0.7 all-gather.3.cloned.1.call-update
  7.3 0.1 fusion.28
  7.4 0.1 fusion.31
  7.5 0.1 convert_bitcast_fusion.1
  7.6 0.6 fusion.27
  8.2 2.0 fusion.3
  10.1 2.0 broadcast_multiply_fusion.1
  12.2 0.5 negate_select_fusion.2
  12.8 1.4 convolution_bitcast_fusion
  14.2 61.0 %all-gather.3.cloned.1.call-done = bf16[8,128,1536]{2,1,0:T(8,128)(2,1)} async-done(((bf16[2,128,1536]{2,1,0:T(8,128)(2,1)}), bf16[8,128,1536]{2,1,0:T(8,128)(2,1)}) %all-gather.3.cloned.1.call-update) | async-done | bytes 3145744 | tf_op jit(solution)/shard_map/all_gather | solution.py:238
  75.2 7.5 %convolution_convert_fusion = bf16[1024,1152]{1,0:T(8,128)(2,1)} fusion(bf16[1024,1536]{1,0:T(8,128)(2,1)} %bitcast.60, bf16[1536,1152]{1,0:T(8,128)(2,1)S(1)} %copy-done), kind=kOutput, calls=%fused_computation.2 | convolution fusion | flops 3625058304 | bytes 9043968 | tf_op jit(solution)/shard_map/dot_general | solution.py:242
  82.7 4.6 %all-to-all-start = ((bf16[8,128,1152]{2,1,0:T(8,128)(2,1)}), bf16[8,128,1152]{2,1,0:T(8,128)(2,1)}, u32[]{:S(2)}, u32[]{:S(2)}) async-start(bf16[8,128,1152]{2,1,0:T(8,128)(2,1)} %bitcast.53), calls=%async_computation | async-start | bytes 4718592 | tf_op jit(solution)/shard_map/all_to_all | solution.py:248
  87.3 0.0 all-gather.5.cloned.1.call-start
  87.4 0.1 compare_convert_fusion
  87.5 54.0 %all-to-all-done = bf16[8,128,1152]{2,1,0:T(8,128)(2,1)} async-done(((bf16[8,128,1152]{2,1,0:T(8,128)(2,1)}), bf16[8,128,1152]{2,1,0:T(8,128)(2,1)}, u32[]{:S(2)}, u32[]{:S(2)}) %all-to-all-start) | async-done | bytes 2359328 | tf_op jit(solution)/shard_map/all_to_all | solution.py:248
  141.4 1.9 copy.27
  143.4 0.1 fusion.42
  143.4 1.3 collective-permute-start
  144.7 1.3 collective-permute-start.1
  146.1 0.1 slice_reduce_fusion.2
  146.2 3.3 %collective-permute-done.1 = bf16[2,1,4608]{2,1,0:T(2,128)(2,1)S(1)} collective-permute-done((bf16[2,1,4608]{2,1,0:T(2,128)(2,1)S(1)}, bf16[2,1,4608]{2,1,0:T(2,128)(2,1)S(1)}, u32[]{:S(2)}, u32[]{:S(2)}) %collective-permute-start.1) | collective-permute-done | bytes 18464 | tf_op jit(solution)/shard_map/ppermute | solution.py:21
  149.6 1.9 multiply_add_fusion
  151.5 0.0 copy-start.9
  151.5 1.7 fusion.41
  153.2 0.0 all-gather.5.cloned.1.call-update
  153.3 1.8 fusion.40
  155.1 0.0 collective-permute-start.2
  155.1 2.0 collective-permute-start.3
  157.1 1.8 collective-permute-start.4
  158.9 0.8 sort.17
  159.7 4.0 %collective-permute-done.2 = f32[129,384]{1,0:T(8,128)} collective-permute-done((f32[129,384]{1,0:T(8,128)}, f32[129,384]{1,0:T(8,128)}, u32[]{:S(2)}, u32[]{:S(2)}) %collective-permute-start.2) | collective-permute-done | bytes 198176 | tf_op jit(solution)/shard_map/ppermute | solution.py:34
  163.7 8.6 %collective-permute-done.3 = f32[129,384]{1,0:T(8,128)} collective-permute-done((f32[129,384]{1,0:T(8,128)}, f32[129,384]{1,0:T(8,128)}, u32[]{:S(2)}, u32[]{:S(2)}) %collective-permute-start.3) | collective-permute-done | bytes 198176 | tf_op jit(solution)/shard_map/ppermute | solution.py:34
  172.2 0.0 collective-permute-done.4
  172.2 2.2 %pad_maximum_fusion.2 = f32[4,129,384]{2,1,0:T(8,128)} fusion(f32[1,129,384]{2,1,0:T(8,128)} %bitcast.13, f32[1,129,384]{2,1,0:T(8,128)} %bitcast.12, f32[1,129,384]{2,1,0:T(8,128)} %bitcast.11, f32[1,129,384]{2,1,0:T(8,128)} %get-tuple-element.22), kind=kLoop, calls=%fused_computation.13 | loop fusion | flops 594432 | bytes 1585152 | tf_op jit(solution)/shard_map/stack | solution.py:36
  174.4 2.7 %gather_fusion = f32[4,129,384]{2,1,0:T(8,128)} fusion(f32[4,129,384]{2,1,0:T(8,128)} %pad_maximum_fusion.2, s32[1024]{0:T(1024)S(1)} %pad_clamp_fusion), kind=kCustom, calls=%fused_computation | custom fusion | bytes 1585168 | tf_op jit(solution)/shard_map/jit(_take)/gather | solution.py:39
  177.1 1.4 select_bitcast_fusion
  178.5 0.1 slice_bitcast_fusion
  178.6 1.0 copy.28
  179.6 0.1 convert_bitcast_fusion
  179.7 0.8 pad_maximum_fusion.4.basis_ref
  180.5 1.9 all-gather.5.cloned.1.call-done.piece_ref
  182.4 1.1 copy-done.1
  183.5 1.4 copy-done.2
  184.9 1.1 copy-done.3
  186.1 1.0 copy-done.4
  187.1 0.9 copy-done.5
  188.0 0.9 copy-done.6
  188.9 22.2 %shard_map.121 = bf16[2,128,1536]{2,1,0:T(8,128)(2,1)} custom-call(bf16[2,512,1536]{2,1,0:T(8,128)(2,1)} %all-gather.5.cloned.1.call-done.piece_ref, bf16[2,4,256,128]{3,2,1,0:T(8,128)(2,1)S(1)} %copy-done.4, f32[128,1536]{1,0:T(8,128)S(1)} %bitcast.49, f32[2,128,1536]{2,1,0:T(8,128)S(1)} %copy-done.2, bf16[2,128,1536]{2,1,0:T(8,128)(2,1)S(1)} %copy-done.1, ...), custom_call_target="tpu_custom_call" | custom-call | tf_op jit(solution)/shard_map/pallas_call | solution.py:180
  (35 shorter events, 0.2 us)
Async XLA Ops:
  6.5 68.6 %copy-start = (bf16[1536,1152]{1,0:T(8,128)(2,1)S(1)}, bf16[1536,1152]{1,0:T(8,128)(2,1)}, u32[]{:S(2)}) copy-start(bf16[1536,1152]{1,0:T(8,128)(2,1)} %param.13) | copy-start | bytes 10616836
  6.5 68.6 %all-gather.3.cloned.1.call-start = ((), (), s32[]{:S(2)}) async-start(), calls=%async_computation.1 | async-start | bytes 3932160 | tf_op jit(solution)/shard_map/all_gather | solution.py:238
  82.7 4.7 %copy-start.10 = (s32[2,1]{0,1:T(1,128)S(1)}, s32[2,1]{0,1:T(1,128)}, u32[]{:S(2)}) copy-start(s32[2,1]{0,1:T(1,128)} %param.21) | copy-start | bytes 28
  82.7 58.7 %all-to-all-start = ((bf16[8,128,1152]{2,1,0:T(8,128)(2,1)}), bf16[8,128,1152]{2,1,0:T(8,128)(2,1)}, u32[]{:S(2)}, u32[]{:S(2)}) async-start(bf16[8,128,1152]{2,1,0:T(8,128)(2,1)} %bitcast.53), calls=%async_computation | async-start | bytes 4718592 | tf_op jit(solution)/shard_map/all_to_all | solution.py:248
  87.3 95.1 %all-gather.5.cloned.1.call-start = ((), (), s32[]{:S(2)}) async-start(), calls=%async_computation.2 | async-start | bytes 3932160 | tf_op jit(solution)/shard_map/all_gather | solution.py:262
  141.4 4.6 %copy-start.8 = (f32[3,4608]{1,0:T(4,128)S(1)}, f32[3,4608]{1,0:T(4,128)}, u32[]{:S(2)}) copy-start(f32[3,4608]{1,0:T(4,128)} %param.14) | copy-start | bytes 165892
  143.4 2.8 %collective-permute-start = (bf16[2,1,4608]{2,1,0:T(2,128)(2,1)S(1)}, bf16[2,1,4608]{2,1,0:T(2,128)(2,1)S(1)}, u32[]{:S(2)}, u32[]{:S(2)}) collective-permute-start(bf16[2,1,4608]{2,1,0:T(2,128)(2,1)S(1)} %get-tuple-element.16), channel_id=1, source_target_pairs={{0,4},{4,8},{8,12},{1,5},{5,9},{9,13},{2,6},{6,10},{10,14},{3,7},{... | collective-permute-start | bytes 55304 | tf_op jit(solution)/shard_map/ppermute | solution.py:19
  144.7 4.8 %collective-permute-start.1 = (bf16[2,1,4608]{2,1,0:T(2,128)(2,1)S(1)}, bf16[2,1,4608]{2,1,0:T(2,128)(2,1)S(1)}, u32[]{:S(2)}, u32[]{:S(2)}) collective-permute-start(bf16[2,1,4608]{2,1,0:T(2,128)(2,1)S(1)} %get-tuple-element.17), channel_id=1, source_target_pairs={{4,0},{8,4},{12,8},{5,1},{9,5},{13,9},{6,2},{10,6},{14,10},{7,3},{... | collective-permute-start | bytes 55304 | tf_op jit(solution)/shard_map/ppermute | solution.py:21
  151.5 1.8 copy-start.9
  155.1 8.6 %collective-permute-start.2 = (f32[129,384]{1,0:T(8,128)}, f32[129,384]{1,0:T(8,128)}, u32[]{:S(2)}, u32[]{:S(2)}) collective-permute-start(f32[129,384]{1,0:T(8,128)} %get-tuple-element.23), channel_id=1, source_target_pairs={{0,1},{1,2},{2,3},{3,0},{4,5},{5,6},{6,7},{7,4},{8,9},{9,10},{10,1... | collective-permute-start | bytes 594440 | tf_op jit(solution)/shard_map/ppermute | solution.py:34
  155.1 17.2 %collective-permute-start.3 = (f32[129,384]{1,0:T(8,128)}, f32[129,384]{1,0:T(8,128)}, u32[]{:S(2)}, u32[]{:S(2)}) collective-permute-start(f32[129,384]{1,0:T(8,128)} %get-tuple-element.23), channel_id=1, source_target_pairs={{0,2},{1,3},{2,0},{3,1},{4,6},{5,7},{6,4},{7,5},{8,10},{9,11},{10,... | collective-permute-start | bytes 594440 | tf_op jit(solution)/shard_map/ppermute | solution.py:34
  157.1 15.2 %collective-permute-start.4 = (f32[129,384]{1,0:T(8,128)}, f32[129,384]{1,0:T(8,128)}, u32[]{:S(2)}, u32[]{:S(2)}) collective-permute-start(f32[129,384]{1,0:T(8,128)} %get-tuple-element.23), channel_id=1, source_target_pairs={{0,3},{1,0},{2,1},{3,2},{4,7},{5,4},{6,5},{7,6},{8,11},{9,8},{10,9... | collective-permute-start | bytes 594440 | tf_op jit(solution)/shard_map/ppermute | solution.py:34
  177.1 2.5 %copy-start.7 = (f32[4,256,128]{2,1,0:T(8,128)S(1)}, f32[4,256,128]{2,1,0:T(8,128)}, u32[]{:S(2)}) copy-start(f32[4,256,128]{2,1,0:T(8,128)} %convolution_bitcast_fusion) | copy-start | bytes 1572868
  182.4 1.1 copy-start.1
  183.5 1.4 copy-start.2
  184.9 1.1 copy-start.3
  186.1 1.0 copy-start.4
  187.1 0.9 copy-start.5
  188.0 0.9 copy-start.6
Sparse Core Ops, SparseCore 0:
  8.9 66.1 all-gather.2
  153.4 28.9 all-gather.4

commit v9 on v8

--- a/solution.py
+++ b/solution.py
@@ -126,46 +126,45 @@
     tables, rows, lanes = carried_ref.shape
     block_total = resp_ref.shape[0]
     cols_hi, cols_lo = split_bf16(out_cols_ref[...])
+    cols = jnp.concatenate([cols_hi, cols_lo, cols_hi], axis=0)
+
+    def dot(a, b):
+        return jnp.dot(a, b, preferred_element_type=jnp.float32)
 
     def fill(block, carry):
-        basis_hi = basis_ref[0, block]
-        resp_ref[block] = (
-            jnp.dot(basis_hi, cols_hi, preferred_element_type=jnp.float32)
-            + jnp.dot(basis_hi, cols_lo, preferred_element_type=jnp.float32)
-            + jnp.dot(basis_ref[1, block], cols_hi, preferred_element_type=jnp.float32)
-        )
+        resp_ref[block] = dot(basis_ref[block], cols)
         return carry
 
     lax.fori_loop(0, block_total, fill, 0)
     first = lax.broadcasted_iota(jnp.int32, (rows, lanes), 0) == 0
-    fwd_hi = fwd_ref[0]
-    fwd_lo = fwd_ref[1]
-
-    def dot(a, b):
-        return jnp.dot(a, b, preferred_element_type=jnp.float32)
+    fwd = fwd_ref[...]
+    inv = inv_ref[...]
 
     for table in range(tables):
 
         def one_block(block, acc):
-            acc_real, acc_imag = acc
+            acc_real, acc_imag, edge = acc
             block_rows = piece_ref[table, pl.ds(pl.multiple_of(block * rows, rows), rows), :]
-            signal = dot(fwd_hi, block_rows) + dot(fwd_lo, block_rows)
+            signal = dot(fwd, jnp.concatenate([block_rows, block_rows], axis=0))
             response = resp_ref[block]
             resp_real = response[:rows]
             resp_imag = response[rows:]
             sig_real = signal[:rows]
             sig_imag = signal[rows:]
-            cross = resp_imag * sig_imag
-            acc_real = acc_real + (resp_real * sig_real - jnp.where(first, 0.0, cross))
-            acc_imag = acc_imag + jnp.where(first, cross, resp_real * sig_imag + resp_imag * sig_real)
-            return acc_real, acc_imag
+            acc_real = acc_real + (resp_real * sig_real - resp_imag * sig_imag)
+            acc_imag = acc_imag + (resp_real * sig_imag + resp_imag * sig_real)
+            edge = edge + resp_imag[0:1] * sig_imag[0:1]
+            return acc_real, acc_imag, edge
 
         zeros = jnp.zeros((rows, lanes), jnp.float32)
-        acc_real, acc_imag = lax.fori_loop(0, block_total, one_block, (zeros, zeros))
+        acc_real, acc_imag, edge = lax.fori_loop(
+            0, block_total, one_block, (zeros, zeros, jnp.zeros((1, lanes), jnp.float32))
+        )
+        acc_real = acc_real + jnp.where(first, edge, 0.0)
+        acc_imag = jnp.where(first, edge, acc_imag)
         spectrum = jnp.concatenate([acc_real, acc_imag], axis=0)
         spec_hi, spec_lo = split_bf16(spectrum)
-        inv_hi = inv_ref[0]
-        conv = dot(inv_hi, spec_hi) + dot(inv_hi, spec_lo) + dot(inv_ref[1], spec_hi)
+        conv = dot(inv, jnp.concatenate([spec_hi, spec_lo, spec_hi], axis=0))
         gated = query_ref[table] * (conv + skip_ref[...] * carried_ref[table].astype(jnp.float32))
         out_ref[table] = gated.astype(out_ref.dtype)
 
@@ -173,22 +172,25 @@
 def fused_conv(piece, basis_spec, out_cols, query_gate, carried, skip):
     tables, rows, width = carried.shape
     block_total = basis_spec.shape[0]
-    basis = jnp.stack(split_bf16(basis_spec))
+    basis_hi, basis_lo = split_bf16(basis_spec)
+    basis = jnp.concatenate([basis_hi, basis_hi, basis_lo], axis=2)
     fwd, inv = dft_tables(rows)
-    lanes = 256 if width % 256 == 0 else width
+    fwd = np.concatenate([fwd[0], fwd[1]], axis=1)
+    inv = np.concatenate([inv[0], inv[0], inv[1]], axis=1)
+    lanes = 768 if width % 768 == 0 else width
     tile3 = lambda i: (0, 0, i)
     return pl.pallas_call(
         conv_kernel,
         grid=(width // lanes,),
         in_specs=[
             pl.BlockSpec((tables, piece.shape[1], lanes), tile3),
-            pl.BlockSpec(basis.shape, lambda i: (0, 0, 0, 0)),
+            pl.BlockSpec(basis.shape, lambda i: (0, 0, 0)),
             pl.BlockSpec((out_cols.shape[0], lanes), lambda i: (0, i)),
             pl.BlockSpec((tables, rows, lanes), tile3),
             pl.BlockSpec((tables, rows, lanes), tile3),
             pl.BlockSpec((1, lanes), lambda i: (0, i)),
-            pl.BlockSpec(fwd.shape, lambda i: (0, 0, 0)),
-            pl.BlockSpec(inv.shape, lambda i: (0, 0, 0)),
+            pl.BlockSpec(fwd.shape, lambda i: (0, 0)),
+            pl.BlockSpec(inv.shape, lambda i: (0, 0)),
         ],
         out_specs=pl.BlockSpec((tables, rows, lanes), tile3),
         out_shape=jax.ShapeDtypeStruct((tables, rows, width), jnp.bfloat16),

time: 220 us -> 210 us (0.955)
  Pallas kernels: 22.2 us -> 13.2 us
    pallas_call x1, Pallas kernels: 22.2 us -> 13.2 us  [fused_conv(): pl.pallas_call(conv_kernel, grid=(width // lanes,), in_specs=[pl.BlockSpe...]
  transfers between devices with their start and end apart: 8 -> 8, of which waited for: 6 -> 6; matrix products, arithmetic and copies ran while one was open for 8% -> 9% of each run, Pallas kernels for 0% -> 0%
where the time goes in v9:
time: 210 us; the launch traced here: 209 us
  waiting for transfers between devices  135 us (64%)
  between operations  13.6 us (6%)
  Pallas kernels  13.2 us (6%)
  matrix products  13 us (6%)
  local copies, waits for them, and re-layouts  12.6 us (6%)
  other arithmetic  12.3 us (6%)
  starting transfers between devices  9.28 us (4%)
    all_gather x1, waiting for transfers between devices, shards(): group_tokens = lax.all_gather(tokens, 'fsdp', axis=0, tiled=True)  60.9 us
    all_to_all x1, waiting for transfers between devices, shards(): projected = lax.all_to_all(partial, 'fsdp', 0, 2, tiled=True)  54 us
    pallas_call x1, Pallas kernels, fused_conv(): pl.pallas_call(conv_kernel, grid=(width // lanes,), in_specs=[pl.BlockSpe...  13.2 us
    ppermute x3, waiting for transfers between devices, gather_by_permutes(): lax.ppermute(values, axis, [(i, (i + shift) % count) for i in range(count)])  12.5 us
    dot_general x1, matrix products, shards(): jnp.dot(group_tokens.reshape(group_rows * block_len, width), in_weight, p...  7.52 us
    unnamed x26, local copies, waits for them, and re-layouts  6.73 us
    all_to_all x1, starting transfers between devices, shards(): projected = lax.all_to_all(partial, 'fsdp', 0, 2, tiled=True)  4.62 us
  transfers between devices with their start and end apart: 8, of which 6 were waited for; matrix products, arithmetic and copies ran while one was open for 9% of the time, Pallas kernels for 0%

profile of v9, /device:TPU:0, one launch (start us, length us, event | category | flops | bytes accessed | tf_op | source)
XLA Modules:
  0.0 209.0 jit_solution(12131780783020043747)
XLA Ops:
  6.5 0.7 all-gather.3.cloned.1.call-update
  7.3 0.1 fusion.27
  7.4 0.1 fusion.30
  7.5 0.1 convert_bitcast_fusion
  7.6 0.6 fusion.26
  8.2 2.0 fusion.3
  10.1 2.0 broadcast_multiply_fusion.1
  12.2 0.5 negate_select_fusion.2
  12.8 1.4 convolution_bitcast_fusion
  14.2 60.9 %all-gather.3.cloned.1.call-done = bf16[8,128,1536]{2,1,0:T(8,128)(2,1)} async-done(((bf16[2,128,1536]{2,1,0:T(8,128)(2,1)}), bf16[8,128,1536]{2,1,0:T(8,128)(2,1)}) %all-gather.3.cloned.1.call-update) | async-done | bytes 3145744 | tf_op jit(solution)/shard_map/all_gather | solution.py:240
  75.2 7.5 %convolution_convert_fusion = bf16[1024,1152]{1,0:T(8,128)(2,1)} fusion(bf16[1024,1536]{1,0:T(8,128)(2,1)} %bitcast.56, bf16[1536,1152]{1,0:T(8,128)(2,1)S(1)} %copy-done), kind=kOutput, calls=%fused_computation.2 | convolution fusion | flops 3625058304 | bytes 9043968 | tf_op jit(solution)/shard_map/dot_general | solution.py:244
  82.7 4.6 %all-to-all-start = ((bf16[8,128,1152]{2,1,0:T(8,128)(2,1)}), bf16[8,128,1152]{2,1,0:T(8,128)(2,1)}, u32[]{:S(2)}, u32[]{:S(2)}) async-start(bf16[8,128,1152]{2,1,0:T(8,128)(2,1)} %bitcast.49), calls=%async_computation | async-start | bytes 4718592 | tf_op jit(solution)/shard_map/all_to_all | solution.py:250
  87.3 0.0 all-gather.5.cloned.1.call-start
  87.4 0.1 compare_convert_fusion
  87.5 54.0 %all-to-all-done = bf16[8,128,1152]{2,1,0:T(8,128)(2,1)} async-done(((bf16[8,128,1152]{2,1,0:T(8,128)(2,1)}), bf16[8,128,1152]{2,1,0:T(8,128)(2,1)}, u32[]{:S(2)}, u32[]{:S(2)}) %all-to-all-start) | async-done | bytes 2359328 | tf_op jit(solution)/shard_map/all_to_all | solution.py:250
  141.4 1.9 copy.27
  143.4 0.1 fusion.41
  143.4 1.3 collective-permute-start
  144.7 1.3 collective-permute-start.1
  146.1 0.1 slice_reduce_fusion.2
  146.2 3.3 %collective-permute-done.1 = bf16[2,1,4608]{2,1,0:T(2,128)(2,1)S(1)} collective-permute-done((bf16[2,1,4608]{2,1,0:T(2,128)(2,1)S(1)}, bf16[2,1,4608]{2,1,0:T(2,128)(2,1)S(1)}, u32[]{:S(2)}, u32[]{:S(2)}) %collective-permute-start.1) | collective-permute-done | bytes 18464 | tf_op jit(solution)/shard_map/ppermute | solution.py:21
  149.6 1.9 multiply_add_fusion
  151.5 0.0 copy-start.9
  151.5 1.7 fusion.40
  153.2 0.0 all-gather.5.cloned.1.call-update
  153.3 1.8 fusion.39
  155.1 0.0 collective-permute-start.3
  155.1 1.5 collective-permute-start.4
  156.5 0.6 collective-permute-start.2
  157.1 0.8 sort.17
  157.9 10.9 %collective-permute-done.3 = f32[129,384]{1,0:T(8,128)} collective-permute-done((f32[129,384]{1,0:T(8,128)}, f32[129,384]{1,0:T(8,128)}, u32[]{:S(2)}, u32[]{:S(2)}) %collective-permute-start.3) | collective-permute-done | bytes 198176 | tf_op jit(solution)/shard_map/ppermute | solution.py:34
  168.8 0.0 collective-permute-done.4
  168.8 1.6 collective-permute-done.2
  170.4 2.2 %pad_maximum_fusion.2 = f32[4,129,384]{2,1,0:T(8,128)} fusion(f32[1,129,384]{2,1,0:T(8,128)} %bitcast.11, f32[1,129,384]{2,1,0:T(8,128)} %bitcast.10, f32[1,129,384]{2,1,0:T(8,128)} %bitcast.9, f32[1,129,384]{2,1,0:T(8,128)} %get-tuple-element.22), kind=kLoop, calls=%fused_computation.13 | loop fusion | flops 594432 | bytes 1585152 | tf_op jit(solution)/shard_map/stack | solution.py:36
  172.6 2.7 %gather_fusion = f32[4,129,384]{2,1,0:T(8,128)} fusion(f32[4,129,384]{2,1,0:T(8,128)} %pad_maximum_fusion.2, s32[1024]{0:T(1024)S(1)} %pad_clamp_fusion), kind=kCustom, calls=%fused_computation | custom fusion | bytes 1585168 | tf_op jit(solution)/shard_map/jit(_take)/gather | solution.py:39
  175.3 1.3 select_bitcast_fusion
  176.6 0.1 slice_bitcast_fusion
  176.7 1.0 copy.28
  177.7 0.1 subtract_convert_fusion
  177.8 1.0 pad_maximum_fusion.3.basis_ref
  178.7 3.7 %all-gather.5.cloned.1.call-done.piece_ref = bf16[2,512,1536]{2,1,0:T(8,128)(2,1)} async-done(((bf16[2,128,1536]{2,1,0:T(8,128)(2,1)}), bf16[2,512,1536]{2,1,0:T(8,128)(2,1)}) %all-gather.5.cloned.1.call-update) | async-done | bytes 3145744 | tf_op jit(solution)/shard_map/all_gather | solution.py:264
  182.4 1.1 copy-done.1
  183.5 1.4 copy-done.2
  184.9 1.1 copy-done.3
  186.1 1.1 copy-done.4
  187.2 0.9 copy-done.5
  188.1 0.9 copy-done.6
  189.0 13.2 %shard_map.121 = bf16[2,128,1536]{2,1,0:T(8,128)(2,1)} custom-call(bf16[2,512,1536]{2,1,0:T(8,128)(2,1)} %all-gather.5.cloned.1.call-done.piece_ref, bf16[4,256,384]{2,1,0:T(8,128)(2,1)S(1)} %copy-done.4, f32[128,1536]{1,0:T(8,128)S(1)} %bitcast.45, f32[2,128,1536]{2,1,0:T(8,128)S(1)} %copy-done.2, bf16[2,128,1536]{2,1,0:T(8,128)(2,1)S(1)} %copy-done.1, ...), custom_call_target="tpu_custom_call" | custom-call | tf_op jit(solution)/shard_map/pallas_call | solution.py:182
  (35 shorter events, 0.2 us)
Async XLA Ops:
  6.5 68.6 %copy-start = (bf16[1536,1152]{1,0:T(8,128)(2,1)S(1)}, bf16[1536,1152]{1,0:T(8,128)(2,1)}, u32[]{:S(2)}) copy-start(bf16[1536,1152]{1,0:T(8,128)(2,1)} %param.13) | copy-start | bytes 10616836
  6.5 68.6 %all-gather.3.cloned.1.call-start = ((), (), s32[]{:S(2)}) async-start(), calls=%async_computation.1 | async-start | bytes 3932160 | tf_op jit(solution)/shard_map/all_gather | solution.py:240
  82.7 4.7 %copy-start.10 = (s32[2,1]{0,1:T(1,128)S(1)}, s32[2,1]{0,1:T(1,128)}, u32[]{:S(2)}) copy-start(s32[2,1]{0,1:T(1,128)} %param.21) | copy-start | bytes 28
  82.7 58.7 %all-to-all-start = ((bf16[8,128,1152]{2,1,0:T(8,128)(2,1)}), bf16[8,128,1152]{2,1,0:T(8,128)(2,1)}, u32[]{:S(2)}, u32[]{:S(2)}) async-start(bf16[8,128,1152]{2,1,0:T(8,128)(2,1)} %bitcast.49), calls=%async_computation | async-start | bytes 4718592 | tf_op jit(solution)/shard_map/all_to_all | solution.py:250
  87.3 95.1 %all-gather.5.cloned.1.call-start = ((), (), s32[]{:S(2)}) async-start(), calls=%async_computation.2 | async-start | bytes 3932160 | tf_op jit(solution)/shard_map/all_gather | solution.py:264
  141.4 4.6 %copy-start.8 = (f32[3,4608]{1,0:T(4,128)S(1)}, f32[3,4608]{1,0:T(4,128)}, u32[]{:S(2)}) copy-start(f32[3,4608]{1,0:T(4,128)} %param.14) | copy-start | bytes 165892
  143.4 2.8 %collective-permute-start = (bf16[2,1,4608]{2,1,0:T(2,128)(2,1)S(1)}, bf16[2,1,4608]{2,1,0:T(2,128)(2,1)S(1)}, u32[]{:S(2)}, u32[]{:S(2)}) collective-permute-start(bf16[2,1,4608]{2,1,0:T(2,128)(2,1)S(1)} %get-tuple-element.18), channel_id=1, source_target_pairs={{0,4},{4,8},{8,12},{1,5},{5,9},{9,13},{2,6},{6,10},{10,14},{3,7},{... | collective-permute-start | bytes 55304 | tf_op jit(solution)/shard_map/ppermute | solution.py:19
  144.7 4.8 %collective-permute-start.1 = (bf16[2,1,4608]{2,1,0:T(2,128)(2,1)S(1)}, bf16[2,1,4608]{2,1,0:T(2,128)(2,1)S(1)}, u32[]{:S(2)}, u32[]{:S(2)}) collective-permute-start(bf16[2,1,4608]{2,1,0:T(2,128)(2,1)S(1)} %get-tuple-element.19), channel_id=1, source_target_pairs={{4,0},{8,4},{12,8},{5,1},{9,5},{13,9},{6,2},{10,6},{14,10},{7,3},{... | collective-permute-start | bytes 55304 | tf_op jit(solution)/shard_map/ppermute | solution.py:21
  151.5 1.8 copy-start.9
  155.1 13.7 %collective-permute-start.3 = (f32[129,384]{1,0:T(8,128)}, f32[129,384]{1,0:T(8,128)}, u32[]{:S(2)}, u32[]{:S(2)}) collective-permute-start(f32[129,384]{1,0:T(8,128)} %get-tuple-element.23), channel_id=1, source_target_pairs={{0,2},{1,3},{2,0},{3,1},{4,6},{5,7},{6,4},{7,5},{8,10},{9,11},{10,... | collective-permute-start | bytes 594440 | tf_op jit(solution)/shard_map/ppermute | solution.py:34
  155.1 13.7 %collective-permute-start.4 = (f32[129,384]{1,0:T(8,128)}, f32[129,384]{1,0:T(8,128)}, u32[]{:S(2)}, u32[]{:S(2)}) collective-permute-start(f32[129,384]{1,0:T(8,128)} %get-tuple-element.23), channel_id=1, source_target_pairs={{0,3},{1,0},{2,1},{3,2},{4,7},{5,4},{6,5},{7,6},{8,11},{9,8},{10,9... | collective-permute-start | bytes 594440 | tf_op jit(solution)/shard_map/ppermute | solution.py:34
  156.5 13.9 %collective-permute-start.2 = (f32[129,384]{1,0:T(8,128)}, f32[129,384]{1,0:T(8,128)}, u32[]{:S(2)}, u32[]{:S(2)}) collective-permute-start(f32[129,384]{1,0:T(8,128)} %get-tuple-element.23), channel_id=1, source_target_pairs={{0,1},{1,2},{2,3},{3,0},{4,5},{5,6},{6,7},{7,4},{8,9},{9,10},{10,1... | collective-permute-start | bytes 594440 | tf_op jit(solution)/shard_map/ppermute | solution.py:34
  175.3 2.4 %copy-start.7 = (f32[4,256,128]{2,1,0:T(8,128)S(1)}, f32[4,256,128]{2,1,0:T(8,128)}, u32[]{:S(2)}) copy-start(f32[4,256,128]{2,1,0:T(8,128)} %convolution_bitcast_fusion) | copy-start | bytes 1572868
  182.4 1.1 copy-start.1
  183.5 1.4 copy-start.2
  184.9 1.1 copy-start.3
  186.1 1.1 copy-start.4
  187.2 0.9 copy-start.5
  188.1 0.9 copy-start.6
Sparse Core Ops, SparseCore 0:
  8.9 66.1 all-gather.2
  153.4 28.9 all-gather.4

commit v10 on v9

--- a/solution.py
+++ b/solution.py
@@ -216,10 +216,13 @@
     params = jnp.concatenate(
         [response_out.reshape(2 * response_out.shape[1], local_ch), skip_gain[None, :]], axis=0
     )
-    gathered = gather_by_permutes(params, "fsdp")
-    gathered = jnp.transpose(gathered, (1, 0, 2)).reshape(params.shape[0], width)
-    stacked_out = gathered[:-1]
-    full_skip = gathered[-1]
+    parts = lax.axis_size("groups") * lax.axis_size("seq")
+    part = lax.axis_index("groups") * lax.axis_size("seq") + lax.axis_index("seq")
+    part_cols = local_ch // parts
+    mine = lax.dynamic_slice_in_dim(params, part * part_cols, part_cols, axis=1)
+    across = lax.all_gather(mine, "fsdp", axis=0, tiled=False)
+    gathered = lax.all_gather(across, ("groups", "seq"), axis=0, tiled=False)
+    gathered = jnp.transpose(gathered, (2, 1, 0, 3)).reshape(params.shape[0], width)
     seq_count = lax.axis_size("seq")
     position = lax.axis_index("seq")
     total_len = float(seq_count * block_len)
@@ -238,7 +241,9 @@
     paired = paired.reshape(block_total, 2 * block_len, paired.shape[-1])
     basis_spec = jnp.einsum("gf,bfk->bgk", forward, paired, precision=lax.Precision.HIGHEST)
     group_tokens = lax.all_gather(tokens, "fsdp", axis=0, tiled=True)
-    group_tokens, basis_spec = lax.optimization_barrier((group_tokens, basis_spec))
+    group_tokens, basis_spec, gathered = lax.optimization_barrier((group_tokens, basis_spec, gathered))
+    stacked_out = gathered[:-1]
+    full_skip = gathered[-1]
     group_rows = group_tokens.shape[0]
     local_cols = in_weight.shape[1]
     partial = jnp.dot(

time: 210 us -> 211 us (level)
  waiting for transfers between devices: 135 us -> 102 us
  blocking collectives: 0 us -> 30.2 us
  local copies, waits for them, and re-layouts: 12.6 us -> 22.2 us
  other arithmetic: 12.3 us -> 8.67 us
    all_gather x1, waiting for transfers between devices: 60.9 us -> 20.3 us  [shards(): group_tokens = lax.all_gather(tokens, 'fsdp', axis=0, tiled=True)]
    all_gather x0 -> x2, blocking collectives: none -> 30.2 us  [the longest x1 16.3 us: shards(): across = lax.all_gather(mine, 'fsdp', axis=0, tiled=False)]
    all_gather x1, waiting for transfers between devices: 3.65 us -> 24 us  [shards(): piece = lax.all_gather(carried, 'seq', axis=1, tiled=True)]
    ppermute x3 -> x0, waiting for transfers between devices: 12.5 us -> none  [gather_by_permutes(): lax.ppermute(values, axis, [(i, (i + shift) % count) for i in range(count)])]
    reshape x0 -> x2, local copies, waits for them, and re-layouts: none -> 5.31 us  [the longest x1 3.57 us: shards(): jnp.transpose(gathered, (2, 1, 0, 3)).reshape(params.shape[0], width)]
    another operation x2 -> x0, other arithmetic: 3.97 us -> none  [gather_by_permutes(): stacked = jnp.stack(received)]
    transpose x0 -> x1, local copies, waits for them, and re-layouts: none -> 3.59 us  [shards(): jnp.transpose(gathered, (2, 1, 0, 3)).reshape(params.shape[0], width)]
    gather x1 -> x0, local copies, waits for them, and re-layouts: 2.69 us -> none  [gather_by_permutes(): return jnp.take(stacked, order, axis=0)]
  transfers between devices with their start and end apart: 8 -> 5, of which waited for: 6 -> 4; matrix products, arithmetic and copies ran while one was open for 9% -> 11% of each run, Pallas kernels for 0% -> 0%
where the time goes in v10:
time: 211 us
  waiting for transfers between devices  102 us (48%)
  blocking collectives  30.2 us (14%)
  local copies, waits for them, and re-layouts  22.2 us (11%)
  between operations  13.6 us (6%)
  Pallas kernels  13.2 us (6%)
  matrix products  13 us (6%)
  other arithmetic  8.67 us (4%)
  starting transfers between devices  7.44 us (4%)
    all_to_all x1, waiting for transfers between devices, shards(): projected = lax.all_to_all(partial, 'fsdp', 0, 2, tiled=True)  54.2 us
    all_gather x1, waiting for transfers between devices, shards(): piece = lax.all_gather(carried, 'seq', axis=1, tiled=True)  24 us
    all_gather x1, waiting for transfers between devices, shards(): group_tokens = lax.all_gather(tokens, 'fsdp', axis=0, tiled=True)  20.3 us
    all_gather x1, blocking collectives, shards(): across = lax.all_gather(mine, 'fsdp', axis=0, tiled=False)  16.3 us
    all_gather x1, blocking collectives, shards(): gathered = lax.all_gather(across, ('groups', 'seq'), axis=0, tiled=False)  13.9 us
    pallas_call x1, Pallas kernels, fused_conv(): pl.pallas_call(conv_kernel, grid=(width // lanes,), in_specs=[pl.BlockSpe...  13.2 us
    dot_general x1, matrix products, shards(): jnp.dot(group_tokens.reshape(group_rows * block_len, width), in_weight, p...  7.56 us
    unnamed x23, local copies, waits for them, and re-layouts  6.67 us
  transfers between devices with their start and end apart: 5, of which 4 were waited for; matrix products, arithmetic and copies ran while one was open for 11% of the time, Pallas kernels for 0%

profile of v10, /device:TPU:0, one launch (start us, length us, event | category | flops | bytes accessed | tf_op | source)
XLA Modules:
  0.0 210.6 jit_solution(7900415473495406285)
XLA Ops:
  6.5 0.0 copy-start
  6.5 0.0 all-gather.6.cloned.1.call-start
  6.5 0.7 all-gather.6.cloned.1.call-update
  7.3 0.1 fusion.29
  7.4 0.1 fusion.32
  7.5 0.1 convert_bitcast_fusion
  7.5 1.5 broadcast_in_dim.25
  9.1 1.7 copy.31
  10.8 0.8 fusion.21
  11.6 16.3 %all-gather.2 = f32[4,129,48]{1,2,0:T(8,128)S(1)} all-gather(f32[1,129,48]{1,2,0:T(8,128)S(1)} %fusion.21), channel_id=2, replica_groups=mesh['groups'=2,'seq'=4,'fsdp'=4] {'fsdp'}, dimensions={0}, use_global_device_ids=true | all-gather | bytes 123840 | tf_op jit(solution)/shard_map/all_gather | solution.py:223
  27.9 13.9 %all-gather.1 = f32[32,129,48]{1,2,0:T(8,128)} all-gather(f32[4,129,48]{1,2,0:T(8,128)S(1)} %all-gather.2), channel_id=3, replica_groups=mesh['groups'=2,'seq'=4,'fsdp'=4] {'groups','seq'}, dimensions={0}, use_global_device_ids=true | all-gather | bytes 891648 | tf_op jit(solution)/shard_map/all_gather | solution.py:224
  41.8 3.6 %copy.33 = f32[129,4,8,48]{3,2,1,0:T(8,128)} copy(f32[129,4,8,48]{0,3,1,2:T(8,128)} %bitcast.43) | data formatting | bytes 1585152 | tf_op jit(solution)/shard_map/transpose | solution.py:225
  45.3 3.6 %reshape.191 = f32[129,1536]{1,0:T(8,128)} reshape(f32[129,4,8,48]{3,2,1,0:T(8,128)} %copy.33) | data formatting | bytes 1585152 | tf_op jit(solution)/shard_map/reshape | solution.py:225
  49.0 0.5 fusion.19
  49.5 0.6 fusion.28
  50.0 2.0 fusion.3
  52.0 2.0 broadcast_multiply_fusion.1
  54.1 0.5 negate_select_fusion.2
  54.6 1.4 convolution_bitcast_fusion
  56.1 20.3 %all-gather.6.cloned.1.call-done = bf16[8,128,1536]{2,1,0:T(8,128)(2,1)} async-done(((bf16[2,128,1536]{2,1,0:T(8,128)(2,1)}), bf16[8,128,1536]{2,1,0:T(8,128)(2,1)}) %all-gather.6.cloned.1.call-update) | async-done | bytes 3145744 | tf_op jit(solution)/shard_map/all_gather | solution.py:243
  76.4 7.6 %convolution_convert_fusion = bf16[1024,1152]{1,0:T(8,128)(2,1)} fusion(bf16[1024,1536]{1,0:T(8,128)(2,1)} %bitcast.51, bf16[1536,1152]{1,0:T(8,128)(2,1)S(1)} %copy-done), kind=kOutput, calls=%fused_computation.1 | convolution fusion | flops 3625058304 | bytes 9043968 | tf_op jit(solution)/shard_map/dot_general | solution.py:249
  83.9 4.6 %all-to-all-start = ((bf16[8,128,1152]{2,1,0:T(8,128)(2,1)}), bf16[8,128,1152]{2,1,0:T(8,128)(2,1)}, u32[]{:S(2)}, u32[]{:S(2)}) async-start(bf16[8,128,1152]{2,1,0:T(8,128)(2,1)} %bitcast.44), calls=%async_computation | async-start | bytes 4718592 | tf_op jit(solution)/shard_map/all_to_all | solution.py:255
  88.6 0.0 all-gather.8.cloned.1.call-start
  88.6 0.0 copy-done.9
  88.6 0.1 compare_convert_fusion
  88.7 54.2 %all-to-all-done = bf16[8,128,1152]{2,1,0:T(8,128)(2,1)} async-done(((bf16[8,128,1152]{2,1,0:T(8,128)(2,1)}), bf16[8,128,1152]{2,1,0:T(8,128)(2,1)}, u32[]{:S(2)}, u32[]{:S(2)}) %all-to-all-start) | async-done | bytes 2359328 | tf_op jit(solution)/shard_map/all_to_all | solution.py:255
  142.9 1.9 copy.37
  144.9 0.1 fusion.41
  144.9 1.3 collective-permute-start
  146.2 1.5 collective-permute-start.1
  147.7 0.1 slice_reduce_fusion.2
  147.9 0.0 collective-permute-done
  147.9 3.2 %collective-permute-done.1 = bf16[2,1,4608]{2,1,0:T(2,128)(2,1)S(1)} collective-permute-done((bf16[2,1,4608]{2,1,0:T(2,128)(2,1)S(1)}, bf16[2,1,4608]{2,1,0:T(2,128)(2,1)S(1)}, u32[]{:S(2)}, u32[]{:S(2)}) %collective-permute-start.1) | collective-permute-done | bytes 18464 | tf_op jit(solution)/shard_map/ppermute | solution.py:21
  151.0 1.9 multiply_add_fusion
  153.0 1.7 fusion.40
  154.7 0.0 all-gather.8.cloned.1.call-update
  154.7 2.1 %slice.47.out_cols_ref = f32[128,1536]{1,0:T(8,128)} slice(f32[129,1536]{1,0:T(8,128)} %reshape.191), slice={[0:128], [0:1536]} | slice | bytes 1572864 | tf_op jit(solution)/shard_map/slice | solution.py:245
  156.9 0.8 slice.49.skip_ref
  157.7 1.3 subtract_convert_fusion
  159.0 1.0 pad_maximum_fusion.2.basis_ref
  160.0 24.0 %all-gather.8.cloned.1.call-done.piece_ref = bf16[2,512,1536]{2,1,0:T(8,128)(2,1)} async-done(((bf16[2,128,1536]{2,1,0:T(8,128)(2,1)}), bf16[2,512,1536]{2,1,0:T(8,128)(2,1)}) %all-gather.8.cloned.1.call-update) | async-done | bytes 3145744 | tf_op jit(solution)/shard_map/all_gather | solution.py:269
  183.9 1.1 copy-done.1
  185.0 1.4 copy-done.2
  186.5 1.1 copy-done.3
  187.6 1.1 copy-done.4
  188.7 0.9 copy-done.5
  189.7 0.9 copy-done.6
  190.6 13.2 %shard_map.121 = bf16[2,128,1536]{2,1,0:T(8,128)(2,1)} custom-call(bf16[2,512,1536]{2,1,0:T(8,128)(2,1)} %all-gather.8.cloned.1.call-done.piece_ref, bf16[4,256,384]{2,1,0:T(8,128)(2,1)S(1)} %copy-done.4, f32[128,1536]{1,0:T(8,128)S(1)} %copy-done.3, f32[2,128,1536]{2,1,0:T(8,128)S(1)} %copy-done.2, bf16[2,128,1536]{2,1,0:T(8,128)(2,1)S(1)} %copy-done.1, ...), custom_call_target="tpu_custom_call" | custom-call | tf_op jit(solution)/shard_map/pallas_call | solution.py:182
  (23 shorter events, 0.1 us)
Async XLA Ops:
  6.5 69.8 %copy-start = (bf16[1536,1152]{1,0:T(8,128)(2,1)S(1)}, bf16[1536,1152]{1,0:T(8,128)(2,1)}, u32[]{:S(2)}) copy-start(bf16[1536,1152]{1,0:T(8,128)(2,1)} %param.13) | copy-start | bytes 10616836
  6.5 69.8 %all-gather.6.cloned.1.call-start = ((), (), s32[]{:S(2)}) async-start(), calls=%async_computation.1 | async-start | bytes 3932160 | tf_op jit(solution)/shard_map/all_gather | solution.py:243
  41.8 8.3 %copy-start.8 = (f32[64]{0:T(128)S(1)}, f32[64]{0:T(128)}, u32[]{:S(2)}) copy-start(f32[64]{0:T(128)} %param.16) | copy-start | bytes 772
  83.9 4.7 %copy-start.9 = (s32[2,1]{0,1:T(1,128)S(1)}, s32[2,1]{0,1:T(1,128)}, u32[]{:S(2)}) copy-start(s32[2,1]{0,1:T(1,128)} %param.21) | copy-start | bytes 28
  83.9 59.0 %all-to-all-start = ((bf16[8,128,1152]{2,1,0:T(8,128)(2,1)}), bf16[8,128,1152]{2,1,0:T(8,128)(2,1)}, u32[]{:S(2)}, u32[]{:S(2)}) async-start(bf16[8,128,1152]{2,1,0:T(8,128)(2,1)} %bitcast.44), calls=%async_computation | async-start | bytes 4718592 | tf_op jit(solution)/shard_map/all_to_all | solution.py:255
  88.6 95.3 %all-gather.8.cloned.1.call-start = ((), (), s32[]{:S(2)}) async-start(), calls=%async_computation.2 | async-start | bytes 3932160 | tf_op jit(solution)/shard_map/all_gather | solution.py:269
  142.9 4.8 %copy-start.7 = (f32[3,4608]{1,0:T(4,128)S(1)}, f32[3,4608]{1,0:T(4,128)}, u32[]{:S(2)}) copy-start(f32[3,4608]{1,0:T(4,128)} %param.14) | copy-start | bytes 165892
  144.9 2.9 %collective-permute-start = (bf16[2,1,4608]{2,1,0:T(2,128)(2,1)S(1)}, bf16[2,1,4608]{2,1,0:T(2,128)(2,1)S(1)}, u32[]{:S(2)}, u32[]{:S(2)}) collective-permute-start(bf16[2,1,4608]{2,1,0:T(2,128)(2,1)S(1)} %get-tuple-element.18), channel_id=1, source_target_pairs={{0,4},{4,8},{8,12},{1,5},{5,9},{9,13},{2,6},{6,10},{10,14},{3,7},{... | collective-permute-start | bytes 55304 | tf_op jit(solution)/shard_map/ppermute | solution.py:19
  146.2 4.8 %collective-permute-start.1 = (bf16[2,1,4608]{2,1,0:T(2,128)(2,1)S(1)}, bf16[2,1,4608]{2,1,0:T(2,128)(2,1)S(1)}, u32[]{:S(2)}, u32[]{:S(2)}) collective-permute-start(bf16[2,1,4608]{2,1,0:T(2,128)(2,1)S(1)} %get-tuple-element.19), channel_id=1, source_target_pairs={{4,0},{8,4},{12,8},{5,1},{9,5},{13,9},{6,2},{10,6},{14,10},{7,3},{... | collective-permute-start | bytes 55304 | tf_op jit(solution)/shard_map/ppermute | solution.py:21
  183.9 1.1 copy-start.1
  185.0 1.4 copy-start.2
  186.5 1.1 copy-start.3
  187.6 1.1 copy-start.4
  188.7 0.9 copy-start.5
  189.7 0.9 copy-start.6
Sparse Core Ops, SparseCore 0:
  8.9 67.3 all-gather.5
  154.9 29.0 all-gather.7

commit v11 on v10

--- a/solution.py
+++ b/solution.py
@@ -244,31 +244,43 @@
     group_tokens, basis_spec, gathered = lax.optimization_barrier((group_tokens, basis_spec, gathered))
     stacked_out = gathered[:-1]
     full_skip = gathered[-1]
-    group_rows = group_tokens.shape[0]
     local_cols = in_weight.shape[1]
-    partial = jnp.dot(
-        group_tokens.reshape(group_rows * block_len, width),
-        in_weight,
-        preferred_element_type=jnp.float32,
-    ).astype(jnp.bfloat16)
-    partial = partial.reshape(group_rows, block_len, local_cols)
-    projected = lax.all_to_all(partial, "fsdp", 0, 2, tiled=True)
-    padded = padded_2(projected, (("seq", 1),), 1)
-    shorted = (
-        short_weight[0] * padded[:, :-2]
-        + short_weight[1] * padded[:, 1:-1]
-        + short_weight[2] * padded[:, 2:]
-    )
-    query_gate = shorted[:, :, :width]
-    key_part = shorted[:, :, width : 2 * width]
-    value_part = shorted[:, :, 2 * width :]
-    valid_mask = (jnp.arange(block_len, dtype=jnp.int32)[None, :] < block_counts).astype(
-        jnp.float32
-    )
-    carried = (key_part * value_part * valid_mask[:, :, None]).astype(jnp.bfloat16)
-    piece = lax.all_gather(carried, "seq", axis=1, tiled=True)
-
-    return fused_conv(piece, basis_spec, stacked_out, query_gate, carried, full_skip)
+    fsdp_count = lax.axis_size("fsdp")
+    grouped = group_tokens.reshape(fsdp_count, seq_dev, block_len, width)
+    partials = []
+    for table in range(seq_dev):
+        partial = jnp.dot(
+            grouped[:, table].reshape(fsdp_count * block_len, width),
+            in_weight,
+            preferred_element_type=jnp.float32,
+        ).astype(jnp.bfloat16)
+        partials.append(partial.reshape(fsdp_count, block_len, local_cols))
+    outputs = []
+    previous = None
+    for table in range(seq_dev):
+        partial = partials[table]
+        if previous is not None:
+            partial, previous = lax.optimization_barrier((partial, previous))
+        projected = lax.all_to_all(partial, "fsdp", 0, 2, tiled=True)
+        if outputs:
+            projected, outputs[-1] = lax.optimization_barrier((projected, outputs[-1]))
+        padded = padded_2(projected, (("seq", 1),), 1)
+        shorted = (
+            short_weight[0] * padded[:, :-2]
+            + short_weight[1] * padded[:, 1:-1]
+            + short_weight[2] * padded[:, 2:]
+        )
+        query_gate = shorted[:, :, :width]
+        key_part = shorted[:, :, width : 2 * width]
+        value_part = shorted[:, :, 2 * width :]
+        valid_mask = (
+            jnp.arange(block_len, dtype=jnp.int32)[None, :] < block_counts[table : table + 1]
+        ).astype(jnp.float32)
+        carried = (key_part * value_part * valid_mask[:, :, None]).astype(jnp.bfloat16)
+        piece = lax.all_gather(carried, "seq", axis=1, tiled=True)
+        previous = carried
+        outputs.append(fused_conv(piece, basis_spec, stacked_out, query_gate, carried, full_skip))
+    return jnp.concatenate(outputs, axis=0)
 
 
 def solution(mesh):

time: 211 us -> 233 us (1.10)
  local copies, waits for them, and re-layouts: 22.2 us -> 38.1 us
  starting transfers between devices: 7.44 us -> 15.6 us
  waiting for transfers between devices: 102 us -> 94.7 us
  other arithmetic: 8.67 us -> 11.2 us
    unnamed x23 -> x55, local copies, waits for them, and re-layouts: 6.67 us -> 15.3 us
    all_gather x1 -> x2, waiting for transfers between devices: 24 us -> 19.6 us  [shards(): piece = lax.all_gather(carried, 'seq', axis=1, tiled=True)]
    all_to_all x1 -> x2, starting transfers between devices: 4.64 us -> 8.7 us  [shards(): projected = lax.all_to_all(partial, 'fsdp', 0, 2, tiled=True)]
    all_to_all x1 -> x2, waiting for transfers between devices: 54.2 us -> 50.3 us  [shards(): projected = lax.all_to_all(partial, 'fsdp', 0, 2, tiled=True)]
    slice x0 -> x2, local copies, waits for them, and re-layouts: none -> 3.84 us  [the longest x1 3.23 us: shards(): grouped[:, table].reshape(fsdp_count * block_len, width)]
    ppermute x1 -> x2, starting transfers between devices: 1.29 us -> 4.09 us  [padded_2(): lax.ppermute(tail, axis, [(i, (i + 1) % count) for i in range(ends)])]
    pallas_call x1 -> x2, Pallas kernels: 13.2 us -> 14.6 us  [fused_conv(): pl.pallas_call(conv_kernel, grid=(width // lanes,), in_specs=[pl.BlockSpe...]
    dot_general x1 -> x2, matrix products: 7.56 us -> 7.93 us  [shards(): jnp.dot(grouped[:, table].reshape(fsdp_count * block_len, width), in_weig...]
  transfers between devices with their start and end apart: 5 -> 9, of which waited for: 4 -> 6; matrix products, arithmetic and copies ran while one was open for 11% -> 15% of each run, Pallas kernels for 0% -> 0%
where the time goes in v11:
time: 233 us; the launch traced here: 231 us
  waiting for transfers between devices  94.7 us (41%)
  local copies, waits for them, and re-layouts  38.1 us (16%)
  blocking collectives  30.2 us (13%)
  starting transfers between devices  15.6 us (7%)
  Pallas kernels  14.6 us (6%)
  matrix products  13.4 us (6%)
  between operations  13.4 us (6%)
  other arithmetic  11.2 us (5%)
    all_to_all x2, waiting for transfers between devices, shards(): projected = lax.all_to_all(partial, 'fsdp', 0, 2, tiled=True)  50.3 us
    all_gather x1, waiting for transfers between devices, shards(): group_tokens = lax.all_gather(tokens, 'fsdp', axis=0, tiled=True)  20.3 us
    all_gather x2, waiting for transfers between devices, shards(): piece = lax.all_gather(carried, 'seq', axis=1, tiled=True)  19.6 us
    all_gather x1, blocking collectives, shards(): across = lax.all_gather(mine, 'fsdp', axis=0, tiled=False)  16.3 us
    unnamed x55, local copies, waits for them, and re-layouts  15.3 us
    pallas_call x2, Pallas kernels, fused_conv(): pl.pallas_call(conv_kernel, grid=(width // lanes,), in_specs=[pl.BlockSpe...  14.6 us
    all_gather x1, blocking collectives, shards(): gathered = lax.all_gather(across, ('groups', 'seq'), axis=0, tiled=False)  13.9 us
    all_to_all x2, starting transfers between devices, shards(): projected = lax.all_to_all(partial, 'fsdp', 0, 2, tiled=True)  8.7 us
  transfers between devices with their start and end apart: 9, of which 6 were waited for; matrix products, arithmetic and copies ran while one was open for 15% of the time, Pallas kernels for 0%

profile of v11, /device:TPU:0, one launch (start us, length us, event | category | flops | bytes accessed | tf_op | source)
XLA Modules:
  0.0 231.3 jit_solution(11817286441370245666)
XLA Ops:
  7.5 1.5 broadcast_in_dim.25
  9.1 1.7 copy.37
  11.6 16.3 %all-gather.2 = f32[4,129,48]{1,2,0:T(8,128)S(1)} all-gather(f32[1,129,48]{1,2,0:T(8,128)S(1)} %fusion.23), channel_id=2, replica_groups=mesh['groups'=2,'seq'=4,'fsdp'=4] {'fsdp'}, dimensions={0}, use_global_device_ids=true | all-gather | bytes 123840 | tf_op jit(solution)/shard_map/all_gather | solution.py:223
  27.9 13.9 %all-gather.1 = f32[32,129,48]{1,2,0:T(8,128)} all-gather(f32[4,129,48]{1,2,0:T(8,128)S(1)} %all-gather.2), channel_id=3, replica_groups=mesh['groups'=2,'seq'=4,'fsdp'=4] {'groups','seq'}, dimensions={0}, use_global_device_ids=true | all-gather | bytes 891648 | tf_op jit(solution)/shard_map/all_gather | solution.py:224
  41.8 3.6 %copy.39 = f32[129,4,8,48]{3,2,1,0:T(8,128)} copy(f32[129,4,8,48]{0,3,1,2:T(8,128)} %bitcast.52) | data formatting | bytes 1585152 | tf_op jit(solution)/shard_map/transpose | solution.py:225
  45.4 3.6 %reshape.241 = f32[129,1536]{1,0:T(8,128)} reshape(f32[129,4,8,48]{3,2,1,0:T(8,128)} %copy.39) | data formatting | bytes 1585152 | tf_op jit(solution)/shard_map/reshape | solution.py:225
  50.1 2.0 fusion.1
  52.1 2.0 broadcast_multiply_fusion.1
  54.7 1.4 convolution_bitcast_fusion
  56.1 20.3 %all-gather.7.cloned.1.call-done = bf16[8,128,1536]{2,1,0:T(8,128)(2,1)} async-done(((bf16[2,128,1536]{2,1,0:T(8,128)(2,1)}), bf16[8,128,1536]{2,1,0:T(8,128)(2,1)}) %all-gather.7.cloned.1.call-update) | async-done | bytes 3145744 | tf_op jit(solution)/shard_map/all_gather | solution.py:243
  76.4 3.2 %fusion.42 = (bf16[4,1,128,1536]{3,2,1,0:T(8,128)(2,1)S(1)}, bf16[4,1,128,1536]{3,2,1,0:T(8,128)(2,1)}) fusion(bf16[4,2,128,1536]{3,2,1,0:T(8,128)(2,1)} %bitcast.57), kind=kLoop, calls=%fused_computation.93 | loop fusion | bytes 6291456 | tf_op jit(solution)/shard_map/slice | solution.py:253
  79.6 3.3 %convolution_convert_fusion = bf16[512,1152]{1,0:T(8,128)(2,1)} fusion(bf16[512,1536]{1,0:T(8,128)(2,1)S(1)} %bitcast.60, bf16[1536,1152]{1,0:T(8,128)(2,1)S(1)} %copy-done), kind=kOutput, calls=%fused_computation | convolution fusion | flops 1812529152 | bytes 6291456 | tf_op jit(solution)/shard_map/dot_general | solution.py:252
  82.9 4.4 %all-to-all-start = ((bf16[4,128,1152]{2,1,0:T(8,128)(2,1)}), bf16[4,128,1152]{2,1,0:T(8,128)(2,1)}, u32[]{:S(2)}, u32[]{:S(2)}) async-start(bf16[4,128,1152]{2,1,0:T(8,128)(2,1)} %bitcast.62), calls=%async_computation | async-start | bytes 2359296 | tf_op jit(solution)/shard_map/all_to_all | solution.py:264
  88.0 1.8 slice_reduce_fusion.2
  89.8 26.6 %all-to-all-done = bf16[4,128,1152]{2,1,0:T(8,128)(2,1)} async-done(((bf16[4,128,1152]{2,1,0:T(8,128)(2,1)}), bf16[4,128,1152]{2,1,0:T(8,128)(2,1)}, u32[]{:S(2)}, u32[]{:S(2)}) %all-to-all-start) | async-done | bytes 1179680 | tf_op jit(solution)/shard_map/all_to_all | solution.py:264
  116.4 1.4 copy.44
  117.8 1.3 collective-permute-start
  119.1 1.5 collective-permute-start.1
  121.2 2.6 %collective-permute-done.1 = bf16[1,1,4608]{2,1,0:T(2,128)(2,1)S(1)} collective-permute-done((bf16[1,1,4608]{2,1,0:T(2,128)(2,1)S(1)}, bf16[1,1,4608]{2,1,0:T(2,128)(2,1)S(1)}, u32[]{:S(2)}, u32[]{:S(2)}) %collective-permute-start.1) | collective-permute-done | bytes 9248 | tf_op jit(solution)/shard_map/ppermute | solution.py:21
  124.7 1.2 fusion.44
  125.9 4.7 %convolution_convert_fusion.1 = bf16[512,1152]{1,0:T(8,128)(2,1)} fusion(bf16[512,1536]{1,0:T(8,128)(2,1)} %bitcast.59, bf16[1536,1152]{1,0:T(8,128)(2,1)S(1)} %copy-done), kind=kOutput, calls=%fused_computation.1 | convolution fusion | flops 1812529152 | bytes 6291456 | tf_op jit(solution)/shard_map/dot_general | solution.py:252
  130.6 4.3 %all-to-all-start.1 = ((bf16[4,128,1152]{2,1,0:T(8,128)(2,1)}), bf16[4,128,1152]{2,1,0:T(8,128)(2,1)}, u32[]{:S(2)}, u32[]{:S(2)}) async-start(bf16[4,128,1152]{2,1,0:T(8,128)(2,1)} %bitcast.61), calls=%async_computation.1 | async-start | bytes 2359296 | tf_op jit(solution)/shard_map/all_to_all | solution.py:264
  134.9 2.1 slice.88.out_cols_ref
  137.8 1.3 subtract_convert_fusion
  139.1 1.0 pad_maximum_fusion.4.basis_ref
  140.1 23.7 %all-to-all-done.1 = bf16[4,128,1152]{2,1,0:T(8,128)(2,1)} async-done(((bf16[4,128,1152]{2,1,0:T(8,128)(2,1)}), bf16[4,128,1152]{2,1,0:T(8,128)(2,1)}, u32[]{:S(2)}, u32[]{:S(2)}) %all-to-all-start.1) | async-done | bytes 1179680 | tf_op jit(solution)/shard_map/all_to_all | solution.py:264
  163.8 2.4 %copy.45 = bf16[1,4,16,8,1152]{4,3,1,2,0:T(8,128)(2,1)} copy(bf16[1,4,16,8,1152]{4,3,2,1,0:T(8,128)(2,1)} %bitcast.24) | data formatting | bytes 2359296 | tf_op jit(solution)/shard_map/all_to_all | solution.py:264
  166.2 1.1 copy-done.1
  167.4 1.1 copy-done.3
  168.5 1.0 copy-done.5
  169.5 1.1 copy-done.7
  170.6 1.4 copy-done.9
  172.0 0.9 copy-done.13
  172.9 0.9 copy-done.15
  173.9 7.3 %shard_map.136 = bf16[1,128,1536]{2,1,0:T(8,128)(2,1)S(1)} custom-call(bf16[1,512,1536]{2,1,0:T(8,128)(2,1)S(1)} %copy-done.9, bf16[4,256,384]{2,1,0:T(8,128)(2,1)S(1)} %copy-done.3, f32[128,1536]{1,0:T(8,128)S(1)} %copy-done.1, f32[1,128,1536]{2,1,0:T(8,128)S(1)} %copy-done.7, bf16[1,128,1536]{2,1,0:T(8,128)(2,1)S(1)} %copy-done.5, ...), custom_call_target="tpu_custom_call" | custom-call | tf_op jit(solution)/shard_map/pallas_call | solution.py:182
  181.3 2.8 %collective-permute-start.2 = (bf16[1,1,4608]{2,1,0:T(2,128)(2,1)S(1)}, bf16[1,1,4608]{2,1,0:T(2,128)(2,1)S(1)}, u32[]{:S(2)}, u32[]{:S(2)}) collective-permute-start(bf16[1,1,4608]{2,1,0:T(2,128)(2,1)S(1)} %get-tuple-element.28), channel_id=1, source_target_pairs={{0,4},{4,8},{8,12},{1,5},{5,9},{9,13},{2,6},{6,10},{10,14},{3,7},{... | collective-permute-start | bytes 27656 | tf_op jit(solution)/shard_map/ppermute | solution.py:19
  184.1 1.3 collective-permute-start.3
  186.0 1.1 collective-permute-done.3
  188.0 1.2 fusion.43
  189.2 19.6 %all-gather.11.cloned.1.call-done.piece_ref = bf16[1,512,1536]{2,1,0:T(8,128)(2,1)} async-done(((bf16[1,128,1536]{2,1,0:T(8,128)(2,1)}), bf16[1,512,1536]{2,1,0:T(8,128)(2,1)}) %all-gather.11.cloned.1.call-update) | async-done | bytes 1572880 | tf_op jit(solution)/shard_map/all_gather | solution.py:280
  208.8 1.1 copy-done.2
  210.0 1.1 copy-done.4
  211.1 1.0 copy-done.6
  212.1 1.1 copy-done.8
  213.2 1.4 copy-done.10
  214.6 0.9 copy-done.14
  216.5 7.3 %shard_map.137 = bf16[1,128,1536]{2,1,0:T(8,128)(2,1)S(1)} custom-call(bf16[1,512,1536]{2,1,0:T(8,128)(2,1)S(1)} %copy-done.10, bf16[4,256,384]{2,1,0:T(8,128)(2,1)S(1)} %copy-done.4, f32[128,1536]{1,0:T(8,128)S(1)} %copy-done.2, f32[1,128,1536]{2,1,0:T(8,128)S(1)} %copy-done.8, bf16[1,128,1536]{2,1,0:T(8,128)(2,1)S(1)} %copy-done.6, ...), custom_call_target="tpu_custom_call" | custom-call | tf_op jit(solution)/shard_map/pallas_call | solution.py:182
  223.8 0.9 pad_maximum_fusion.5
  (74 shorter events, 8.8 us)
Async XLA Ops:
  6.5 73.1 %copy-start = (bf16[1536,1152]{1,0:T(8,128)(2,1)S(1)}, bf16[1536,1152]{1,0:T(8,128)(2,1)}, u32[]{:S(2)}) copy-start(bf16[1536,1152]{1,0:T(8,128)(2,1)} %param.15) | copy-start | bytes 10616836
  6.5 69.8 %all-gather.7.cloned.1.call-start = ((), (), s32[]{:S(2)}) async-start(), calls=%async_computation.2 | async-start | bytes 3932160 | tf_op jit(solution)/shard_map/all_gather | solution.py:243
  45.4 4.7 %copy-start.25 = (f32[64]{0:T(128)S(1)}, f32[64]{0:T(128)}, u32[]{:S(2)}) copy-start(f32[64]{0:T(128)} %param.18) | copy-start | bytes 772
  82.9 4.5 %copy-start.24 = (s32[2,1]{0,1:T(1,128)S(1)}, s32[2,1]{0,1:T(1,128)}, u32[]{:S(2)}) copy-start(s32[2,1]{0,1:T(1,128)} %param.23) | copy-start | bytes 28
  82.9 33.5 %all-to-all-start = ((bf16[4,128,1152]{2,1,0:T(8,128)(2,1)}), bf16[4,128,1152]{2,1,0:T(8,128)(2,1)}, u32[]{:S(2)}, u32[]{:S(2)}) async-start(bf16[4,128,1152]{2,1,0:T(8,128)(2,1)} %bitcast.62), calls=%async_computation | async-start | bytes 2359296 | tf_op jit(solution)/shard_map/all_to_all | solution.py:264
  87.3 78.9 %all-gather.9.cloned.1.call-start = ((), (), s32[]{:S(2)}) async-start(), calls=%async_computation.3 | async-start | bytes 1966080 | tf_op jit(solution)/shard_map/all_gather | solution.py:280
  116.4 7.5 %copy-start.18 = (f32[4608]{0:T(1024)S(1)}, f32[4608]{0:T(1024)}, u32[]{:S(2)}) copy-start(f32[4608]{0:T(1024)} %get-tuple-element.17) | copy-start | bytes 55300
  116.4 7.5 %copy-start.20 = (f32[4608]{0:T(1024)S(1)}, f32[4608]{0:T(1024)}, u32[]{:S(2)}) copy-start(f32[4608]{0:T(1024)} %get-tuple-element.18) | copy-start | bytes 55300
  116.4 7.5 %copy-start.22 = (f32[4608]{0:T(1024)S(1)}, f32[4608]{0:T(1024)}, u32[]{:S(2)}) copy-start(f32[4608]{0:T(1024)} %get-tuple-element.19) | copy-start | bytes 55300
  117.8 3.4 %collective-permute-start = (bf16[1,1,4608]{2,1,0:T(2,128)(2,1)S(1)}, bf16[1,1,4608]{2,1,0:T(2,128)(2,1)S(1)}, u32[]{:S(2)}, u32[]{:S(2)}) collective-permute-start(bf16[1,1,4608]{2,1,0:T(2,128)(2,1)S(1)} %get-tuple-element.30), channel_id=1, source_target_pairs={{0,4},{4,8},{8,12},{1,5},{5,9},{9,13},{2,6},{6,10},{10,14},{3,7},{... | collective-permute-start | bytes 27656 | tf_op jit(solution)/shard_map/ppermute | solution.py:19
  119.1 4.8 %collective-permute-start.1 = (bf16[1,1,4608]{2,1,0:T(2,128)(2,1)S(1)}, bf16[1,1,4608]{2,1,0:T(2,128)(2,1)S(1)}, u32[]{:S(2)}, u32[]{:S(2)}) collective-permute-start(bf16[1,1,4608]{2,1,0:T(2,128)(2,1)S(1)} %get-tuple-element.31), channel_id=1, source_target_pairs={{4,0},{8,4},{12,8},{5,1},{9,5},{13,9},{6,2},{10,6},{14,10},{7,3},{... | collective-permute-start | bytes 27656 | tf_op jit(solution)/shard_map/ppermute | solution.py:21
  130.6 33.2 %all-to-all-start.1 = ((bf16[4,128,1152]{2,1,0:T(8,128)(2,1)}), bf16[4,128,1152]{2,1,0:T(8,128)(2,1)}, u32[]{:S(2)}, u32[]{:S(2)}) async-start(bf16[4,128,1152]{2,1,0:T(8,128)(2,1)} %bitcast.61), calls=%async_computation.1 | async-start | bytes 2359296 | tf_op jit(solution)/shard_map/all_to_all | solution.py:264
  134.9 73.9 %all-gather.11.cloned.1.call-start = ((), (), s32[]{:S(2)}) async-start(), calls=%async_computation.4 | async-start | bytes 1966080 | tf_op jit(solution)/shard_map/all_gather | solution.py:280
  166.2 1.1 copy-start.1
  167.3 1.1 copy-start.3
  168.5 1.0 copy-start.5
  169.5 1.1 copy-start.7
  170.6 1.4 copy-start.9
  172.0 0.9 copy-start.13
  172.9 0.9 copy-start.15
  173.9 7.4 %copy-start.17 = (bf16[1,4,16,8,1152]{4,3,1,2,0:T(8,128)(2,1)S(1)}, bf16[1,4,16,8,1152]{4,3,1,2,0:T(8,128)(2,1)}, u32[]{:S(2)}) copy-start(bf16[1,4,16,8,1152]{4,3,1,2,0:T(8,128)(2,1)} %copy.45) | copy-start | bytes 3538948
  173.9 13.3 %copy-start.19 = (f32[4608]{0:T(1024)S(1)}, f32[4608]{0:T(1024)}, u32[]{:S(2)}) copy-start(f32[4608]{0:T(1024)} %get-tuple-element.17) | copy-start | bytes 55300
  173.9 13.3 %copy-start.21 = (f32[4608]{0:T(1024)S(1)}, f32[4608]{0:T(1024)}, u32[]{:S(2)}) copy-start(f32[4608]{0:T(1024)} %get-tuple-element.18) | copy-start | bytes 55300
  173.9 13.3 %copy-start.23 = (f32[4608]{0:T(1024)S(1)}, f32[4608]{0:T(1024)}, u32[]{:S(2)}) copy-start(f32[4608]{0:T(1024)} %get-tuple-element.19) | copy-start | bytes 55300
  181.2 8.0 %copy-start.11 = (bf16[1,128,1536]{2,1,0:T(8,128)(2,1)}, bf16[1,128,1536]{2,1,0:T(8,128)(2,1)S(1)}, u32[]{:S(2)}) copy-start(bf16[1,128,1536]{2,1,0:T(8,128)(2,1)S(1)} %shard_map.136) | copy-start | bytes 1179652
  181.3 4.7 %collective-permute-start.2 = (bf16[1,1,4608]{2,1,0:T(2,128)(2,1)S(1)}, bf16[1,1,4608]{2,1,0:T(2,128)(2,1)S(1)}, u32[]{:S(2)}, u32[]{:S(2)}) collective-permute-start(bf16[1,1,4608]{2,1,0:T(2,128)(2,1)S(1)} %get-tuple-element.28), channel_id=1, source_target_pairs={{0,4},{4,8},{8,12},{1,5},{5,9},{9,13},{2,6},{6,10},{10,14},{3,7},{... | collective-permute-start | bytes 27656 | tf_op jit(solution)/shard_map/ppermute | solution.py:19
  184.1 3.1 %collective-permute-start.3 = (bf16[1,1,4608]{2,1,0:T(2,128)(2,1)S(1)}, bf16[1,1,4608]{2,1,0:T(2,128)(2,1)S(1)}, u32[]{:S(2)}, u32[]{:S(2)}) collective-permute-start(bf16[1,1,4608]{2,1,0:T(2,128)(2,1)S(1)} %get-tuple-element.29), channel_id=1, source_target_pairs={{4,0},{8,4},{12,8},{5,1},{9,5},{13,9},{6,2},{10,6},{14,10},{7,3},{... | collective-permute-start | bytes 27656 | tf_op jit(solution)/shard_map/ppermute | solution.py:21
  208.8 1.1 copy-start.2
  210.0 1.1 copy-start.4
  211.1 1.0 copy-start.6
  212.1 1.1 copy-start.8
  213.2 1.4 copy-start.10
  214.6 0.9 copy-start.14
  215.6 0.9 copy-start.16
  216.5 7.3 %copy-start.12 = (bf16[1,128,1536]{2,1,0:T(8,128)(2,1)S(1)}, bf16[1,128,1536]{2,1,0:T(8,128)(2,1)}, u32[]{:S(2)}) copy-start(bf16[1,128,1536]{2,1,0:T(8,128)(2,1)} %copy-done.11) | copy-start | bytes 1179652
Sparse Core Ops, SparseCore 0:
  8.9 67.3 all-gather.6
  126.1 19.9 all-gather.8
  189.3 19.4 all-gather.10

commit v12 on v9

--- a/solution.py
+++ b/solution.py
@@ -120,12 +120,14 @@
 
 
 def conv_kernel(
-    piece_ref, basis_ref, out_cols_ref, query_ref, carried_ref, skip_ref, fwd_ref, inv_ref,
+    piece_ref, basis_ref, out_cols_ref, query_ref, carried_ref, fwd_ref, inv_ref,
     out_ref, resp_ref,
 ):
     tables, rows, lanes = carried_ref.shape
     block_total = resp_ref.shape[0]
-    cols_hi, cols_lo = split_bf16(out_cols_ref[...])
+    out_cols = out_cols_ref[...]
+    cols_hi, cols_lo = split_bf16(out_cols[:-1])
+    skip = out_cols[out_cols.shape[0] - 1 :]
     cols = jnp.concatenate([cols_hi, cols_lo, cols_hi], axis=0)
 
     def dot(a, b):
@@ -165,11 +167,11 @@
         spectrum = jnp.concatenate([acc_real, acc_imag], axis=0)
         spec_hi, spec_lo = split_bf16(spectrum)
         conv = dot(inv, jnp.concatenate([spec_hi, spec_lo, spec_hi], axis=0))
-        gated = query_ref[table] * (conv + skip_ref[...] * carried_ref[table].astype(jnp.float32))
+        gated = query_ref[table] * (conv + skip * carried_ref[table].astype(jnp.float32))
         out_ref[table] = gated.astype(out_ref.dtype)
 
 
-def fused_conv(piece, basis_spec, out_cols, query_gate, carried, skip):
+def fused_conv(piece, basis_spec, out_cols, query_gate, carried):
     tables, rows, width = carried.shape
     block_total = basis_spec.shape[0]
     basis_hi, basis_lo = split_bf16(basis_spec)
@@ -188,7 +190,6 @@
             pl.BlockSpec((out_cols.shape[0], lanes), lambda i: (0, i)),
             pl.BlockSpec((tables, rows, lanes), tile3),
             pl.BlockSpec((tables, rows, lanes), tile3),
-            pl.BlockSpec((1, lanes), lambda i: (0, i)),
             pl.BlockSpec(fwd.shape, lambda i: (0, 0)),
             pl.BlockSpec(inv.shape, lambda i: (0, 0)),
         ],
@@ -196,7 +197,7 @@
         out_shape=jax.ShapeDtypeStruct((tables, rows, width), jnp.bfloat16),
         scratch_shapes=[pltpu.VMEM((block_total, 2 * rows, lanes), jnp.float32)],
         compiler_params=pltpu.CompilerParams(vmem_limit_bytes=48 * 1024 * 1024),
-    )(piece, basis, out_cols, query_gate, carried, skip.reshape(1, width), jnp.asarray(fwd), jnp.asarray(inv))
+    )(piece, basis, out_cols, query_gate, carried, jnp.asarray(fwd), jnp.asarray(inv))
 
 
 def shards(
@@ -218,8 +219,6 @@
     )
     gathered = gather_by_permutes(params, "fsdp")
     gathered = jnp.transpose(gathered, (1, 0, 2)).reshape(params.shape[0], width)
-    stacked_out = gathered[:-1]
-    full_skip = gathered[-1]
     seq_count = lax.axis_size("seq")
     position = lax.axis_index("seq")
     total_len = float(seq_count * block_len)
@@ -263,7 +262,7 @@
     carried = (key_part * value_part * valid_mask[:, :, None]).astype(jnp.bfloat16)
     piece = lax.all_gather(carried, "seq", axis=1, tiled=True)
 
-    return fused_conv(piece, basis_spec, stacked_out, query_gate, carried, full_skip)
+    return fused_conv(piece, basis_spec, gathered, query_gate, carried)
 
 
 def solution(mesh):

time: 210 us -> 210 us (level)
    unnamed x26 -> x27, local copies, waits for them, and re-layouts: 6.73 us -> 7.83 us
where the time goes in v12:
time: 210 us; the launch traced here: 209 us
  waiting for transfers between devices  135 us (64%)
  between operations  13.6 us (6%)
  Pallas kernels  13.1 us (6%)
  matrix products  13 us (6%)
  local copies, waits for them, and re-layouts  12.9 us (6%)
  other arithmetic  12.3 us (6%)
  starting transfers between devices  9.28 us (4%)
    all_gather x1, waiting for transfers between devices, shards(): group_tokens = lax.all_gather(tokens, 'fsdp', axis=0, tiled=True)  60.9 us
    all_to_all x1, waiting for transfers between devices, shards(): projected = lax.all_to_all(partial, 'fsdp', 0, 2, tiled=True)  54 us
    pallas_call x1, Pallas kernels, fused_conv(): pl.pallas_call(conv_kernel, grid=(width // lanes,), in_specs=[pl.BlockSpe...  13.1 us
    ppermute x3, waiting for transfers between devices, gather_by_permutes(): lax.ppermute(values, axis, [(i, (i + shift) % count) for i in range(count)])  12.5 us
    unnamed x27, local copies, waits for them, and re-layouts  7.83 us
    dot_general x1, matrix products, shards(): jnp.dot(group_tokens.reshape(group_rows * block_len, width), in_weight, p...  7.52 us
    all_to_all x1, starting transfers between devices, shards(): projected = lax.all_to_all(partial, 'fsdp', 0, 2, tiled=True)  4.62 us
  transfers between devices with their start and end apart: 8, of which 6 were waited for; matrix products, arithmetic and copies ran while one was open for 9% of the time, Pallas kernels for 0%

profile of v12, /device:TPU:0, one launch (start us, length us, event | category | flops | bytes accessed | tf_op | source)
XLA Modules:
  0.0 209.0 jit_solution(9843092231810214930)
XLA Ops:
  6.5 0.7 all-gather.3.cloned.1.call-update
  7.3 0.1 fusion.27
  7.4 0.1 fusion.30
  7.5 0.1 convert_bitcast_fusion
  7.6 0.6 fusion.26
  8.2 2.0 fusion.3
  10.1 2.0 broadcast_multiply_fusion.1
  12.2 0.5 negate_select_fusion.2
  12.8 1.4 convolution_bitcast_fusion
  14.2 60.9 %all-gather.3.cloned.1.call-done = bf16[8,128,1536]{2,1,0:T(8,128)(2,1)} async-done(((bf16[2,128,1536]{2,1,0:T(8,128)(2,1)}), bf16[8,128,1536]{2,1,0:T(8,128)(2,1)}) %all-gather.3.cloned.1.call-update) | async-done | bytes 3145744 | tf_op jit(solution)/shard_map/all_gather | solution.py:239
  75.2 7.5 %convolution_convert_fusion = bf16[1024,1152]{1,0:T(8,128)(2,1)} fusion(bf16[1024,1536]{1,0:T(8,128)(2,1)} %bitcast.55, bf16[1536,1152]{1,0:T(8,128)(2,1)S(1)} %copy-done), kind=kOutput, calls=%fused_computation.2 | convolution fusion | flops 3625058304 | bytes 9043968 | tf_op jit(solution)/shard_map/dot_general | solution.py:243
  82.7 4.6 %all-to-all-start = ((bf16[8,128,1152]{2,1,0:T(8,128)(2,1)}), bf16[8,128,1152]{2,1,0:T(8,128)(2,1)}, u32[]{:S(2)}, u32[]{:S(2)}) async-start(bf16[8,128,1152]{2,1,0:T(8,128)(2,1)} %bitcast.48), calls=%async_computation | async-start | bytes 4718592 | tf_op jit(solution)/shard_map/all_to_all | solution.py:249
  87.3 0.0 all-gather.5.cloned.1.call-start
  87.4 0.1 compare_convert_fusion
  87.5 54.0 %all-to-all-done = bf16[8,128,1152]{2,1,0:T(8,128)(2,1)} async-done(((bf16[8,128,1152]{2,1,0:T(8,128)(2,1)}), bf16[8,128,1152]{2,1,0:T(8,128)(2,1)}, u32[]{:S(2)}, u32[]{:S(2)}) %all-to-all-start) | async-done | bytes 2359328 | tf_op jit(solution)/shard_map/all_to_all | solution.py:249
  141.4 1.9 copy.27
  143.4 0.1 fusion.41
  143.4 1.3 collective-permute-start
  144.7 1.3 collective-permute-start.1
  146.1 0.1 slice_reduce_fusion.2
  146.2 3.3 %collective-permute-done.1 = bf16[2,1,4608]{2,1,0:T(2,128)(2,1)S(1)} collective-permute-done((bf16[2,1,4608]{2,1,0:T(2,128)(2,1)S(1)}, bf16[2,1,4608]{2,1,0:T(2,128)(2,1)S(1)}, u32[]{:S(2)}, u32[]{:S(2)}) %collective-permute-start.1) | collective-permute-done | bytes 18464 | tf_op jit(solution)/shard_map/ppermute | solution.py:21
  149.6 1.9 multiply_add_fusion
  151.5 0.0 copy-start.9
  151.5 1.7 fusion.40
  153.2 0.0 all-gather.5.cloned.1.call-update
  153.3 1.8 fusion.39
  155.1 0.0 collective-permute-start.3
  155.1 1.5 collective-permute-start.4
  156.5 0.6 collective-permute-start.2
  157.1 0.8 sort.17
  157.9 10.9 %collective-permute-done.3 = f32[129,384]{1,0:T(8,128)} collective-permute-done((f32[129,384]{1,0:T(8,128)}, f32[129,384]{1,0:T(8,128)}, u32[]{:S(2)}, u32[]{:S(2)}) %collective-permute-start.3) | collective-permute-done | bytes 198176 | tf_op jit(solution)/shard_map/ppermute | solution.py:34
  168.8 1.6 collective-permute-done.2
  170.4 2.2 %pad_maximum_fusion.2 = f32[4,129,384]{2,1,0:T(8,128)} fusion(f32[1,129,384]{2,1,0:T(8,128)} %bitcast.11, f32[1,129,384]{2,1,0:T(8,128)} %bitcast.10, f32[1,129,384]{2,1,0:T(8,128)} %bitcast.9, f32[1,129,384]{2,1,0:T(8,128)} %get-tuple-element.22), kind=kLoop, calls=%fused_computation.13 | loop fusion | flops 594432 | bytes 1585152 | tf_op jit(solution)/shard_map/stack | solution.py:36
  172.6 2.7 %gather_fusion = f32[4,129,384]{2,1,0:T(8,128)} fusion(f32[4,129,384]{2,1,0:T(8,128)} %pad_maximum_fusion.2, s32[1024]{0:T(1024)S(1)} %pad_clamp_fusion), kind=kCustom, calls=%fused_computation | custom fusion | bytes 1585168 | tf_op jit(solution)/shard_map/jit(_take)/gather | solution.py:39
  175.3 1.3 select_bitcast_fusion
  176.6 0.2 copy.24
  176.8 0.1 pad.25
  177.0 1.0 copy.31
  178.0 0.1 subtract_convert_fusion
  178.0 1.0 pad_maximum_fusion.3.basis_ref
  179.0 3.4 %all-gather.5.cloned.1.call-done.piece_ref = bf16[2,512,1536]{2,1,0:T(8,128)(2,1)} async-done(((bf16[2,128,1536]{2,1,0:T(8,128)(2,1)}), bf16[2,512,1536]{2,1,0:T(8,128)(2,1)}) %all-gather.5.cloned.1.call-update) | async-done | bytes 3145744 | tf_op jit(solution)/shard_map/all_gather | solution.py:263
  182.4 1.1 copy-done.1
  183.5 1.4 copy-done.2
  184.9 1.1 copy-done.3
  186.1 1.1 copy-done.4
  187.2 0.9 copy-done.5
  188.2 0.9 copy-done.6
  189.1 13.1 %shard_map.121 = bf16[2,128,1536]{2,1,0:T(8,128)(2,1)} custom-call(bf16[2,512,1536]{2,1,0:T(8,128)(2,1)} %all-gather.5.cloned.1.call-done.piece_ref, bf16[4,256,384]{2,1,0:T(8,128)(2,1)S(1)} %copy-done.4, f32[129,1536]{1,0:T(8,128)S(1)} %bitcast.44, f32[2,128,1536]{2,1,0:T(8,128)S(1)} %copy-done.2, bf16[2,128,1536]{2,1,0:T(8,128)(2,1)S(1)} %copy-done.1, ...), custom_call_target="tpu_custom_call" | custom-call | tf_op jit(solution)/shard_map/pallas_call | solution.py:184
  (35 shorter events, 0.2 us)
Async XLA Ops:
  6.5 68.6 %copy-start = (bf16[1536,1152]{1,0:T(8,128)(2,1)S(1)}, bf16[1536,1152]{1,0:T(8,128)(2,1)}, u32[]{:S(2)}) copy-start(bf16[1536,1152]{1,0:T(8,128)(2,1)} %param.13) | copy-start | bytes 10616836
  6.5 68.6 %all-gather.3.cloned.1.call-start = ((), (), s32[]{:S(2)}) async-start(), calls=%async_computation.1 | async-start | bytes 3932160 | tf_op jit(solution)/shard_map/all_gather | solution.py:239
  82.7 4.7 %copy-start.10 = (s32[2,1]{0,1:T(1,128)S(1)}, s32[2,1]{0,1:T(1,128)}, u32[]{:S(2)}) copy-start(s32[2,1]{0,1:T(1,128)} %param.21) | copy-start | bytes 28
  82.7 58.7 %all-to-all-start = ((bf16[8,128,1152]{2,1,0:T(8,128)(2,1)}), bf16[8,128,1152]{2,1,0:T(8,128)(2,1)}, u32[]{:S(2)}, u32[]{:S(2)}) async-start(bf16[8,128,1152]{2,1,0:T(8,128)(2,1)} %bitcast.48), calls=%async_computation | async-start | bytes 4718592 | tf_op jit(solution)/shard_map/all_to_all | solution.py:249
  87.3 95.1 %all-gather.5.cloned.1.call-start = ((), (), s32[]{:S(2)}) async-start(), calls=%async_computation.2 | async-start | bytes 3932160 | tf_op jit(solution)/shard_map/all_gather | solution.py:263
  141.4 4.6 %copy-start.8 = (f32[3,4608]{1,0:T(4,128)S(1)}, f32[3,4608]{1,0:T(4,128)}, u32[]{:S(2)}) copy-start(f32[3,4608]{1,0:T(4,128)} %param.14) | copy-start | bytes 165892
  143.4 2.8 %collective-permute-start = (bf16[2,1,4608]{2,1,0:T(2,128)(2,1)S(1)}, bf16[2,1,4608]{2,1,0:T(2,128)(2,1)S(1)}, u32[]{:S(2)}, u32[]{:S(2)}) collective-permute-start(bf16[2,1,4608]{2,1,0:T(2,128)(2,1)S(1)} %get-tuple-element.18), channel_id=1, source_target_pairs={{0,4},{4,8},{8,12},{1,5},{5,9},{9,13},{2,6},{6,10},{10,14},{3,7},{... | collective-permute-start | bytes 55304 | tf_op jit(solution)/shard_map/ppermute | solution.py:19
  144.7 4.8 %collective-permute-start.1 = (bf16[2,1,4608]{2,1,0:T(2,128)(2,1)S(1)}, bf16[2,1,4608]{2,1,0:T(2,128)(2,1)S(1)}, u32[]{:S(2)}, u32[]{:S(2)}) collective-permute-start(bf16[2,1,4608]{2,1,0:T(2,128)(2,1)S(1)} %get-tuple-element.19), channel_id=1, source_target_pairs={{4,0},{8,4},{12,8},{5,1},{9,5},{13,9},{6,2},{10,6},{14,10},{7,3},{... | collective-permute-start | bytes 55304 | tf_op jit(solution)/shard_map/ppermute | solution.py:21
  151.5 1.8 copy-start.9
  155.1 13.7 %collective-permute-start.3 = (f32[129,384]{1,0:T(8,128)}, f32[129,384]{1,0:T(8,128)}, u32[]{:S(2)}, u32[]{:S(2)}) collective-permute-start(f32[129,384]{1,0:T(8,128)} %get-tuple-element.23), channel_id=1, source_target_pairs={{0,2},{1,3},{2,0},{3,1},{4,6},{5,7},{6,4},{7,5},{8,10},{9,11},{10,... | collective-permute-start | bytes 594440 | tf_op jit(solution)/shard_map/ppermute | solution.py:34
  155.1 13.7 %collective-permute-start.4 = (f32[129,384]{1,0:T(8,128)}, f32[129,384]{1,0:T(8,128)}, u32[]{:S(2)}, u32[]{:S(2)}) collective-permute-start(f32[129,384]{1,0:T(8,128)} %get-tuple-element.23), channel_id=1, source_target_pairs={{0,3},{1,0},{2,1},{3,2},{4,7},{5,4},{6,5},{7,6},{8,11},{9,8},{10,9... | collective-permute-start | bytes 594440 | tf_op jit(solution)/shard_map/ppermute | solution.py:34
  156.5 13.9 %collective-permute-start.2 = (f32[129,384]{1,0:T(8,128)}, f32[129,384]{1,0:T(8,128)}, u32[]{:S(2)}, u32[]{:S(2)}) collective-permute-start(f32[129,384]{1,0:T(8,128)} %get-tuple-element.23), channel_id=1, source_target_pairs={{0,1},{1,2},{2,3},{3,0},{4,5},{5,6},{6,7},{7,4},{8,9},{9,10},{10,1... | collective-permute-start | bytes 594440 | tf_op jit(solution)/shard_map/ppermute | solution.py:34
  175.3 2.7 %copy-start.7 = (f32[4,256,128]{2,1,0:T(8,128)S(1)}, f32[4,256,128]{2,1,0:T(8,128)}, u32[]{:S(2)}) copy-start(f32[4,256,128]{2,1,0:T(8,128)} %convolution_bitcast_fusion) | copy-start | bytes 1572868
  182.4 1.1 copy-start.1
  183.5 1.4 copy-start.2
  184.9 1.1 copy-start.3
  186.1 1.1 copy-start.4
  187.2 0.9 copy-start.5
  188.2 0.9 copy-start.6
Sparse Core Ops, SparseCore 0:
  8.9 66.1 all-gather.2
  153.4 28.9 all-gather.4

commit v13 on v12

--- a/solution.py
+++ b/solution.py
@@ -146,7 +146,7 @@
 
         def one_block(block, acc):
             acc_real, acc_imag, edge = acc
-            block_rows = piece_ref[table, pl.ds(pl.multiple_of(block * rows, rows), rows), :]
+            block_rows = piece_ref[block, table]
             signal = dot(fwd, jnp.concatenate([block_rows, block_rows], axis=0))
             response = resp_ref[block]
             resp_real = response[:rows]
@@ -185,7 +185,7 @@
         conv_kernel,
         grid=(width // lanes,),
         in_specs=[
-            pl.BlockSpec((tables, piece.shape[1], lanes), tile3),
+            pl.BlockSpec((block_total, tables, rows, lanes), lambda i: (0, 0, 0, i)),
             pl.BlockSpec(basis.shape, lambda i: (0, 0, 0)),
             pl.BlockSpec((out_cols.shape[0], lanes), lambda i: (0, i)),
             pl.BlockSpec((tables, rows, lanes), tile3),
@@ -217,8 +217,13 @@
     params = jnp.concatenate(
         [response_out.reshape(2 * response_out.shape[1], local_ch), skip_gain[None, :]], axis=0
     )
-    gathered = gather_by_permutes(params, "fsdp")
-    gathered = jnp.transpose(gathered, (1, 0, 2)).reshape(params.shape[0], width)
+    parts = lax.axis_size("groups") * lax.axis_size("seq")
+    part = lax.axis_index("groups") * lax.axis_size("seq") + lax.axis_index("seq")
+    part_cols = local_ch // parts
+    mine = lax.dynamic_slice_in_dim(params, part * part_cols, part_cols, axis=1)
+    across = lax.all_gather(mine, "fsdp", axis=0, tiled=False)
+    gathered = lax.all_gather(across, ("groups", "seq"), axis=0, tiled=False)
+    gathered = jnp.transpose(gathered, (2, 1, 0, 3)).reshape(params.shape[0], width)
     seq_count = lax.axis_size("seq")
     position = lax.axis_index("seq")
     total_len = float(seq_count * block_len)
@@ -229,7 +234,11 @@
     wrapped = jnp.where(circular < block_len, circular, circular - 2 * block_len)
 
     block_total = seq_count
-    offsets = (position - jnp.arange(block_total, dtype=jnp.int32)) * block_len
+    chips = seq_count // 2
+    chip, core = position // 2, position % 2
+    ring = (chip - jnp.arange(chips, dtype=jnp.int32)) % chips
+    order = jnp.concatenate([2 * ring + core, 2 * ring + 1 - core])
+    offsets = (position - order) * block_len
     lag_values = (offsets[:, None] + wrapped[None, :]).reshape(-1)
     basis_rows = filter_basis(lag_values, total_len, basis_in, basis_bias, basis_mid, basis_shift)
     ahead_mask = (lag_values >= 0).astype(jnp.float32)[:, None]
@@ -237,7 +246,7 @@
     paired = paired.reshape(block_total, 2 * block_len, paired.shape[-1])
     basis_spec = jnp.einsum("gf,bfk->bgk", forward, paired, precision=lax.Precision.HIGHEST)
     group_tokens = lax.all_gather(tokens, "fsdp", axis=0, tiled=True)
-    group_tokens, basis_spec = lax.optimization_barrier((group_tokens, basis_spec))
+    group_tokens, basis_spec, gathered = lax.optimization_barrier((group_tokens, basis_spec, gathered))
     group_rows = group_tokens.shape[0]
     local_cols = in_weight.shape[1]
     partial = jnp.dot(
@@ -260,7 +269,16 @@
         jnp.float32
     )
     carried = (key_part * value_part * valid_mask[:, :, None]).astype(jnp.bfloat16)
-    piece = lax.all_gather(carried, "seq", axis=1, tiled=True)
+    same_core = [carried]
+    for shift in range(1, chips):
+        same_core.append(
+            lax.ppermute(
+                carried, "seq", [(i, (i + 2 * shift) % seq_count) for i in range(seq_count)]
+            )
+        )
+    same_core = jnp.stack(same_core)
+    other_core = lax.ppermute(same_core, "seq", [(i, i ^ 1) for i in range(seq_count)])
+    piece = jnp.concatenate([same_core, other_core], axis=0)
 
     return fused_conv(piece, basis_spec, gathered, query_gate, carried)
 

time: 210 us -> 200 us (0.952)
  waiting for transfers between devices: 135 us -> 98.5 us
  blocking collectives: 0 us -> 30.3 us
  other arithmetic: 12.3 us -> 7.29 us
    all_gather x1, waiting for transfers between devices: 60.9 us -> 20.2 us  [shards(): group_tokens = lax.all_gather(tokens, 'fsdp', axis=0, tiled=True)]
    all_gather x0 -> x2, blocking collectives: none -> 30.3 us  [the longest x1 16.3 us: shards(): across = lax.all_gather(mine, 'fsdp', axis=0, tiled=False)]
    unnamed x27 -> x19, local copies, waits for them, and re-layouts: 7.83 us -> 0.06 us
    ppermute x3 -> x2, waiting for transfers between devices: 12.5 us -> 20.2 us  [the longest x1 17.4 us: shards(): lax.ppermute(carried, 'seq', [(i, (i + 2 * shift) % seq_count) for i in r...]
    reshape x0 -> x2, local copies, waits for them, and re-layouts: none -> 5.32 us  [the longest x1 3.59 us: shards(): jnp.transpose(gathered, (2, 1, 0, 3)).reshape(params.shape[0], width)]
    another operation x2 -> x1, other arithmetic: 3.97 us -> 0.15 us  [shards(): same_core = jnp.stack(same_core)]
    transpose x0 -> x1, local copies, waits for them, and re-layouts: none -> 3.6 us  [shards(): jnp.transpose(gathered, (2, 1, 0, 3)).reshape(params.shape[0], width)]
    all_gather x1 -> x0, waiting for transfers between devices: 3.4 us -> none  [shards(): piece = lax.all_gather(carried, 'seq', axis=1, tiled=True)]
  transfers between devices with their start and end apart: 8 -> 6, of which waited for: 6 -> 5; matrix products, arithmetic and copies ran while one was open for 9% -> 10% of each run, Pallas kernels for 0% -> 0%
where the time goes in v13:
time: 200 us; the launch traced here: 199 us
  waiting for transfers between devices  98.5 us (49%)
  blocking collectives  30.3 us (15%)
  between operations  13.6 us (7%)
  Pallas kernels  13.1 us (7%)
  matrix products  13 us (6%)
  local copies, waits for them, and re-layouts  12.6 us (6%)
  starting transfers between devices  10.9 us (5%)
  other arithmetic  7.29 us (4%)
    all_to_all x1, waiting for transfers between devices, shards(): projected = lax.all_to_all(partial, 'fsdp', 0, 2, tiled=True)  54.2 us
    all_gather x1, waiting for transfers between devices, shards(): group_tokens = lax.all_gather(tokens, 'fsdp', axis=0, tiled=True)  20.2 us
    ppermute x1, waiting for transfers between devices, shards(): lax.ppermute(carried, 'seq', [(i, (i + 2 * shift) % seq_count) for i in r...  17.4 us
    all_gather x1, blocking collectives, shards(): across = lax.all_gather(mine, 'fsdp', axis=0, tiled=False)  16.3 us
    all_gather x1, blocking collectives, shards(): gathered = lax.all_gather(across, ('groups', 'seq'), axis=0, tiled=False)  14 us
    pallas_call x1, Pallas kernels, fused_conv(): pl.pallas_call(conv_kernel, grid=(width // lanes,), in_specs=[pl.BlockSpe...  13.1 us
    dot_general x1, matrix products, shards(): jnp.dot(group_tokens.reshape(group_rows * block_len, width), in_weight, p...  7.58 us
    all_to_all x1, starting transfers between devices, shards(): projected = lax.all_to_all(partial, 'fsdp', 0, 2, tiled=True)  4.62 us
  transfers between devices with their start and end apart: 6, of which 5 were waited for; matrix products, arithmetic and copies ran while one was open for 10% of the time, Pallas kernels for 0%

profile of v13, /device:TPU:0, one launch (start us, length us, event | category | flops | bytes accessed | tf_op | source)
XLA Modules:
  0.0 199.4 jit_solution(2478612088084502907)
XLA Ops:
  6.5 0.0 copy-start
  6.5 0.0 all-gather.5.cloned.1.call-start
  6.5 0.7 all-gather.5.cloned.1.call-update
  7.3 0.1 fusion.39
  7.4 0.1 fusion.29
  7.5 0.1 fusion.32
  7.5 0.1 convert_bitcast_fusion
  7.6 1.5 broadcast_in_dim.25
  9.1 1.7 copy.31
  10.8 0.8 fusion.21
  11.6 16.3 %all-gather.2 = f32[4,129,48]{1,2,0:T(8,128)S(1)} all-gather(f32[1,129,48]{1,2,0:T(8,128)S(1)} %fusion.21), channel_id=2, replica_groups=mesh['groups'=2,'seq'=4,'fsdp'=4] {'fsdp'}, dimensions={0}, use_global_device_ids=true | all-gather | bytes 123840 | tf_op jit(solution)/shard_map/all_gather | solution.py:224
  27.9 14.0 %all-gather.1 = f32[32,129,48]{1,2,0:T(8,128)} all-gather(f32[4,129,48]{1,2,0:T(8,128)S(1)} %all-gather.2), channel_id=3, replica_groups=mesh['groups'=2,'seq'=4,'fsdp'=4] {'groups','seq'}, dimensions={0}, use_global_device_ids=true | all-gather | bytes 891648 | tf_op jit(solution)/shard_map/all_gather | solution.py:225
  41.9 3.6 %copy.33 = f32[129,4,8,48]{3,2,1,0:T(8,128)} copy(f32[129,4,8,48]{0,3,1,2:T(8,128)} %bitcast.47) | data formatting | bytes 1585152 | tf_op jit(solution)/shard_map/transpose | solution.py:226
  45.5 3.6 %reshape.200.out_cols_ref = f32[129,1536]{1,0:T(8,128)} reshape(f32[129,4,8,48]{3,2,1,0:T(8,128)} %copy.33) | data formatting | bytes 1585152 | tf_op jit(solution)/shard_map/reshape | solution.py:226
  49.1 0.5 fusion.19
  49.6 0.6 fusion.28
  50.2 2.0 fusion.3
  52.2 2.0 %broadcast_multiply_fusion.1 = (f32[1024,64]{0,1:T(8,128)S(1)}, f32[1024,64]{0,1:T(8,128)S(1)}) fusion(f32[1024]{0:T(1024)S(1)} %bitcast.54, f32[1024]{0:T(1024)S(1)} %broadcast_subtract_fusion, f32[64]{0:T(128)} %param.18, f32[1024,64]{0,1:T(8,128)S(1)} %fusion.3, f32[64,64]{1,0:T(8,128)} %param.17), kind=kOutput, calls=%fused_computation.34 | convolution fusion | flops 50528256 | bytes 811264 | tf_op jit(solution)/shard_map/dot_general | solution.py:55
  54.2 0.5 negate_select_fusion.2
  54.8 1.4 convolution_bitcast_fusion
  56.2 20.2 %all-gather.5.cloned.1.call-done = bf16[8,128,1536]{2,1,0:T(8,128)(2,1)} async-done(((bf16[2,128,1536]{2,1,0:T(8,128)(2,1)}), bf16[8,128,1536]{2,1,0:T(8,128)(2,1)}) %all-gather.5.cloned.1.call-update) | async-done | bytes 3145744 | tf_op jit(solution)/shard_map/all_gather | solution.py:248
  76.4 7.6 %convolution_convert_fusion = bf16[1024,1152]{1,0:T(8,128)(2,1)} fusion(bf16[1024,1536]{1,0:T(8,128)(2,1)} %bitcast.57, bf16[1536,1152]{1,0:T(8,128)(2,1)S(1)} %copy-done), kind=kOutput, calls=%fused_computation.1 | convolution fusion | flops 3625058304 | bytes 9043968 | tf_op jit(solution)/shard_map/dot_general | solution.py:252
  84.0 4.6 %all-to-all-start = ((bf16[8,128,1152]{2,1,0:T(8,128)(2,1)}), bf16[8,128,1152]{2,1,0:T(8,128)(2,1)}, u32[]{:S(2)}, u32[]{:S(2)}) async-start(bf16[8,128,1152]{2,1,0:T(8,128)(2,1)} %bitcast.50), calls=%async_computation | async-start | bytes 4718592 | tf_op jit(solution)/shard_map/all_to_all | solution.py:258
  88.6 0.1 compare_convert_fusion
  88.7 54.2 %all-to-all-done = bf16[8,128,1152]{2,1,0:T(8,128)(2,1)} async-done(((bf16[8,128,1152]{2,1,0:T(8,128)(2,1)}), bf16[8,128,1152]{2,1,0:T(8,128)(2,1)}, u32[]{:S(2)}, u32[]{:S(2)}) %all-to-all-start) | async-done | bytes 2359328 | tf_op jit(solution)/shard_map/all_to_all | solution.py:258
  142.9 1.9 copy.37
  144.9 0.1 fusion.44
  144.9 1.3 collective-permute-start
  146.2 1.5 collective-permute-start.1
  147.7 0.0 copy-done.5
  147.7 0.1 slice_reduce_fusion.2
  147.9 0.0 collective-permute-done
  147.9 3.2 %collective-permute-done.1 = bf16[2,1,4608]{2,1,0:T(2,128)(2,1)S(1)} collective-permute-done((bf16[2,1,4608]{2,1,0:T(2,128)(2,1)S(1)}, bf16[2,1,4608]{2,1,0:T(2,128)(2,1)S(1)}, u32[]{:S(2)}, u32[]{:S(2)}) %collective-permute-start.1) | collective-permute-done | bytes 18464 | tf_op jit(solution)/shard_map/ppermute | solution.py:21
  151.1 1.9 multiply_add_fusion
  153.0 0.3 fusion.43
  153.3 0.0 copy-start.4
  153.3 2.6 %collective-permute-start.2 = (bf16[2,128,1536]{2,1,0:T(8,128)(2,1)S(1)}, bf16[2,128,1536]{2,1,0:T(8,128)(2,1)S(1)}, u32[]{:S(2)}, u32[]{:S(2)}) collective-permute-start(bf16[2,128,1536]{2,1,0:T(8,128)(2,1)S(1)} %get-tuple-element.17.carried_ref), channel_id=1, source_target_pairs={{0,8},{4,12},{8,0},{12,4},{1,9},{5,13},{9,1},{13,5},{2,10},{6,14},... | collective-permute-start | bytes 2359304 | tf_op jit(solution)/shard_map/ppermute | solution.py:275
  155.9 17.4 %collective-permute-done.2 = bf16[2,128,1536]{2,1,0:T(8,128)(2,1)S(1)} collective-permute-done((bf16[2,128,1536]{2,1,0:T(8,128)(2,1)S(1)}, bf16[2,128,1536]{2,1,0:T(8,128)(2,1)S(1)}, u32[]{:S(2)}, u32[]{:S(2)}) %collective-permute-start.2) | collective-permute-done | bytes 786464 | tf_op jit(solution)/shard_map/ppermute | solution.py:275
  173.3 0.1 pad_maximum_fusion.3
  173.5 0.9 collective-permute-start.3
  174.4 0.1 subtract_convert_fusion
  174.5 0.1 pad_maximum_fusion.4.basis_ref
  174.6 0.0 copy-start.2
  174.6 0.0 copy-start.3
  174.6 2.8 %collective-permute-done.3 = bf16[2,2,128,1536]{3,2,1,0:T(8,128)(2,1)S(1)} collective-permute-done((bf16[2,2,128,1536]{3,2,1,0:T(8,128)(2,1)S(1)}, bf16[2,2,128,1536]{3,2,1,0:T(8,128)(2,1)S(1)}, u32[]{:S(2)}, u32[]{:S(2)}) %collective-permute-start.3) | collective-permute-done | bytes 1572896 | tf_op jit(solution)/shard_map/ppermute | solution.py:280
  177.4 2.0 pad_maximum_fusion.piece_ref
  179.4 0.0 copy-done.2
  179.4 13.1 %shard_map.121 = bf16[2,128,1536]{2,1,0:T(8,128)(2,1)} custom-call(bf16[4,2,128,1536]{3,2,1,0:T(8,128)(2,1)} %pad_maximum_fusion.piece_ref, bf16[4,256,384]{2,1,0:T(8,128)(2,1)S(1)} %pad_maximum_fusion.4.basis_ref, f32[129,1536]{1,0:T(8,128)S(1)} %copy-done.1, f32[2,128,1536]{2,1,0:T(8,128)S(1)} %get-tuple-element.16.query_ref, ...), custom_call_target="tpu_custom_call" | custom-call | tf_op jit(solution)/shard_map/pallas_call | solution.py:184
  (21 shorter events, 0.1 us)
Async XLA Ops:
  6.5 69.8 %copy-start = (bf16[1536,1152]{1,0:T(8,128)(2,1)S(1)}, bf16[1536,1152]{1,0:T(8,128)(2,1)}, u32[]{:S(2)}) copy-start(bf16[1536,1152]{1,0:T(8,128)(2,1)} %param.13) | copy-start | bytes 10616836
  6.5 69.8 %all-gather.5.cloned.1.call-start = ((), (), s32[]{:S(2)}) async-start(), calls=%async_computation.1 | async-start | bytes 3932160 | tf_op jit(solution)/shard_map/all_gather | solution.py:248
  41.9 8.3 %copy-start.6 = (f32[64]{0:T(128)S(1)}, f32[64]{0:T(128)}, u32[]{:S(2)}) copy-start(f32[64]{0:T(128)} %param.16) | copy-start | bytes 772
  84.0 4.6 %copy-start.7 = (s32[2,1]{0,1:T(1,128)S(1)}, s32[2,1]{0,1:T(1,128)}, u32[]{:S(2)}) copy-start(s32[2,1]{0,1:T(1,128)} %param.21) | copy-start | bytes 28
  84.0 59.0 %all-to-all-start = ((bf16[8,128,1152]{2,1,0:T(8,128)(2,1)}), bf16[8,128,1152]{2,1,0:T(8,128)(2,1)}, u32[]{:S(2)}, u32[]{:S(2)}) async-start(bf16[8,128,1152]{2,1,0:T(8,128)(2,1)} %bitcast.50), calls=%async_computation | async-start | bytes 4718592 | tf_op jit(solution)/shard_map/all_to_all | solution.py:258
  142.9 4.8 %copy-start.5 = (f32[3,4608]{1,0:T(4,128)S(1)}, f32[3,4608]{1,0:T(4,128)}, u32[]{:S(2)}) copy-start(f32[3,4608]{1,0:T(4,128)} %param.14) | copy-start | bytes 165892
  144.9 2.9 %collective-permute-start = (bf16[2,1,4608]{2,1,0:T(2,128)(2,1)S(1)}, bf16[2,1,4608]{2,1,0:T(2,128)(2,1)S(1)}, u32[]{:S(2)}, u32[]{:S(2)}) collective-permute-start(bf16[2,1,4608]{2,1,0:T(2,128)(2,1)S(1)} %get-tuple-element.18), channel_id=1, source_target_pairs={{0,4},{4,8},{8,12},{1,5},{5,9},{9,13},{2,6},{6,10},{10,14},{3,7},{... | collective-permute-start | bytes 55304 | tf_op jit(solution)/shard_map/ppermute | solution.py:19
  146.2 4.8 %collective-permute-start.1 = (bf16[2,1,4608]{2,1,0:T(2,128)(2,1)S(1)}, bf16[2,1,4608]{2,1,0:T(2,128)(2,1)S(1)}, u32[]{:S(2)}, u32[]{:S(2)}) collective-permute-start(bf16[2,1,4608]{2,1,0:T(2,128)(2,1)S(1)} %get-tuple-element.19), channel_id=1, source_target_pairs={{4,0},{8,4},{12,8},{5,1},{9,5},{13,9},{6,2},{10,6},{14,10},{7,3},{... | collective-permute-start | bytes 55304 | tf_op jit(solution)/shard_map/ppermute | solution.py:21
  153.3 21.1 %copy-start.4 = (f32[4,256,128]{2,1,0:T(8,128)S(1)}, f32[4,256,128]{2,1,0:T(8,128)}, u32[]{:S(2)}) copy-start(f32[4,256,128]{2,1,0:T(8,128)} %convolution_bitcast_fusion) | copy-start | bytes 1572868
  153.3 20.0 %collective-permute-start.2 = (bf16[2,128,1536]{2,1,0:T(8,128)(2,1)S(1)}, bf16[2,128,1536]{2,1,0:T(8,128)(2,1)S(1)}, u32[]{:S(2)}, u32[]{:S(2)}) collective-permute-start(bf16[2,128,1536]{2,1,0:T(8,128)(2,1)S(1)} %get-tuple-element.17.carried_ref), channel_id=1, source_target_pairs={{0,8},{4,12},{8,0},{12,4},{1,9},{5,13},{9,1},{13,5},{2,10},{6,14},... | collective-permute-start | bytes 2359304 | tf_op jit(solution)/shard_map/ppermute | solution.py:275
  173.5 4.0 %collective-permute-start.3 = (bf16[2,2,128,1536]{3,2,1,0:T(8,128)(2,1)S(1)}, bf16[2,2,128,1536]{3,2,1,0:T(8,128)(2,1)S(1)}, u32[]{:S(2)}, u32[]{:S(2)}) collective-permute-start(bf16[2,2,128,1536]{3,2,1,0:T(8,128)(2,1)S(1)} %pad_maximum_fusion.3), channel_id=1, source_target_pairs={{0,4},{4,0},{8,12},{12,8},{1,5},{5,1},{9,13},{13,9},{2,6},{6,2},{1... | collective-permute-start | bytes 4718600 | tf_op jit(solution)/shard_map/ppermute | solution.py:280
  174.5 4.8 %copy-start.1 = (f32[129,1536]{1,0:T(8,128)S(1)}, f32[129,1536]{1,0:T(8,128)}, u32[]{:S(2)}) copy-start(f32[129,1536]{1,0:T(8,128)} %reshape.200.out_cols_ref) | copy-start | bytes 2377732
  174.6 4.8 %copy-start.2 = (bf16[128,768]{1,0:T(8,128)(2,1)S(1)}, bf16[128,768]{1,0:T(8,128)(2,1)}, u32[]{:S(2)}) copy-start(bf16[128,768]{1,0:T(8,128)(2,1)} %constant.123.clone.inv_ref) | copy-start | bytes 589828
  174.6 4.8 %copy-start.3 = (bf16[256,256]{1,0:T(8,128)(2,1)S(1)}, bf16[256,256]{1,0:T(8,128)(2,1)}, u32[]{:S(2)}) copy-start(bf16[256,256]{1,0:T(8,128)(2,1)} %constant.122.clone.fwd_ref) | copy-start | bytes 393220
Sparse Core Ops, SparseCore 0:
  8.9 67.3 all-gather.4

commit v14 on v13

--- a/solution.py
+++ b/solution.py
@@ -119,61 +119,68 @@
     return split_table(forward), split_table(inverse)
 
 
-def conv_kernel(
-    piece_ref, basis_ref, out_cols_ref, query_ref, carried_ref, fwd_ref, inv_ref,
-    out_ref, resp_ref,
-):
-    tables, rows, lanes = carried_ref.shape
-    block_total = resp_ref.shape[0]
-    out_cols = out_cols_ref[...]
-    cols_hi, cols_lo = split_bf16(out_cols[:-1])
-    skip = out_cols[out_cols.shape[0] - 1 :]
-    cols = jnp.concatenate([cols_hi, cols_lo, cols_hi], axis=0)
-
-    def dot(a, b):
-        return jnp.dot(a, b, preferred_element_type=jnp.float32)
-
-    def fill(block, carry):
-        resp_ref[block] = dot(basis_ref[block], cols)
-        return carry
-
-    lax.fori_loop(0, block_total, fill, 0)
-    first = lax.broadcasted_iota(jnp.int32, (rows, lanes), 0) == 0
-    fwd = fwd_ref[...]
-    inv = inv_ref[...]
-
-    for table in range(tables):
-
-        def one_block(block, acc):
-            acc_real, acc_imag, edge = acc
-            block_rows = piece_ref[block, table]
-            signal = dot(fwd, jnp.concatenate([block_rows, block_rows], axis=0))
-            response = resp_ref[block]
-            resp_real = response[:rows]
-            resp_imag = response[rows:]
-            sig_real = signal[:rows]
-            sig_imag = signal[rows:]
-            acc_real = acc_real + (resp_real * sig_real - resp_imag * sig_imag)
-            acc_imag = acc_imag + (resp_real * sig_imag + resp_imag * sig_real)
-            edge = edge + resp_imag[0:1] * sig_imag[0:1]
-            return acc_real, acc_imag, edge
-
-        zeros = jnp.zeros((rows, lanes), jnp.float32)
-        acc_real, acc_imag, edge = lax.fori_loop(
-            0, block_total, one_block, (zeros, zeros, jnp.zeros((1, lanes), jnp.float32))
-        )
-        acc_real = acc_real + jnp.where(first, edge, 0.0)
-        acc_imag = jnp.where(first, edge, acc_imag)
-        spectrum = jnp.concatenate([acc_real, acc_imag], axis=0)
-        spec_hi, spec_lo = split_bf16(spectrum)
-        conv = dot(inv, jnp.concatenate([spec_hi, spec_lo, spec_hi], axis=0))
-        gated = query_ref[table] * (conv + skip * carried_ref[table].astype(jnp.float32))
-        out_ref[table] = gated.astype(out_ref.dtype)
-
-
-def fused_conv(piece, basis_spec, out_cols, query_gate, carried):
-    tables, rows, width = carried.shape
-    block_total = basis_spec.shape[0]
+def conv_body(finish):
+    def kernel(*refs):
+        if finish:
+            (piece_ref, basis_ref, out_cols_ref, spec_in_ref, query_ref, carried_ref,
+             fwd_ref, inv_ref, out_ref, resp_ref) = refs
+        else:
+            piece_ref, basis_ref, out_cols_ref, fwd_ref, out_ref, resp_ref = refs
+        block_total, tables, rows, lanes = piece_ref.shape
+        out_cols = out_cols_ref[...]
+        cols_hi, cols_lo = split_bf16(out_cols[:-1])
+        skip = out_cols[out_cols.shape[0] - 1 :]
+        cols = jnp.concatenate([cols_hi, cols_lo, cols_hi], axis=0)
+
+        def dot(a, b):
+            return jnp.dot(a, b, preferred_element_type=jnp.float32)
+
+        def fill(block, carry):
+            resp_ref[block] = dot(basis_ref[block], cols)
+            return carry
+
+        lax.fori_loop(0, block_total, fill, 0)
+        first = lax.broadcasted_iota(jnp.int32, (rows, lanes), 0) == 0
+        fwd = fwd_ref[...]
+
+        for table in range(tables):
+
+            def one_block(block, acc):
+                acc_real, acc_imag, edge = acc
+                block_rows = piece_ref[block, table]
+                signal = dot(fwd, jnp.concatenate([block_rows, block_rows], axis=0))
+                response = resp_ref[block]
+                resp_real = response[:rows]
+                resp_imag = response[rows:]
+                sig_real = signal[:rows]
+                sig_imag = signal[rows:]
+                acc_real = acc_real + (resp_real * sig_real - resp_imag * sig_imag)
+                acc_imag = acc_imag + (resp_real * sig_imag + resp_imag * sig_real)
+                edge = edge + resp_imag[0:1] * sig_imag[0:1]
+                return acc_real, acc_imag, edge
+
+            zeros = jnp.zeros((rows, lanes), jnp.float32)
+            acc_real, acc_imag, edge = lax.fori_loop(
+                0, block_total, one_block, (zeros, zeros, jnp.zeros((1, lanes), jnp.float32))
+            )
+            acc_real = acc_real + jnp.where(first, edge, 0.0)
+            acc_imag = jnp.where(first, edge, acc_imag)
+            spectrum = jnp.concatenate([acc_real, acc_imag], axis=0)
+            if not finish:
+                out_ref[table] = spectrum
+                continue
+            spectrum = spectrum + spec_in_ref[table]
+            spec_hi, spec_lo = split_bf16(spectrum)
+            conv = dot(inv_ref[...], jnp.concatenate([spec_hi, spec_lo, spec_hi], axis=0))
+            gated = query_ref[table] * (conv + skip * carried_ref[table].astype(jnp.float32))
+            out_ref[table] = gated.astype(out_ref.dtype)
+
+    return kernel
+
+
+def fused_conv(piece, basis_spec, out_cols, query_gate=None, carried=None, spec_in=None):
+    block_total, tables, rows, width = piece.shape
+    finish = spec_in is not None
     basis_hi, basis_lo = split_bf16(basis_spec)
     basis = jnp.concatenate([basis_hi, basis_hi, basis_lo], axis=2)
     fwd, inv = dft_tables(rows)
@@ -181,23 +188,38 @@
     inv = np.concatenate([inv[0], inv[0], inv[1]], axis=1)
     lanes = 768 if width % 768 == 0 else width
     tile3 = lambda i: (0, 0, i)
-    return pl.pallas_call(
-        conv_kernel,
-        grid=(width // lanes,),
-        in_specs=[
-            pl.BlockSpec((block_total, tables, rows, lanes), lambda i: (0, 0, 0, i)),
-            pl.BlockSpec(basis.shape, lambda i: (0, 0, 0)),
-            pl.BlockSpec((out_cols.shape[0], lanes), lambda i: (0, i)),
+    specs = [
+        pl.BlockSpec((block_total, tables, rows, lanes), lambda i: (0, 0, 0, i)),
+        pl.BlockSpec(basis.shape, lambda i: (0, 0, 0)),
+        pl.BlockSpec((out_cols.shape[0], lanes), lambda i: (0, i)),
+    ]
+    operands = [piece, basis, out_cols]
+    if finish:
+        specs += [
+            pl.BlockSpec((tables, 2 * rows, lanes), tile3),
             pl.BlockSpec((tables, rows, lanes), tile3),
             pl.BlockSpec((tables, rows, lanes), tile3),
-            pl.BlockSpec(fwd.shape, lambda i: (0, 0)),
-            pl.BlockSpec(inv.shape, lambda i: (0, 0)),
-        ],
-        out_specs=pl.BlockSpec((tables, rows, lanes), tile3),
-        out_shape=jax.ShapeDtypeStruct((tables, rows, width), jnp.bfloat16),
+        ]
+        operands += [spec_in, query_gate, carried]
+    specs.append(pl.BlockSpec(fwd.shape, lambda i: (0, 0)))
+    operands.append(jnp.asarray(fwd))
+    if finish:
+        specs.append(pl.BlockSpec(inv.shape, lambda i: (0, 0)))
+        operands.append(jnp.asarray(inv))
+        out_block = (tables, rows, lanes)
+        out_shape = jax.ShapeDtypeStruct((tables, rows, width), jnp.bfloat16)
+    else:
+        out_block = (tables, 2 * rows, lanes)
+        out_shape = jax.ShapeDtypeStruct((tables, 2 * rows, width), jnp.float32)
+    return pl.pallas_call(
+        conv_body(finish),
+        grid=(width // lanes,),
+        in_specs=specs,
+        out_specs=pl.BlockSpec(out_block, tile3),
+        out_shape=out_shape,
         scratch_shapes=[pltpu.VMEM((block_total, 2 * rows, lanes), jnp.float32)],
         compiler_params=pltpu.CompilerParams(vmem_limit_bytes=48 * 1024 * 1024),
-    )(piece, basis, out_cols, query_gate, carried, jnp.asarray(fwd), jnp.asarray(inv))
+    )(*operands)
 
 
 def shards(
@@ -237,7 +259,9 @@
     chips = seq_count // 2
     chip, core = position // 2, position % 2
     ring = (chip - jnp.arange(chips, dtype=jnp.int32)) % chips
-    order = jnp.concatenate([2 * ring + core, 2 * ring + 1 - core])
+    order = jnp.concatenate(
+        [2 * ring[:1] + core, 2 * ring[:1] + 1 - core, 2 * ring[1:] + core, 2 * ring[1:] + 1 - core]
+    )
     offsets = (position - order) * block_len
     lag_values = (offsets[:, None] + wrapped[None, :]).reshape(-1)
     basis_rows = filter_basis(lag_values, total_len, basis_in, basis_bias, basis_mid, basis_shift)
@@ -269,18 +293,21 @@
         jnp.float32
     )
     carried = (key_part * value_part * valid_mask[:, :, None]).astype(jnp.bfloat16)
-    same_core = [carried]
+    partner = [(i, i ^ 1) for i in range(seq_count)]
+    near = jnp.stack([carried, lax.ppermute(carried, "seq", partner)])
+    far = []
     for shift in range(1, chips):
-        same_core.append(
+        far.append(
             lax.ppermute(
                 carried, "seq", [(i, (i + 2 * shift) % seq_count) for i in range(seq_count)]
             )
         )
-    same_core = jnp.stack(same_core)
-    other_core = lax.ppermute(same_core, "seq", [(i, i ^ 1) for i in range(seq_count)])
-    piece = jnp.concatenate([same_core, other_core], axis=0)
-
-    return fused_conv(piece, basis_spec, gathered, query_gate, carried)
+    far = jnp.stack(far)
+    near_count = near.shape[0]
+    spectrum = fused_conv(near, basis_spec[:near_count], gathered)
+    far, spectrum = lax.optimization_barrier((far, spectrum))
+    far = jnp.concatenate([far, lax.ppermute(far, "seq", partner)], axis=0)
+    return fused_conv(far, basis_spec[near_count:], gathered, query_gate, carried, spectrum)
 
 
 def solution(mesh):

time: 200 us -> 194 us (0.970)
  waiting for transfers between devices: 98.5 us -> 91 us
  local copies, waits for them, and re-layouts: 12.6 us -> 14.8 us
    ppermute x1, waiting for transfers between devices: 17.4 us -> 10.3 us  [shards(): lax.ppermute(carried, 'seq', [(i, (i + 2 * shift) % seq_count) for i in r...]
    ppermute x1, starting transfers between devices: 2.62 us -> 0.01 us  [shards(): lax.ppermute(carried, 'seq', [(i, (i + 2 * shift) % seq_count) for i in r...]
    ppermute x1 -> x2, waiting for transfers between devices: 2.84 us -> 4.02 us  [the longest x1 2.24 us: shards(): far = jnp.concatenate([far, lax.ppermute(far, 'seq', partner)], axis=0)]
    pallas_call x1 -> x2, Pallas kernels: 13.1 us -> 14.1 us  [fused_conv(): pl.pallas_call(conv_body(finish), grid=(width // lanes,), in_specs=specs,...]
  transfers between devices with their start and end apart: 6 -> 7, of which waited for: 5 -> 6; matrix products, arithmetic and copies ran while one was open for 10% -> 10% of each run, Pallas kernels for 0% -> 3%
where the time goes in v14:
time: 194 us
  waiting for transfers between devices  91 us (47%)
  blocking collectives  30.3 us (16%)
  between operations  14.9 us (8%)
  local copies, waits for them, and re-layouts  14.8 us (8%)
  Pallas kernels  14.1 us (7%)
  matrix products  13 us (7%)
  starting transfers between devices  10.1 us (5%)
  other arithmetic  5.47 us (3%)
    all_to_all x1, waiting for transfers between devices, shards(): projected = lax.all_to_all(partial, 'fsdp', 0, 2, tiled=True)  54.1 us
    all_gather x1, waiting for transfers between devices, shards(): group_tokens = lax.all_gather(tokens, 'fsdp', axis=0, tiled=True)  18.6 us
    all_gather x1, blocking collectives, shards(): across = lax.all_gather(mine, 'fsdp', axis=0, tiled=False)  16.4 us
    pallas_call x2, Pallas kernels, fused_conv(): pl.pallas_call(conv_body(finish), grid=(width // lanes,), in_specs=specs,...  14.1 us
    all_gather x1, blocking collectives, shards(): gathered = lax.all_gather(across, ('groups', 'seq'), axis=0, tiled=False)  13.9 us
    ppermute x1, waiting for transfers between devices, shards(): lax.ppermute(carried, 'seq', [(i, (i + 2 * shift) % seq_count) for i in r...  10.3 us
    dot_general x1, matrix products, shards(): jnp.dot(group_tokens.reshape(group_rows * block_len, width), in_weight, p...  7.57 us
    all_to_all x1, starting transfers between devices, shards(): projected = lax.all_to_all(partial, 'fsdp', 0, 2, tiled=True)  4.64 us
  transfers between devices with their start and end apart: 7, of which 6 were waited for; matrix products, arithmetic and copies ran while one was open for 10% of the time, Pallas kernels for 3%

profile of v14, /device:TPU:0, one launch (start us, length us, event | category | flops | bytes accessed | tf_op | source)
XLA Modules:
  0.0 193.7 jit_solution(12907098696594091333)
XLA Ops:
  6.5 0.7 all-gather.5.cloned.1.call-update
  7.3 0.6 fusion.44
  9.1 0.1 fusion.38
  9.2 0.1 fusion.29
  9.3 0.1 fusion.32
  9.3 0.1 convert_bitcast_fusion
  9.4 1.5 broadcast_in_dim.25
  10.9 1.7 copy.32
  12.6 0.8 fusion.21
  13.4 16.4 %all-gather.2 = f32[4,129,48]{1,2,0:T(8,128)S(1)} all-gather(f32[1,129,48]{1,2,0:T(8,128)S(1)} %fusion.21), channel_id=2, replica_groups=mesh['groups'=2,'seq'=4,'fsdp'=4] {'fsdp'}, dimensions={0}, use_global_device_ids=true | all-gather | bytes 123840 | tf_op jit(solution)/shard_map/all_gather | solution.py:246
  29.8 13.9 %all-gather.1 = f32[32,129,48]{1,2,0:T(8,128)} all-gather(f32[4,129,48]{1,2,0:T(8,128)S(1)} %all-gather.2), channel_id=3, replica_groups=mesh['groups'=2,'seq'=4,'fsdp'=4] {'groups','seq'}, dimensions={0}, use_global_device_ids=true | all-gather | bytes 891648 | tf_op jit(solution)/shard_map/all_gather | solution.py:247
  43.7 3.6 %copy.34 = f32[129,4,8,48]{3,2,1,0:T(8,128)} copy(f32[129,4,8,48]{0,3,1,2:T(8,128)} %bitcast.48) | data formatting | bytes 1585152 | tf_op jit(solution)/shard_map/transpose | solution.py:248
  47.3 3.6 %reshape.216.refs_2_ = f32[129,1536]{1,0:T(8,128)} reshape(f32[129,4,8,48]{3,2,1,0:T(8,128)} %copy.34) | data formatting | bytes 1585152 | tf_op jit(solution)/shard_map/reshape | solution.py:248
  51.0 0.5 fusion.19
  51.5 0.6 fusion.28
  52.0 2.0 %fusion.3 = f32[1024,64]{0,1:T(8,128)S(1)} fusion(f32[17,64]{1,0:T(8,128)} %param.16, f32[64]{0:T(128)S(1)} %copy-done.7, f32[1024,8]{0,1:T(8,128)S(1)} %get-tuple-element.31, f32[1024,8]{0,1:T(8,128)S(1)} %get-tuple-element.30, f32[1024,1]{0,1:T(1,128)S(1)} %bitcast.57), kind=kOutput, calls=%fused_computation.13 | convolution fusion | flops 13469696 | bytes 336384 | tf_op jit(solution)/shard_map/dot_general | solution.py:54
  54.0 2.0 %broadcast_multiply_fusion.1 = (f32[1024,64]{0,1:T(8,128)S(1)}, f32[1024,64]{0,1:T(8,128)S(1)}) fusion(f32[1024]{0:T(1024)S(1)} %bitcast.56, f32[1024]{0:T(1024)S(1)} %broadcast_subtract_fusion, f32[64]{0:T(128)} %param.19, f32[1024,64]{0,1:T(8,128)S(1)} %fusion.3, f32[64,64]{1,0:T(8,128)} %param.18), kind=kOutput, calls=%fused_computation.38 | convolution fusion | flops 50528256 | bytes 811264 | tf_op jit(solution)/shard_map/dot_general | solution.py:55
  56.1 0.5 negate_select_fusion.2
  56.6 1.4 convolution_bitcast_fusion
  58.1 18.6 %all-gather.5.cloned.1.call-done = bf16[8,128,1536]{2,1,0:T(8,128)(2,1)} async-done(((bf16[2,128,1536]{2,1,0:T(8,128)(2,1)}), bf16[8,128,1536]{2,1,0:T(8,128)(2,1)}) %all-gather.5.cloned.1.call-update) | async-done | bytes 3145744 | tf_op jit(solution)/shard_map/all_gather | solution.py:272
  76.7 7.6 %convolution_convert_fusion = bf16[1024,1152]{1,0:T(8,128)(2,1)} fusion(bf16[1024,1536]{1,0:T(8,128)(2,1)} %bitcast.59, bf16[1536,1152]{1,0:T(8,128)(2,1)S(1)} %copy-done), kind=kOutput, calls=%fused_computation.1 | convolution fusion | flops 3625058304 | bytes 9043968 | tf_op jit(solution)/shard_map/dot_general | solution.py:276
  84.3 4.6 %all-to-all-start = ((bf16[8,128,1152]{2,1,0:T(8,128)(2,1)}), bf16[8,128,1152]{2,1,0:T(8,128)(2,1)}, u32[]{:S(2)}, u32[]{:S(2)}) async-start(bf16[8,128,1152]{2,1,0:T(8,128)(2,1)} %bitcast.49), calls=%async_computation | async-start | bytes 4718592 | tf_op jit(solution)/shard_map/all_to_all | solution.py:282
  88.9 0.1 compare_convert_fusion
  89.0 54.1 %all-to-all-done = bf16[8,128,1152]{2,1,0:T(8,128)(2,1)} async-done(((bf16[8,128,1152]{2,1,0:T(8,128)(2,1)}), bf16[8,128,1152]{2,1,0:T(8,128)(2,1)}, u32[]{:S(2)}, u32[]{:S(2)}) %all-to-all-start) | async-done | bytes 2359328 | tf_op jit(solution)/shard_map/all_to_all | solution.py:282
  143.1 1.9 copy.38
  145.0 0.1 fusion.43
  145.1 1.3 collective-permute-start
  146.4 1.5 collective-permute-start.1
  147.9 0.1 slice_reduce_fusion.2
  148.0 0.0 collective-permute-done
  148.0 3.2 %collective-permute-done.1 = bf16[2,1,4608]{2,1,0:T(2,128)(2,1)S(1)} collective-permute-done((bf16[2,1,4608]{2,1,0:T(2,128)(2,1)S(1)}, bf16[2,1,4608]{2,1,0:T(2,128)(2,1)S(1)}, u32[]{:S(2)}, u32[]{:S(2)}) %collective-permute-start.1) | collective-permute-done | bytes 18464 | tf_op jit(solution)/shard_map/ppermute | solution.py:21
  151.3 1.9 multiply_add_fusion
  153.2 0.0 copy-start.5
  153.2 0.3 fusion.42
  153.5 0.0 copy-start.3
  153.6 2.7 %collective-permute-start.3 = (bf16[2,128,1536]{2,1,0:T(8,128)(2,1)S(1)}, bf16[2,128,1536]{2,1,0:T(8,128)(2,1)S(1)}, u32[]{:S(2)}, u32[]{:S(2)}) collective-permute-start(bf16[2,128,1536]{2,1,0:T(8,128)(2,1)S(1)} %get-tuple-element.23.refs_5_), channel_id=1, source_target_pairs={{0,4},{4,0},{8,12},{12,8},{1,5},{5,1},{9,13},{13,9},{2,6},{6,2},{1... | collective-permute-start | bytes 2359304 | tf_op jit(solution)/shard_map/ppermute | solution.py:297
  156.3 0.0 collective-permute-start.2
  156.3 0.1 subtract_convert_fusion
  156.4 1.8 collective-permute-done.3
  158.2 0.1 pad_maximum_fusion.2.refs_0_
  158.4 0.0 copy-done.2
  158.4 5.5 %shard_map.130.refs_3_ = f32[2,256,1536]{2,1,0:T(8,128)S(1)} custom-call(bf16[2,2,128,1536]{3,2,1,0:T(8,128)(2,1)S(1)} %pad_maximum_fusion.2.refs_0_, bf16[2,256,384]{2,1,0:T(8,128)(2,1)S(1)} %pad_maximum_fusion.5.refs_1_, f32[129,1536]{1,0:T(8,128)S(1)} %copy-done.2, bf16[256,256]{1,0:T(8,128)(2,1)S(1)} %copy-done.3), custom_call_target="tpu_custom_call" | custom-call | tf_op jit(solution)/shard_map/pallas_call | solution.py:214
  163.9 1.6 copy-done.1
  165.6 10.3 %collective-permute-done.2 = bf16[2,128,1536]{2,1,0:T(8,128)(2,1)S(1)} collective-permute-done((bf16[2,128,1536]{2,1,0:T(8,128)(2,1)S(1)}, bf16[2,128,1536]{2,1,0:T(8,128)(2,1)S(1)}, u32[]{:S(2)}, u32[]{:S(2)}) %collective-permute-start.2) | collective-permute-done | bytes 786464 | tf_op jit(solution)/shard_map/ppermute | solution.py:301
  175.8 0.0 collective-permute-start.4
  175.9 2.2 %collective-permute-done.4 = bf16[1,2,128,1536]{3,2,1,0:T(8,128)(2,1)S(1)} collective-permute-done((bf16[1,2,128,1536]{3,2,1,0:T(8,128)(2,1)S(1)}, bf16[1,2,128,1536]{3,2,1,0:T(8,128)(2,1)S(1)}, u32[]{:S(2)}, u32[]{:S(2)}) %collective-permute-start.4) | collective-permute-done | bytes 786464 | tf_op jit(solution)/shard_map/ppermute | solution.py:309
  178.1 0.1 pad_maximum_fusion.3.refs_0_
  178.3 8.6 %shard_map.131 = bf16[2,128,1536]{2,1,0:T(8,128)(2,1)} custom-call(bf16[2,2,128,1536]{3,2,1,0:T(8,128)(2,1)S(1)} %pad_maximum_fusion.3.refs_0_, bf16[2,256,384]{2,1,0:T(8,128)(2,1)S(1)} %pad_maximum_fusion.6.refs_1_, f32[129,1536]{1,0:T(8,128)S(1)} %copy-done.2, f32[2,256,1536]{2,1,0:T(8,128)} %copy-done.1, f32[2,128,1536]{2,1,0:T(8,128)S(1)} %get-tuple-element.22.refs_4_, ...), custom_call_target="tpu_custom_call" | custom-call | tf_op jit(solution)/shard_map/pallas_call | solution.py:214
  (28 shorter events, 0.2 us)
Async XLA Ops:
  6.5 70.2 %copy-start = (bf16[1536,1152]{1,0:T(8,128)(2,1)S(1)}, bf16[1536,1152]{1,0:T(8,128)(2,1)}, u32[]{:S(2)}) copy-start(bf16[1536,1152]{1,0:T(8,128)(2,1)} %param.14) | copy-start | bytes 10616836
  6.5 70.1 %all-gather.5.cloned.1.call-start = ((), (), s32[]{:S(2)}) async-start(), calls=%async_computation.1 | async-start | bytes 3932160 | tf_op jit(solution)/shard_map/all_gather | solution.py:272
  43.7 8.3 %copy-start.7 = (f32[64]{0:T(128)S(1)}, f32[64]{0:T(128)}, u32[]{:S(2)}) copy-start(f32[64]{0:T(128)} %param.17) | copy-start | bytes 772
  84.3 4.6 %copy-start.8 = (s32[2,1]{0,1:T(1,128)S(1)}, s32[2,1]{0,1:T(1,128)}, u32[]{:S(2)}) copy-start(s32[2,1]{0,1:T(1,128)} %param.22) | copy-start | bytes 28
  84.3 58.8 %all-to-all-start = ((bf16[8,128,1152]{2,1,0:T(8,128)(2,1)}), bf16[8,128,1152]{2,1,0:T(8,128)(2,1)}, u32[]{:S(2)}, u32[]{:S(2)}) async-start(bf16[8,128,1152]{2,1,0:T(8,128)(2,1)} %bitcast.49), calls=%async_computation | async-start | bytes 4718592 | tf_op jit(solution)/shard_map/all_to_all | solution.py:282
  143.1 4.8 %copy-start.6 = (f32[3,4608]{1,0:T(4,128)S(1)}, f32[3,4608]{1,0:T(4,128)}, u32[]{:S(2)}) copy-start(f32[3,4608]{1,0:T(4,128)} %param.15) | copy-start | bytes 165892
  145.1 2.9 %collective-permute-start = (bf16[2,1,4608]{2,1,0:T(2,128)(2,1)S(1)}, bf16[2,1,4608]{2,1,0:T(2,128)(2,1)S(1)}, u32[]{:S(2)}, u32[]{:S(2)}) collective-permute-start(bf16[2,1,4608]{2,1,0:T(2,128)(2,1)S(1)} %get-tuple-element.24), channel_id=1, source_target_pairs={{0,4},{4,8},{8,12},{1,5},{5,9},{9,13},{2,6},{6,10},{10,14},{3,7},{... | collective-permute-start | bytes 55304 | tf_op jit(solution)/shard_map/ppermute | solution.py:19
  146.4 4.9 %collective-permute-start.1 = (bf16[2,1,4608]{2,1,0:T(2,128)(2,1)S(1)}, bf16[2,1,4608]{2,1,0:T(2,128)(2,1)S(1)}, u32[]{:S(2)}, u32[]{:S(2)}) collective-permute-start(bf16[2,1,4608]{2,1,0:T(2,128)(2,1)S(1)} %get-tuple-element.25), channel_id=1, source_target_pairs={{4,0},{8,4},{12,8},{5,1},{9,5},{13,9},{6,2},{10,6},{14,10},{7,3},{... | collective-permute-start | bytes 55304 | tf_op jit(solution)/shard_map/ppermute | solution.py:21
  153.2 3.1 %copy-start.5 = (f32[4,256,128]{2,1,0:T(8,128)S(1)}, f32[4,256,128]{2,1,0:T(8,128)}, u32[]{:S(2)}) copy-start(f32[4,256,128]{2,1,0:T(8,128)} %convolution_bitcast_fusion) | copy-start | bytes 1572868
  153.5 4.8 %copy-start.2 = (f32[129,1536]{1,0:T(8,128)S(1)}, f32[129,1536]{1,0:T(8,128)}, u32[]{:S(2)}) copy-start(f32[129,1536]{1,0:T(8,128)} %reshape.216.refs_2_) | copy-start | bytes 2377732
  153.5 4.8 %copy-start.3 = (bf16[256,256]{1,0:T(8,128)(2,1)S(1)}, bf16[256,256]{1,0:T(8,128)(2,1)}, u32[]{:S(2)}) copy-start(bf16[256,256]{1,0:T(8,128)(2,1)} %constant.124.clone.refs_3_.refs_6_) | copy-start | bytes 393220
  153.6 4.6 %collective-permute-start.3 = (bf16[2,128,1536]{2,1,0:T(8,128)(2,1)S(1)}, bf16[2,128,1536]{2,1,0:T(8,128)(2,1)S(1)}, u32[]{:S(2)}, u32[]{:S(2)}) collective-permute-start(bf16[2,128,1536]{2,1,0:T(8,128)(2,1)S(1)} %get-tuple-element.23.refs_5_), channel_id=1, source_target_pairs={{0,4},{4,0},{8,12},{12,8},{1,5},{5,1},{9,13},{13,9},{2,6},{6,2},{1... | collective-permute-start | bytes 2359304 | tf_op jit(solution)/shard_map/ppermute | solution.py:297
  156.3 19.5 %collective-permute-start.2 = (bf16[2,128,1536]{2,1,0:T(8,128)(2,1)S(1)}, bf16[2,128,1536]{2,1,0:T(8,128)(2,1)S(1)}, u32[]{:S(2)}, u32[]{:S(2)}) collective-permute-start(bf16[2,128,1536]{2,1,0:T(8,128)(2,1)S(1)} %get-tuple-element.23.refs_5_), channel_id=1, source_target_pairs={{0,8},{4,12},{8,0},{12,4},{1,9},{5,13},{9,1},{13,5},{2,10},{6,14},... | collective-permute-start | bytes 2359304 | tf_op jit(solution)/shard_map/ppermute | solution.py:301
  163.9 1.6 copy-start.1
  165.6 12.7 %copy-start.4 = (bf16[128,768]{1,0:T(8,128)(2,1)S(1)}, bf16[128,768]{1,0:T(8,128)(2,1)}, u32[]{:S(2)}) copy-start(bf16[128,768]{1,0:T(8,128)(2,1)} %constant.125.clone.refs_7_) | copy-start | bytes 589828
  175.8 2.3 %collective-permute-start.4 = (bf16[1,2,128,1536]{3,2,1,0:T(8,128)(2,1)S(1)}, bf16[1,2,128,1536]{3,2,1,0:T(8,128)(2,1)S(1)}, u32[]{:S(2)}, u32[]{:S(2)}) collective-permute-start(bf16[1,2,128,1536]{3,2,1,0:T(8,128)(2,1)S(1)} %bitcast.51), channel_id=1, source_target_pairs={{0,4},{4,0},{8,12},{12,8},{1,5},{5,1},{9,13},{13,9},{2,6},{6,2},{1... | collective-permute-start | bytes 2359304 | tf_op jit(solution)/shard_map/ppermute | solution.py:309
Sparse Core Ops, SparseCore 0:
  8.9 67.7 all-gather.4

commit v15 on v14

--- a/solution.py
+++ b/solution.py
@@ -37,6 +37,26 @@
     sources = (own - jnp.arange(count, dtype=jnp.int32)) % count
     order = jnp.argsort(sources)
     return jnp.take(stacked, order, axis=0)
+
+
+def relay_gather(values, axis):
+    count = lax.axis_size(axis)
+    own = lax.axis_index(axis)
+    from_left, from_right = [], []
+    rightward, leftward = values, values
+    for step in range(1, count):
+        rightward = lax.ppermute(rightward, axis, [(j, j + 1) for j in range(step - 1, count - 1)])
+        leftward = lax.ppermute(leftward, axis, [(j, j - 1) for j in range(1, count - step + 1)])
+        from_left.append(rightward)
+        from_right.append(leftward)
+    chunks = []
+    for target in range(count):
+        chunk = values
+        for step in range(1, count):
+            chunk = jnp.where(own - step == target, from_left[step - 1], chunk)
+            chunk = jnp.where(own + step == target, from_right[step - 1], chunk)
+        chunks.append(chunk)
+    return jnp.concatenate(chunks, axis=0)
 
 
 def filter_basis(lag_values, total_len, basis_in, basis_bias, basis_mid, basis_shift):
@@ -269,7 +289,7 @@
     paired = jnp.concatenate([basis_rows * ahead_mask, basis_rows * (1.0 - ahead_mask)], axis=1)
     paired = paired.reshape(block_total, 2 * block_len, paired.shape[-1])
     basis_spec = jnp.einsum("gf,bfk->bgk", forward, paired, precision=lax.Precision.HIGHEST)
-    group_tokens = lax.all_gather(tokens, "fsdp", axis=0, tiled=True)
+    group_tokens = relay_gather(tokens, "fsdp")
     group_tokens, basis_spec, gathered = lax.optimization_barrier((group_tokens, basis_spec, gathered))
     group_rows = group_tokens.shape[0]
     local_cols = in_weight.shape[1]

time: 194 us -> 211 us (1.088)
  between operations: 14.9 us -> 1.57 us
  starting transfers between devices: 10.1 us -> 23.3 us
  waiting for transfers between devices: 91 us -> 102 us
  blocking collectives: 30.3 us -> 34.4 us
  other arithmetic: 5.47 us -> 9.5 us
    ppermute x0 -> x6, waiting for transfers between devices: none -> 32.9 us  [the longest x3 32.9 us: relay_gather(): lax.ppermute(leftward, axis, [(j, j - 1) for j in range(1, count - step +...]
    all_gather x1 -> x0, waiting for transfers between devices: 18.6 us -> none  [shards(): group_tokens = lax.all_gather(tokens, 'fsdp', axis=0, tiled=True)]
    ppermute x0 -> x6, starting transfers between devices: none -> 12 us  [the longest x3 7.88 us: relay_gather(): lax.ppermute(rightward, axis, [(j, j + 1) for j in range(step - 1, count...]
    all_gather x1, blocking collectives: 16.4 us -> 20.4 us  [shards(): across = lax.all_gather(mine, 'fsdp', axis=0, tiled=False)]
    select_n x0 -> x2, other arithmetic: none -> 3.58 us  [relay_gather(): chunk = jnp.where(own + step == target, from_right[step - 1], chunk)]
  transfers between devices with their start and end apart: 7 -> 12, of which waited for: 6 -> 7; matrix products, arithmetic and copies ran while one was open for 10% -> 9% of each run, Pallas kernels for 3% -> 3%
where the time goes in v15:
time: 211 us
  waiting for transfers between devices  102 us (48%)
  blocking collectives  34.4 us (16%)
  starting transfers between devices  23.3 us (11%)
  local copies, waits for them, and re-layouts  14.8 us (7%)
  Pallas kernels  14.1 us (7%)
  matrix products  10.9 us (5%)
  other arithmetic  9.5 us (5%)
    all_to_all x1, waiting for transfers between devices, shards(): projected = lax.all_to_all(partial, 'fsdp', 0, 2, tiled=True)  52.6 us
    ppermute x3, waiting for transfers between devices, relay_gather(): lax.ppermute(leftward, axis, [(j, j - 1) for j in range(1, count - step +...  32.9 us
    all_gather x1, blocking collectives, shards(): across = lax.all_gather(mine, 'fsdp', axis=0, tiled=False)  20.4 us
    pallas_call x2, Pallas kernels, fused_conv(): pl.pallas_call(conv_body(finish), grid=(width // lanes,), in_specs=specs,...  14.1 us
    all_gather x1, blocking collectives, shards(): gathered = lax.all_gather(across, ('groups', 'seq'), axis=0, tiled=False)  14 us
    ppermute x1, waiting for transfers between devices, shards(): lax.ppermute(carried, 'seq', [(i, (i + 2 * shift) % seq_count) for i in r...  10.3 us
    ppermute x3, starting transfers between devices, relay_gather(): lax.ppermute(rightward, axis, [(j, j + 1) for j in range(step - 1, count...  7.88 us
    all_to_all x1, starting transfers between devices, shards(): projected = lax.all_to_all(partial, 'fsdp', 0, 2, tiled=True)  5.77 us
  transfers between devices with their start and end apart: 12, of which 7 were waited for; matrix products, arithmetic and copies ran while one was open for 9% of the time, Pallas kernels for 3%

profile of v15, /device:TPU:0, one launch (start us, length us, event | category | flops | bytes accessed | tf_op | source)
XLA Modules:
  0.0 210.6 jit_solution(15430498109391771296)
XLA Ops:
  0.0 1.5 collective-permute-start
  1.6 6.5 %collective-permute-start.3 = (bf16[2,128,1536]{2,1,0:T(8,128)(2,1)}, bf16[2,128,1536]{2,1,0:T(8,128)(2,1)}, u32[]{:S(2)}, u32[]{:S(2)}) collective-permute-start(bf16[2,128,1536]{2,1,0:T(8,128)(2,1)} %param.13), channel_id=1, source_target_pairs={{0,1},{1,2},{2,3},{4,5},{5,6},{6,7},{8,9},{9,10},{10,11},{12,13},{... | collective-permute-start | bytes 2359304 | tf_op jit(solution)/shard_map/ppermute | solution.py:48
  8.0 0.6 fusion.44
  9.8 0.1 fusion.38
  9.9 0.1 fusion.29
  10.0 0.1 fusion.32
  10.0 0.1 convert_bitcast_fusion
  10.1 1.5 broadcast_in_dim.25
  11.6 1.7 copy.32
  13.4 0.8 fusion.21
  14.1 20.4 %all-gather.2 = f32[4,129,48]{1,2,0:T(8,128)S(1)} all-gather(f32[1,129,48]{1,2,0:T(8,128)S(1)} %fusion.21), channel_id=2, replica_groups=mesh['groups'=2,'seq'=4,'fsdp'=4] {'fsdp'}, dimensions={0}, use_global_device_ids=true | all-gather | bytes 123840 | tf_op jit(solution)/shard_map/all_gather | solution.py:266
  34.5 14.0 %all-gather.1 = f32[32,129,48]{1,2,0:T(8,128)} all-gather(f32[4,129,48]{1,2,0:T(8,128)S(1)} %all-gather.2), channel_id=3, replica_groups=mesh['groups'=2,'seq'=4,'fsdp'=4] {'groups','seq'}, dimensions={0}, use_global_device_ids=true | all-gather | bytes 891648 | tf_op jit(solution)/shard_map/all_gather | solution.py:267
  48.5 3.6 %copy.34 = f32[129,4,8,48]{3,2,1,0:T(8,128)} copy(f32[129,4,8,48]{0,3,1,2:T(8,128)} %bitcast.48) | data formatting | bytes 1585152 | tf_op jit(solution)/shard_map/transpose | solution.py:268
  52.2 3.6 %reshape.216.refs_2_ = f32[129,1536]{1,0:T(8,128)} reshape(f32[129,4,8,48]{3,2,1,0:T(8,128)} %copy.34) | data formatting | bytes 1585152 | tf_op jit(solution)/shard_map/reshape | solution.py:268
  55.8 0.5 fusion.19
  56.3 1.3 collective-permute-start.1
  57.6 0.7 collective-permute-start.4
  58.4 0.6 fusion.28
  58.9 2.0 fusion.3
  60.9 17.8 %collective-permute-done.1 = bf16[2,128,1536]{2,1,0:T(8,128)(2,1)S(1)} collective-permute-done((bf16[2,128,1536]{2,1,0:T(8,128)(2,1)}, bf16[2,128,1536]{2,1,0:T(8,128)(2,1)S(1)}, u32[]{:S(2)}, u32[]{:S(2)}) %collective-permute-start.1) | collective-permute-done | bytes 786464 | tf_op jit(solution)/shard_map/ppermute | solution.py:49
  78.7 1.3 collective-permute-start.2
  80.0 0.7 collective-permute-start.5
  80.7 2.0 broadcast_multiply_fusion.1
  82.8 0.5 negate_select_fusion.2
  83.3 1.4 convolution_bitcast_fusion
  84.8 15.0 %collective-permute-done.2 = bf16[2,128,1536]{2,1,0:T(8,128)(2,1)S(1)} collective-permute-done((bf16[2,128,1536]{2,1,0:T(8,128)(2,1)S(1)}, bf16[2,128,1536]{2,1,0:T(8,128)(2,1)S(1)}, u32[]{:S(2)}, u32[]{:S(2)}) %collective-permute-start.2) | collective-permute-done | bytes 786464 | tf_op jit(solution)/shard_map/ppermute | solution.py:49
  99.8 1.8 select_select_fusion.2
  101.6 1.8 select_select_fusion.3
  103.4 0.4 pad_maximum_fusion
  103.9 5.5 %convolution_convert_fusion = bf16[1024,1152]{1,0:T(8,128)(2,1)} fusion(bf16[1024,1536]{1,0:T(8,128)(2,1)S(1)} %bitcast.49, bf16[1536,1152]{1,0:T(8,128)(2,1)S(1)} %copy-done), kind=kOutput, calls=%fused_computation.1 | convolution fusion | flops 3625058304 | bytes 9043968 | tf_op jit(solution)/shard_map/dot_general | solution.py:296
  109.4 5.8 %all-to-all-start = ((bf16[8,128,1152]{2,1,0:T(8,128)(2,1)}), bf16[8,128,1152]{2,1,0:T(8,128)(2,1)}, u32[]{:S(2)}, u32[]{:S(2)}) async-start(bf16[8,128,1152]{2,1,0:T(8,128)(2,1)} %bitcast.50), calls=%async_computation | async-start | bytes 4718592 | tf_op jit(solution)/shard_map/all_to_all | solution.py:302
  115.2 52.6 %all-to-all-done = bf16[8,128,1152]{2,1,0:T(8,128)(2,1)} async-done(((bf16[8,128,1152]{2,1,0:T(8,128)(2,1)}), bf16[8,128,1152]{2,1,0:T(8,128)(2,1)}, u32[]{:S(2)}, u32[]{:S(2)}) %all-to-all-start) | async-done | bytes 2359328 | tf_op jit(solution)/shard_map/all_to_all | solution.py:302
  167.9 1.9 copy.38
  169.9 1.3 collective-permute-start.6
  171.2 1.5 collective-permute-start.7
  172.7 0.1 slice_reduce_fusion.2
  172.9 2.2 %collective-permute-done.7 = bf16[2,1,4608]{2,1,0:T(2,128)(2,1)S(1)} collective-permute-done((bf16[2,1,4608]{2,1,0:T(2,128)(2,1)S(1)}, bf16[2,1,4608]{2,1,0:T(2,128)(2,1)S(1)}, u32[]{:S(2)}, u32[]{:S(2)}) %collective-permute-start.7) | collective-permute-done | bytes 18464 | tf_op jit(solution)/shard_map/ppermute | solution.py:21
  175.0 1.9 multiply_add_fusion
  177.0 0.3 fusion.42
  177.3 2.7 %collective-permute-start.9 = (bf16[2,128,1536]{2,1,0:T(8,128)(2,1)S(1)}, bf16[2,128,1536]{2,1,0:T(8,128)(2,1)S(1)}, u32[]{:S(2)}, u32[]{:S(2)}) collective-permute-start(bf16[2,128,1536]{2,1,0:T(8,128)(2,1)S(1)} %get-tuple-element.27.refs_5_), channel_id=1, source_target_pairs={{0,4},{4,0},{8,12},{12,8},{1,5},{5,1},{9,13},{13,9},{2,6},{6,2},{1... | collective-permute-start | bytes 2359304 | tf_op jit(solution)/shard_map/ppermute | solution.py:317
  180.2 1.8 collective-permute-done.9
  182.0 0.1 pad_maximum_fusion.3.refs_0_
  182.1 5.5 %shard_map.130.refs_3_ = f32[2,256,1536]{2,1,0:T(8,128)S(1)} custom-call(bf16[2,2,128,1536]{3,2,1,0:T(8,128)(2,1)S(1)} %pad_maximum_fusion.3.refs_0_, bf16[2,256,384]{2,1,0:T(8,128)(2,1)S(1)} %pad_maximum_fusion.6.refs_1_, f32[129,1536]{1,0:T(8,128)S(1)} %copy-done.2, bf16[256,256]{1,0:T(8,128)(2,1)S(1)} %copy-done.3), custom_call_target="tpu_custom_call" | custom-call | tf_op jit(solution)/shard_map/pallas_call | solution.py:234
  187.7 1.6 copy-done.1
  189.3 10.3 %collective-permute-done.8 = bf16[2,128,1536]{2,1,0:T(8,128)(2,1)S(1)} collective-permute-done((bf16[2,128,1536]{2,1,0:T(8,128)(2,1)S(1)}, bf16[2,128,1536]{2,1,0:T(8,128)(2,1)S(1)}, u32[]{:S(2)}, u32[]{:S(2)}) %collective-permute-start.8) | collective-permute-done | bytes 786464 | tf_op jit(solution)/shard_map/ppermute | solution.py:321
  199.6 2.2 %collective-permute-done.10 = bf16[1,2,128,1536]{3,2,1,0:T(8,128)(2,1)S(1)} collective-permute-done((bf16[1,2,128,1536]{3,2,1,0:T(8,128)(2,1)S(1)}, bf16[1,2,128,1536]{3,2,1,0:T(8,128)(2,1)S(1)}, u32[]{:S(2)}, u32[]{:S(2)}) %collective-permute-start.10) | collective-permute-done | bytes 786464 | tf_op jit(solution)/shard_map/ppermute | solution.py:329
  201.9 0.1 pad_maximum_fusion.4.refs_0_
  202.0 8.6 %shard_map.131 = bf16[2,128,1536]{2,1,0:T(8,128)(2,1)} custom-call(bf16[2,2,128,1536]{3,2,1,0:T(8,128)(2,1)S(1)} %pad_maximum_fusion.4.refs_0_, bf16[2,256,384]{2,1,0:T(8,128)(2,1)S(1)} %pad_maximum_fusion.7.refs_1_, f32[129,1536]{1,0:T(8,128)S(1)} %copy-done.2, f32[2,256,1536]{2,1,0:T(8,128)} %copy-done.1, f32[2,128,1536]{2,1,0:T(8,128)S(1)} %get-tuple-element.26.refs_4_, ...), custom_call_target="tpu_custom_call" | custom-call | tf_op jit(solution)/shard_map/pallas_call | solution.py:234
  (42 shorter events, 0.5 us)
Async XLA Ops:
  0.0 103.9 %copy-start = (bf16[1536,1152]{1,0:T(8,128)(2,1)S(1)}, bf16[1536,1152]{1,0:T(8,128)(2,1)}, u32[]{:S(2)}) copy-start(bf16[1536,1152]{1,0:T(8,128)(2,1)} %param.14) | copy-start | bytes 10616836
  0.0 56.3 %collective-permute-start = (bf16[2,128,1536]{2,1,0:T(8,128)(2,1)}, bf16[2,128,1536]{2,1,0:T(8,128)(2,1)}, u32[]{:S(2)}, u32[]{:S(2)}) collective-permute-start(bf16[2,128,1536]{2,1,0:T(8,128)(2,1)} %param.13), channel_id=1, source_target_pairs={{1,0},{2,1},{3,2},{5,4},{6,5},{7,6},{9,8},{10,9},{11,10},{13,12},{... | collective-permute-start | bytes 2359304 | tf_op jit(solution)/shard_map/ppermute | solution.py:49
  1.6 56.0 %collective-permute-start.3 = (bf16[2,128,1536]{2,1,0:T(8,128)(2,1)}, bf16[2,128,1536]{2,1,0:T(8,128)(2,1)}, u32[]{:S(2)}, u32[]{:S(2)}) collective-permute-start(bf16[2,128,1536]{2,1,0:T(8,128)(2,1)} %param.13), channel_id=1, source_target_pairs={{0,1},{1,2},{2,3},{4,5},{5,6},{6,7},{8,9},{9,10},{10,11},{12,13},{... | collective-permute-start | bytes 2359304 | tf_op jit(solution)/shard_map/ppermute | solution.py:48
  48.5 10.4 %copy-start.8 = (f32[64]{0:T(128)S(1)}, f32[64]{0:T(128)}, u32[]{:S(2)}) copy-start(f32[64]{0:T(128)} %param.17) | copy-start | bytes 772
  55.7 44.1 %copy-start.6 = (bf16[2,128,1536]{2,1,0:T(8,128)(2,1)S(1)}, bf16[2,128,1536]{2,1,0:T(8,128)(2,1)}, u32[]{:S(2)}) copy-start(bf16[2,128,1536]{2,1,0:T(8,128)(2,1)} %param.13) | copy-start | bytes 2359300
  56.3 22.4 %collective-permute-start.1 = (bf16[2,128,1536]{2,1,0:T(8,128)(2,1)}, bf16[2,128,1536]{2,1,0:T(8,128)(2,1)S(1)}, u32[]{:S(2)}, u32[]{:S(2)}) collective-permute-start(bf16[2,128,1536]{2,1,0:T(8,128)(2,1)} %collective-permute-done), channel_id=1, source_target_pairs={{1,0},{2,1},{5,4},{6,5},{9,8},{10,9},{13,12},{14,13},{17,16},{18,1... | collective-permute-start | bytes 2359304 | tf_op jit(solution)/shard_map/ppermute | solution.py:49
  57.6 22.4 %collective-permute-start.4 = (bf16[2,128,1536]{2,1,0:T(8,128)(2,1)}, bf16[2,128,1536]{2,1,0:T(8,128)(2,1)S(1)}, u32[]{:S(2)}, u32[]{:S(2)}) collective-permute-start(bf16[2,128,1536]{2,1,0:T(8,128)(2,1)} %collective-permute-done.3), channel_id=1, source_target_pairs={{1,2},{2,3},{5,6},{6,7},{9,10},{10,11},{13,14},{14,15},{17,18},{18... | collective-permute-start | bytes 2359304 | tf_op jit(solution)/shard_map/ppermute | solution.py:48
  78.7 21.1 %collective-permute-start.2 = (bf16[2,128,1536]{2,1,0:T(8,128)(2,1)S(1)}, bf16[2,128,1536]{2,1,0:T(8,128)(2,1)S(1)}, u32[]{:S(2)}, u32[]{:S(2)}) collective-permute-start(bf16[2,128,1536]{2,1,0:T(8,128)(2,1)S(1)} %collective-permute-done.1), channel_id=1, source_target_pairs={{1,0},{5,4},{9,8},{13,12},{17,16},{21,20},{25,24},{29,28}} | collective-permute-start | bytes 2359304 | tf_op jit(solution)/shard_map/ppermute | solution.py:49
  80.0 19.8 %collective-permute-start.5 = (bf16[2,128,1536]{2,1,0:T(8,128)(2,1)S(1)}, bf16[2,128,1536]{2,1,0:T(8,128)(2,1)S(1)}, u32[]{:S(2)}, u32[]{:S(2)}) collective-permute-start(bf16[2,128,1536]{2,1,0:T(8,128)(2,1)S(1)} %collective-permute-done.4), channel_id=1, source_target_pairs={{2,3},{6,7},{10,11},{14,15},{18,19},{22,23},{26,27},{30,31}} | collective-permute-start | bytes 2359304 | tf_op jit(solution)/shard_map/ppermute | solution.py:48
  109.4 5.8 %copy-start.9 = (s32[2,1]{0,1:T(1,128)S(1)}, s32[2,1]{0,1:T(1,128)}, u32[]{:S(2)}) copy-start(s32[2,1]{0,1:T(1,128)} %param.22) | copy-start | bytes 28
  109.4 58.5 %all-to-all-start = ((bf16[8,128,1152]{2,1,0:T(8,128)(2,1)}), bf16[8,128,1152]{2,1,0:T(8,128)(2,1)}, u32[]{:S(2)}, u32[]{:S(2)}) async-start(bf16[8,128,1152]{2,1,0:T(8,128)(2,1)} %bitcast.50), calls=%async_computation | async-start | bytes 4718592 | tf_op jit(solution)/shard_map/all_to_all | solution.py:302
  167.9 4.8 %copy-start.7 = (f32[3,4608]{1,0:T(4,128)S(1)}, f32[3,4608]{1,0:T(4,128)}, u32[]{:S(2)}) copy-start(f32[3,4608]{1,0:T(4,128)} %param.15) | copy-start | bytes 165892
  169.9 2.9 %collective-permute-start.6 = (bf16[2,1,4608]{2,1,0:T(2,128)(2,1)S(1)}, bf16[2,1,4608]{2,1,0:T(2,128)(2,1)S(1)}, u32[]{:S(2)}, u32[]{:S(2)}) collective-permute-start(bf16[2,1,4608]{2,1,0:T(2,128)(2,1)S(1)} %get-tuple-element.28), channel_id=1, source_target_pairs={{0,4},{4,8},{8,12},{1,5},{5,9},{9,13},{2,6},{6,10},{10,14},{3,7},{... | collective-permute-start | bytes 55304 | tf_op jit(solution)/shard_map/ppermute | solution.py:19
  171.2 3.8 %collective-permute-start.7 = (bf16[2,1,4608]{2,1,0:T(2,128)(2,1)S(1)}, bf16[2,1,4608]{2,1,0:T(2,128)(2,1)S(1)}, u32[]{:S(2)}, u32[]{:S(2)}) collective-permute-start(bf16[2,1,4608]{2,1,0:T(2,128)(2,1)S(1)} %get-tuple-element.29), channel_id=1, source_target_pairs={{4,0},{8,4},{12,8},{5,1},{9,5},{13,9},{6,2},{10,6},{14,10},{7,3},{... | collective-permute-start | bytes 55304 | tf_op jit(solution)/shard_map/ppermute | solution.py:21
  177.0 3.1 %copy-start.5 = (f32[4,256,128]{2,1,0:T(8,128)S(1)}, f32[4,256,128]{2,1,0:T(8,128)}, u32[]{:S(2)}) copy-start(f32[4,256,128]{2,1,0:T(8,128)} %convolution_bitcast_fusion) | copy-start | bytes 1572868
  177.3 4.8 %copy-start.2 = (f32[129,1536]{1,0:T(8,128)S(1)}, f32[129,1536]{1,0:T(8,128)}, u32[]{:S(2)}) copy-start(f32[129,1536]{1,0:T(8,128)} %reshape.216.refs_2_) | copy-start | bytes 2377732
  177.3 4.8 %copy-start.3 = (bf16[256,256]{1,0:T(8,128)(2,1)S(1)}, bf16[256,256]{1,0:T(8,128)(2,1)}, u32[]{:S(2)}) copy-start(bf16[256,256]{1,0:T(8,128)(2,1)} %constant.133.clone.refs_3_.refs_6_) | copy-start | bytes 393220
  177.3 4.6 %collective-permute-start.9 = (bf16[2,128,1536]{2,1,0:T(8,128)(2,1)S(1)}, bf16[2,128,1536]{2,1,0:T(8,128)(2,1)S(1)}, u32[]{:S(2)}, u32[]{:S(2)}) collective-permute-start(bf16[2,128,1536]{2,1,0:T(8,128)(2,1)S(1)} %get-tuple-element.27.refs_5_), channel_id=1, source_target_pairs={{0,4},{4,0},{8,12},{12,8},{1,5},{5,1},{9,13},{13,9},{2,6},{6,2},{1... | collective-permute-start | bytes 2359304 | tf_op jit(solution)/shard_map/ppermute | solution.py:317
  180.1 19.5 %collective-permute-start.8 = (bf16[2,128,1536]{2,1,0:T(8,128)(2,1)S(1)}, bf16[2,128,1536]{2,1,0:T(8,128)(2,1)S(1)}, u32[]{:S(2)}, u32[]{:S(2)}) collective-permute-start(bf16[2,128,1536]{2,1,0:T(8,128)(2,1)S(1)} %get-tuple-element.27.refs_5_), channel_id=1, source_target_pairs={{0,8},{4,12},{8,0},{12,4},{1,9},{5,13},{9,1},{13,5},{2,10},{6,14},... | collective-permute-start | bytes 2359304 | tf_op jit(solution)/shard_map/ppermute | solution.py:321
  187.7 1.6 copy-start.1
  189.3 12.7 %copy-start.4 = (bf16[128,768]{1,0:T(8,128)(2,1)S(1)}, bf16[128,768]{1,0:T(8,128)(2,1)}, u32[]{:S(2)}) copy-start(bf16[128,768]{1,0:T(8,128)(2,1)} %constant.134.clone.refs_7_) | copy-start | bytes 589828
  199.6 2.3 %collective-permute-start.10 = (bf16[1,2,128,1536]{3,2,1,0:T(8,128)(2,1)S(1)}, bf16[1,2,128,1536]{3,2,1,0:T(8,128)(2,1)S(1)}, u32[]{:S(2)}, u32[]{:S(2)}) collective-permute-start(bf16[1,2,128,1536]{3,2,1,0:T(8,128)(2,1)S(1)} %bitcast.52), channel_id=1, source_target_pairs={{0,4},{4,0},{8,12},{12,8},{1,5},{5,1},{9,13},{13,9},{2,6},{6,2},{1... | collective-permute-start | bytes 2359304 | tf_op jit(solution)/shard_map/ppermute | solution.py:329

commit v16 on v15

--- a/solution.py
+++ b/solution.py
@@ -290,7 +290,7 @@
     paired = paired.reshape(block_total, 2 * block_len, paired.shape[-1])
     basis_spec = jnp.einsum("gf,bfk->bgk", forward, paired, precision=lax.Precision.HIGHEST)
     group_tokens = relay_gather(tokens, "fsdp")
-    group_tokens, basis_spec, gathered = lax.optimization_barrier((group_tokens, basis_spec, gathered))
+    group_tokens, basis_spec = lax.optimization_barrier((group_tokens, basis_spec))
     group_rows = group_tokens.shape[0]
     local_cols = in_weight.shape[1]
     partial = jnp.dot(
@@ -300,6 +300,7 @@
     ).astype(jnp.bfloat16)
     partial = partial.reshape(group_rows, block_len, local_cols)
     projected = lax.all_to_all(partial, "fsdp", 0, 2, tiled=True)
+    projected, gathered = lax.optimization_barrier((projected, gathered))
     padded = padded_2(projected, (("seq", 1),), 1)
     shorted = (
         short_weight[0] * padded[:, :-2]

time: 211 us -> 203 us (0.962)
  waiting for transfers between devices: 102 us -> 57.8 us
  blocking collectives: 34.4 us -> 68.6 us
    all_to_all x1, waiting for transfers between devices: 52.6 us -> 0.01 us  [shards(): projected = lax.all_to_all(partial, 'fsdp', 0, 2, tiled=True)]
    all_gather x1, blocking collectives: 20.4 us -> 54.6 us  [shards(): across = lax.all_gather(mine, 'fsdp', axis=0, tiled=False)]
    ppermute x3, waiting for transfers between devices: 32.9 us -> 42 us  [relay_gather(): lax.ppermute(leftward, axis, [(j, j - 1) for j in range(1, count - step +...]
where the time goes in v16:
time: 203 us; the launch traced here: 202 us
  blocking collectives  68.6 us (34%)
  waiting for transfers between devices  57.8 us (28%)
  starting transfers between devices  25.1 us (12%)
  local copies, waits for them, and re-layouts  14.2 us (7%)
  Pallas kernels  14.1 us (7%)
  matrix products  11 us (5%)
  other arithmetic  9.5 us (5%)
    all_gather x1, blocking collectives, shards(): across = lax.all_gather(mine, 'fsdp', axis=0, tiled=False)  54.6 us
    ppermute x3, waiting for transfers between devices, relay_gather(): lax.ppermute(leftward, axis, [(j, j - 1) for j in range(1, count - step +...  42 us
    pallas_call x2, Pallas kernels, fused_conv(): pl.pallas_call(conv_body(finish), grid=(width // lanes,), in_specs=specs,...  14.1 us
    all_gather x1, blocking collectives, shards(): gathered = lax.all_gather(across, ('groups', 'seq'), axis=0, tiled=False)  14 us
    ppermute x1, waiting for transfers between devices, shards(): lax.ppermute(carried, 'seq', [(i, (i + 2 * shift) % seq_count) for i in r...  10.3 us
    ppermute x3, starting transfers between devices, relay_gather(): lax.ppermute(rightward, axis, [(j, j + 1) for j in range(step - 1, count...  7.91 us
    all_to_all x1, starting transfers between devices, shards(): projected = lax.all_to_all(partial, 'fsdp', 0, 2, tiled=True)  6.83 us
    dot_general x1, matrix products, shards(): jnp.dot(group_tokens.reshape(group_rows * block_len, width), in_weight, p...  5.51 us
  transfers between devices with their start and end apart: 12, of which 7 were waited for; matrix products, arithmetic and copies ran while one was open for 9% of the time, Pallas kernels for 3%

profile of v16, /device:TPU:0, one launch (start us, length us, event | category | flops | bytes accessed | tf_op | source)
XLA Modules:
  0.0 201.9 jit_solution(14750060684589303513)
XLA Ops:
  0.0 1.5 collective-permute-start
  1.6 6.5 %collective-permute-start.3 = (bf16[2,128,1536]{2,1,0:T(8,128)(2,1)}, bf16[2,128,1536]{2,1,0:T(8,128)(2,1)}, u32[]{:S(2)}, u32[]{:S(2)}) collective-permute-start(bf16[2,128,1536]{2,1,0:T(8,128)(2,1)} %param.13), channel_id=1, source_target_pairs={{0,1},{1,2},{2,3},{4,5},{5,6},{6,7},{8,9},{9,10},{10,11},{12,13},{... | collective-permute-start | bytes 2359304 | tf_op jit(solution)/shard_map/ppermute | solution.py:48
  8.1 0.6 fusion.44
  10.0 0.1 fusion.38
  10.1 0.1 fusion.29
  10.2 0.1 fusion.32
  10.2 0.1 convert_bitcast_fusion
  10.4 0.5 fusion.19
  10.9 12.2 %collective-permute-done = bf16[2,128,1536]{2,1,0:T(8,128)(2,1)} collective-permute-done((bf16[2,128,1536]{2,1,0:T(8,128)(2,1)}, bf16[2,128,1536]{2,1,0:T(8,128)(2,1)}, u32[]{:S(2)}, u32[]{:S(2)}) %collective-permute-start) | collective-permute-done | bytes 786464 | tf_op jit(solution)/shard_map/ppermute | solution.py:49
  23.0 1.3 collective-permute-start.1
  24.3 0.7 collective-permute-start.4
  25.1 0.6 fusion.28
  25.6 2.0 fusion.3
  27.6 16.2 %collective-permute-done.1 = bf16[2,128,1536]{2,1,0:T(8,128)(2,1)S(1)} collective-permute-done((bf16[2,128,1536]{2,1,0:T(8,128)(2,1)}, bf16[2,128,1536]{2,1,0:T(8,128)(2,1)S(1)}, u32[]{:S(2)}, u32[]{:S(2)}) %collective-permute-start.1) | collective-permute-done | bytes 786464 | tf_op jit(solution)/shard_map/ppermute | solution.py:49
  43.9 1.3 collective-permute-start.2
  45.2 0.7 collective-permute-start.5
  45.9 2.0 %broadcast_multiply_fusion.1 = (f32[1024,64]{0,1:T(8,128)S(1)}, f32[1024,64]{0,1:T(8,128)S(1)}) fusion(f32[1024]{0:T(1024)S(1)} %bitcast.57, f32[1024]{0:T(1024)S(1)} %broadcast_subtract_fusion, f32[64]{0:T(128)} %param.19, f32[1024,64]{0,1:T(8,128)S(1)} %fusion.3, f32[64,64]{1,0:T(8,128)} %param.18), kind=kOutput, calls=%fused_computation.43 | convolution fusion | flops 50528256 | bytes 811264 | tf_op jit(solution)/shard_map/dot_general | solution.py:75
  48.0 0.5 negate_select_fusion.2
  48.5 1.4 convolution_bitcast_fusion
  49.9 13.6 %collective-permute-done.2 = bf16[2,128,1536]{2,1,0:T(8,128)(2,1)S(1)} collective-permute-done((bf16[2,128,1536]{2,1,0:T(8,128)(2,1)S(1)}, bf16[2,128,1536]{2,1,0:T(8,128)(2,1)S(1)}, u32[]{:S(2)}, u32[]{:S(2)}) %collective-permute-start.2) | collective-permute-done | bytes 786464 | tf_op jit(solution)/shard_map/ppermute | solution.py:49
  63.6 1.8 select_select_fusion.2
  65.3 1.8 select_select_fusion.3
  67.1 0.4 pad_maximum_fusion
  67.6 5.5 %convolution_convert_fusion = bf16[1024,1152]{1,0:T(8,128)(2,1)} fusion(bf16[1024,1536]{1,0:T(8,128)(2,1)S(1)} %bitcast.49, bf16[1536,1152]{1,0:T(8,128)(2,1)S(1)} %copy-done), kind=kOutput, calls=%fused_computation.1 | convolution fusion | flops 3625058304 | bytes 9043968 | tf_op jit(solution)/shard_map/dot_general | solution.py:296
  73.1 6.8 %all-to-all-start = ((bf16[8,128,1152]{2,1,0:T(8,128)(2,1)}), bf16[8,128,1152]{2,1,0:T(8,128)(2,1)}, u32[]{:S(2)}, u32[]{:S(2)}) async-start(bf16[8,128,1152]{2,1,0:T(8,128)(2,1)} %bitcast.50), calls=%async_computation | async-start | bytes 4718592 | tf_op jit(solution)/shard_map/all_to_all | solution.py:302
  80.0 0.8 broadcast_in_dim.25
  80.8 1.8 copy.33
  82.5 0.8 fusion.21
  83.3 54.6 %all-gather.2 = f32[4,129,48]{1,2,0:T(8,128)S(1)} all-gather(f32[1,129,48]{1,2,0:T(8,128)S(1)} %fusion.21), channel_id=2, replica_groups=mesh['groups'=2,'seq'=4,'fsdp'=4] {'fsdp'}, dimensions={0}, use_global_device_ids=true | all-gather | bytes 123840 | tf_op jit(solution)/shard_map/all_gather | solution.py:266
  137.9 14.0 %all-gather.1 = f32[32,129,48]{1,2,0:T(8,128)} all-gather(f32[4,129,48]{1,2,0:T(8,128)S(1)} %all-gather.2), channel_id=3, replica_groups=mesh['groups'=2,'seq'=4,'fsdp'=4] {'groups','seq'}, dimensions={0}, use_global_device_ids=true | all-gather | bytes 891648 | tf_op jit(solution)/shard_map/all_gather | solution.py:267
  151.9 3.6 %copy.35 = f32[129,4,8,48]{3,2,1,0:T(8,128)} copy(f32[129,4,8,48]{0,3,1,2:T(8,128)} %bitcast.48) | data formatting | bytes 1585152 | tf_op jit(solution)/shard_map/transpose | solution.py:268
  155.5 3.6 %reshape.218.refs_2_ = f32[129,1536]{1,0:T(8,128)} reshape(f32[129,4,8,48]{3,2,1,0:T(8,128)} %copy.35) | data formatting | bytes 1585152 | tf_op jit(solution)/shard_map/reshape | solution.py:268
  159.2 1.9 copy.38
  161.2 2.3 %collective-permute-start.6 = (bf16[2,1,4608]{2,1,0:T(2,128)(2,1)S(1)}, bf16[2,1,4608]{2,1,0:T(2,128)(2,1)S(1)}, u32[]{:S(2)}, u32[]{:S(2)}) collective-permute-start(bf16[2,1,4608]{2,1,0:T(2,128)(2,1)S(1)} %get-tuple-element.30), channel_id=1, source_target_pairs={{0,4},{4,8},{8,12},{1,5},{5,9},{9,13},{2,6},{6,10},{10,14},{3,7},{... | collective-permute-start | bytes 55304 | tf_op jit(solution)/shard_map/ppermute | solution.py:19
  163.5 1.5 collective-permute-start.7
  164.9 0.1 slice_reduce_fusion.2
  165.1 1.5 collective-permute-done.7
  166.6 1.9 multiply_add_fusion
  168.5 0.3 fusion.42
  168.8 2.5 %collective-permute-start.9 = (bf16[2,128,1536]{2,1,0:T(8,128)(2,1)S(1)}, bf16[2,128,1536]{2,1,0:T(8,128)(2,1)S(1)}, u32[]{:S(2)}, u32[]{:S(2)}) collective-permute-start(bf16[2,128,1536]{2,1,0:T(8,128)(2,1)S(1)} %get-tuple-element.29.refs_5_), channel_id=1, source_target_pairs={{0,4},{4,0},{8,12},{12,8},{1,5},{5,1},{9,13},{13,9},{2,6},{6,2},{1... | collective-permute-start | bytes 2359304 | tf_op jit(solution)/shard_map/ppermute | solution.py:318
  171.5 1.8 collective-permute-done.9
  173.2 0.1 pad_maximum_fusion.3.refs_0_
  173.4 5.5 %shard_map.130.refs_3_ = f32[2,256,1536]{2,1,0:T(8,128)S(1)} custom-call(bf16[2,2,128,1536]{3,2,1,0:T(8,128)(2,1)S(1)} %pad_maximum_fusion.3.refs_0_, bf16[2,256,384]{2,1,0:T(8,128)(2,1)S(1)} %pad_maximum_fusion.6.refs_1_, f32[129,1536]{1,0:T(8,128)S(1)} %copy-done.2, bf16[256,256]{1,0:T(8,128)(2,1)S(1)} %copy-done.3), custom_call_target="tpu_custom_call" | custom-call | tf_op jit(solution)/shard_map/pallas_call | solution.py:234
  178.9 1.6 copy-done.1
  180.6 10.3 %collective-permute-done.8 = bf16[2,128,1536]{2,1,0:T(8,128)(2,1)S(1)} collective-permute-done((bf16[2,128,1536]{2,1,0:T(8,128)(2,1)S(1)}, bf16[2,128,1536]{2,1,0:T(8,128)(2,1)S(1)}, u32[]{:S(2)}, u32[]{:S(2)}) %collective-permute-start.8) | collective-permute-done | bytes 786464 | tf_op jit(solution)/shard_map/ppermute | solution.py:322
  190.9 2.2 %collective-permute-done.10 = bf16[1,2,128,1536]{3,2,1,0:T(8,128)(2,1)S(1)} collective-permute-done((bf16[1,2,128,1536]{3,2,1,0:T(8,128)(2,1)S(1)}, bf16[1,2,128,1536]{3,2,1,0:T(8,128)(2,1)S(1)}, u32[]{:S(2)}, u32[]{:S(2)}) %collective-permute-start.10) | collective-permute-done | bytes 786464 | tf_op jit(solution)/shard_map/ppermute | solution.py:330
  193.1 0.1 pad_maximum_fusion.4.refs_0_
  193.3 8.6 %shard_map.131 = bf16[2,128,1536]{2,1,0:T(8,128)(2,1)} custom-call(bf16[2,2,128,1536]{3,2,1,0:T(8,128)(2,1)S(1)} %pad_maximum_fusion.4.refs_0_, bf16[2,256,384]{2,1,0:T(8,128)(2,1)S(1)} %pad_maximum_fusion.7.refs_1_, f32[129,1536]{1,0:T(8,128)S(1)} %copy-done.2, f32[2,256,1536]{2,1,0:T(8,128)} %copy-done.1, f32[2,128,1536]{2,1,0:T(8,128)S(1)} %get-tuple-element.28.refs_4_, ...), custom_call_target="tpu_custom_call" | custom-call | tf_op jit(solution)/shard_map/pallas_call | solution.py:234
  (42 shorter events, 0.5 us)
Async XLA Ops:
  0.0 67.6 %copy-start = (bf16[1536,1152]{1,0:T(8,128)(2,1)S(1)}, bf16[1536,1152]{1,0:T(8,128)(2,1)}, u32[]{:S(2)}) copy-start(bf16[1536,1152]{1,0:T(8,128)(2,1)} %param.14) | copy-start | bytes 10616836
  0.0 23.0 %collective-permute-start = (bf16[2,128,1536]{2,1,0:T(8,128)(2,1)}, bf16[2,128,1536]{2,1,0:T(8,128)(2,1)}, u32[]{:S(2)}, u32[]{:S(2)}) collective-permute-start(bf16[2,128,1536]{2,1,0:T(8,128)(2,1)} %param.13), channel_id=1, source_target_pairs={{1,0},{2,1},{3,2},{5,4},{6,5},{7,6},{9,8},{10,9},{11,10},{13,12},{... | collective-permute-start | bytes 2359304 | tf_op jit(solution)/shard_map/ppermute | solution.py:49
  1.6 22.8 %collective-permute-start.3 = (bf16[2,128,1536]{2,1,0:T(8,128)(2,1)}, bf16[2,128,1536]{2,1,0:T(8,128)(2,1)}, u32[]{:S(2)}, u32[]{:S(2)}) collective-permute-start(bf16[2,128,1536]{2,1,0:T(8,128)(2,1)} %param.13), channel_id=1, source_target_pairs={{0,1},{1,2},{2,3},{4,5},{5,6},{6,7},{8,9},{9,10},{10,11},{12,13},{... | collective-permute-start | bytes 2359304 | tf_op jit(solution)/shard_map/ppermute | solution.py:48
  10.2 53.3 %copy-start.6 = (bf16[2,128,1536]{2,1,0:T(8,128)(2,1)S(1)}, bf16[2,128,1536]{2,1,0:T(8,128)(2,1)}, u32[]{:S(2)}) copy-start(bf16[2,128,1536]{2,1,0:T(8,128)(2,1)} %param.13) | copy-start | bytes 2359300
  23.0 20.8 %collective-permute-start.1 = (bf16[2,128,1536]{2,1,0:T(8,128)(2,1)}, bf16[2,128,1536]{2,1,0:T(8,128)(2,1)S(1)}, u32[]{:S(2)}, u32[]{:S(2)}) collective-permute-start(bf16[2,128,1536]{2,1,0:T(8,128)(2,1)} %collective-permute-done), channel_id=1, source_target_pairs={{1,0},{2,1},{5,4},{6,5},{9,8},{10,9},{13,12},{14,13},{17,16},{18,1... | collective-permute-start | bytes 2359304 | tf_op jit(solution)/shard_map/ppermute | solution.py:49
  24.3 20.8 %collective-permute-start.4 = (bf16[2,128,1536]{2,1,0:T(8,128)(2,1)}, bf16[2,128,1536]{2,1,0:T(8,128)(2,1)S(1)}, u32[]{:S(2)}, u32[]{:S(2)}) collective-permute-start(bf16[2,128,1536]{2,1,0:T(8,128)(2,1)} %collective-permute-done.3), channel_id=1, source_target_pairs={{1,2},{2,3},{5,6},{6,7},{9,10},{10,11},{13,14},{14,15},{17,18},{18... | collective-permute-start | bytes 2359304 | tf_op jit(solution)/shard_map/ppermute | solution.py:48
  43.9 19.7 %collective-permute-start.2 = (bf16[2,128,1536]{2,1,0:T(8,128)(2,1)S(1)}, bf16[2,128,1536]{2,1,0:T(8,128)(2,1)S(1)}, u32[]{:S(2)}, u32[]{:S(2)}) collective-permute-start(bf16[2,128,1536]{2,1,0:T(8,128)(2,1)S(1)} %collective-permute-done.1), channel_id=1, source_target_pairs={{1,0},{5,4},{9,8},{13,12},{17,16},{21,20},{25,24},{29,28}} | collective-permute-start | bytes 2359304 | tf_op jit(solution)/shard_map/ppermute | solution.py:49
  45.2 18.4 %collective-permute-start.5 = (bf16[2,128,1536]{2,1,0:T(8,128)(2,1)S(1)}, bf16[2,128,1536]{2,1,0:T(8,128)(2,1)S(1)}, u32[]{:S(2)}, u32[]{:S(2)}) collective-permute-start(bf16[2,128,1536]{2,1,0:T(8,128)(2,1)S(1)} %collective-permute-done.4), channel_id=1, source_target_pairs={{2,3},{6,7},{10,11},{14,15},{18,19},{22,23},{26,27},{30,31}} | collective-permute-start | bytes 2359304 | tf_op jit(solution)/shard_map/ppermute | solution.py:48
  73.1 6.8 %copy-start.8 = (f32[384]{0:T(512)S(1)}, f32[384]{0:T(512)}, u32[]{:S(2)}) copy-start(f32[384]{0:T(512)} %param.21) | copy-start | bytes 4612
  73.1 86.1 %all-to-all-start = ((bf16[8,128,1152]{2,1,0:T(8,128)(2,1)}), bf16[8,128,1152]{2,1,0:T(8,128)(2,1)}, u32[]{:S(2)}, u32[]{:S(2)}) async-start(bf16[8,128,1152]{2,1,0:T(8,128)(2,1)} %bitcast.50), calls=%async_computation | async-start | bytes 4718592 | tf_op jit(solution)/shard_map/all_to_all | solution.py:302
  151.9 7.2 %copy-start.9 = (s32[2,1]{0,1:T(1,128)S(1)}, s32[2,1]{0,1:T(1,128)}, u32[]{:S(2)}) copy-start(s32[2,1]{0,1:T(1,128)} %param.22) | copy-start | bytes 28
  159.2 5.8 %copy-start.7 = (f32[3,4608]{1,0:T(4,128)S(1)}, f32[3,4608]{1,0:T(4,128)}, u32[]{:S(2)}) copy-start(f32[3,4608]{1,0:T(4,128)} %param.15) | copy-start | bytes 165892
  161.2 3.9 %collective-permute-start.6 = (bf16[2,1,4608]{2,1,0:T(2,128)(2,1)S(1)}, bf16[2,1,4608]{2,1,0:T(2,128)(2,1)S(1)}, u32[]{:S(2)}, u32[]{:S(2)}) collective-permute-start(bf16[2,1,4608]{2,1,0:T(2,128)(2,1)S(1)} %get-tuple-element.30), channel_id=1, source_target_pairs={{0,4},{4,8},{8,12},{1,5},{5,9},{9,13},{2,6},{6,10},{10,14},{3,7},{... | collective-permute-start | bytes 55304 | tf_op jit(solution)/shard_map/ppermute | solution.py:19
  163.5 3.1 %collective-permute-start.7 = (bf16[2,1,4608]{2,1,0:T(2,128)(2,1)S(1)}, bf16[2,1,4608]{2,1,0:T(2,128)(2,1)S(1)}, u32[]{:S(2)}, u32[]{:S(2)}) collective-permute-start(bf16[2,1,4608]{2,1,0:T(2,128)(2,1)S(1)} %get-tuple-element.31), channel_id=1, source_target_pairs={{4,0},{8,4},{12,8},{5,1},{9,5},{13,9},{6,2},{10,6},{14,10},{7,3},{... | collective-permute-start | bytes 55304 | tf_op jit(solution)/shard_map/ppermute | solution.py:21
  168.5 2.8 %copy-start.5 = (f32[4,256,128]{2,1,0:T(8,128)S(1)}, f32[4,256,128]{2,1,0:T(8,128)}, u32[]{:S(2)}) copy-start(f32[4,256,128]{2,1,0:T(8,128)} %convolution_bitcast_fusion) | copy-start | bytes 1572868
  168.8 4.6 %copy-start.2 = (f32[129,1536]{1,0:T(8,128)S(1)}, f32[129,1536]{1,0:T(8,128)}, u32[]{:S(2)}) copy-start(f32[129,1536]{1,0:T(8,128)} %reshape.218.refs_2_) | copy-start | bytes 2377732
  168.8 4.6 %copy-start.3 = (bf16[256,256]{1,0:T(8,128)(2,1)S(1)}, bf16[256,256]{1,0:T(8,128)(2,1)}, u32[]{:S(2)}) copy-start(bf16[256,256]{1,0:T(8,128)(2,1)} %constant.133.clone.refs_3_.refs_6_) | copy-start | bytes 393220
  168.8 4.4 %collective-permute-start.9 = (bf16[2,128,1536]{2,1,0:T(8,128)(2,1)S(1)}, bf16[2,128,1536]{2,1,0:T(8,128)(2,1)S(1)}, u32[]{:S(2)}, u32[]{:S(2)}) collective-permute-start(bf16[2,128,1536]{2,1,0:T(8,128)(2,1)S(1)} %get-tuple-element.29.refs_5_), channel_id=1, source_target_pairs={{0,4},{4,0},{8,12},{12,8},{1,5},{5,1},{9,13},{13,9},{2,6},{6,2},{1... | collective-permute-start | bytes 2359304 | tf_op jit(solution)/shard_map/ppermute | solution.py:318
  171.3 19.5 %collective-permute-start.8 = (bf16[2,128,1536]{2,1,0:T(8,128)(2,1)S(1)}, bf16[2,128,1536]{2,1,0:T(8,128)(2,1)S(1)}, u32[]{:S(2)}, u32[]{:S(2)}) collective-permute-start(bf16[2,128,1536]{2,1,0:T(8,128)(2,1)S(1)} %get-tuple-element.29.refs_5_), channel_id=1, source_target_pairs={{0,8},{4,12},{8,0},{12,4},{1,9},{5,13},{9,1},{13,5},{2,10},{6,14},... | collective-permute-start | bytes 2359304 | tf_op jit(solution)/shard_map/ppermute | solution.py:322
  178.9 1.6 copy-start.1
  180.6 12.7 %copy-start.4 = (bf16[128,768]{1,0:T(8,128)(2,1)S(1)}, bf16[128,768]{1,0:T(8,128)(2,1)}, u32[]{:S(2)}) copy-start(bf16[128,768]{1,0:T(8,128)(2,1)} %constant.134.clone.refs_7_) | copy-start | bytes 589828
  190.9 2.3 %collective-permute-start.10 = (bf16[1,2,128,1536]{3,2,1,0:T(8,128)(2,1)S(1)}, bf16[1,2,128,1536]{3,2,1,0:T(8,128)(2,1)S(1)}, u32[]{:S(2)}, u32[]{:S(2)}) collective-permute-start(bf16[1,2,128,1536]{3,2,1,0:T(8,128)(2,1)S(1)} %bitcast.52), channel_id=1, source_target_pairs={{0,4},{4,0},{8,12},{12,8},{1,5},{5,1},{9,13},{13,9},{2,6},{6,2},{1... | collective-permute-start | bytes 2359304 | tf_op jit(solution)/shard_map/ppermute | solution.py:330

commit v17 on v15

--- a/solution.py
+++ b/solution.py
@@ -57,6 +57,21 @@
             chunk = jnp.where(own + step == target, from_right[step - 1], chunk)
         chunks.append(chunk)
     return jnp.concatenate(chunks, axis=0)
+
+
+def permute_gather(values, axis, count, own):
+    received = [values]
+    for shift in range(1, count):
+        received.append(
+            lax.ppermute(values, axis, [(i, (i + shift) % count) for i in range(count)])
+        )
+    chunks = []
+    for target in range(count):
+        chunk = received[0]
+        for shift in range(1, count):
+            chunk = jnp.where((own - shift) % count == target, received[shift], chunk)
+        chunks.append(chunk)
+    return jnp.stack(chunks)
 
 
 def filter_basis(lag_values, total_len, basis_in, basis_bias, basis_mid, basis_shift):
@@ -263,8 +278,8 @@
     part = lax.axis_index("groups") * lax.axis_size("seq") + lax.axis_index("seq")
     part_cols = local_ch // parts
     mine = lax.dynamic_slice_in_dim(params, part * part_cols, part_cols, axis=1)
-    across = lax.all_gather(mine, "fsdp", axis=0, tiled=False)
-    gathered = lax.all_gather(across, ("groups", "seq"), axis=0, tiled=False)
+    across = permute_gather(mine, "fsdp", lax.axis_size("fsdp"), lax.axis_index("fsdp"))
+    gathered = permute_gather(across, ("groups", "seq"), parts, part)
     gathered = jnp.transpose(gathered, (2, 1, 0, 3)).reshape(params.shape[0], width)
     seq_count = lax.axis_size("seq")
     position = lax.axis_index("seq")

time: 211 us -> 215 us (1.019)
  blocking collectives: 34.4 us -> 0 us
  starting transfers between devices: 23.3 us -> 42 us
  other arithmetic: 9.5 us -> 24.7 us
  waiting for transfers between devices: 102 us -> 108 us
  local copies, waits for them, and re-layouts: 14.8 us -> 12 us
    all_gather x2 -> x0, blocking collectives: 34.4 us -> none  [the longest x1 20.4 us: shards(): across = lax.all_gather(mine, 'fsdp', axis=0, tiled=False)]
    ppermute x0 -> x10, starting transfers between devices: none -> 17.2 us  [permute_gather(): lax.ppermute(values, axis, [(i, (i + shift) % count) for i in range(count)])]
    ppermute x0 -> x10, waiting for transfers between devices: none -> 10.5 us  [permute_gather(): lax.ppermute(values, axis, [(i, (i + shift) % count) for i in range(count)])]
    ppermute x3, waiting for transfers between devices: 32.9 us -> 25.7 us  [relay_gather(): lax.ppermute(leftward, axis, [(j, j - 1) for j in range(1, count - step +...]
    unnamed x4 -> x10, other arithmetic: 0.98 us -> 7.9 us
    another operation x0 -> x3, other arithmetic: none -> 2.97 us  [permute_gather(): return jnp.stack(chunks)]
    ppermute x1, waiting for transfers between devices: 2.18 us -> 5.02 us  [padded_2(): lax.ppermute(head, axis, [((i + 1) % count, i) for i in range(ends)])]
  transfers between devices with their start and end apart: 12 -> 22, of which waited for: 7 -> 13; matrix products, arithmetic and copies ran while one was open for 9% -> 13% of each run, Pallas kernels for 3% -> 3%
where the time goes in v17:
time: 215 us; the launch traced here: 214 us
  waiting for transfers between devices  108 us (50%)
  starting transfers between devices  42 us (20%)
  other arithmetic  24.7 us (11%)
  Pallas kernels  14.1 us (7%)
  local copies, waits for them, and re-layouts  12 us (6%)
  matrix products  12 us (6%)
    all_to_all x1, waiting for transfers between devices, shards(): projected = lax.all_to_all(partial, 'fsdp', 0, 2, tiled=True)  52.2 us
    ppermute x3, waiting for transfers between devices, relay_gather(): lax.ppermute(leftward, axis, [(j, j - 1) for j in range(1, count - step +...  25.7 us
    ppermute x10, starting transfers between devices, permute_gather(): lax.ppermute(values, axis, [(i, (i + shift) % count) for i in range(count)])  17.2 us
    pallas_call x2, Pallas kernels, fused_conv(): pl.pallas_call(conv_body(finish), grid=(width // lanes,), in_specs=specs,...  14.1 us
    ppermute x10, waiting for transfers between devices, permute_gather(): lax.ppermute(values, axis, [(i, (i + shift) % count) for i in range(count)])  10.5 us
    ppermute x1, waiting for transfers between devices, shards(): lax.ppermute(carried, 'seq', [(i, (i + 2 * shift) % seq_count) for i in r...  10.3 us
    ppermute x3, starting transfers between devices, relay_gather(): lax.ppermute(rightward, axis, [(j, j + 1) for j in range(step - 1, count...  9.06 us
    unnamed x10, other arithmetic  7.9 us
  transfers between devices with their start and end apart: 22, of which 13 were waited for; matrix products, arithmetic and copies ran while one was open for 13% of the time, Pallas kernels for 3%

profile of v17, /device:TPU:0, one launch (start us, length us, event | category | flops | bytes accessed | tf_op | source)
XLA Modules:
  0.0 214.3 jit_solution(7671983653887198529)
XLA Ops:
  0.8 1.8 fusion.19
  2.6 5.0 %collective-permute-start.6 = (f32[129,48]{1,0:T(8,128)}, f32[129,48]{1,0:T(8,128)}, u32[]{:S(2)}, u32[]{:S(2)}) collective-permute-start(f32[129,48]{1,0:T(8,128)} %fusion.19), channel_id=1, source_target_pairs={{0,3},{1,0},{2,1},{3,2},{4,7},{5,4},{6,5},{7,6},{8,11},{9,8},{10,9... | collective-permute-start | bytes 74312 | tf_op jit(solution)/shard_map/ppermute | solution.py:66
  8.7 1.3 collective-permute-start
  12.3 1.2 negate_select_fusion.2
  14.0 2.0 fusion.3
  16.0 2.0 broadcast_multiply_fusion.1
  18.9 1.1 select_bitcast_fusion.3
  21.3 2.3 %collective-permute-start.10 = (f32[4,129,48]{2,1,0:T(8,128)}, f32[4,129,48]{2,1,0:T(8,128)}, u32[]{:S(2)}, u32[]{:S(2)}) collective-permute-start(f32[4,129,48]{2,1,0:T(8,128)} %pad_maximum_fusion.8), channel_id=1, source_target_pairs={{0,24},{4,28},{8,0},{12,4},{16,8},{20,12},{24,16},{28,20},{1,25},{... | collective-permute-start | bytes 297224 | tf_op jit(solution)/shard_map/ppermute | solution.py:66
  24.4 1.4 collective-permute-start.13
  26.2 5.0 %collective-permute-done.10 = f32[4,129,48]{2,1,0:T(8,128)} collective-permute-done((f32[4,129,48]{2,1,0:T(8,128)}, f32[4,129,48]{2,1,0:T(8,128)}, u32[]{:S(2)}, u32[]{:S(2)}) %collective-permute-start.10) | collective-permute-done | bytes 99104 | tf_op jit(solution)/shard_map/ppermute | solution.py:66
  31.2 5.9 %collective-permute-start.3 = (bf16[2,128,1536]{2,1,0:T(8,128)(2,1)}, bf16[2,128,1536]{2,1,0:T(8,128)(2,1)}, u32[]{:S(2)}, u32[]{:S(2)}) collective-permute-start(bf16[2,128,1536]{2,1,0:T(8,128)(2,1)} %param.13), channel_id=1, source_target_pairs={{0,1},{1,2},{2,3},{4,5},{5,6},{6,7},{8,9},{9,10},{10,11},{12,13},{... | collective-permute-start | bytes 2359304 | tf_op jit(solution)/shard_map/ppermute | solution.py:48
  37.2 2.5 %collective-permute-start.14 = (f32[4,129,48]{2,1,0:T(8,128)}, f32[4,129,48]{2,1,0:T(8,128)}, u32[]{:S(2)}, u32[]{:S(2)}) collective-permute-start(f32[4,129,48]{2,1,0:T(8,128)} %pad_maximum_fusion.8), channel_id=1, source_target_pairs={{0,8},{4,12},{8,16},{12,20},{16,24},{20,28},{24,0},{28,4},{1,9},{5... | collective-permute-start | bytes 297224 | tf_op jit(solution)/shard_map/ppermute | solution.py:66
  40.0 1.1 collective-permute-done.13
  41.1 4.2 %collective-permute-start.9 = (f32[4,129,48]{2,1,0:T(8,128)}, f32[4,129,48]{2,1,0:T(8,128)}, u32[]{:S(2)}, u32[]{:S(2)}) collective-permute-start(f32[4,129,48]{2,1,0:T(8,128)} %pad_maximum_fusion.8), channel_id=1, source_target_pairs={{0,28},{4,0},{8,4},{12,8},{16,12},{20,16},{24,20},{28,24},{1,29},{... | collective-permute-start | bytes 297224 | tf_op jit(solution)/shard_map/ppermute | solution.py:66
  45.2 2.5 %convolution_bitcast_fusion = f32[4,256,128]{2,1,0:T(8,128)} fusion(f32[16,4,8,256]{3,2,1,0:T(8,128)} %bitcast.71, f32[128,256]{1,0:T(8,128)} %negate_select_fusion.2, f32[128,256]{1,0:T(8,128)S(1)} %fusion.20), kind=kOutput, calls=%fused_computation.10 | convolution fusion | flops 402718720 | bytes 1310720 | tf_op jit(solution)/shard_map/gf,bfk->bgk/dot_general | solution.py:306
  48.3 3.2 %collective-permute-done.15 = f32[4,129,48]{2,1,0:T(8,128)} collective-permute-done((f32[4,129,48]{2,1,0:T(8,128)}, f32[4,129,48]{2,1,0:T(8,128)}, u32[]{:S(2)}, u32[]{:S(2)}) %collective-permute-start.15) | collective-permute-done | bytes 99104 | tf_op jit(solution)/shard_map/ppermute | solution.py:66
  52.0 1.1 bitcast_dynamic-update-slice_fusion.7
  53.1 1.1 bitcast_dynamic-update-slice_fusion.6
  54.2 1.3 collective-permute-start.1
  55.6 1.5 collective-permute-start.4
  58.2 1.1 bitcast_dynamic-update-slice_fusion.4
  59.3 1.1 bitcast_dynamic-update-slice_fusion.3
  60.4 17.1 %collective-permute-done.1 = bf16[2,128,1536]{2,1,0:T(8,128)(2,1)} collective-permute-done((bf16[2,128,1536]{2,1,0:T(8,128)(2,1)}, bf16[2,128,1536]{2,1,0:T(8,128)(2,1)}, u32[]{:S(2)}, u32[]{:S(2)}) %collective-permute-start.1) | collective-permute-done | bytes 786464 | tf_op jit(solution)/shard_map/ppermute | solution.py:49
  77.5 1.3 collective-permute-start.2
  78.8 1.6 collective-permute-start.5
  80.4 1.1 bitcast_dynamic-update-slice_fusion.2
  81.4 1.1 bitcast_dynamic-update-slice_fusion.1
  82.6 1.1 bitcast_dynamic-update-slice_fusion
  83.7 2.6 %copy.44 = f32[129,4,8,48]{3,2,1,0:T(8,128)} copy(f32[129,4,8,48]{3,0,1,2:T(8,128)S(1)} %bitcast.69) | data formatting | bytes 1585152 | tf_op jit(solution)/shard_map/transpose | solution.py:283
  86.3 3.6 %reshape.216.refs_2_ = f32[129,1536]{1,0:T(8,128)} reshape(f32[129,4,8,48]{3,2,1,0:T(8,128)} %copy.44) | data formatting | bytes 1585152 | tf_op jit(solution)/shard_map/reshape | solution.py:283
  89.9 8.6 %collective-permute-done.2 = bf16[2,128,1536]{2,1,0:T(8,128)(2,1)} collective-permute-done((bf16[2,128,1536]{2,1,0:T(8,128)(2,1)}, bf16[2,128,1536]{2,1,0:T(8,128)(2,1)}, u32[]{:S(2)}, u32[]{:S(2)}) %collective-permute-start.2) | collective-permute-done | bytes 786464 | tf_op jit(solution)/shard_map/ppermute | solution.py:49
  98.5 2.9 %select_select_fusion.2 = (bf16[2,128,1536]{2,1,0:T(8,128)(2,1)S(1)}, bf16[2,128,1536]{2,1,0:T(8,128)(2,1)S(1)}) fusion(bf16[2,128,1536]{2,1,0:T(8,128)(2,1)} %collective-permute-done.2, bf16[2,128,1536]{2,1,0:T(8,128)(2,1)} %collective-permute-done.5, bf16[2,128,1536]{2,1,0:T(8,128)(2,1)} %collective-permute-done.1, ...), kind=kLoop, calls=%fused_computation.17 | loop fusion | flops 4718592 | bytes 7077900 | tf_op jit(solution)/shard_map/jit(_where)/select_n | solution.py:57
  101.4 2.7 %select_select_fusion.3 = (bf16[2,128,1536]{2,1,0:T(8,128)(2,1)S(1)}, bf16[2,128,1536]{2,1,0:T(8,128)(2,1)S(1)}) fusion(bf16[2,128,1536]{2,1,0:T(8,128)(2,1)} %collective-permute-done.2, bf16[2,128,1536]{2,1,0:T(8,128)(2,1)} %collective-permute-done.5, bf16[2,128,1536]{2,1,0:T(8,128)(2,1)} %collective-permute-done.1, ...), kind=kLoop, calls=%fused_computation.18 | loop fusion | flops 4718592 | bytes 7077900 | tf_op jit(solution)/shard_map/jit(_where)/select_n | solution.py:57
  104.6 5.5 %convolution_convert_fusion = bf16[1024,1152]{1,0:T(8,128)(2,1)} fusion(bf16[1024,1536]{1,0:T(8,128)(2,1)S(1)} %bitcast.68, bf16[1536,1152]{1,0:T(8,128)(2,1)S(1)} %copy-done), kind=kOutput, calls=%fused_computation.1 | convolution fusion | flops 3625058304 | bytes 9043968 | tf_op jit(solution)/shard_map/dot_general | solution.py:311
  110.1 6.5 %all-to-all-start = ((bf16[8,128,1152]{2,1,0:T(8,128)(2,1)}), bf16[8,128,1152]{2,1,0:T(8,128)(2,1)}, u32[]{:S(2)}, u32[]{:S(2)}) async-start(bf16[8,128,1152]{2,1,0:T(8,128)(2,1)} %bitcast.70), calls=%async_computation | async-start | bytes 4718592 | tf_op jit(solution)/shard_map/all_to_all | solution.py:317
  116.7 52.2 %all-to-all-done = bf16[8,128,1152]{2,1,0:T(8,128)(2,1)} async-done(((bf16[8,128,1152]{2,1,0:T(8,128)(2,1)}), bf16[8,128,1152]{2,1,0:T(8,128)(2,1)}, u32[]{:S(2)}, u32[]{:S(2)}) %all-to-all-start) | async-done | bytes 2359328 | tf_op jit(solution)/shard_map/all_to_all | solution.py:317
  168.9 1.9 copy.49
  170.9 1.3 collective-permute-start.16
  172.2 1.3 collective-permute-start.17
  173.6 5.0 %collective-permute-done.17 = bf16[2,1,4608]{2,1,0:T(2,128)(2,1)S(1)} collective-permute-done((bf16[2,1,4608]{2,1,0:T(2,128)(2,1)S(1)}, bf16[2,1,4608]{2,1,0:T(2,128)(2,1)S(1)}, u32[]{:S(2)}, u32[]{:S(2)}) %collective-permute-start.17) | collective-permute-done | bytes 18464 | tf_op jit(solution)/shard_map/ppermute | solution.py:21
  178.7 1.9 multiply_add_fusion
  180.9 2.7 %collective-permute-start.19 = (bf16[2,128,1536]{2,1,0:T(8,128)(2,1)S(1)}, bf16[2,128,1536]{2,1,0:T(8,128)(2,1)S(1)}, u32[]{:S(2)}, u32[]{:S(2)}) collective-permute-start(bf16[2,128,1536]{2,1,0:T(8,128)(2,1)S(1)} %get-tuple-element.27.refs_5_), channel_id=1, source_target_pairs={{0,4},{4,0},{8,12},{12,8},{1,5},{5,1},{9,13},{13,9},{2,6},{6,2},{1... | collective-permute-start | bytes 2359304 | tf_op jit(solution)/shard_map/ppermute | solution.py:332
  183.8 1.8 collective-permute-done.19
  185.8 5.5 %shard_map.130.refs_3_ = f32[2,256,1536]{2,1,0:T(8,128)S(1)} custom-call(bf16[2,2,128,1536]{3,2,1,0:T(8,128)(2,1)S(1)} %pad_maximum_fusion.3.refs_0_, bf16[2,256,384]{2,1,0:T(8,128)(2,1)S(1)} %pad_maximum_fusion.6.refs_1_, f32[129,1536]{1,0:T(8,128)S(1)} %copy-done.2, bf16[256,256]{1,0:T(8,128)(2,1)S(1)} %copy-done.3), custom_call_target="tpu_custom_call" | custom-call | tf_op jit(solution)/shard_map/pallas_call | solution.py:249
  191.3 1.6 copy-done.1
  192.9 10.3 %collective-permute-done.18 = bf16[2,128,1536]{2,1,0:T(8,128)(2,1)S(1)} collective-permute-done((bf16[2,128,1536]{2,1,0:T(8,128)(2,1)S(1)}, bf16[2,128,1536]{2,1,0:T(8,128)(2,1)S(1)}, u32[]{:S(2)}, u32[]{:S(2)}) %collective-permute-start.18) | collective-permute-done | bytes 786464 | tf_op jit(solution)/shard_map/ppermute | solution.py:336
  203.2 2.2 %collective-permute-done.20 = bf16[1,2,128,1536]{3,2,1,0:T(8,128)(2,1)S(1)} collective-permute-done((bf16[1,2,128,1536]{3,2,1,0:T(8,128)(2,1)S(1)}, bf16[1,2,128,1536]{3,2,1,0:T(8,128)(2,1)S(1)}, u32[]{:S(2)}, u32[]{:S(2)}) %collective-permute-start.20) | collective-permute-done | bytes 786464 | tf_op jit(solution)/shard_map/ppermute | solution.py:344
  205.6 8.6 %shard_map.131 = bf16[2,128,1536]{2,1,0:T(8,128)(2,1)} custom-call(bf16[2,2,128,1536]{3,2,1,0:T(8,128)(2,1)S(1)} %pad_maximum_fusion.4.refs_0_, bf16[2,256,384]{2,1,0:T(8,128)(2,1)S(1)} %pad_maximum_fusion.7.refs_1_, f32[129,1536]{1,0:T(8,128)S(1)} %copy-done.2, f32[2,256,1536]{2,1,0:T(8,128)} %copy-done.1, f32[2,128,1536]{2,1,0:T(8,128)S(1)} %get-tuple-element.26.refs_4_, ...), custom_call_target="tpu_custom_call" | custom-call | tf_op jit(solution)/shard_map/pallas_call | solution.py:249
  (83 shorter events, 10.6 us)
Async XLA Ops:
  0.0 104.6 %copy-start = (bf16[1536,1152]{1,0:T(8,128)(2,1)S(1)}, bf16[1536,1152]{1,0:T(8,128)(2,1)}, u32[]{:S(2)}) copy-start(bf16[1536,1152]{1,0:T(8,128)(2,1)} %param.14) | copy-start | bytes 10616836
  2.6 16.2 %collective-permute-start.6 = (f32[129,48]{1,0:T(8,128)}, f32[129,48]{1,0:T(8,128)}, u32[]{:S(2)}, u32[]{:S(2)}) collective-permute-start(f32[129,48]{1,0:T(8,128)} %fusion.19), channel_id=1, source_target_pairs={{0,3},{1,0},{2,1},{3,2},{4,7},{5,4},{6,5},{7,6},{8,11},{9,8},{10,9... | collective-permute-start | bytes 74312 | tf_op jit(solution)/shard_map/ppermute | solution.py:66
  7.7 11.2 %collective-permute-start.7 = (f32[129,48]{1,0:T(8,128)}, f32[129,48]{1,0:T(8,128)}, u32[]{:S(2)}, u32[]{:S(2)}) collective-permute-start(f32[129,48]{1,0:T(8,128)} %fusion.19), channel_id=1, source_target_pairs={{0,2},{1,3},{2,0},{3,1},{4,6},{5,7},{6,4},{7,5},{8,10},{9,11},{10,... | collective-permute-start | bytes 74312 | tf_op jit(solution)/shard_map/ppermute | solution.py:66
  7.7 11.2 %collective-permute-start.8 = (f32[129,48]{1,0:T(8,128)}, f32[129,48]{1,0:T(8,128)}, u32[]{:S(2)}, u32[]{:S(2)}) collective-permute-start(f32[129,48]{1,0:T(8,128)} %fusion.19), channel_id=1, source_target_pairs={{0,1},{1,2},{2,3},{3,0},{4,5},{5,6},{6,7},{7,4},{8,9},{9,10},{10,1... | collective-permute-start | bytes 74312 | tf_op jit(solution)/shard_map/ppermute | solution.py:66
  8.7 45.5 %collective-permute-start = (bf16[2,128,1536]{2,1,0:T(8,128)(2,1)}, bf16[2,128,1536]{2,1,0:T(8,128)(2,1)}, u32[]{:S(2)}, u32[]{:S(2)}) collective-permute-start(bf16[2,128,1536]{2,1,0:T(8,128)(2,1)} %param.13), channel_id=1, source_target_pairs={{1,0},{2,1},{3,2},{5,4},{6,5},{7,6},{9,8},{10,9},{11,10},{13,12},{... | collective-permute-start | bytes 2359304 | tf_op jit(solution)/shard_map/ppermute | solution.py:49
  20.0 0.6 copy-start.5
  20.0 1.3 copy-start.7
  20.0 3.7 %copy-start.9 = (f32[1,129,48]{2,1,0:T(8,128)}, f32[1,129,48]{2,1,0:T(8,128)S(1)}, u32[]{:S(2)}) copy-start(f32[1,129,48]{2,1,0:T(8,128)S(1)} %get-tuple-element.34) | copy-start | bytes 74308
  20.0 3.7 %copy-start.11 = (f32[1,129,48]{2,1,0:T(8,128)}, f32[1,129,48]{2,1,0:T(8,128)S(1)}, u32[]{:S(2)}) copy-start(f32[1,129,48]{2,1,0:T(8,128)S(1)} %get-tuple-element.35) | copy-start | bytes 74308
  21.3 9.9 %collective-permute-start.10 = (f32[4,129,48]{2,1,0:T(8,128)}, f32[4,129,48]{2,1,0:T(8,128)}, u32[]{:S(2)}, u32[]{:S(2)}) collective-permute-start(f32[4,129,48]{2,1,0:T(8,128)} %pad_maximum_fusion.8), channel_id=1, source_target_pairs={{0,24},{4,28},{8,0},{12,4},{16,8},{20,12},{24,16},{28,20},{1,25},{... | collective-permute-start | bytes 297224 | tf_op jit(solution)/shard_map/ppermute | solution.py:66
  23.7 13.5 %collective-permute-start.11 = (f32[4,129,48]{2,1,0:T(8,128)}, f32[4,129,48]{2,1,0:T(8,128)}, u32[]{:S(2)}, u32[]{:S(2)}) collective-permute-start(f32[4,129,48]{2,1,0:T(8,128)} %pad_maximum_fusion.8), channel_id=1, source_target_pairs={{0,20},{4,24},{8,28},{12,0},{16,4},{20,8},{24,12},{28,16},{1,21},{... | collective-permute-start | bytes 297224 | tf_op jit(solution)/shard_map/ppermute | solution.py:66
  23.7 16.2 %collective-permute-start.12 = (f32[4,129,48]{2,1,0:T(8,128)}, f32[4,129,48]{2,1,0:T(8,128)}, u32[]{:S(2)}, u32[]{:S(2)}) collective-permute-start(f32[4,129,48]{2,1,0:T(8,128)} %pad_maximum_fusion.8), channel_id=1, source_target_pairs={{0,16},{4,20},{8,24},{12,28},{16,0},{20,4},{24,8},{28,12},{1,17},{... | collective-permute-start | bytes 297224 | tf_op jit(solution)/shard_map/ppermute | solution.py:66
  24.4 16.7 %collective-permute-start.13 = (f32[4,129,48]{2,1,0:T(8,128)}, f32[4,129,48]{2,1,0:T(8,128)}, u32[]{:S(2)}, u32[]{:S(2)}) collective-permute-start(f32[4,129,48]{2,1,0:T(8,128)} %pad_maximum_fusion.8), channel_id=1, source_target_pairs={{0,12},{4,16},{8,20},{12,24},{16,28},{20,0},{24,4},{28,8},{1,13},{... | collective-permute-start | bytes 297224 | tf_op jit(solution)/shard_map/ppermute | solution.py:66
  31.2 24.3 %collective-permute-start.3 = (bf16[2,128,1536]{2,1,0:T(8,128)(2,1)}, bf16[2,128,1536]{2,1,0:T(8,128)(2,1)}, u32[]{:S(2)}, u32[]{:S(2)}) collective-permute-start(bf16[2,128,1536]{2,1,0:T(8,128)(2,1)} %param.13), channel_id=1, source_target_pairs={{0,1},{1,2},{2,3},{4,5},{5,6},{6,7},{8,9},{9,10},{10,11},{12,13},{... | collective-permute-start | bytes 2359304 | tf_op jit(solution)/shard_map/ppermute | solution.py:48
  37.2 11.1 %collective-permute-start.14 = (f32[4,129,48]{2,1,0:T(8,128)}, f32[4,129,48]{2,1,0:T(8,128)}, u32[]{:S(2)}, u32[]{:S(2)}) collective-permute-start(f32[4,129,48]{2,1,0:T(8,128)} %pad_maximum_fusion.8), channel_id=1, source_target_pairs={{0,8},{4,12},{8,16},{12,20},{16,24},{20,28},{24,0},{28,4},{1,9},{5... | collective-permute-start | bytes 297224 | tf_op jit(solution)/shard_map/ppermute | solution.py:66
  39.9 11.6 %collective-permute-start.15 = (f32[4,129,48]{2,1,0:T(8,128)}, f32[4,129,48]{2,1,0:T(8,128)}, u32[]{:S(2)}, u32[]{:S(2)}) collective-permute-start(f32[4,129,48]{2,1,0:T(8,128)} %pad_maximum_fusion.8), channel_id=1, source_target_pairs={{0,4},{4,8},{8,12},{12,16},{16,20},{20,24},{24,28},{28,0},{1,5},{5... | collective-permute-start | bytes 297224 | tf_op jit(solution)/shard_map/ppermute | solution.py:66
  41.1 10.9 %collective-permute-start.9 = (f32[4,129,48]{2,1,0:T(8,128)}, f32[4,129,48]{2,1,0:T(8,128)}, u32[]{:S(2)}, u32[]{:S(2)}) collective-permute-start(f32[4,129,48]{2,1,0:T(8,128)} %pad_maximum_fusion.8), channel_id=1, source_target_pairs={{0,28},{4,0},{8,4},{12,8},{16,12},{20,16},{24,20},{28,24},{1,29},{... | collective-permute-start | bytes 297224 | tf_op jit(solution)/shard_map/ppermute | solution.py:66
  47.8 5.3 %copy-start.6 = (f32[1,129,48]{2,1,0:T(8,128)S(1)}, f32[1,129,48]{2,1,0:T(8,128)}, u32[]{:S(2)}) copy-start(f32[1,129,48]{2,1,0:T(8,128)} %copy-done.5) | copy-start | bytes 74308
  47.8 5.3 %copy-start.8 = (f32[1,129,48]{2,1,0:T(8,128)S(1)}, f32[1,129,48]{2,1,0:T(8,128)}, u32[]{:S(2)}) copy-start(f32[1,129,48]{2,1,0:T(8,128)} %copy-done.7) | copy-start | bytes 74308
  47.8 5.3 %copy-start.10 = (f32[1,129,48]{2,1,0:T(8,128)S(1)}, f32[1,129,48]{2,1,0:T(8,128)}, u32[]{:S(2)}) copy-start(f32[1,129,48]{2,1,0:T(8,128)} %copy-done.9) | copy-start | bytes 74308
  47.8 5.3 %copy-start.12 = (f32[1,129,48]{2,1,0:T(8,128)S(1)}, f32[1,129,48]{2,1,0:T(8,128)}, u32[]{:S(2)}) copy-start(f32[1,129,48]{2,1,0:T(8,128)} %copy-done.11) | copy-start | bytes 74308
  54.2 23.2 %collective-permute-start.1 = (bf16[2,128,1536]{2,1,0:T(8,128)(2,1)}, bf16[2,128,1536]{2,1,0:T(8,128)(2,1)}, u32[]{:S(2)}, u32[]{:S(2)}) collective-permute-start(bf16[2,128,1536]{2,1,0:T(8,128)(2,1)} %collective-permute-done), channel_id=1, source_target_pairs={{1,0},{2,1},{5,4},{6,5},{9,8},{10,9},{13,12},{14,13},{17,16},{18,1... | collective-permute-start | bytes 2359304 | tf_op jit(solution)/shard_map/ppermute | solution.py:49
  55.6 23.2 %collective-permute-start.4 = (bf16[2,128,1536]{2,1,0:T(8,128)(2,1)}, bf16[2,128,1536]{2,1,0:T(8,128)(2,1)}, u32[]{:S(2)}, u32[]{:S(2)}) collective-permute-start(bf16[2,128,1536]{2,1,0:T(8,128)(2,1)} %collective-permute-done.3), channel_id=1, source_target_pairs={{1,2},{2,3},{5,6},{6,7},{9,10},{10,11},{13,14},{14,15},{17,18},{18... | collective-permute-start | bytes 2359304 | tf_op jit(solution)/shard_map/ppermute | solution.py:48
  77.5 21.1 %collective-permute-start.2 = (bf16[2,128,1536]{2,1,0:T(8,128)(2,1)}, bf16[2,128,1536]{2,1,0:T(8,128)(2,1)}, u32[]{:S(2)}, u32[]{:S(2)}) collective-permute-start(bf16[2,128,1536]{2,1,0:T(8,128)(2,1)} %collective-permute-done.1), channel_id=1, source_target_pairs={{1,0},{5,4},{9,8},{13,12},{17,16},{21,20},{25,24},{29,28}} | collective-permute-start | bytes 2359304 | tf_op jit(solution)/shard_map/ppermute | solution.py:49
  78.8 19.8 %collective-permute-start.5 = (bf16[2,128,1536]{2,1,0:T(8,128)(2,1)}, bf16[2,128,1536]{2,1,0:T(8,128)(2,1)}, u32[]{:S(2)}, u32[]{:S(2)}) collective-permute-start(bf16[2,128,1536]{2,1,0:T(8,128)(2,1)} %collective-permute-done.4), channel_id=1, source_target_pairs={{2,3},{6,7},{10,11},{14,15},{18,19},{22,23},{26,27},{30,31}} | collective-permute-start | bytes 2359304 | tf_op jit(solution)/shard_map/ppermute | solution.py:48
  89.9 11.5 %copy-start.14 = (bf16[2,128,1536]{2,1,0:T(8,128)(2,1)S(1)}, bf16[2,128,1536]{2,1,0:T(8,128)(2,1)}, u32[]{:S(2)}) copy-start(bf16[2,128,1536]{2,1,0:T(8,128)(2,1)} %param.13) | copy-start | bytes 2359300
  110.1 6.5 %copy-start.16 = (s32[2,1]{0,1:T(1,128)S(1)}, s32[2,1]{0,1:T(1,128)}, u32[]{:S(2)}) copy-start(s32[2,1]{0,1:T(1,128)} %param.22) | copy-start | bytes 28
  110.1 58.8 %all-to-all-start = ((bf16[8,128,1152]{2,1,0:T(8,128)(2,1)}), bf16[8,128,1152]{2,1,0:T(8,128)(2,1)}, u32[]{:S(2)}, u32[]{:S(2)}) async-start(bf16[8,128,1152]{2,1,0:T(8,128)(2,1)} %bitcast.70), calls=%async_computation | async-start | bytes 4718592 | tf_op jit(solution)/shard_map/all_to_all | solution.py:317
  168.9 4.6 %copy-start.15 = (f32[3,4608]{1,0:T(4,128)S(1)}, f32[3,4608]{1,0:T(4,128)}, u32[]{:S(2)}) copy-start(f32[3,4608]{1,0:T(4,128)} %param.15) | copy-start | bytes 165892
  170.9 2.8 %collective-permute-start.16 = (bf16[2,1,4608]{2,1,0:T(2,128)(2,1)S(1)}, bf16[2,1,4608]{2,1,0:T(2,128)(2,1)S(1)}, u32[]{:S(2)}, u32[]{:S(2)}) collective-permute-start(bf16[2,1,4608]{2,1,0:T(2,128)(2,1)S(1)} %get-tuple-element.28), channel_id=1, source_target_pairs={{0,4},{4,8},{8,12},{1,5},{5,9},{9,13},{2,6},{6,10},{10,14},{3,7},{... | collective-permute-start | bytes 55304 | tf_op jit(solution)/shard_map/ppermute | solution.py:19
  172.2 6.5 %collective-permute-start.17 = (bf16[2,1,4608]{2,1,0:T(2,128)(2,1)S(1)}, bf16[2,1,4608]{2,1,0:T(2,128)(2,1)S(1)}, u32[]{:S(2)}, u32[]{:S(2)}) collective-permute-start(bf16[2,1,4608]{2,1,0:T(2,128)(2,1)S(1)} %get-tuple-element.29), channel_id=1, source_target_pairs={{4,0},{8,4},{12,8},{5,1},{9,5},{13,9},{6,2},{10,6},{14,10},{7,3},{... | collective-permute-start | bytes 55304 | tf_op jit(solution)/shard_map/ppermute | solution.py:21
  180.6 3.1 %copy-start.13 = (f32[4,256,128]{2,1,0:T(8,128)S(1)}, f32[4,256,128]{2,1,0:T(8,128)}, u32[]{:S(2)}) copy-start(f32[4,256,128]{2,1,0:T(8,128)} %convolution_bitcast_fusion) | copy-start | bytes 1572868
  180.9 4.8 %copy-start.2 = (f32[129,1536]{1,0:T(8,128)S(1)}, f32[129,1536]{1,0:T(8,128)}, u32[]{:S(2)}) copy-start(f32[129,1536]{1,0:T(8,128)} %reshape.216.refs_2_) | copy-start | bytes 2377732
  180.9 4.8 %copy-start.3 = (bf16[256,256]{1,0:T(8,128)(2,1)S(1)}, bf16[256,256]{1,0:T(8,128)(2,1)}, u32[]{:S(2)}) copy-start(bf16[256,256]{1,0:T(8,128)(2,1)} %constant.314.clone.refs_3_.refs_6_) | copy-start | bytes 393220
  180.9 4.6 %collective-permute-start.19 = (bf16[2,128,1536]{2,1,0:T(8,128)(2,1)S(1)}, bf16[2,128,1536]{2,1,0:T(8,128)(2,1)S(1)}, u32[]{:S(2)}, u32[]{:S(2)}) collective-permute-start(bf16[2,128,1536]{2,1,0:T(8,128)(2,1)S(1)} %get-tuple-element.27.refs_5_), channel_id=1, source_target_pairs={{0,4},{4,0},{8,12},{12,8},{1,5},{5,1},{9,13},{13,9},{2,6},{6,2},{1... | collective-permute-start | bytes 2359304 | tf_op jit(solution)/shard_map/ppermute | solution.py:332
  183.7 19.5 %collective-permute-start.18 = (bf16[2,128,1536]{2,1,0:T(8,128)(2,1)S(1)}, bf16[2,128,1536]{2,1,0:T(8,128)(2,1)S(1)}, u32[]{:S(2)}, u32[]{:S(2)}) collective-permute-start(bf16[2,128,1536]{2,1,0:T(8,128)(2,1)S(1)} %get-tuple-element.27.refs_5_), channel_id=1, source_target_pairs={{0,8},{4,12},{8,0},{12,4},{1,9},{5,13},{9,1},{13,5},{2,10},{6,14},... | collective-permute-start | bytes 2359304 | tf_op jit(solution)/shard_map/ppermute | solution.py:336
  191.3 1.6 copy-start.1
  192.9 12.7 %copy-start.4 = (bf16[128,768]{1,0:T(8,128)(2,1)S(1)}, bf16[128,768]{1,0:T(8,128)(2,1)}, u32[]{:S(2)}) copy-start(bf16[128,768]{1,0:T(8,128)(2,1)} %constant.315.clone.refs_7_) | copy-start | bytes 589828
  203.2 2.3 %collective-permute-start.20 = (bf16[1,2,128,1536]{3,2,1,0:T(8,128)(2,1)S(1)}, bf16[1,2,128,1536]{3,2,1,0:T(8,128)(2,1)S(1)}, u32[]{:S(2)}, u32[]{:S(2)}) collective-permute-start(bf16[1,2,128,1536]{3,2,1,0:T(8,128)(2,1)S(1)} %bitcast.72), channel_id=1, source_target_pairs={{0,4},{4,0},{8,12},{12,8},{1,5},{5,1},{9,13},{13,9},{2,6},{6,2},{1... | collective-permute-start | bytes 2359304 | tf_op jit(solution)/shard_map/ppermute | solution.py:344

commit v18 on v17

--- a/solution.py
+++ b/solution.py
@@ -279,8 +279,6 @@
     part_cols = local_ch // parts
     mine = lax.dynamic_slice_in_dim(params, part * part_cols, part_cols, axis=1)
     across = permute_gather(mine, "fsdp", lax.axis_size("fsdp"), lax.axis_index("fsdp"))
-    gathered = permute_gather(across, ("groups", "seq"), parts, part)
-    gathered = jnp.transpose(gathered, (2, 1, 0, 3)).reshape(params.shape[0], width)
     seq_count = lax.axis_size("seq")
     position = lax.axis_index("seq")
     total_len = float(seq_count * block_len)
@@ -305,7 +303,9 @@
     paired = paired.reshape(block_total, 2 * block_len, paired.shape[-1])
     basis_spec = jnp.einsum("gf,bfk->bgk", forward, paired, precision=lax.Precision.HIGHEST)
     group_tokens = relay_gather(tokens, "fsdp")
-    group_tokens, basis_spec, gathered = lax.optimization_barrier((group_tokens, basis_spec, gathered))
+    group_tokens, basis_spec, across = lax.optimization_barrier((group_tokens, basis_spec, across))
+    gathered = lax.all_gather(across, ("groups", "seq"), axis=0, tiled=False)
+    gathered = jnp.transpose(gathered, (2, 1, 0, 3)).reshape(params.shape[0], width)
     group_rows = group_tokens.shape[0]
     local_cols = in_weight.shape[1]
     partial = jnp.dot(
@@ -315,6 +315,7 @@
     ).astype(jnp.bfloat16)
     partial = partial.reshape(group_rows, block_len, local_cols)
     projected = lax.all_to_all(partial, "fsdp", 0, 2, tiled=True)
+    projected, gathered = lax.optimization_barrier((projected, gathered))
     padded = padded_2(projected, (("seq", 1),), 1)
     shorted = (
         short_weight[0] * padded[:, :-2]

time: 215 us -> 179 us (0.83)
  waiting for transfers between devices: 108 us -> 76.8 us
  blocking collectives: 0 us -> 15.3 us
  other arithmetic: 24.7 us -> 13.8 us
  starting transfers between devices: 42 us -> 31.2 us
    all_to_all x1, waiting for transfers between devices: 52.2 us -> 28.2 us  [shards(): projected = lax.all_to_all(partial, 'fsdp', 0, 2, tiled=True)]
    all_gather x0 -> x1, blocking collectives: none -> 15.3 us  [shards(): gathered = lax.all_gather(across, ('groups', 'seq'), axis=0, tiled=False)]
    ppermute x10 -> x3, starting transfers between devices: 17.2 us -> 5.02 us  [permute_gather(): lax.ppermute(values, axis, [(i, (i + shift) % count) for i in range(count)])]
    ppermute x10 -> x3, waiting for transfers between devices: 10.5 us -> 0.01 us  [permute_gather(): lax.ppermute(values, axis, [(i, (i + shift) % count) for i in range(count)])]
    ppermute x3, waiting for transfers between devices: 25.7 us -> 34.9 us  [relay_gather(): lax.ppermute(leftward, axis, [(j, j - 1) for j in range(1, count - step +...]
    unnamed x10 -> x3, other arithmetic: 7.9 us -> 0.22 us
    ppermute x1, waiting for transfers between devices: 5.02 us -> 0.01 us  [padded_2(): lax.ppermute(head, axis, [((i + 1) % count, i) for i in range(ends)])]
    ppermute x1, starting transfers between devices: 0.01 us -> 2.28 us  [shards(): lax.ppermute(carried, 'seq', [(i, (i + 2 * shift) % seq_count) for i in r...]
  transfers between devices with their start and end apart: 22 -> 15, of which waited for: 13 -> 8; matrix products, arithmetic and copies ran while one was open for 13% -> 12% of each run, Pallas kernels for 3% -> 3%
where the time goes in v18:
time: 179 us; the launch traced here: 178 us
  waiting for transfers between devices  76.8 us (43%)
  starting transfers between devices  31.2 us (17%)
  blocking collectives  15.3 us (9%)
  local copies, waits for them, and re-layouts  14.1 us (8%)
  Pallas kernels  14.1 us (8%)
  other arithmetic  13.8 us (8%)
  matrix products  11 us (6%)
    ppermute x3, waiting for transfers between devices, relay_gather(): lax.ppermute(leftward, axis, [(j, j - 1) for j in range(1, count - step +...  34.9 us
    all_to_all x1, waiting for transfers between devices, shards(): projected = lax.all_to_all(partial, 'fsdp', 0, 2, tiled=True)  28.2 us
    all_gather x1, blocking collectives, shards(): gathered = lax.all_gather(across, ('groups', 'seq'), axis=0, tiled=False)  15.3 us
    pallas_call x2, Pallas kernels, fused_conv(): pl.pallas_call(conv_body(finish), grid=(width // lanes,), in_specs=specs,...  14.1 us
    ppermute x1, waiting for transfers between devices, shards(): lax.ppermute(carried, 'seq', [(i, (i + 2 * shift) % seq_count) for i in r...  10.7 us
    ppermute x3, starting transfers between devices, relay_gather(): lax.ppermute(rightward, axis, [(j, j + 1) for j in range(step - 1, count...  9.6 us
    select_n x2, other arithmetic, relay_gather(): chunk = jnp.where(own + step == target, from_right[step - 1], chunk)  5.61 us
    dot_general x1, matrix products, shards(): jnp.dot(group_tokens.reshape(group_rows * block_len, width), in_weight, p...  5.52 us
  transfers between devices with their start and end apart: 15, of which 8 were waited for; matrix products, arithmetic and copies ran while one was open for 12% of the time, Pallas kernels for 3%

profile of v18, /device:TPU:0, one launch (start us, length us, event | category | flops | bytes accessed | tf_op | source)
XLA Modules:
  0.0 177.7 jit_solution(13064118157913956987)
XLA Ops:
  0.0 1.5 collective-permute-start
  1.6 6.5 %collective-permute-start.3 = (bf16[2,128,1536]{2,1,0:T(8,128)(2,1)}, bf16[2,128,1536]{2,1,0:T(8,128)(2,1)}, u32[]{:S(2)}, u32[]{:S(2)}) collective-permute-start(bf16[2,128,1536]{2,1,0:T(8,128)(2,1)} %param.13), channel_id=1, source_target_pairs={{0,1},{1,2},{2,3},{4,5},{5,6},{6,7},{8,9},{9,10},{10,11},{12,13},{... | collective-permute-start | bytes 2359304 | tf_op jit(solution)/shard_map/ppermute | solution.py:48
  8.0 0.7 broadcast_in_dim.24
  8.7 1.6 fusion.19
  10.4 1.8 %collective-permute-start.6 = (f32[129,48]{1,0:T(8,128)}, f32[129,48]{1,0:T(8,128)}, u32[]{:S(2)}, u32[]{:S(2)}) collective-permute-start(f32[129,48]{1,0:T(8,128)} %fusion.19), channel_id=1, source_target_pairs={{0,3},{1,0},{2,1},{3,2},{4,7},{5,4},{6,5},{7,6},{8,11},{9,8},{10,9... | collective-permute-start | bytes 74312 | tf_op jit(solution)/shard_map/ppermute | solution.py:66
  12.2 1.2 collective-permute-start.7
  13.4 2.0 %collective-permute-start.8 = (f32[129,48]{1,0:T(8,128)}, f32[129,48]{1,0:T(8,128)}, u32[]{:S(2)}, u32[]{:S(2)}) collective-permute-start(f32[129,48]{1,0:T(8,128)} %fusion.19), channel_id=1, source_target_pairs={{0,1},{1,2},{2,3},{3,0},{4,5},{5,6},{6,7},{7,4},{8,9},{9,10},{10,1... | collective-permute-start | bytes 74312 | tf_op jit(solution)/shard_map/ppermute | solution.py:66
  15.4 0.6 fusion.43
  17.6 6.2 %collective-permute-done = bf16[2,128,1536]{2,1,0:T(8,128)(2,1)} collective-permute-done((bf16[2,128,1536]{2,1,0:T(8,128)(2,1)}, bf16[2,128,1536]{2,1,0:T(8,128)(2,1)}, u32[]{:S(2)}, u32[]{:S(2)}) %collective-permute-start) | collective-permute-done | bytes 786464 | tf_op jit(solution)/shard_map/ppermute | solution.py:49
  23.8 1.3 collective-permute-start.1
  25.1 0.3 collective-permute-done.3
  25.4 1.5 collective-permute-start.4
  26.9 0.6 fusion.27
  27.5 2.0 %fusion.3 = f32[1024,64]{0,1:T(8,128)S(1)} fusion(f32[17,64]{1,0:T(8,128)} %param.16, f32[64]{0:T(128)} %param.17, f32[1024,8]{0,1:T(8,128)S(1)} %get-tuple-element.43, f32[1024,8]{0,1:T(8,128)S(1)} %get-tuple-element.42, f32[1024,1]{0,1:T(1,128)S(1)} %bitcast.65), kind=kOutput, calls=%fused_computation.14 | convolution fusion | flops 13469696 | bytes 336384 | tf_op jit(solution)/shard_map/dot_general | solution.py:89
  29.5 2.0 %broadcast_multiply_fusion.1 = (f32[1024,64]{0,1:T(8,128)S(1)}, f32[1024,64]{0,1:T(8,128)S(1)}) fusion(f32[1024]{0:T(1024)S(1)} %bitcast.64, f32[1024]{0:T(1024)S(1)} %broadcast_subtract_fusion, f32[64]{0:T(128)} %param.19, f32[1024,64]{0,1:T(8,128)S(1)} %fusion.3, f32[64,64]{1,0:T(8,128)} %param.18), kind=kOutput, calls=%fused_computation.44 | convolution fusion | flops 50528256 | bytes 811264 | tf_op jit(solution)/shard_map/dot_general | solution.py:90
  31.5 14.7 %collective-permute-done.1 = bf16[2,128,1536]{2,1,0:T(8,128)(2,1)} collective-permute-done((bf16[2,128,1536]{2,1,0:T(8,128)(2,1)}, bf16[2,128,1536]{2,1,0:T(8,128)(2,1)}, u32[]{:S(2)}, u32[]{:S(2)}) %collective-permute-start.1) | collective-permute-done | bytes 786464 | tf_op jit(solution)/shard_map/ppermute | solution.py:49
  46.2 1.3 collective-permute-start.2
  47.5 1.6 collective-permute-start.5
  49.0 0.5 negate_select_fusion.2
  49.6 1.4 convolution_bitcast_fusion
  51.1 1.1 select_bitcast_fusion.3
  52.2 0.7 pad_maximum_fusion.8
  53.0 14.0 %collective-permute-done.2 = bf16[2,128,1536]{2,1,0:T(8,128)(2,1)} collective-permute-done((bf16[2,128,1536]{2,1,0:T(8,128)(2,1)}, bf16[2,128,1536]{2,1,0:T(8,128)(2,1)}, u32[]{:S(2)}, u32[]{:S(2)}) %collective-permute-start.2) | collective-permute-done | bytes 786464 | tf_op jit(solution)/shard_map/ppermute | solution.py:49
  67.0 2.9 %select_select_fusion.2 = (bf16[2,128,1536]{2,1,0:T(8,128)(2,1)S(1)}, bf16[2,128,1536]{2,1,0:T(8,128)(2,1)S(1)}) fusion(bf16[2,128,1536]{2,1,0:T(8,128)(2,1)} %collective-permute-done.2, bf16[2,128,1536]{2,1,0:T(8,128)(2,1)} %collective-permute-done.5, bf16[2,128,1536]{2,1,0:T(8,128)(2,1)} %collective-permute-done.1, ...), kind=kLoop, calls=%fused_computation.17 | loop fusion | flops 4718592 | bytes 7077900 | tf_op jit(solution)/shard_map/jit(_where)/select_n | solution.py:57
  69.9 2.7 %select_select_fusion.3 = (bf16[2,128,1536]{2,1,0:T(8,128)(2,1)S(1)}, bf16[2,128,1536]{2,1,0:T(8,128)(2,1)S(1)}) fusion(bf16[2,128,1536]{2,1,0:T(8,128)(2,1)} %collective-permute-done.2, bf16[2,128,1536]{2,1,0:T(8,128)(2,1)} %collective-permute-done.5, bf16[2,128,1536]{2,1,0:T(8,128)(2,1)} %collective-permute-done.1, ...), kind=kLoop, calls=%fused_computation.18 | loop fusion | flops 4718592 | bytes 7077900 | tf_op jit(solution)/shard_map/jit(_where)/select_n | solution.py:57
  72.6 0.4 pad_maximum_fusion
  73.1 5.5 %convolution_convert_fusion = bf16[1024,1152]{1,0:T(8,128)(2,1)} fusion(bf16[1024,1536]{1,0:T(8,128)(2,1)S(1)} %bitcast.55, bf16[1536,1152]{1,0:T(8,128)(2,1)S(1)} %copy-done), kind=kOutput, calls=%fused_computation.1 | convolution fusion | flops 3625058304 | bytes 9043968 | tf_op jit(solution)/shard_map/dot_general | solution.py:311
  78.6 4.7 %all-to-all-start = ((bf16[8,128,1152]{2,1,0:T(8,128)(2,1)}), bf16[8,128,1152]{2,1,0:T(8,128)(2,1)}, u32[]{:S(2)}, u32[]{:S(2)}) async-start(bf16[8,128,1152]{2,1,0:T(8,128)(2,1)} %bitcast.56), calls=%async_computation | async-start | bytes 4718592 | tf_op jit(solution)/shard_map/all_to_all | solution.py:317
  83.3 1.8 %copy.32 = f32[4,129,48]{1,2,0:T(8,128)} copy(f32[4,129,48]{2,1,0:T(8,128)} %pad_maximum_fusion.8) | data formatting | bytes 198144 | tf_op jit(solution)/shard_map/optimization_barrier | solution.py:306
  85.2 15.3 %all-gather = f32[32,129,48]{1,2,0:T(8,128)} all-gather(f32[4,129,48]{1,2,0:T(8,128)} %copy.32), channel_id=2, replica_groups=mesh['groups'=2,'seq'=4,'fsdp'=4] {'groups','seq'}, dimensions={0}, use_global_device_ids=true | all-gather | bytes 891648 | tf_op jit(solution)/shard_map/all_gather | solution.py:307
  100.4 3.6 %copy.33 = f32[129,4,8,48]{3,2,1,0:T(8,128)} copy(f32[129,4,8,48]{0,3,1,2:T(8,128)} %bitcast.54) | data formatting | bytes 1585152 | tf_op jit(solution)/shard_map/transpose | solution.py:308
  104.0 3.6 %reshape.218.refs_2_ = f32[129,1536]{1,0:T(8,128)} reshape(f32[129,4,8,48]{3,2,1,0:T(8,128)} %copy.33) | data formatting | bytes 1585152 | tf_op jit(solution)/shard_map/reshape | solution.py:308
  107.6 28.2 %all-to-all-done = bf16[8,128,1152]{2,1,0:T(8,128)(2,1)} async-done(((bf16[8,128,1152]{2,1,0:T(8,128)(2,1)}), bf16[8,128,1152]{2,1,0:T(8,128)(2,1)}, u32[]{:S(2)}, u32[]{:S(2)}) %all-to-all-start) | async-done | bytes 2359328 | tf_op jit(solution)/shard_map/all_to_all | solution.py:317
  135.8 1.9 %copy.36 = bf16[4,2,16,8,1152]{4,3,0,2,1:T(8,128)(2,1)S(1)} copy(bf16[4,2,16,8,1152]{4,3,2,1,0:T(8,128)(2,1)} %bitcast.22) | data formatting | bytes 4718592 | tf_op jit(solution)/shard_map/all_to_all | solution.py:317
  137.8 1.3 collective-permute-start.10
  139.1 3.2 %collective-permute-start.9 = (bf16[2,1,4608]{2,1,0:T(2,128)(2,1)S(1)}, bf16[2,1,4608]{2,1,0:T(2,128)(2,1)S(1)}, u32[]{:S(2)}, u32[]{:S(2)}) collective-permute-start(bf16[2,1,4608]{2,1,0:T(2,128)(2,1)S(1)} %get-tuple-element.32), channel_id=1, source_target_pairs={{0,4},{4,8},{8,12},{1,5},{5,9},{9,13},{2,6},{6,10},{10,14},{3,7},{... | collective-permute-start | bytes 55304 | tf_op jit(solution)/shard_map/ppermute | solution.py:19
  142.3 0.1 slice_reduce_fusion.2
  142.5 0.5 collective-permute-done.9
  143.0 1.9 %multiply_add_fusion = f32[2,128,4608]{2,1,0:T(8,128)S(1)} fusion(bf16[2,128,4608]{2,1,0:T(8,128)(2,1)S(1)} %bitcast.53, bf16[2,1,4608]{2,1,0:T(2,128)(2,1)S(1)} %collective-permute-done.10, bf16[2,1,4608]{2,1,0:T(2,128)(2,1)S(1)} %collective-permute-done.9, f32[4608]{0:T(1024)S(1)} %get-tuple-element.20, f32[4608]{0:T(1024)S(1)} %get-tuple-element.21, ...), kind=kLoop, calls=%fused_computation | loop fusion | flops 16515072 | bytes 7170048 | tf_op jit(solution)/shard_map/add | solution.py:321
  144.9 0.3 fusion.41
  145.3 1.0 collective-permute-start.12
  146.2 2.3 %collective-permute-start.11 = (bf16[2,128,1536]{2,1,0:T(8,128)(2,1)S(1)}, bf16[2,128,1536]{2,1,0:T(8,128)(2,1)S(1)}, u32[]{:S(2)}, u32[]{:S(2)}) collective-permute-start(bf16[2,128,1536]{2,1,0:T(8,128)(2,1)S(1)} %get-tuple-element.31.refs_5_), channel_id=1, source_target_pairs={{0,8},{4,12},{8,0},{12,4},{1,9},{5,13},{9,1},{13,5},{2,10},{6,14},... | collective-permute-start | bytes 2359304 | tf_op jit(solution)/shard_map/ppermute | solution.py:337
  148.7 0.1 pad_maximum_fusion.3.refs_0_
  148.8 5.5 %shard_map.130.refs_3_ = f32[2,256,1536]{2,1,0:T(8,128)S(1)} custom-call(bf16[2,2,128,1536]{3,2,1,0:T(8,128)(2,1)S(1)} %pad_maximum_fusion.3.refs_0_, bf16[2,256,384]{2,1,0:T(8,128)(2,1)S(1)} %pad_maximum_fusion.6.refs_1_, f32[129,1536]{1,0:T(8,128)S(1)} %copy-done.2, bf16[256,256]{1,0:T(8,128)(2,1)S(1)} %copy-done.3), custom_call_target="tpu_custom_call" | custom-call | tf_op jit(solution)/shard_map/pallas_call | solution.py:249
  154.4 1.6 copy-done.1
  156.0 10.7 %collective-permute-done.11 = bf16[2,128,1536]{2,1,0:T(8,128)(2,1)S(1)} collective-permute-done((bf16[2,128,1536]{2,1,0:T(8,128)(2,1)S(1)}, bf16[2,128,1536]{2,1,0:T(8,128)(2,1)S(1)}, u32[]{:S(2)}, u32[]{:S(2)}) %collective-permute-start.11) | collective-permute-done | bytes 786464 | tf_op jit(solution)/shard_map/ppermute | solution.py:337
  166.7 2.2 %collective-permute-done.13 = bf16[1,2,128,1536]{3,2,1,0:T(8,128)(2,1)S(1)} collective-permute-done((bf16[1,2,128,1536]{3,2,1,0:T(8,128)(2,1)S(1)}, bf16[1,2,128,1536]{3,2,1,0:T(8,128)(2,1)S(1)}, u32[]{:S(2)}, u32[]{:S(2)}) %collective-permute-start.13) | collective-permute-done | bytes 786464 | tf_op jit(solution)/shard_map/ppermute | solution.py:345
  169.1 8.6 %shard_map.131 = bf16[2,128,1536]{2,1,0:T(8,128)(2,1)} custom-call(bf16[2,2,128,1536]{3,2,1,0:T(8,128)(2,1)S(1)} %pad_maximum_fusion.4.refs_0_, bf16[2,256,384]{2,1,0:T(8,128)(2,1)S(1)} %pad_maximum_fusion.7.refs_1_, f32[129,1536]{1,0:T(8,128)S(1)} %copy-done.2, f32[2,256,1536]{2,1,0:T(8,128)} %copy-done.1, f32[2,128,1536]{2,1,0:T(8,128)S(1)} %get-tuple-element.30.refs_4_, ...), custom_call_target="tpu_custom_call" | custom-call | tf_op jit(solution)/shard_map/pallas_call | solution.py:249
  (46 shorter events, 0.9 us)
Async XLA Ops:
  0.0 73.0 %copy-start = (bf16[1536,1152]{1,0:T(8,128)(2,1)S(1)}, bf16[1536,1152]{1,0:T(8,128)(2,1)}, u32[]{:S(2)}) copy-start(bf16[1536,1152]{1,0:T(8,128)(2,1)} %param.14) | copy-start | bytes 10616836
  0.0 23.8 %collective-permute-start = (bf16[2,128,1536]{2,1,0:T(8,128)(2,1)}, bf16[2,128,1536]{2,1,0:T(8,128)(2,1)}, u32[]{:S(2)}, u32[]{:S(2)}) collective-permute-start(bf16[2,128,1536]{2,1,0:T(8,128)(2,1)} %param.13), channel_id=1, source_target_pairs={{1,0},{2,1},{3,2},{5,4},{6,5},{7,6},{9,8},{10,9},{11,10},{13,12},{... | collective-permute-start | bytes 2359304 | tf_op jit(solution)/shard_map/ppermute | solution.py:49
  1.6 23.8 %collective-permute-start.3 = (bf16[2,128,1536]{2,1,0:T(8,128)(2,1)}, bf16[2,128,1536]{2,1,0:T(8,128)(2,1)}, u32[]{:S(2)}, u32[]{:S(2)}) collective-permute-start(bf16[2,128,1536]{2,1,0:T(8,128)(2,1)} %param.13), channel_id=1, source_target_pairs={{0,1},{1,2},{2,3},{4,5},{5,6},{6,7},{8,9},{9,10},{10,11},{12,13},{... | collective-permute-start | bytes 2359304 | tf_op jit(solution)/shard_map/ppermute | solution.py:48
  10.4 40.7 %collective-permute-start.6 = (f32[129,48]{1,0:T(8,128)}, f32[129,48]{1,0:T(8,128)}, u32[]{:S(2)}, u32[]{:S(2)}) collective-permute-start(f32[129,48]{1,0:T(8,128)} %fusion.19), channel_id=1, source_target_pairs={{0,3},{1,0},{2,1},{3,2},{4,7},{5,4},{6,5},{7,6},{8,11},{9,8},{10,9... | collective-permute-start | bytes 74312 | tf_op jit(solution)/shard_map/ppermute | solution.py:66
  12.2 38.9 %collective-permute-start.7 = (f32[129,48]{1,0:T(8,128)}, f32[129,48]{1,0:T(8,128)}, u32[]{:S(2)}, u32[]{:S(2)}) collective-permute-start(f32[129,48]{1,0:T(8,128)} %fusion.19), channel_id=1, source_target_pairs={{0,2},{1,3},{2,0},{3,1},{4,6},{5,7},{6,4},{7,5},{8,10},{9,11},{10,... | collective-permute-start | bytes 74312 | tf_op jit(solution)/shard_map/ppermute | solution.py:66
  13.4 37.7 %collective-permute-start.8 = (f32[129,48]{1,0:T(8,128)}, f32[129,48]{1,0:T(8,128)}, u32[]{:S(2)}, u32[]{:S(2)}) collective-permute-start(f32[129,48]{1,0:T(8,128)} %fusion.19), channel_id=1, source_target_pairs={{0,1},{1,2},{2,3},{3,0},{4,5},{5,6},{6,7},{7,4},{8,9},{9,10},{10,1... | collective-permute-start | bytes 74312 | tf_op jit(solution)/shard_map/ppermute | solution.py:66
  23.8 22.4 %collective-permute-start.1 = (bf16[2,128,1536]{2,1,0:T(8,128)(2,1)}, bf16[2,128,1536]{2,1,0:T(8,128)(2,1)}, u32[]{:S(2)}, u32[]{:S(2)}) collective-permute-start(bf16[2,128,1536]{2,1,0:T(8,128)(2,1)} %collective-permute-done), channel_id=1, source_target_pairs={{1,0},{2,1},{5,4},{6,5},{9,8},{10,9},{13,12},{14,13},{17,16},{18,1... | collective-permute-start | bytes 2359304 | tf_op jit(solution)/shard_map/ppermute | solution.py:49
  25.4 22.1 %collective-permute-start.4 = (bf16[2,128,1536]{2,1,0:T(8,128)(2,1)}, bf16[2,128,1536]{2,1,0:T(8,128)(2,1)}, u32[]{:S(2)}, u32[]{:S(2)}) collective-permute-start(bf16[2,128,1536]{2,1,0:T(8,128)(2,1)} %collective-permute-done.3), channel_id=1, source_target_pairs={{1,2},{2,3},{5,6},{6,7},{9,10},{10,11},{13,14},{14,15},{17,18},{18... | collective-permute-start | bytes 2359304 | tf_op jit(solution)/shard_map/ppermute | solution.py:48
  46.2 20.8 %collective-permute-start.2 = (bf16[2,128,1536]{2,1,0:T(8,128)(2,1)}, bf16[2,128,1536]{2,1,0:T(8,128)(2,1)}, u32[]{:S(2)}, u32[]{:S(2)}) collective-permute-start(bf16[2,128,1536]{2,1,0:T(8,128)(2,1)} %collective-permute-done.1), channel_id=1, source_target_pairs={{1,0},{5,4},{9,8},{13,12},{17,16},{21,20},{25,24},{29,28}} | collective-permute-start | bytes 2359304 | tf_op jit(solution)/shard_map/ppermute | solution.py:49
  47.5 19.5 %collective-permute-start.5 = (bf16[2,128,1536]{2,1,0:T(8,128)(2,1)}, bf16[2,128,1536]{2,1,0:T(8,128)(2,1)}, u32[]{:S(2)}, u32[]{:S(2)}) collective-permute-start(bf16[2,128,1536]{2,1,0:T(8,128)(2,1)} %collective-permute-done.4), channel_id=1, source_target_pairs={{2,3},{6,7},{10,11},{14,15},{18,19},{22,23},{26,27},{30,31}} | collective-permute-start | bytes 2359304 | tf_op jit(solution)/shard_map/ppermute | solution.py:48
  53.0 16.9 %copy-start.6 = (bf16[2,128,1536]{2,1,0:T(8,128)(2,1)S(1)}, bf16[2,128,1536]{2,1,0:T(8,128)(2,1)}, u32[]{:S(2)}) copy-start(bf16[2,128,1536]{2,1,0:T(8,128)(2,1)} %param.13) | copy-start | bytes 2359300
  78.6 4.7 %copy-start.8 = (s32[2,1]{0,1:T(1,128)S(1)}, s32[2,1]{0,1:T(1,128)}, u32[]{:S(2)}) copy-start(s32[2,1]{0,1:T(1,128)} %param.22) | copy-start | bytes 28
  78.6 57.2 %all-to-all-start = ((bf16[8,128,1152]{2,1,0:T(8,128)(2,1)}), bf16[8,128,1152]{2,1,0:T(8,128)(2,1)}, u32[]{:S(2)}, u32[]{:S(2)}) async-start(bf16[8,128,1152]{2,1,0:T(8,128)(2,1)} %bitcast.56), calls=%async_computation | async-start | bytes 4718592 | tf_op jit(solution)/shard_map/all_to_all | solution.py:317
  135.8 6.5 %copy-start.7 = (f32[3,4608]{1,0:T(4,128)S(1)}, f32[3,4608]{1,0:T(4,128)}, u32[]{:S(2)}) copy-start(f32[3,4608]{1,0:T(4,128)} %param.15) | copy-start | bytes 165892
  137.8 4.7 %collective-permute-start.10 = (bf16[2,1,4608]{2,1,0:T(2,128)(2,1)S(1)}, bf16[2,1,4608]{2,1,0:T(2,128)(2,1)S(1)}, u32[]{:S(2)}, u32[]{:S(2)}) collective-permute-start(bf16[2,1,4608]{2,1,0:T(2,128)(2,1)S(1)} %get-tuple-element.33), channel_id=1, source_target_pairs={{4,0},{8,4},{12,8},{5,1},{9,5},{13,9},{6,2},{10,6},{14,10},{7,3},{... | collective-permute-start | bytes 55304 | tf_op jit(solution)/shard_map/ppermute | solution.py:21
  139.1 3.9 %collective-permute-start.9 = (bf16[2,1,4608]{2,1,0:T(2,128)(2,1)S(1)}, bf16[2,1,4608]{2,1,0:T(2,128)(2,1)S(1)}, u32[]{:S(2)}, u32[]{:S(2)}) collective-permute-start(bf16[2,1,4608]{2,1,0:T(2,128)(2,1)S(1)} %get-tuple-element.32), channel_id=1, source_target_pairs={{0,4},{4,8},{8,12},{1,5},{5,9},{9,13},{2,6},{6,10},{10,14},{3,7},{... | collective-permute-start | bytes 55304 | tf_op jit(solution)/shard_map/ppermute | solution.py:19
  144.9 3.6 %copy-start.5 = (f32[4,256,128]{2,1,0:T(8,128)S(1)}, f32[4,256,128]{2,1,0:T(8,128)}, u32[]{:S(2)}) copy-start(f32[4,256,128]{2,1,0:T(8,128)} %convolution_bitcast_fusion) | copy-start | bytes 1572868
  145.2 3.6 %copy-start.2 = (f32[129,1536]{1,0:T(8,128)S(1)}, f32[129,1536]{1,0:T(8,128)}, u32[]{:S(2)}) copy-start(f32[129,1536]{1,0:T(8,128)} %reshape.218.refs_2_) | copy-start | bytes 2377732
  145.2 3.6 %copy-start.3 = (bf16[256,256]{1,0:T(8,128)(2,1)S(1)}, bf16[256,256]{1,0:T(8,128)(2,1)}, u32[]{:S(2)}) copy-start(bf16[256,256]{1,0:T(8,128)(2,1)} %constant.166.clone.refs_3_.refs_6_) | copy-start | bytes 393220
  145.3 3.4 %collective-permute-start.12 = (bf16[2,128,1536]{2,1,0:T(8,128)(2,1)S(1)}, bf16[2,128,1536]{2,1,0:T(8,128)(2,1)S(1)}, u32[]{:S(2)}, u32[]{:S(2)}) collective-permute-start(bf16[2,128,1536]{2,1,0:T(8,128)(2,1)S(1)} %get-tuple-element.31.refs_5_), channel_id=1, source_target_pairs={{0,4},{4,0},{8,12},{12,8},{1,5},{5,1},{9,13},{13,9},{2,6},{6,2},{1... | collective-permute-start | bytes 2359304 | tf_op jit(solution)/shard_map/ppermute | solution.py:333
  146.2 20.4 %collective-permute-start.11 = (bf16[2,128,1536]{2,1,0:T(8,128)(2,1)S(1)}, bf16[2,128,1536]{2,1,0:T(8,128)(2,1)S(1)}, u32[]{:S(2)}, u32[]{:S(2)}) collective-permute-start(bf16[2,128,1536]{2,1,0:T(8,128)(2,1)S(1)} %get-tuple-element.31.refs_5_), channel_id=1, source_target_pairs={{0,8},{4,12},{8,0},{12,4},{1,9},{5,13},{9,1},{13,5},{2,10},{6,14},... | collective-permute-start | bytes 2359304 | tf_op jit(solution)/shard_map/ppermute | solution.py:337
  154.4 1.6 copy-start.1
  156.0 13.1 %copy-start.4 = (bf16[128,768]{1,0:T(8,128)(2,1)S(1)}, bf16[128,768]{1,0:T(8,128)(2,1)}, u32[]{:S(2)}) copy-start(bf16[128,768]{1,0:T(8,128)(2,1)} %constant.167.clone.refs_7_) | copy-start | bytes 589828
  166.7 2.3 %collective-permute-start.13 = (bf16[1,2,128,1536]{3,2,1,0:T(8,128)(2,1)S(1)}, bf16[1,2,128,1536]{3,2,1,0:T(8,128)(2,1)S(1)}, u32[]{:S(2)}, u32[]{:S(2)}) collective-permute-start(bf16[1,2,128,1536]{3,2,1,0:T(8,128)(2,1)S(1)} %bitcast.58), channel_id=1, source_target_pairs={{0,4},{4,0},{8,12},{12,8},{1,5},{5,1},{9,13},{13,9},{2,6},{6,2},{1... | collective-permute-start | bytes 2359304 | tf_op jit(solution)/shard_map/ppermute | solution.py:345

commit v19 on v18

--- a/solution.py
+++ b/solution.py
@@ -39,7 +39,7 @@
     return jnp.take(stacked, order, axis=0)
 
 
-def relay_gather(values, axis):
+def relay_gather(values, axis, apply=lambda block: block):
     count = lax.axis_size(axis)
     own = lax.axis_index(axis)
     from_left, from_right = [], []
@@ -49,6 +49,9 @@
         leftward = lax.ppermute(leftward, axis, [(j, j - 1) for j in range(1, count - step + 1)])
         from_left.append(rightward)
         from_right.append(leftward)
+    values = apply(values)
+    from_left = [apply(block) for block in from_left]
+    from_right = [apply(block) for block in from_right]
     chunks = []
     for target in range(count):
         chunk = values
@@ -302,18 +305,20 @@
     paired = jnp.concatenate([basis_rows * ahead_mask, basis_rows * (1.0 - ahead_mask)], axis=1)
     paired = paired.reshape(block_total, 2 * block_len, paired.shape[-1])
     basis_spec = jnp.einsum("gf,bfk->bgk", forward, paired, precision=lax.Precision.HIGHEST)
-    group_tokens = relay_gather(tokens, "fsdp")
-    group_tokens, basis_spec, across = lax.optimization_barrier((group_tokens, basis_spec, across))
+    local_cols = in_weight.shape[1]
+
+    def project(block):
+        rows = jnp.dot(
+            block.reshape(seq_dev * block_len, width),
+            in_weight,
+            preferred_element_type=jnp.float32,
+        ).astype(jnp.bfloat16)
+        return rows.reshape(seq_dev, block_len, local_cols)
+
+    partial = relay_gather(tokens, "fsdp", project)
+    partial, basis_spec, across = lax.optimization_barrier((partial, basis_spec, across))
     gathered = lax.all_gather(across, ("groups", "seq"), axis=0, tiled=False)
     gathered = jnp.transpose(gathered, (2, 1, 0, 3)).reshape(params.shape[0], width)
-    group_rows = group_tokens.shape[0]
-    local_cols = in_weight.shape[1]
-    partial = jnp.dot(
-        group_tokens.reshape(group_rows * block_len, width),
-        in_weight,
-        preferred_element_type=jnp.float32,
-    ).astype(jnp.bfloat16)
-    partial = partial.reshape(group_rows, block_len, local_cols)
     projected = lax.all_to_all(partial, "fsdp", 0, 2, tiled=True)
     projected, gathered = lax.optimization_barrier((projected, gathered))
     padded = padded_2(projected, (("seq", 1),), 1)

time: 179 us -> 174 us (0.972)
  waiting for transfers between devices: 76.8 us -> 68.3 us
  matrix products: 11 us -> 19.3 us
  other arithmetic: 13.8 us -> 9.86 us
    ppermute x3, waiting for transfers between devices: 34.9 us -> 24.3 us  [relay_gather(): lax.ppermute(leftward, axis, [(j, j - 1) for j in range(1, count - step +...]
    dot_general x1 -> x7, matrix products: 5.52 us -> 13.8 us  [project(): jnp.dot(block.reshape(seq_dev * block_len, width), in_weight, preferred_e...]
    select_n x2 -> x1, other arithmetic: 5.61 us -> 0.31 us  [relay_gather(): chunk = jnp.where(own + step == target, from_right[step - 1], chunk)]
    ppermute x3, waiting for transfers between devices: 0.01 us -> 4.82 us  [permute_gather(): lax.ppermute(values, axis, [(i, (i + shift) % count) for i in range(count)])]
    all_to_all x1, waiting for transfers between devices: 28.2 us -> 25.8 us  [shards(): projected = lax.all_to_all(partial, 'fsdp', 0, 2, tiled=True)]
  transfers between devices with their start and end apart: 15 -> 15, of which waited for: 8 -> 8; matrix products, arithmetic and copies ran while one was open for 12% -> 19% of each run, Pallas kernels for 3% -> 3%
where the time goes in v19:
time: 174 us; the launch traced here: 173 us
  waiting for transfers between devices  68.3 us (39%)
  starting transfers between devices  30.5 us (18%)
  matrix products  19.3 us (11%)
  blocking collectives  15.5 us (9%)
  local copies, waits for them, and re-layouts  14.1 us (8%)
  Pallas kernels  14.1 us (8%)
  other arithmetic  9.86 us (6%)
    all_to_all x1, waiting for transfers between devices, shards(): projected = lax.all_to_all(partial, 'fsdp', 0, 2, tiled=True)  25.8 us
    ppermute x3, waiting for transfers between devices, relay_gather(): lax.ppermute(leftward, axis, [(j, j - 1) for j in range(1, count - step +...  24.3 us
    all_gather x1, blocking collectives, shards(): gathered = lax.all_gather(across, ('groups', 'seq'), axis=0, tiled=False)  15.5 us
    pallas_call x2, Pallas kernels, fused_conv(): pl.pallas_call(conv_body(finish), grid=(width // lanes,), in_specs=specs,...  14.1 us
    dot_general x7, matrix products, project(): jnp.dot(block.reshape(seq_dev * block_len, width), in_weight, preferred_e...  13.8 us
    ppermute x1, waiting for transfers between devices, shards(): lax.ppermute(carried, 'seq', [(i, (i + 2 * shift) % seq_count) for i in r...  10.6 us
    ppermute x3, starting transfers between devices, relay_gather(): lax.ppermute(rightward, axis, [(j, j + 1) for j in range(step - 1, count...  8.37 us
    ppermute x3, starting transfers between devices, permute_gather(): lax.ppermute(values, axis, [(i, (i + shift) % count) for i in range(count)])  5.26 us
  transfers between devices with their start and end apart: 15, of which 8 were waited for; matrix products, arithmetic and copies ran while one was open for 19% of the time, Pallas kernels for 3%

profile of v19, /device:TPU:0, one launch (start us, length us, event | category | flops | bytes accessed | tf_op | source)
XLA Modules:
  0.0 173.3 jit_solution(4709595358266758357)
XLA Ops:
  0.0 6.1 %collective-permute-start.3 = (bf16[2,128,1536]{2,1,0:T(8,128)(2,1)}, bf16[2,128,1536]{2,1,0:T(8,128)(2,1)}, u32[]{:S(2)}, u32[]{:S(2)}) collective-permute-start(bf16[2,128,1536]{2,1,0:T(8,128)(2,1)} %param.13), channel_id=1, source_target_pairs={{0,1},{1,2},{2,3},{4,5},{5,6},{6,7},{8,9},{9,10},{10,11},{12,13},{... | collective-permute-start | bytes 2359304 | tf_op jit(solution)/shard_map/ppermute | solution.py:48
  6.1 1.3 collective-permute-start
  7.4 0.7 broadcast_in_dim.24
  8.1 1.6 fusion.19
  9.7 4.7 %collective-permute-start.6 = (f32[129,48]{1,0:T(8,128)}, f32[129,48]{1,0:T(8,128)}, u32[]{:S(2)}, u32[]{:S(2)}) collective-permute-start(f32[129,48]{1,0:T(8,128)} %fusion.19), channel_id=1, source_target_pairs={{0,3},{1,0},{2,1},{3,2},{4,7},{5,4},{6,5},{7,6},{8,11},{9,8},{10,9... | collective-permute-start | bytes 74312 | tf_op jit(solution)/shard_map/ppermute | solution.py:69
  14.4 0.6 collective-permute-start.8
  15.0 0.6 fusion.43
  17.1 0.6 fusion.27
  17.7 2.0 %fusion.3 = f32[1024,64]{0,1:T(8,128)S(1)} fusion(f32[17,64]{1,0:T(8,128)} %param.16, f32[64]{0:T(128)} %param.17, f32[1024,8]{0,1:T(8,128)S(1)} %get-tuple-element.43, f32[1024,8]{0,1:T(8,128)S(1)} %get-tuple-element.42, f32[1024,1]{0,1:T(1,128)S(1)} %bitcast.88), kind=kOutput, calls=%fused_computation.20 | convolution fusion | flops 13469696 | bytes 336384 | tf_op jit(solution)/shard_map/dot_general | solution.py:92
  19.7 2.0 %broadcast_multiply_fusion.1 = (f32[1024,64]{0,1:T(8,128)S(1)}, f32[1024,64]{0,1:T(8,128)S(1)}) fusion(f32[1024]{0:T(1024)S(1)} %bitcast.87, f32[1024]{0:T(1024)S(1)} %broadcast_subtract_fusion, f32[64]{0:T(128)} %param.19, f32[1024,64]{0,1:T(8,128)S(1)} %fusion.3, f32[64,64]{1,0:T(8,128)} %param.18), kind=kOutput, calls=%fused_computation.50 | convolution fusion | flops 50528256 | bytes 811264 | tf_op jit(solution)/shard_map/dot_general | solution.py:93
  21.8 3.1 %convolution_convert_fusion = bf16[256,1152]{1,0:T(8,128)(2,1)} fusion(bf16[256,1536]{1,0:T(8,128)(2,1)} %bitcast.90, bf16[1536,1152]{1,0:T(8,128)(2,1)S(1)} %copy-done), kind=kOutput, calls=%fused_computation.1 | convolution fusion | flops 906264576 | bytes 4915200 | tf_op jit(solution)/shard_map/dot_general | solution.py:311
  24.9 0.5 negate_select_fusion.2
  25.5 1.6 collective-permute-start.4
  27.1 1.5 convolution_bitcast_fusion
  28.6 1.0 collective-permute-done.6
  29.5 3.9 %collective-permute-done.7 = f32[129,48]{1,0:T(8,128)} collective-permute-done((f32[129,48]{1,0:T(8,128)}, f32[129,48]{1,0:T(8,128)}, u32[]{:S(2)}, u32[]{:S(2)}) %collective-permute-start.7) | collective-permute-done | bytes 24800 | tf_op jit(solution)/shard_map/ppermute | solution.py:69
  33.4 1.1 select_bitcast_fusion.3
  34.5 1.3 collective-permute-start.1
  35.8 0.7 pad_maximum_fusion.8
  36.6 2.3 %convolution_convert_fusion.1 = bf16[256,1152]{1,0:T(8,128)(2,1)S(1)} fusion(bf16[256,1536]{1,0:T(8,128)(2,1)} %bitcast.5, bf16[1536,1152]{1,0:T(8,128)(2,1)S(1)} %copy-done), kind=kOutput, calls=%fused_computation.2 | convolution fusion | flops 906264576 | bytes 4915200 | tf_op jit(solution)/shard_map/dot_general | solution.py:311
  38.9 0.7 collective-permute-start.5
  39.6 2.3 %convolution_convert_fusion.2 = bf16[256,1152]{1,0:T(8,128)(2,1)S(1)} fusion(bf16[256,1536]{1,0:T(8,128)(2,1)} %bitcast.4, bf16[1536,1152]{1,0:T(8,128)(2,1)S(1)} %copy-done), kind=kOutput, calls=%fused_computation.3 | convolution fusion | flops 906264576 | bytes 4915200 | tf_op jit(solution)/shard_map/dot_general | solution.py:311
  41.9 12.1 %collective-permute-done.1 = bf16[2,128,1536]{2,1,0:T(8,128)(2,1)S(1)} collective-permute-done((bf16[2,128,1536]{2,1,0:T(8,128)(2,1)}, bf16[2,128,1536]{2,1,0:T(8,128)(2,1)S(1)}, u32[]{:S(2)}, u32[]{:S(2)}) %collective-permute-start.1) | collective-permute-done | bytes 786464 | tf_op jit(solution)/shard_map/ppermute | solution.py:49
  54.0 1.5 collective-permute-start.2
  55.5 2.3 %convolution_convert_fusion.3 = bf16[256,1152]{1,0:T(8,128)(2,1)S(1)} fusion(bf16[256,1536]{1,0:T(8,128)(2,1)} %bitcast.3, bf16[1536,1152]{1,0:T(8,128)(2,1)S(1)} %copy-done), kind=kOutput, calls=%fused_computation.4 | convolution fusion | flops 906264576 | bytes 4915200 | tf_op jit(solution)/shard_map/dot_general | solution.py:311
  57.8 1.2 convolution_convert_fusion.4
  59.1 1.2 convolution_convert_fusion.5
  60.3 12.1 %collective-permute-done.2 = bf16[2,128,1536]{2,1,0:T(8,128)(2,1)S(1)} collective-permute-done((bf16[2,128,1536]{2,1,0:T(8,128)(2,1)S(1)}, bf16[2,128,1536]{2,1,0:T(8,128)(2,1)S(1)}, u32[]{:S(2)}, u32[]{:S(2)}) %collective-permute-start.2) | collective-permute-done | bytes 786464 | tf_op jit(solution)/shard_map/ppermute | solution.py:49
  72.4 1.3 select_select_fusion.2
  74.0 1.8 %pad_maximum_fusion.2 = bf16[8,128,1152]{2,1,0:T(8,128)(2,1)} fusion(bf16[2,128,1152]{2,1,0:T(8,128)(2,1)S(1)} %bitcast.85, bf16[2,128,1152]{2,1,0:T(8,128)(2,1)S(1)} %bitcast.77, bf16[2,128,1152]{2,1,0:T(8,128)(2,1)S(1)} %bitcast.84, bf16[2,128,1152]{2,1,0:T(8,128)(2,1)S(1)} %bitcast.76), kind=kLoop, calls=%fused_computation.10 | loop fusion | flops 3538944 | bytes 4718592 | tf_op jit(solution)/shard_map/concatenate | solution.py:62
  75.8 4.7 %all-to-all-start = ((bf16[8,128,1152]{2,1,0:T(8,128)(2,1)}), bf16[8,128,1152]{2,1,0:T(8,128)(2,1)}, u32[]{:S(2)}, u32[]{:S(2)}) async-start(bf16[8,128,1152]{2,1,0:T(8,128)(2,1)} %pad_maximum_fusion.2), calls=%async_computation | async-start | bytes 4718592 | tf_op jit(solution)/shard_map/all_to_all | solution.py:322
  80.6 1.8 %copy.32 = f32[4,129,48]{1,2,0:T(8,128)} copy(f32[4,129,48]{2,1,0:T(8,128)} %pad_maximum_fusion.8) | data formatting | bytes 198144 | tf_op jit(solution)/shard_map/optimization_barrier | solution.py:319
  82.4 15.5 %all-gather = f32[32,129,48]{1,2,0:T(8,128)} all-gather(f32[4,129,48]{1,2,0:T(8,128)} %copy.32), channel_id=2, replica_groups=mesh['groups'=2,'seq'=4,'fsdp'=4] {'groups','seq'}, dimensions={0}, use_global_device_ids=true | all-gather | bytes 891648 | tf_op jit(solution)/shard_map/all_gather | solution.py:320
  97.9 3.6 %copy.33 = f32[129,4,8,48]{3,2,1,0:T(8,128)} copy(f32[129,4,8,48]{0,3,1,2:T(8,128)} %bitcast.75) | data formatting | bytes 1585152 | tf_op jit(solution)/shard_map/transpose | solution.py:321
  101.5 3.6 %reshape.283.refs_2_ = f32[129,1536]{1,0:T(8,128)} reshape(f32[129,4,8,48]{3,2,1,0:T(8,128)} %copy.33) | data formatting | bytes 1585152 | tf_op jit(solution)/shard_map/reshape | solution.py:321
  105.1 25.8 %all-to-all-done = bf16[8,128,1152]{2,1,0:T(8,128)(2,1)} async-done(((bf16[8,128,1152]{2,1,0:T(8,128)(2,1)}), bf16[8,128,1152]{2,1,0:T(8,128)(2,1)}, u32[]{:S(2)}, u32[]{:S(2)}) %all-to-all-start) | async-done | bytes 2359328 | tf_op jit(solution)/shard_map/all_to_all | solution.py:322
  131.0 1.9 %copy.36 = bf16[4,2,16,8,1152]{4,3,0,2,1:T(8,128)(2,1)S(1)} copy(bf16[4,2,16,8,1152]{4,3,2,1,0:T(8,128)(2,1)} %bitcast.31) | data formatting | bytes 4718592 | tf_op jit(solution)/shard_map/all_to_all | solution.py:322
  133.0 1.3 collective-permute-start.10
  134.3 3.3 %collective-permute-start.9 = (bf16[2,1,4608]{2,1,0:T(2,128)(2,1)S(1)}, bf16[2,1,4608]{2,1,0:T(2,128)(2,1)S(1)}, u32[]{:S(2)}, u32[]{:S(2)}) collective-permute-start(bf16[2,1,4608]{2,1,0:T(2,128)(2,1)S(1)} %get-tuple-element.32), channel_id=1, source_target_pairs={{0,4},{4,8},{8,12},{1,5},{5,9},{9,13},{2,6},{6,10},{10,14},{3,7},{... | collective-permute-start | bytes 55304 | tf_op jit(solution)/shard_map/ppermute | solution.py:19
  137.7 0.5 collective-permute-done.9
  138.1 1.9 %multiply_add_fusion = f32[2,128,4608]{2,1,0:T(8,128)S(1)} fusion(bf16[2,128,4608]{2,1,0:T(8,128)(2,1)S(1)} %bitcast.74, bf16[2,1,4608]{2,1,0:T(2,128)(2,1)S(1)} %collective-permute-done.10, bf16[2,1,4608]{2,1,0:T(2,128)(2,1)S(1)} %collective-permute-done.9, f32[4608]{0:T(1024)S(1)} %get-tuple-element.20, f32[4608]{0:T(1024)S(1)} %get-tuple-element.21, ...), kind=kLoop, calls=%fused_computation | loop fusion | flops 16515072 | bytes 7170048 | tf_op jit(solution)/shard_map/add | solution.py:326
  140.4 1.4 collective-permute-start.12
  141.8 2.3 %collective-permute-start.11 = (bf16[2,128,1536]{2,1,0:T(8,128)(2,1)S(1)}, bf16[2,128,1536]{2,1,0:T(8,128)(2,1)S(1)}, u32[]{:S(2)}, u32[]{:S(2)}) collective-permute-start(bf16[2,128,1536]{2,1,0:T(8,128)(2,1)S(1)} %get-tuple-element.27.refs_5_), channel_id=1, source_target_pairs={{0,8},{4,12},{8,0},{12,4},{1,9},{5,13},{9,1},{13,5},{2,10},{6,14},... | collective-permute-start | bytes 2359304 | tf_op jit(solution)/shard_map/ppermute | solution.py:342
  144.4 5.5 %shard_map.130.refs_3_ = f32[2,256,1536]{2,1,0:T(8,128)S(1)} custom-call(bf16[2,2,128,1536]{3,2,1,0:T(8,128)(2,1)S(1)} %pad_maximum_fusion.3.refs_0_, bf16[2,256,384]{2,1,0:T(8,128)(2,1)S(1)} %pad_maximum_fusion.6.refs_1_, f32[129,1536]{1,0:T(8,128)S(1)} %copy-done.2, bf16[256,256]{1,0:T(8,128)(2,1)S(1)} %copy-done.3), custom_call_target="tpu_custom_call" | custom-call | tf_op jit(solution)/shard_map/pallas_call | solution.py:252
  149.9 1.6 copy-done.1
  151.6 10.6 %collective-permute-done.11 = bf16[2,128,1536]{2,1,0:T(8,128)(2,1)S(1)} collective-permute-done((bf16[2,128,1536]{2,1,0:T(8,128)(2,1)S(1)}, bf16[2,128,1536]{2,1,0:T(8,128)(2,1)S(1)}, u32[]{:S(2)}, u32[]{:S(2)}) %collective-permute-start.11) | collective-permute-done | bytes 786464 | tf_op jit(solution)/shard_map/ppermute | solution.py:342
  162.3 2.2 %collective-permute-done.13 = bf16[1,2,128,1536]{3,2,1,0:T(8,128)(2,1)S(1)} collective-permute-done((bf16[1,2,128,1536]{3,2,1,0:T(8,128)(2,1)S(1)}, bf16[1,2,128,1536]{3,2,1,0:T(8,128)(2,1)S(1)}, u32[]{:S(2)}, u32[]{:S(2)}) %collective-permute-start.13) | collective-permute-done | bytes 786464 | tf_op jit(solution)/shard_map/ppermute | solution.py:350
  164.7 8.6 %shard_map.131 = bf16[2,128,1536]{2,1,0:T(8,128)(2,1)} custom-call(bf16[2,2,128,1536]{3,2,1,0:T(8,128)(2,1)S(1)} %pad_maximum_fusion.4.refs_0_, bf16[2,256,384]{2,1,0:T(8,128)(2,1)S(1)} %pad_maximum_fusion.7.refs_1_, f32[129,1536]{1,0:T(8,128)S(1)} %copy-done.2, f32[2,256,1536]{2,1,0:T(8,128)} %copy-done.1, f32[2,128,1536]{2,1,0:T(8,128)S(1)} %get-tuple-element.26.refs_4_, ...), custom_call_target="tpu_custom_call" | custom-call | tf_op jit(solution)/shard_map/pallas_call | solution.py:252
  (51 shorter events, 1.8 us)
Async XLA Ops:
  0.0 21.8 %copy-start = (bf16[1536,1152]{1,0:T(8,128)(2,1)S(1)}, bf16[1536,1152]{1,0:T(8,128)(2,1)}, u32[]{:S(2)}) copy-start(bf16[1536,1152]{1,0:T(8,128)(2,1)} %param.14) | copy-start | bytes 10616836
  0.0 25.5 %collective-permute-start.3 = (bf16[2,128,1536]{2,1,0:T(8,128)(2,1)}, bf16[2,128,1536]{2,1,0:T(8,128)(2,1)}, u32[]{:S(2)}, u32[]{:S(2)}) collective-permute-start(bf16[2,128,1536]{2,1,0:T(8,128)(2,1)} %param.13), channel_id=1, source_target_pairs={{0,1},{1,2},{2,3},{4,5},{5,6},{6,7},{8,9},{9,10},{10,11},{12,13},{... | collective-permute-start | bytes 2359304 | tf_op jit(solution)/shard_map/ppermute | solution.py:48
  6.1 28.4 %collective-permute-start = (bf16[2,128,1536]{2,1,0:T(8,128)(2,1)}, bf16[2,128,1536]{2,1,0:T(8,128)(2,1)}, u32[]{:S(2)}, u32[]{:S(2)}) collective-permute-start(bf16[2,128,1536]{2,1,0:T(8,128)(2,1)} %param.13), channel_id=1, source_target_pairs={{1,0},{2,1},{3,2},{5,4},{6,5},{7,6},{9,8},{10,9},{11,10},{13,12},{... | collective-permute-start | bytes 2359304 | tf_op jit(solution)/shard_map/ppermute | solution.py:49
  9.7 19.8 %collective-permute-start.6 = (f32[129,48]{1,0:T(8,128)}, f32[129,48]{1,0:T(8,128)}, u32[]{:S(2)}, u32[]{:S(2)}) collective-permute-start(f32[129,48]{1,0:T(8,128)} %fusion.19), channel_id=1, source_target_pairs={{0,3},{1,0},{2,1},{3,2},{4,7},{5,4},{6,5},{7,6},{8,11},{9,8},{10,9... | collective-permute-start | bytes 74312 | tf_op jit(solution)/shard_map/ppermute | solution.py:69
  14.4 19.0 %collective-permute-start.7 = (f32[129,48]{1,0:T(8,128)}, f32[129,48]{1,0:T(8,128)}, u32[]{:S(2)}, u32[]{:S(2)}) collective-permute-start(f32[129,48]{1,0:T(8,128)} %fusion.19), channel_id=1, source_target_pairs={{0,2},{1,3},{2,0},{3,1},{4,6},{5,7},{6,4},{7,5},{8,10},{9,11},{10,... | collective-permute-start | bytes 74312 | tf_op jit(solution)/shard_map/ppermute | solution.py:69
  14.4 19.0 %collective-permute-start.8 = (f32[129,48]{1,0:T(8,128)}, f32[129,48]{1,0:T(8,128)}, u32[]{:S(2)}, u32[]{:S(2)}) collective-permute-start(f32[129,48]{1,0:T(8,128)} %fusion.19), channel_id=1, source_target_pairs={{0,1},{1,2},{2,3},{3,0},{4,5},{5,6},{6,7},{7,4},{8,9},{9,10},{10,1... | collective-permute-start | bytes 74312 | tf_op jit(solution)/shard_map/ppermute | solution.py:69
  25.5 13.4 %collective-permute-start.4 = (bf16[2,128,1536]{2,1,0:T(8,128)(2,1)}, bf16[2,128,1536]{2,1,0:T(8,128)(2,1)}, u32[]{:S(2)}, u32[]{:S(2)}) collective-permute-start(bf16[2,128,1536]{2,1,0:T(8,128)(2,1)} %collective-permute-done.3), channel_id=1, source_target_pairs={{1,2},{2,3},{5,6},{6,7},{9,10},{10,11},{13,14},{14,15},{17,18},{18... | collective-permute-start | bytes 2359304 | tf_op jit(solution)/shard_map/ppermute | solution.py:48
  34.5 19.5 %collective-permute-start.1 = (bf16[2,128,1536]{2,1,0:T(8,128)(2,1)}, bf16[2,128,1536]{2,1,0:T(8,128)(2,1)S(1)}, u32[]{:S(2)}, u32[]{:S(2)}) collective-permute-start(bf16[2,128,1536]{2,1,0:T(8,128)(2,1)} %collective-permute-done), channel_id=1, source_target_pairs={{1,0},{2,1},{5,4},{6,5},{9,8},{10,9},{13,12},{14,13},{17,16},{18,1... | collective-permute-start | bytes 2359304 | tf_op jit(solution)/shard_map/ppermute | solution.py:49
  38.9 20.2 %collective-permute-start.5 = (bf16[2,128,1536]{2,1,0:T(8,128)(2,1)}, bf16[2,128,1536]{2,1,0:T(8,128)(2,1)S(1)}, u32[]{:S(2)}, u32[]{:S(2)}) collective-permute-start(bf16[2,128,1536]{2,1,0:T(8,128)(2,1)} %collective-permute-done.4), channel_id=1, source_target_pairs={{2,3},{6,7},{10,11},{14,15},{18,19},{22,23},{26,27},{30,31}} | collective-permute-start | bytes 2359304 | tf_op jit(solution)/shard_map/ppermute | solution.py:48
  54.0 18.4 %collective-permute-start.2 = (bf16[2,128,1536]{2,1,0:T(8,128)(2,1)S(1)}, bf16[2,128,1536]{2,1,0:T(8,128)(2,1)S(1)}, u32[]{:S(2)}, u32[]{:S(2)}) collective-permute-start(bf16[2,128,1536]{2,1,0:T(8,128)(2,1)S(1)} %collective-permute-done.1), channel_id=1, source_target_pairs={{1,0},{5,4},{9,8},{13,12},{17,16},{21,20},{25,24},{29,28}} | collective-permute-start | bytes 2359304 | tf_op jit(solution)/shard_map/ppermute | solution.py:49
  59.0 13.4 %copy-start.6 = (bf16[256,1152]{1,0:T(8,128)(2,1)S(1)}, bf16[256,1152]{1,0:T(8,128)(2,1)}, u32[]{:S(2)}) copy-start(bf16[256,1152]{1,0:T(8,128)(2,1)} %convolution_convert_fusion) | copy-start | bytes 1769476
  75.8 4.7 %copy-start.8 = (s32[2,1]{0,1:T(1,128)S(1)}, s32[2,1]{0,1:T(1,128)}, u32[]{:S(2)}) copy-start(s32[2,1]{0,1:T(1,128)} %param.22) | copy-start | bytes 28
  75.8 55.1 %all-to-all-start = ((bf16[8,128,1152]{2,1,0:T(8,128)(2,1)}), bf16[8,128,1152]{2,1,0:T(8,128)(2,1)}, u32[]{:S(2)}, u32[]{:S(2)}) async-start(bf16[8,128,1152]{2,1,0:T(8,128)(2,1)} %pad_maximum_fusion.2), calls=%async_computation | async-start | bytes 4718592 | tf_op jit(solution)/shard_map/all_to_all | solution.py:322
  130.9 6.6 %copy-start.7 = (f32[3,4608]{1,0:T(4,128)S(1)}, f32[3,4608]{1,0:T(4,128)}, u32[]{:S(2)}) copy-start(f32[3,4608]{1,0:T(4,128)} %param.15) | copy-start | bytes 165892
  133.0 4.7 %collective-permute-start.10 = (bf16[2,1,4608]{2,1,0:T(2,128)(2,1)S(1)}, bf16[2,1,4608]{2,1,0:T(2,128)(2,1)S(1)}, u32[]{:S(2)}, u32[]{:S(2)}) collective-permute-start(bf16[2,1,4608]{2,1,0:T(2,128)(2,1)S(1)} %get-tuple-element.33), channel_id=1, source_target_pairs={{4,0},{8,4},{12,8},{5,1},{9,5},{13,9},{6,2},{10,6},{14,10},{7,3},{... | collective-permute-start | bytes 55304 | tf_op jit(solution)/shard_map/ppermute | solution.py:21
  134.3 3.9 %collective-permute-start.9 = (bf16[2,1,4608]{2,1,0:T(2,128)(2,1)S(1)}, bf16[2,1,4608]{2,1,0:T(2,128)(2,1)S(1)}, u32[]{:S(2)}, u32[]{:S(2)}) collective-permute-start(bf16[2,1,4608]{2,1,0:T(2,128)(2,1)S(1)} %get-tuple-element.32), channel_id=1, source_target_pairs={{0,4},{4,8},{8,12},{1,5},{5,9},{9,13},{2,6},{6,10},{10,14},{3,7},{... | collective-permute-start | bytes 55304 | tf_op jit(solution)/shard_map/ppermute | solution.py:19
  140.1 4.0 %copy-start.5 = (f32[4,256,128]{2,1,0:T(8,128)S(1)}, f32[4,256,128]{2,1,0:T(8,128)}, u32[]{:S(2)}) copy-start(f32[4,256,128]{2,1,0:T(8,128)} %convolution_bitcast_fusion) | copy-start | bytes 1572868
  140.4 4.0 %copy-start.2 = (f32[129,1536]{1,0:T(8,128)S(1)}, f32[129,1536]{1,0:T(8,128)}, u32[]{:S(2)}) copy-start(f32[129,1536]{1,0:T(8,128)} %reshape.283.refs_2_) | copy-start | bytes 2377732
  140.4 4.0 %copy-start.3 = (bf16[256,256]{1,0:T(8,128)(2,1)S(1)}, bf16[256,256]{1,0:T(8,128)(2,1)}, u32[]{:S(2)}) copy-start(bf16[256,256]{1,0:T(8,128)(2,1)} %constant.166.clone.refs_3_.refs_6_) | copy-start | bytes 393220
  140.4 3.8 %collective-permute-start.12 = (bf16[2,128,1536]{2,1,0:T(8,128)(2,1)S(1)}, bf16[2,128,1536]{2,1,0:T(8,128)(2,1)S(1)}, u32[]{:S(2)}, u32[]{:S(2)}) collective-permute-start(bf16[2,128,1536]{2,1,0:T(8,128)(2,1)S(1)} %get-tuple-element.27.refs_5_), channel_id=1, source_target_pairs={{0,4},{4,0},{8,12},{12,8},{1,5},{5,1},{9,13},{13,9},{2,6},{6,2},{1... | collective-permute-start | bytes 2359304 | tf_op jit(solution)/shard_map/ppermute | solution.py:338
  141.8 20.4 %collective-permute-start.11 = (bf16[2,128,1536]{2,1,0:T(8,128)(2,1)S(1)}, bf16[2,128,1536]{2,1,0:T(8,128)(2,1)S(1)}, u32[]{:S(2)}, u32[]{:S(2)}) collective-permute-start(bf16[2,128,1536]{2,1,0:T(8,128)(2,1)S(1)} %get-tuple-element.27.refs_5_), channel_id=1, source_target_pairs={{0,8},{4,12},{8,0},{12,4},{1,9},{5,13},{9,1},{13,5},{2,10},{6,14},... | collective-permute-start | bytes 2359304 | tf_op jit(solution)/shard_map/ppermute | solution.py:342
  144.4 20.3 %copy-start.4 = (bf16[128,768]{1,0:T(8,128)(2,1)S(1)}, bf16[128,768]{1,0:T(8,128)(2,1)}, u32[]{:S(2)}) copy-start(bf16[128,768]{1,0:T(8,128)(2,1)} %constant.167.clone.refs_7_) | copy-start | bytes 589828
  149.9 1.6 copy-start.1
  162.2 2.3 %collective-permute-start.13 = (bf16[1,2,128,1536]{3,2,1,0:T(8,128)(2,1)S(1)}, bf16[1,2,128,1536]{3,2,1,0:T(8,128)(2,1)S(1)}, u32[]{:S(2)}, u32[]{:S(2)}) collective-permute-start(bf16[1,2,128,1536]{3,2,1,0:T(8,128)(2,1)S(1)} %bitcast.79), channel_id=1, source_target_pairs={{0,4},{4,0},{8,12},{12,8},{1,5},{5,1},{9,13},{13,9},{2,6},{6,2},{1... | collective-permute-start | bytes 2359304 | tf_op jit(solution)/shard_map/ppermute | solution.py:350

commit v20 on v19

--- a/solution.py
+++ b/solution.py
@@ -224,7 +224,7 @@
     fwd, inv = dft_tables(rows)
     fwd = np.concatenate([fwd[0], fwd[1]], axis=1)
     inv = np.concatenate([inv[0], inv[0], inv[1]], axis=1)
-    lanes = 768 if width % 768 == 0 else width
+    lanes = width if block_total <= 4 or width % 768 else 768
     tile3 = lambda i: (0, 0, i)
     specs = [
         pl.BlockSpec((block_total, tables, rows, lanes), lambda i: (0, 0, 0, i)),

time: 174 us -> 174 us (level)
  transfers between devices with their start and end apart: 15 -> 15, of which waited for: 8 -> 8; matrix products, arithmetic and copies ran while one was open for 19% -> 20% of each run, Pallas kernels for 3% -> 3%
where the time goes in v20:
time: 174 us; the launch traced here: 173 us
  waiting for transfers between devices  69.3 us (40%)
  starting transfers between devices  30.5 us (18%)
  matrix products  19.3 us (11%)
  blocking collectives  15.5 us (9%)
  local copies, waits for them, and re-layouts  14.1 us (8%)
  Pallas kernels  12.7 us (7%)
  other arithmetic  9.86 us (6%)
    all_to_all x1, waiting for transfers between devices, shards(): projected = lax.all_to_all(partial, 'fsdp', 0, 2, tiled=True)  25.8 us
    ppermute x3, waiting for transfers between devices, relay_gather(): lax.ppermute(leftward, axis, [(j, j - 1) for j in range(1, count - step +...  24.3 us
    all_gather x1, blocking collectives, shards(): gathered = lax.all_gather(across, ('groups', 'seq'), axis=0, tiled=False)  15.5 us
    dot_general x7, matrix products, project(): jnp.dot(block.reshape(seq_dev * block_len, width), in_weight, preferred_e...  13.8 us
    pallas_call x2, Pallas kernels, fused_conv(): pl.pallas_call(conv_body(finish), grid=(width // lanes,), in_specs=specs,...  12.7 us
    ppermute x1, waiting for transfers between devices, shards(): lax.ppermute(carried, 'seq', [(i, (i + 2 * shift) % seq_count) for i in r...  11.7 us
    ppermute x3, starting transfers between devices, relay_gather(): lax.ppermute(rightward, axis, [(j, j + 1) for j in range(step - 1, count...  8.37 us
    ppermute x3, starting transfers between devices, permute_gather(): lax.ppermute(values, axis, [(i, (i + shift) % count) for i in range(count)])  5.26 us
  transfers between devices with their start and end apart: 15, of which 8 were waited for; matrix products, arithmetic and copies ran while one was open for 20% of the time, Pallas kernels for 3%

profile of v20, /device:TPU:0, one launch (start us, length us, event | category | flops | bytes accessed | tf_op | source)
XLA Modules:
  0.0 172.9 jit_solution(4907990988592907016)
XLA Ops:
  0.0 6.1 %collective-permute-start.3 = (bf16[2,128,1536]{2,1,0:T(8,128)(2,1)}, bf16[2,128,1536]{2,1,0:T(8,128)(2,1)}, u32[]{:S(2)}, u32[]{:S(2)}) collective-permute-start(bf16[2,128,1536]{2,1,0:T(8,128)(2,1)} %param.13), channel_id=1, source_target_pairs={{0,1},{1,2},{2,3},{4,5},{5,6},{6,7},{8,9},{9,10},{10,11},{12,13},{... | collective-permute-start | bytes 2359304 | tf_op jit(solution)/shard_map/ppermute | solution.py:48
  6.1 1.3 collective-permute-start
  7.4 0.7 broadcast_in_dim.24
  8.1 1.6 fusion.19
  9.7 4.7 %collective-permute-start.6 = (f32[129,48]{1,0:T(8,128)}, f32[129,48]{1,0:T(8,128)}, u32[]{:S(2)}, u32[]{:S(2)}) collective-permute-start(f32[129,48]{1,0:T(8,128)} %fusion.19), channel_id=1, source_target_pairs={{0,3},{1,0},{2,1},{3,2},{4,7},{5,4},{6,5},{7,6},{8,11},{9,8},{10,9... | collective-permute-start | bytes 74312 | tf_op jit(solution)/shard_map/ppermute | solution.py:69
  14.4 0.6 collective-permute-start.8
  15.0 0.6 fusion.43
  17.1 0.6 fusion.27
  17.7 2.0 %fusion.3 = f32[1024,64]{0,1:T(8,128)S(1)} fusion(f32[17,64]{1,0:T(8,128)} %param.16, f32[64]{0:T(128)} %param.17, f32[1024,8]{0,1:T(8,128)S(1)} %get-tuple-element.43, f32[1024,8]{0,1:T(8,128)S(1)} %get-tuple-element.42, f32[1024,1]{0,1:T(1,128)S(1)} %bitcast.88), kind=kOutput, calls=%fused_computation.20 | convolution fusion | flops 13469696 | bytes 336384 | tf_op jit(solution)/shard_map/dot_general | solution.py:92
  19.7 2.0 %broadcast_multiply_fusion.1 = (f32[1024,64]{0,1:T(8,128)S(1)}, f32[1024,64]{0,1:T(8,128)S(1)}) fusion(f32[1024]{0:T(1024)S(1)} %bitcast.87, f32[1024]{0:T(1024)S(1)} %broadcast_subtract_fusion, f32[64]{0:T(128)} %param.19, f32[1024,64]{0,1:T(8,128)S(1)} %fusion.3, f32[64,64]{1,0:T(8,128)} %param.18), kind=kOutput, calls=%fused_computation.50 | convolution fusion | flops 50528256 | bytes 811264 | tf_op jit(solution)/shard_map/dot_general | solution.py:93
  21.8 3.1 %convolution_convert_fusion = bf16[256,1152]{1,0:T(8,128)(2,1)} fusion(bf16[256,1536]{1,0:T(8,128)(2,1)} %bitcast.90, bf16[1536,1152]{1,0:T(8,128)(2,1)S(1)} %copy-done), kind=kOutput, calls=%fused_computation.1 | convolution fusion | flops 906264576 | bytes 4915200 | tf_op jit(solution)/shard_map/dot_general | solution.py:311
  24.9 0.5 negate_select_fusion.2
  25.5 1.6 collective-permute-start.4
  27.1 1.5 convolution_bitcast_fusion
  28.6 1.0 collective-permute-done.6
  29.5 3.9 %collective-permute-done.7 = f32[129,48]{1,0:T(8,128)} collective-permute-done((f32[129,48]{1,0:T(8,128)}, f32[129,48]{1,0:T(8,128)}, u32[]{:S(2)}, u32[]{:S(2)}) %collective-permute-start.7) | collective-permute-done | bytes 24800 | tf_op jit(solution)/shard_map/ppermute | solution.py:69
  33.4 1.1 select_bitcast_fusion.3
  34.5 1.3 collective-permute-start.1
  35.8 0.7 pad_maximum_fusion.8
  36.6 2.3 %convolution_convert_fusion.1 = bf16[256,1152]{1,0:T(8,128)(2,1)S(1)} fusion(bf16[256,1536]{1,0:T(8,128)(2,1)} %bitcast.5, bf16[1536,1152]{1,0:T(8,128)(2,1)S(1)} %copy-done), kind=kOutput, calls=%fused_computation.2 | convolution fusion | flops 906264576 | bytes 4915200 | tf_op jit(solution)/shard_map/dot_general | solution.py:311
  38.9 0.7 collective-permute-start.5
  39.6 2.3 %convolution_convert_fusion.2 = bf16[256,1152]{1,0:T(8,128)(2,1)S(1)} fusion(bf16[256,1536]{1,0:T(8,128)(2,1)} %bitcast.4, bf16[1536,1152]{1,0:T(8,128)(2,1)S(1)} %copy-done), kind=kOutput, calls=%fused_computation.3 | convolution fusion | flops 906264576 | bytes 4915200 | tf_op jit(solution)/shard_map/dot_general | solution.py:311
  41.9 12.1 %collective-permute-done.1 = bf16[2,128,1536]{2,1,0:T(8,128)(2,1)S(1)} collective-permute-done((bf16[2,128,1536]{2,1,0:T(8,128)(2,1)}, bf16[2,128,1536]{2,1,0:T(8,128)(2,1)S(1)}, u32[]{:S(2)}, u32[]{:S(2)}) %collective-permute-start.1) | collective-permute-done | bytes 786464 | tf_op jit(solution)/shard_map/ppermute | solution.py:49
  54.0 1.5 collective-permute-start.2
  55.5 2.3 %convolution_convert_fusion.3 = bf16[256,1152]{1,0:T(8,128)(2,1)S(1)} fusion(bf16[256,1536]{1,0:T(8,128)(2,1)} %bitcast.3, bf16[1536,1152]{1,0:T(8,128)(2,1)S(1)} %copy-done), kind=kOutput, calls=%fused_computation.4 | convolution fusion | flops 906264576 | bytes 4915200 | tf_op jit(solution)/shard_map/dot_general | solution.py:311
  57.8 1.2 convolution_convert_fusion.4
  59.1 1.2 convolution_convert_fusion.5
  60.3 12.1 %collective-permute-done.2 = bf16[2,128,1536]{2,1,0:T(8,128)(2,1)S(1)} collective-permute-done((bf16[2,128,1536]{2,1,0:T(8,128)(2,1)S(1)}, bf16[2,128,1536]{2,1,0:T(8,128)(2,1)S(1)}, u32[]{:S(2)}, u32[]{:S(2)}) %collective-permute-start.2) | collective-permute-done | bytes 786464 | tf_op jit(solution)/shard_map/ppermute | solution.py:49
  72.4 1.3 select_select_fusion.2
  74.0 1.8 %pad_maximum_fusion.2 = bf16[8,128,1152]{2,1,0:T(8,128)(2,1)} fusion(bf16[2,128,1152]{2,1,0:T(8,128)(2,1)S(1)} %bitcast.85, bf16[2,128,1152]{2,1,0:T(8,128)(2,1)S(1)} %bitcast.77, bf16[2,128,1152]{2,1,0:T(8,128)(2,1)S(1)} %bitcast.84, bf16[2,128,1152]{2,1,0:T(8,128)(2,1)S(1)} %bitcast.76), kind=kLoop, calls=%fused_computation.10 | loop fusion | flops 3538944 | bytes 4718592 | tf_op jit(solution)/shard_map/concatenate | solution.py:62
  75.8 4.7 %all-to-all-start = ((bf16[8,128,1152]{2,1,0:T(8,128)(2,1)}), bf16[8,128,1152]{2,1,0:T(8,128)(2,1)}, u32[]{:S(2)}, u32[]{:S(2)}) async-start(bf16[8,128,1152]{2,1,0:T(8,128)(2,1)} %pad_maximum_fusion.2), calls=%async_computation | async-start | bytes 4718592 | tf_op jit(solution)/shard_map/all_to_all | solution.py:322
  80.6 1.8 %copy.32 = f32[4,129,48]{1,2,0:T(8,128)} copy(f32[4,129,48]{2,1,0:T(8,128)} %pad_maximum_fusion.8) | data formatting | bytes 198144 | tf_op jit(solution)/shard_map/optimization_barrier | solution.py:319
  82.4 15.5 %all-gather = f32[32,129,48]{1,2,0:T(8,128)} all-gather(f32[4,129,48]{1,2,0:T(8,128)} %copy.32), channel_id=2, replica_groups=mesh['groups'=2,'seq'=4,'fsdp'=4] {'groups','seq'}, dimensions={0}, use_global_device_ids=true | all-gather | bytes 891648 | tf_op jit(solution)/shard_map/all_gather | solution.py:320
  97.9 3.6 %copy.33 = f32[129,4,8,48]{3,2,1,0:T(8,128)} copy(f32[129,4,8,48]{0,3,1,2:T(8,128)} %bitcast.75) | data formatting | bytes 1585152 | tf_op jit(solution)/shard_map/transpose | solution.py:321
  101.5 3.6 %reshape.283.refs_2_ = f32[129,1536]{1,0:T(8,128)} reshape(f32[129,4,8,48]{3,2,1,0:T(8,128)} %copy.33) | data formatting | bytes 1585152 | tf_op jit(solution)/shard_map/reshape | solution.py:321
  105.1 25.8 %all-to-all-done = bf16[8,128,1152]{2,1,0:T(8,128)(2,1)} async-done(((bf16[8,128,1152]{2,1,0:T(8,128)(2,1)}), bf16[8,128,1152]{2,1,0:T(8,128)(2,1)}, u32[]{:S(2)}, u32[]{:S(2)}) %all-to-all-start) | async-done | bytes 2359328 | tf_op jit(solution)/shard_map/all_to_all | solution.py:322
  131.0 1.9 %copy.36 = bf16[4,2,16,8,1152]{4,3,0,2,1:T(8,128)(2,1)S(1)} copy(bf16[4,2,16,8,1152]{4,3,2,1,0:T(8,128)(2,1)} %bitcast.31) | data formatting | bytes 4718592 | tf_op jit(solution)/shard_map/all_to_all | solution.py:322
  133.0 1.3 collective-permute-start.10
  134.3 3.3 %collective-permute-start.9 = (bf16[2,1,4608]{2,1,0:T(2,128)(2,1)S(1)}, bf16[2,1,4608]{2,1,0:T(2,128)(2,1)S(1)}, u32[]{:S(2)}, u32[]{:S(2)}) collective-permute-start(bf16[2,1,4608]{2,1,0:T(2,128)(2,1)S(1)} %get-tuple-element.32), channel_id=1, source_target_pairs={{0,4},{4,8},{8,12},{1,5},{5,9},{9,13},{2,6},{6,10},{10,14},{3,7},{... | collective-permute-start | bytes 55304 | tf_op jit(solution)/shard_map/ppermute | solution.py:19
  137.7 0.5 collective-permute-done.9
  138.1 1.9 %multiply_add_fusion = f32[2,128,4608]{2,1,0:T(8,128)S(1)} fusion(bf16[2,128,4608]{2,1,0:T(8,128)(2,1)S(1)} %bitcast.74, bf16[2,1,4608]{2,1,0:T(2,128)(2,1)S(1)} %collective-permute-done.10, bf16[2,1,4608]{2,1,0:T(2,128)(2,1)S(1)} %collective-permute-done.9, f32[4608]{0:T(1024)S(1)} %get-tuple-element.20, f32[4608]{0:T(1024)S(1)} %get-tuple-element.21, ...), kind=kLoop, calls=%fused_computation | loop fusion | flops 16515072 | bytes 7170048 | tf_op jit(solution)/shard_map/add | solution.py:326
  140.4 1.4 collective-permute-start.12
  141.8 2.3 %collective-permute-start.11 = (bf16[2,128,1536]{2,1,0:T(8,128)(2,1)S(1)}, bf16[2,128,1536]{2,1,0:T(8,128)(2,1)S(1)}, u32[]{:S(2)}, u32[]{:S(2)}) collective-permute-start(bf16[2,128,1536]{2,1,0:T(8,128)(2,1)S(1)} %get-tuple-element.27.refs_5_), channel_id=1, source_target_pairs={{0,8},{4,12},{8,0},{12,4},{1,9},{5,13},{9,1},{13,5},{2,10},{6,14},... | collective-permute-start | bytes 2359304 | tf_op jit(solution)/shard_map/ppermute | solution.py:342
  144.4 4.4 %shard_map.130.refs_3_ = f32[2,256,1536]{2,1,0:T(8,128)S(1)} custom-call(bf16[2,2,128,1536]{3,2,1,0:T(8,128)(2,1)S(1)} %pad_maximum_fusion.3.refs_0_, bf16[2,256,384]{2,1,0:T(8,128)(2,1)S(1)} %pad_maximum_fusion.6.refs_1_, f32[129,1536]{1,0:T(8,128)S(1)} %copy-done.2, bf16[256,256]{1,0:T(8,128)(2,1)S(1)} %copy-done.3), custom_call_target="tpu_custom_call" | custom-call | tf_op jit(solution)/shard_map/pallas_call | solution.py:252
  148.9 1.6 copy-done.1
  150.5 11.7 %collective-permute-done.11 = bf16[2,128,1536]{2,1,0:T(8,128)(2,1)S(1)} collective-permute-done((bf16[2,128,1536]{2,1,0:T(8,128)(2,1)S(1)}, bf16[2,128,1536]{2,1,0:T(8,128)(2,1)S(1)}, u32[]{:S(2)}, u32[]{:S(2)}) %collective-permute-start.11) | collective-permute-done | bytes 786464 | tf_op jit(solution)/shard_map/ppermute | solution.py:342
  162.3 2.2 %collective-permute-done.13 = bf16[1,2,128,1536]{3,2,1,0:T(8,128)(2,1)S(1)} collective-permute-done((bf16[1,2,128,1536]{3,2,1,0:T(8,128)(2,1)S(1)}, bf16[1,2,128,1536]{3,2,1,0:T(8,128)(2,1)S(1)}, u32[]{:S(2)}, u32[]{:S(2)}) %collective-permute-start.13) | collective-permute-done | bytes 786464 | tf_op jit(solution)/shard_map/ppermute | solution.py:350
  164.7 8.3 %shard_map.131 = bf16[2,128,1536]{2,1,0:T(8,128)(2,1)} custom-call(bf16[2,2,128,1536]{3,2,1,0:T(8,128)(2,1)S(1)} %pad_maximum_fusion.4.refs_0_, bf16[2,256,384]{2,1,0:T(8,128)(2,1)S(1)} %pad_maximum_fusion.7.refs_1_, f32[129,1536]{1,0:T(8,128)S(1)} %copy-done.2, f32[2,256,1536]{2,1,0:T(8,128)} %copy-done.1, f32[2,128,1536]{2,1,0:T(8,128)S(1)} %get-tuple-element.26.refs_4_, ...), custom_call_target="tpu_custom_call" | custom-call | tf_op jit(solution)/shard_map/pallas_call | solution.py:252
  (51 shorter events, 1.8 us)
Async XLA Ops:
  0.0 21.8 %copy-start = (bf16[1536,1152]{1,0:T(8,128)(2,1)S(1)}, bf16[1536,1152]{1,0:T(8,128)(2,1)}, u32[]{:S(2)}) copy-start(bf16[1536,1152]{1,0:T(8,128)(2,1)} %param.14) | copy-start | bytes 10616836
  0.0 25.5 %collective-permute-start.3 = (bf16[2,128,1536]{2,1,0:T(8,128)(2,1)}, bf16[2,128,1536]{2,1,0:T(8,128)(2,1)}, u32[]{:S(2)}, u32[]{:S(2)}) collective-permute-start(bf16[2,128,1536]{2,1,0:T(8,128)(2,1)} %param.13), channel_id=1, source_target_pairs={{0,1},{1,2},{2,3},{4,5},{5,6},{6,7},{8,9},{9,10},{10,11},{12,13},{... | collective-permute-start | bytes 2359304 | tf_op jit(solution)/shard_map/ppermute | solution.py:48
  6.1 28.4 %collective-permute-start = (bf16[2,128,1536]{2,1,0:T(8,128)(2,1)}, bf16[2,128,1536]{2,1,0:T(8,128)(2,1)}, u32[]{:S(2)}, u32[]{:S(2)}) collective-permute-start(bf16[2,128,1536]{2,1,0:T(8,128)(2,1)} %param.13), channel_id=1, source_target_pairs={{1,0},{2,1},{3,2},{5,4},{6,5},{7,6},{9,8},{10,9},{11,10},{13,12},{... | collective-permute-start | bytes 2359304 | tf_op jit(solution)/shard_map/ppermute | solution.py:49
  9.7 19.8 %collective-permute-start.6 = (f32[129,48]{1,0:T(8,128)}, f32[129,48]{1,0:T(8,128)}, u32[]{:S(2)}, u32[]{:S(2)}) collective-permute-start(f32[129,48]{1,0:T(8,128)} %fusion.19), channel_id=1, source_target_pairs={{0,3},{1,0},{2,1},{3,2},{4,7},{5,4},{6,5},{7,6},{8,11},{9,8},{10,9... | collective-permute-start | bytes 74312 | tf_op jit(solution)/shard_map/ppermute | solution.py:69
  14.4 19.0 %collective-permute-start.7 = (f32[129,48]{1,0:T(8,128)}, f32[129,48]{1,0:T(8,128)}, u32[]{:S(2)}, u32[]{:S(2)}) collective-permute-start(f32[129,48]{1,0:T(8,128)} %fusion.19), channel_id=1, source_target_pairs={{0,2},{1,3},{2,0},{3,1},{4,6},{5,7},{6,4},{7,5},{8,10},{9,11},{10,... | collective-permute-start | bytes 74312 | tf_op jit(solution)/shard_map/ppermute | solution.py:69
  14.4 19.0 %collective-permute-start.8 = (f32[129,48]{1,0:T(8,128)}, f32[129,48]{1,0:T(8,128)}, u32[]{:S(2)}, u32[]{:S(2)}) collective-permute-start(f32[129,48]{1,0:T(8,128)} %fusion.19), channel_id=1, source_target_pairs={{0,1},{1,2},{2,3},{3,0},{4,5},{5,6},{6,7},{7,4},{8,9},{9,10},{10,1... | collective-permute-start | bytes 74312 | tf_op jit(solution)/shard_map/ppermute | solution.py:69
  25.5 13.4 %collective-permute-start.4 = (bf16[2,128,1536]{2,1,0:T(8,128)(2,1)}, bf16[2,128,1536]{2,1,0:T(8,128)(2,1)}, u32[]{:S(2)}, u32[]{:S(2)}) collective-permute-start(bf16[2,128,1536]{2,1,0:T(8,128)(2,1)} %collective-permute-done.3), channel_id=1, source_target_pairs={{1,2},{2,3},{5,6},{6,7},{9,10},{10,11},{13,14},{14,15},{17,18},{18... | collective-permute-start | bytes 2359304 | tf_op jit(solution)/shard_map/ppermute | solution.py:48
  34.5 19.5 %collective-permute-start.1 = (bf16[2,128,1536]{2,1,0:T(8,128)(2,1)}, bf16[2,128,1536]{2,1,0:T(8,128)(2,1)S(1)}, u32[]{:S(2)}, u32[]{:S(2)}) collective-permute-start(bf16[2,128,1536]{2,1,0:T(8,128)(2,1)} %collective-permute-done), channel_id=1, source_target_pairs={{1,0},{2,1},{5,4},{6,5},{9,8},{10,9},{13,12},{14,13},{17,16},{18,1... | collective-permute-start | bytes 2359304 | tf_op jit(solution)/shard_map/ppermute | solution.py:49
  38.9 20.2 %collective-permute-start.5 = (bf16[2,128,1536]{2,1,0:T(8,128)(2,1)}, bf16[2,128,1536]{2,1,0:T(8,128)(2,1)S(1)}, u32[]{:S(2)}, u32[]{:S(2)}) collective-permute-start(bf16[2,128,1536]{2,1,0:T(8,128)(2,1)} %collective-permute-done.4), channel_id=1, source_target_pairs={{2,3},{6,7},{10,11},{14,15},{18,19},{22,23},{26,27},{30,31}} | collective-permute-start | bytes 2359304 | tf_op jit(solution)/shard_map/ppermute | solution.py:48
  54.0 18.4 %collective-permute-start.2 = (bf16[2,128,1536]{2,1,0:T(8,128)(2,1)S(1)}, bf16[2,128,1536]{2,1,0:T(8,128)(2,1)S(1)}, u32[]{:S(2)}, u32[]{:S(2)}) collective-permute-start(bf16[2,128,1536]{2,1,0:T(8,128)(2,1)S(1)} %collective-permute-done.1), channel_id=1, source_target_pairs={{1,0},{5,4},{9,8},{13,12},{17,16},{21,20},{25,24},{29,28}} | collective-permute-start | bytes 2359304 | tf_op jit(solution)/shard_map/ppermute | solution.py:49
  59.0 13.4 %copy-start.6 = (bf16[256,1152]{1,0:T(8,128)(2,1)S(1)}, bf16[256,1152]{1,0:T(8,128)(2,1)}, u32[]{:S(2)}) copy-start(bf16[256,1152]{1,0:T(8,128)(2,1)} %convolution_convert_fusion) | copy-start | bytes 1769476
  75.8 4.7 %copy-start.8 = (s32[2,1]{0,1:T(1,128)S(1)}, s32[2,1]{0,1:T(1,128)}, u32[]{:S(2)}) copy-start(s32[2,1]{0,1:T(1,128)} %param.22) | copy-start | bytes 28
  75.8 55.1 %all-to-all-start = ((bf16[8,128,1152]{2,1,0:T(8,128)(2,1)}), bf16[8,128,1152]{2,1,0:T(8,128)(2,1)}, u32[]{:S(2)}, u32[]{:S(2)}) async-start(bf16[8,128,1152]{2,1,0:T(8,128)(2,1)} %pad_maximum_fusion.2), calls=%async_computation | async-start | bytes 4718592 | tf_op jit(solution)/shard_map/all_to_all | solution.py:322
  130.9 6.6 %copy-start.7 = (f32[3,4608]{1,0:T(4,128)S(1)}, f32[3,4608]{1,0:T(4,128)}, u32[]{:S(2)}) copy-start(f32[3,4608]{1,0:T(4,128)} %param.15) | copy-start | bytes 165892
  133.0 4.7 %collective-permute-start.10 = (bf16[2,1,4608]{2,1,0:T(2,128)(2,1)S(1)}, bf16[2,1,4608]{2,1,0:T(2,128)(2,1)S(1)}, u32[]{:S(2)}, u32[]{:S(2)}) collective-permute-start(bf16[2,1,4608]{2,1,0:T(2,128)(2,1)S(1)} %get-tuple-element.33), channel_id=1, source_target_pairs={{4,0},{8,4},{12,8},{5,1},{9,5},{13,9},{6,2},{10,6},{14,10},{7,3},{... | collective-permute-start | bytes 55304 | tf_op jit(solution)/shard_map/ppermute | solution.py:21
  134.3 3.9 %collective-permute-start.9 = (bf16[2,1,4608]{2,1,0:T(2,128)(2,1)S(1)}, bf16[2,1,4608]{2,1,0:T(2,128)(2,1)S(1)}, u32[]{:S(2)}, u32[]{:S(2)}) collective-permute-start(bf16[2,1,4608]{2,1,0:T(2,128)(2,1)S(1)} %get-tuple-element.32), channel_id=1, source_target_pairs={{0,4},{4,8},{8,12},{1,5},{5,9},{9,13},{2,6},{6,10},{10,14},{3,7},{... | collective-permute-start | bytes 55304 | tf_op jit(solution)/shard_map/ppermute | solution.py:19
  140.1 4.0 %copy-start.5 = (f32[4,256,128]{2,1,0:T(8,128)S(1)}, f32[4,256,128]{2,1,0:T(8,128)}, u32[]{:S(2)}) copy-start(f32[4,256,128]{2,1,0:T(8,128)} %convolution_bitcast_fusion) | copy-start | bytes 1572868
  140.4 4.0 %copy-start.2 = (f32[129,1536]{1,0:T(8,128)S(1)}, f32[129,1536]{1,0:T(8,128)}, u32[]{:S(2)}) copy-start(f32[129,1536]{1,0:T(8,128)} %reshape.283.refs_2_) | copy-start | bytes 2377732
  140.4 4.0 %copy-start.3 = (bf16[256,256]{1,0:T(8,128)(2,1)S(1)}, bf16[256,256]{1,0:T(8,128)(2,1)}, u32[]{:S(2)}) copy-start(bf16[256,256]{1,0:T(8,128)(2,1)} %constant.166.clone.refs_3_.refs_6_) | copy-start | bytes 393220
  140.4 3.8 %collective-permute-start.12 = (bf16[2,128,1536]{2,1,0:T(8,128)(2,1)S(1)}, bf16[2,128,1536]{2,1,0:T(8,128)(2,1)S(1)}, u32[]{:S(2)}, u32[]{:S(2)}) collective-permute-start(bf16[2,128,1536]{2,1,0:T(8,128)(2,1)S(1)} %get-tuple-element.27.refs_5_), channel_id=1, source_target_pairs={{0,4},{4,0},{8,12},{12,8},{1,5},{5,1},{9,13},{13,9},{2,6},{6,2},{1... | collective-permute-start | bytes 2359304 | tf_op jit(solution)/shard_map/ppermute | solution.py:338
  141.8 20.4 %collective-permute-start.11 = (bf16[2,128,1536]{2,1,0:T(8,128)(2,1)S(1)}, bf16[2,128,1536]{2,1,0:T(8,128)(2,1)S(1)}, u32[]{:S(2)}, u32[]{:S(2)}) collective-permute-start(bf16[2,128,1536]{2,1,0:T(8,128)(2,1)S(1)} %get-tuple-element.27.refs_5_), channel_id=1, source_target_pairs={{0,8},{4,12},{8,0},{12,4},{1,9},{5,13},{9,1},{13,5},{2,10},{6,14},... | collective-permute-start | bytes 2359304 | tf_op jit(solution)/shard_map/ppermute | solution.py:342
  144.4 20.3 %copy-start.4 = (bf16[128,768]{1,0:T(8,128)(2,1)S(1)}, bf16[128,768]{1,0:T(8,128)(2,1)}, u32[]{:S(2)}) copy-start(bf16[128,768]{1,0:T(8,128)(2,1)} %constant.167.clone.refs_7_) | copy-start | bytes 589828
  148.9 1.6 copy-start.1
  162.2 2.3 %collective-permute-start.13 = (bf16[1,2,128,1536]{3,2,1,0:T(8,128)(2,1)S(1)}, bf16[1,2,128,1536]{3,2,1,0:T(8,128)(2,1)S(1)}, u32[]{:S(2)}, u32[]{:S(2)}) collective-permute-start(bf16[1,2,128,1536]{3,2,1,0:T(8,128)(2,1)S(1)} %bitcast.79), channel_id=1, source_target_pairs={{0,4},{4,0},{8,12},{12,8},{1,5},{5,1},{9,13},{13,9},{2,6},{6,2},{1... | collective-permute-start | bytes 2359304 | tf_op jit(solution)/shard_map/ppermute | solution.py:350

commit v21 on v20

--- a/solution.py
+++ b/solution.py
@@ -160,8 +160,8 @@
 def conv_body(finish):
     def kernel(*refs):
         if finish:
-            (piece_ref, basis_ref, out_cols_ref, spec_in_ref, query_ref, carried_ref,
-             fwd_ref, inv_ref, out_ref, resp_ref) = refs
+            (piece_ref, resp_ref, out_cols_ref, spec_in_ref, query_ref, carried_ref,
+             fwd_ref, inv_ref, out_ref) = refs
         else:
             piece_ref, basis_ref, out_cols_ref, fwd_ref, out_ref, resp_ref = refs
         block_total, tables, rows, lanes = piece_ref.shape
@@ -177,7 +177,8 @@
             resp_ref[block] = dot(basis_ref[block], cols)
             return carry
 
-        lax.fori_loop(0, block_total, fill, 0)
+        if not finish:
+            lax.fori_loop(0, block_total, fill, 0)
         first = lax.broadcasted_iota(jnp.int32, (rows, lanes), 0) == 0
         fwd = fwd_ref[...]
 
@@ -226,12 +227,20 @@
     inv = np.concatenate([inv[0], inv[0], inv[1]], axis=1)
     lanes = width if block_total <= 4 or width % 768 else 768
     tile3 = lambda i: (0, 0, i)
+    if finish:
+        cols_hi, cols_lo = split_bf16(out_cols[:-1])
+        cols = jnp.concatenate([cols_hi, cols_lo, cols_hi], axis=0)
+        response = jnp.einsum("bgk,kd->bgd", basis, cols, preferred_element_type=jnp.float32)
+        second = pl.BlockSpec((block_total, 2 * rows, lanes), lambda i: (0, 0, i))
+    else:
+        response = basis
+        second = pl.BlockSpec(basis.shape, lambda i: (0, 0, 0))
     specs = [
         pl.BlockSpec((block_total, tables, rows, lanes), lambda i: (0, 0, 0, i)),
-        pl.BlockSpec(basis.shape, lambda i: (0, 0, 0)),
+        second,
         pl.BlockSpec((out_cols.shape[0], lanes), lambda i: (0, i)),
     ]
-    operands = [piece, basis, out_cols]
+    operands = [piece, response, out_cols]
     if finish:
         specs += [
             pl.BlockSpec((tables, 2 * rows, lanes), tile3),
@@ -255,7 +264,7 @@
         in_specs=specs,
         out_specs=pl.BlockSpec(out_block, tile3),
         out_shape=out_shape,
-        scratch_shapes=[pltpu.VMEM((block_total, 2 * rows, lanes), jnp.float32)],
+        scratch_shapes=[] if finish else [pltpu.VMEM((block_total, 2 * rows, lanes), jnp.float32)],
         compiler_params=pltpu.CompilerParams(vmem_limit_bytes=48 * 1024 * 1024),
     )(*operands)
 

time: 174 us -> 175 us (level)
    dot_general x0 -> x1, matrix products: none -> 2.61 us  [fused_conv(): jnp.einsum('bgk,kd->bgd', basis, cols, preferred_element_type=jnp.float32)]
    ppermute x1, waiting for transfers between devices: 2.24 us -> 0.01 us  [shards(): far = jnp.concatenate([far, lax.ppermute(far, 'seq', partner)], axis=0)]
  transfers between devices with their start and end apart: 15 -> 15, of which waited for: 8 -> 7; matrix products, arithmetic and copies ran while one was open for 20% -> 20% of each run, Pallas kernels for 3% -> 3%
where the time goes in v21:
time: 175 us; the launch traced here: 174 us
  waiting for transfers between devices  69.7 us (40%)
  starting transfers between devices  30.5 us (17%)
  matrix products  20.8 us (12%)
  blocking collectives  15.5 us (9%)
  local copies, waits for them, and re-layouts  13.2 us (8%)
  Pallas kernels  12.6 us (7%)
  other arithmetic  9.89 us (6%)
    all_to_all x1, waiting for transfers between devices, shards(): projected = lax.all_to_all(partial, 'fsdp', 0, 2, tiled=True)  25.8 us
    ppermute x3, waiting for transfers between devices, relay_gather(): lax.ppermute(leftward, axis, [(j, j - 1) for j in range(1, count - step +...  24.2 us
    all_gather x1, blocking collectives, shards(): gathered = lax.all_gather(across, ('groups', 'seq'), axis=0, tiled=False)  15.5 us
    ppermute x1, waiting for transfers between devices, shards(): lax.ppermute(carried, 'seq', [(i, (i + 2 * shift) % seq_count) for i in r...  13.4 us
    dot_general x7, matrix products, project(): jnp.dot(block.reshape(seq_dev * block_len, width), in_weight, preferred_e...  12.6 us
    pallas_call x2, Pallas kernels, fused_conv(): pl.pallas_call(conv_body(finish), grid=(width // lanes,), in_specs=specs,...  12.6 us
    ppermute x3, starting transfers between devices, relay_gather(): lax.ppermute(rightward, axis, [(j, j + 1) for j in range(step - 1, count...  8.37 us
    ppermute x3, waiting for transfers between devices, permute_gather(): lax.ppermute(values, axis, [(i, (i + shift) % count) for i in range(count)])  5.84 us
  transfers between devices with their start and end apart: 15, of which 7 were waited for; matrix products, arithmetic and copies ran while one was open for 20% of the time, Pallas kernels for 3%

profile of v21, /device:TPU:0, one launch (start us, length us, event | category | flops | bytes accessed | tf_op | source)
XLA Modules:
  0.0 173.9 jit_solution(13692975647463209024)
XLA Ops:
  0.0 6.1 %collective-permute-start.3 = (bf16[2,128,1536]{2,1,0:T(8,128)(2,1)}, bf16[2,128,1536]{2,1,0:T(8,128)(2,1)}, u32[]{:S(2)}, u32[]{:S(2)}) collective-permute-start(bf16[2,128,1536]{2,1,0:T(8,128)(2,1)} %param.13), channel_id=1, source_target_pairs={{0,1},{1,2},{2,3},{4,5},{5,6},{6,7},{8,9},{9,10},{10,11},{12,13},{... | collective-permute-start | bytes 2359304 | tf_op jit(solution)/shard_map/ppermute | solution.py:48
  6.1 1.3 collective-permute-start
  7.4 0.7 broadcast_in_dim.24
  8.1 1.6 fusion.29
  9.7 4.7 %collective-permute-start.6 = (f32[129,48]{1,0:T(8,128)}, f32[129,48]{1,0:T(8,128)}, u32[]{:S(2)}, u32[]{:S(2)}) collective-permute-start(f32[129,48]{1,0:T(8,128)} %fusion.29), channel_id=1, source_target_pairs={{0,3},{1,0},{2,1},{3,2},{4,7},{5,4},{6,5},{7,6},{8,11},{9,8},{10,9... | collective-permute-start | bytes 74312 | tf_op jit(solution)/shard_map/ppermute | solution.py:69
  14.4 0.6 collective-permute-start.8
  15.0 0.6 fusion.54
  17.3 0.6 fusion.37
  17.8 2.0 %fusion.8 = f32[1024,64]{0,1:T(8,128)S(1)} fusion(f32[17,64]{1,0:T(8,128)} %param.16, f32[64]{0:T(128)} %param.17, f32[1024,8]{0,1:T(8,128)S(1)} %get-tuple-element.45, f32[1024,8]{0,1:T(8,128)S(1)} %get-tuple-element.44, f32[1024,1]{0,1:T(1,128)S(1)} %bitcast.91), kind=kOutput, calls=%fused_computation.26 | convolution fusion | flops 13469696 | bytes 336384 | tf_op jit(solution)/shard_map/dot_general | solution.py:92
  19.8 2.0 %broadcast_multiply_fusion.1 = (f32[1024,64]{0,1:T(8,128)S(1)}, f32[1024,64]{0,1:T(8,128)S(1)}) fusion(f32[1024]{0:T(1024)S(1)} %bitcast.90, f32[1024]{0:T(1024)S(1)} %broadcast_subtract_fusion, f32[64]{0:T(128)} %param.19, f32[1024,64]{0,1:T(8,128)S(1)} %fusion.8, f32[64,64]{1,0:T(8,128)} %param.18), kind=kOutput, calls=%fused_computation.62 | convolution fusion | flops 50528256 | bytes 811264 | tf_op jit(solution)/shard_map/dot_general | solution.py:93
  21.9 2.0 %convolution_convert_fusion = bf16[256,1152]{1,0:T(8,128)(2,1)} fusion(bf16[256,1536]{1,0:T(8,128)(2,1)S(1)} %bitcast.93, bf16[1536,1152]{1,0:T(8,128)(2,1)S(1)} %copy-done), kind=kOutput, calls=%fused_computation.1 | convolution fusion | flops 906264576 | bytes 4915200 | tf_op jit(solution)/shard_map/dot_general | solution.py:320
  23.9 0.5 negate_select_fusion.2
  24.5 1.6 collective-permute-start.4
  26.0 1.5 convolution_bitcast_fusion
  27.6 2.0 %collective-permute-done.6 = f32[129,48]{1,0:T(8,128)} collective-permute-done((f32[129,48]{1,0:T(8,128)}, f32[129,48]{1,0:T(8,128)}, u32[]{:S(2)}, u32[]{:S(2)}) %collective-permute-start.6) | collective-permute-done | bytes 24800 | tf_op jit(solution)/shard_map/ppermute | solution.py:69
  29.5 3.9 %collective-permute-done.7 = f32[129,48]{1,0:T(8,128)} collective-permute-done((f32[129,48]{1,0:T(8,128)}, f32[129,48]{1,0:T(8,128)}, u32[]{:S(2)}, u32[]{:S(2)}) %collective-permute-start.7) | collective-permute-done | bytes 24800 | tf_op jit(solution)/shard_map/ppermute | solution.py:69
  33.4 1.1 select_bitcast_fusion.3
  34.5 1.3 collective-permute-start.1
  35.8 0.7 pad_maximum_fusion.7
  36.6 2.3 %convolution_convert_fusion.2 = bf16[256,1152]{1,0:T(8,128)(2,1)S(1)} fusion(bf16[256,1536]{1,0:T(8,128)(2,1)} %bitcast.4, bf16[1536,1152]{1,0:T(8,128)(2,1)S(1)} %copy-done), kind=kOutput, calls=%fused_computation.3 | convolution fusion | flops 906264576 | bytes 4915200 | tf_op jit(solution)/shard_map/dot_general | solution.py:320
  38.9 0.7 collective-permute-start.5
  39.6 2.3 %convolution_convert_fusion.1 = bf16[256,1152]{1,0:T(8,128)(2,1)S(1)} fusion(bf16[256,1536]{1,0:T(8,128)(2,1)} %bitcast.5, bf16[1536,1152]{1,0:T(8,128)(2,1)S(1)} %copy-done), kind=kOutput, calls=%fused_computation.2 | convolution fusion | flops 906264576 | bytes 4915200 | tf_op jit(solution)/shard_map/dot_general | solution.py:320
  41.9 12.1 %collective-permute-done.1 = bf16[2,128,1536]{2,1,0:T(8,128)(2,1)S(1)} collective-permute-done((bf16[2,128,1536]{2,1,0:T(8,128)(2,1)}, bf16[2,128,1536]{2,1,0:T(8,128)(2,1)S(1)}, u32[]{:S(2)}, u32[]{:S(2)}) %collective-permute-start.1) | collective-permute-done | bytes 786464 | tf_op jit(solution)/shard_map/ppermute | solution.py:49
  54.0 1.5 collective-permute-start.2
  55.5 1.2 convolution_convert_fusion.4
  56.7 2.3 %convolution_convert_fusion.3 = bf16[256,1152]{1,0:T(8,128)(2,1)S(1)} fusion(bf16[256,1536]{1,0:T(8,128)(2,1)} %bitcast.3, bf16[1536,1152]{1,0:T(8,128)(2,1)S(1)} %copy-done), kind=kOutput, calls=%fused_computation.4 | convolution fusion | flops 906264576 | bytes 4915200 | tf_op jit(solution)/shard_map/dot_general | solution.py:320
  59.1 1.2 convolution_convert_fusion.5
  60.3 12.1 %collective-permute-done.2 = bf16[2,128,1536]{2,1,0:T(8,128)(2,1)S(1)} collective-permute-done((bf16[2,128,1536]{2,1,0:T(8,128)(2,1)S(1)}, bf16[2,128,1536]{2,1,0:T(8,128)(2,1)S(1)}, u32[]{:S(2)}, u32[]{:S(2)}) %collective-permute-start.2) | collective-permute-done | bytes 786464 | tf_op jit(solution)/shard_map/ppermute | solution.py:49
  72.4 1.3 select_select_fusion.2
  74.0 1.8 %pad_maximum_fusion.2 = bf16[8,128,1152]{2,1,0:T(8,128)(2,1)} fusion(bf16[2,128,1152]{2,1,0:T(8,128)(2,1)S(1)} %bitcast.88, bf16[2,128,1152]{2,1,0:T(8,128)(2,1)S(1)} %bitcast.80, bf16[2,128,1152]{2,1,0:T(8,128)(2,1)S(1)} %bitcast.87, bf16[2,128,1152]{2,1,0:T(8,128)(2,1)S(1)} %bitcast.79), kind=kLoop, calls=%fused_computation.10 | loop fusion | flops 3538944 | bytes 4718592 | tf_op jit(solution)/shard_map/concatenate | solution.py:62
  75.9 4.6 %all-to-all-start = ((bf16[8,128,1152]{2,1,0:T(8,128)(2,1)}), bf16[8,128,1152]{2,1,0:T(8,128)(2,1)}, u32[]{:S(2)}, u32[]{:S(2)}) async-start(bf16[8,128,1152]{2,1,0:T(8,128)(2,1)} %pad_maximum_fusion.2), calls=%async_computation | async-start | bytes 4718592 | tf_op jit(solution)/shard_map/all_to_all | solution.py:331
  80.6 1.8 %copy.32 = f32[4,129,48]{1,2,0:T(8,128)} copy(f32[4,129,48]{2,1,0:T(8,128)} %pad_maximum_fusion.7) | data formatting | bytes 198144 | tf_op jit(solution)/shard_map/optimization_barrier | solution.py:328
  82.4 15.5 %all-gather = f32[32,129,48]{1,2,0:T(8,128)} all-gather(f32[4,129,48]{1,2,0:T(8,128)} %copy.32), channel_id=2, replica_groups=mesh['groups'=2,'seq'=4,'fsdp'=4] {'groups','seq'}, dimensions={0}, use_global_device_ids=true | all-gather | bytes 891648 | tf_op jit(solution)/shard_map/all_gather | solution.py:329
  97.9 3.6 %copy.33 = f32[129,4,8,48]{3,2,1,0:T(8,128)} copy(f32[129,4,8,48]{0,3,1,2:T(8,128)} %bitcast.78) | data formatting | bytes 1585152 | tf_op jit(solution)/shard_map/transpose | solution.py:330
  101.5 3.6 %reshape.283.refs_2_ = f32[129,1536]{1,0:T(8,128)} reshape(f32[129,4,8,48]{3,2,1,0:T(8,128)} %copy.33) | data formatting | bytes 1585152 | tf_op jit(solution)/shard_map/reshape | solution.py:330
  105.1 25.8 %all-to-all-done = bf16[8,128,1152]{2,1,0:T(8,128)(2,1)} async-done(((bf16[8,128,1152]{2,1,0:T(8,128)(2,1)}), bf16[8,128,1152]{2,1,0:T(8,128)(2,1)}, u32[]{:S(2)}, u32[]{:S(2)}) %all-to-all-start) | async-done | bytes 2359328 | tf_op jit(solution)/shard_map/all_to_all | solution.py:331
  130.9 1.9 %copy.36 = bf16[4,2,16,8,1152]{4,3,0,2,1:T(8,128)(2,1)S(1)} copy(bf16[4,2,16,8,1152]{4,3,2,1,0:T(8,128)(2,1)} %bitcast.32) | data formatting | bytes 4718592 | tf_op jit(solution)/shard_map/all_to_all | solution.py:331
  132.9 1.3 collective-permute-start.10
  134.2 3.3 %collective-permute-start.9 = (bf16[2,1,4608]{2,1,0:T(2,128)(2,1)S(1)}, bf16[2,1,4608]{2,1,0:T(2,128)(2,1)S(1)}, u32[]{:S(2)}, u32[]{:S(2)}) collective-permute-start(bf16[2,1,4608]{2,1,0:T(2,128)(2,1)S(1)} %get-tuple-element.34), channel_id=1, source_target_pairs={{0,4},{4,8},{8,12},{1,5},{5,9},{9,13},{2,6},{6,10},{10,14},{3,7},{... | collective-permute-start | bytes 55304 | tf_op jit(solution)/shard_map/ppermute | solution.py:19
  137.7 0.5 collective-permute-done.9
  138.1 1.9 %multiply_add_fusion = f32[2,128,4608]{2,1,0:T(8,128)S(1)} fusion(bf16[2,128,4608]{2,1,0:T(8,128)(2,1)S(1)} %bitcast.77, bf16[2,1,4608]{2,1,0:T(2,128)(2,1)S(1)} %collective-permute-done.10, bf16[2,1,4608]{2,1,0:T(2,128)(2,1)S(1)} %collective-permute-done.9, f32[4608]{0:T(1024)S(1)} %get-tuple-element.20, f32[4608]{0:T(1024)S(1)} %get-tuple-element.21, ...), kind=kLoop, calls=%fused_computation | loop fusion | flops 16515072 | bytes 7170048 | tf_op jit(solution)/shard_map/add | solution.py:335
  140.4 1.4 collective-permute-start.12
  141.8 2.3 %collective-permute-start.11 = (bf16[2,128,1536]{2,1,0:T(8,128)(2,1)S(1)}, bf16[2,128,1536]{2,1,0:T(8,128)(2,1)S(1)}, u32[]{:S(2)}, u32[]{:S(2)}) collective-permute-start(bf16[2,128,1536]{2,1,0:T(8,128)(2,1)S(1)} %get-tuple-element.29.refs_5_), channel_id=1, source_target_pairs={{0,8},{4,12},{8,0},{12,4},{1,9},{5,13},{9,1},{13,5},{2,10},{6,14},... | collective-permute-start | bytes 2359304 | tf_op jit(solution)/shard_map/ppermute | solution.py:351
  144.4 4.5 %shard_map.130.refs_3_ = f32[2,256,1536]{2,1,0:T(8,128)S(1)} custom-call(bf16[2,2,128,1536]{3,2,1,0:T(8,128)(2,1)S(1)} %pad_maximum_fusion.3.refs_0_, bf16[2,256,384]{2,1,0:T(8,128)(2,1)S(1)} %pad_maximum_fusion.6.refs_1_, f32[129,1536]{1,0:T(8,128)S(1)} %copy-done.1, bf16[256,256]{1,0:T(8,128)(2,1)S(1)} %copy-done.3), custom_call_target="tpu_custom_call" | custom-call | tf_op jit(solution)/shard_map/pallas_call | solution.py:261
  148.8 13.4 %collective-permute-done.11 = bf16[2,128,1536]{2,1,0:T(8,128)(2,1)S(1)} collective-permute-done((bf16[2,128,1536]{2,1,0:T(8,128)(2,1)S(1)}, bf16[2,128,1536]{2,1,0:T(8,128)(2,1)S(1)}, u32[]{:S(2)}, u32[]{:S(2)}) %collective-permute-start.11) | collective-permute-done | bytes 786464 | tf_op jit(solution)/shard_map/ppermute | solution.py:351
  162.3 2.6 %fusion.2.refs_1_ = f32[2,256,1536]{2,1,0:T(8,128)} fusion(bf16[128,1536]{1,0:T(8,128)(2,1)S(1)} %get-tuple-element.25, bf16[128,1536]{1,0:T(8,128)(2,1)S(1)} %get-tuple-element.24, bf16[2,256,128]{2,1,0:T(8,128)(2,1)S(1)} %get-tuple-element.22, bf16[2,256,128]{2,1,0:T(8,128)(2,1)S(1)} %get-tuple-element.23), kind=kOutput, calls=%fused_computation.18 | convolution fusion | flops 608698368 | bytes 4194304 | tf_op jit(solution)/shard_map/bgk,kd->bgd/dot_general | solution.py:233
  165.0 0.8 copy-done.4
  165.8 8.1 %shard_map.131 = bf16[2,128,1536]{2,1,0:T(8,128)(2,1)} custom-call(bf16[2,2,128,1536]{3,2,1,0:T(8,128)(2,1)S(1)} %pad_maximum_fusion.4.refs_0_, f32[2,256,1536]{2,1,0:T(8,128)} %fusion.2.refs_1_, f32[129,1536]{1,0:T(8,128)S(1)} %copy-done.1, f32[2,256,1536]{2,1,0:T(8,128)} %copy-done.2, f32[2,128,1536]{2,1,0:T(8,128)S(1)} %get-tuple-element.28.refs_4_, ...), custom_call_target="tpu_custom_call" | custom-call | tf_op jit(solution)/shard_map/pallas_call | solution.py:261
  (54 shorter events, 1.9 us)
Async XLA Ops:
  0.0 21.9 %copy-start = (bf16[1536,1152]{1,0:T(8,128)(2,1)S(1)}, bf16[1536,1152]{1,0:T(8,128)(2,1)}, u32[]{:S(2)}) copy-start(bf16[1536,1152]{1,0:T(8,128)(2,1)} %param.14) | copy-start | bytes 10616836
  0.0 24.5 %collective-permute-start.3 = (bf16[2,128,1536]{2,1,0:T(8,128)(2,1)}, bf16[2,128,1536]{2,1,0:T(8,128)(2,1)}, u32[]{:S(2)}, u32[]{:S(2)}) collective-permute-start(bf16[2,128,1536]{2,1,0:T(8,128)(2,1)} %param.13), channel_id=1, source_target_pairs={{0,1},{1,2},{2,3},{4,5},{5,6},{6,7},{8,9},{9,10},{10,11},{12,13},{... | collective-permute-start | bytes 2359304 | tf_op jit(solution)/shard_map/ppermute | solution.py:48
  6.1 28.4 %collective-permute-start = (bf16[2,128,1536]{2,1,0:T(8,128)(2,1)}, bf16[2,128,1536]{2,1,0:T(8,128)(2,1)}, u32[]{:S(2)}, u32[]{:S(2)}) collective-permute-start(bf16[2,128,1536]{2,1,0:T(8,128)(2,1)} %param.13), channel_id=1, source_target_pairs={{1,0},{2,1},{3,2},{5,4},{6,5},{7,6},{9,8},{10,9},{11,10},{13,12},{... | collective-permute-start | bytes 2359304 | tf_op jit(solution)/shard_map/ppermute | solution.py:49
  9.7 19.8 %collective-permute-start.6 = (f32[129,48]{1,0:T(8,128)}, f32[129,48]{1,0:T(8,128)}, u32[]{:S(2)}, u32[]{:S(2)}) collective-permute-start(f32[129,48]{1,0:T(8,128)} %fusion.29), channel_id=1, source_target_pairs={{0,3},{1,0},{2,1},{3,2},{4,7},{5,4},{6,5},{7,6},{8,11},{9,8},{10,9... | collective-permute-start | bytes 74312 | tf_op jit(solution)/shard_map/ppermute | solution.py:69
  14.4 19.0 %collective-permute-start.7 = (f32[129,48]{1,0:T(8,128)}, f32[129,48]{1,0:T(8,128)}, u32[]{:S(2)}, u32[]{:S(2)}) collective-permute-start(f32[129,48]{1,0:T(8,128)} %fusion.29), channel_id=1, source_target_pairs={{0,2},{1,3},{2,0},{3,1},{4,6},{5,7},{6,4},{7,5},{8,10},{9,11},{10,... | collective-permute-start | bytes 74312 | tf_op jit(solution)/shard_map/ppermute | solution.py:69
  14.4 19.0 %collective-permute-start.8 = (f32[129,48]{1,0:T(8,128)}, f32[129,48]{1,0:T(8,128)}, u32[]{:S(2)}, u32[]{:S(2)}) collective-permute-start(f32[129,48]{1,0:T(8,128)} %fusion.29), channel_id=1, source_target_pairs={{0,1},{1,2},{2,3},{3,0},{4,5},{5,6},{6,7},{7,4},{8,9},{9,10},{10,1... | collective-permute-start | bytes 74312 | tf_op jit(solution)/shard_map/ppermute | solution.py:69
  16.1 5.7 %copy-start.8 = (bf16[2,128,1536]{2,1,0:T(8,128)(2,1)S(1)}, bf16[2,128,1536]{2,1,0:T(8,128)(2,1)}, u32[]{:S(2)}) copy-start(bf16[2,128,1536]{2,1,0:T(8,128)(2,1)} %param.13) | copy-start | bytes 2359300
  24.5 14.4 %collective-permute-start.4 = (bf16[2,128,1536]{2,1,0:T(8,128)(2,1)}, bf16[2,128,1536]{2,1,0:T(8,128)(2,1)}, u32[]{:S(2)}, u32[]{:S(2)}) collective-permute-start(bf16[2,128,1536]{2,1,0:T(8,128)(2,1)} %collective-permute-done.3), channel_id=1, source_target_pairs={{1,2},{2,3},{5,6},{6,7},{9,10},{10,11},{13,14},{14,15},{17,18},{18... | collective-permute-start | bytes 2359304 | tf_op jit(solution)/shard_map/ppermute | solution.py:48
  34.5 19.5 %collective-permute-start.1 = (bf16[2,128,1536]{2,1,0:T(8,128)(2,1)}, bf16[2,128,1536]{2,1,0:T(8,128)(2,1)S(1)}, u32[]{:S(2)}, u32[]{:S(2)}) collective-permute-start(bf16[2,128,1536]{2,1,0:T(8,128)(2,1)} %collective-permute-done), channel_id=1, source_target_pairs={{1,0},{2,1},{5,4},{6,5},{9,8},{10,9},{13,12},{14,13},{17,16},{18,1... | collective-permute-start | bytes 2359304 | tf_op jit(solution)/shard_map/ppermute | solution.py:49
  38.9 20.1 %collective-permute-start.5 = (bf16[2,128,1536]{2,1,0:T(8,128)(2,1)}, bf16[2,128,1536]{2,1,0:T(8,128)(2,1)S(1)}, u32[]{:S(2)}, u32[]{:S(2)}) collective-permute-start(bf16[2,128,1536]{2,1,0:T(8,128)(2,1)} %collective-permute-done.4), channel_id=1, source_target_pairs={{2,3},{6,7},{10,11},{14,15},{18,19},{22,23},{26,27},{30,31}} | collective-permute-start | bytes 2359304 | tf_op jit(solution)/shard_map/ppermute | solution.py:48
  54.0 18.4 %collective-permute-start.2 = (bf16[2,128,1536]{2,1,0:T(8,128)(2,1)S(1)}, bf16[2,128,1536]{2,1,0:T(8,128)(2,1)S(1)}, u32[]{:S(2)}, u32[]{:S(2)}) collective-permute-start(bf16[2,128,1536]{2,1,0:T(8,128)(2,1)S(1)} %collective-permute-done.1), channel_id=1, source_target_pairs={{1,0},{5,4},{9,8},{13,12},{17,16},{21,20},{25,24},{29,28}} | collective-permute-start | bytes 2359304 | tf_op jit(solution)/shard_map/ppermute | solution.py:49
  59.1 13.4 %copy-start.6 = (bf16[256,1152]{1,0:T(8,128)(2,1)S(1)}, bf16[256,1152]{1,0:T(8,128)(2,1)}, u32[]{:S(2)}) copy-start(bf16[256,1152]{1,0:T(8,128)(2,1)} %convolution_convert_fusion) | copy-start | bytes 1769476
  75.9 4.6 %copy-start.9 = (s32[2,1]{0,1:T(1,128)S(1)}, s32[2,1]{0,1:T(1,128)}, u32[]{:S(2)}) copy-start(s32[2,1]{0,1:T(1,128)} %param.22) | copy-start | bytes 28
  75.9 55.1 %all-to-all-start = ((bf16[8,128,1152]{2,1,0:T(8,128)(2,1)}), bf16[8,128,1152]{2,1,0:T(8,128)(2,1)}, u32[]{:S(2)}, u32[]{:S(2)}) async-start(bf16[8,128,1152]{2,1,0:T(8,128)(2,1)} %pad_maximum_fusion.2), calls=%async_computation | async-start | bytes 4718592 | tf_op jit(solution)/shard_map/all_to_all | solution.py:331
  130.9 6.6 %copy-start.7 = (f32[3,4608]{1,0:T(4,128)S(1)}, f32[3,4608]{1,0:T(4,128)}, u32[]{:S(2)}) copy-start(f32[3,4608]{1,0:T(4,128)} %param.15) | copy-start | bytes 165892
  132.9 4.7 %collective-permute-start.10 = (bf16[2,1,4608]{2,1,0:T(2,128)(2,1)S(1)}, bf16[2,1,4608]{2,1,0:T(2,128)(2,1)S(1)}, u32[]{:S(2)}, u32[]{:S(2)}) collective-permute-start(bf16[2,1,4608]{2,1,0:T(2,128)(2,1)S(1)} %get-tuple-element.35), channel_id=1, source_target_pairs={{4,0},{8,4},{12,8},{5,1},{9,5},{13,9},{6,2},{10,6},{14,10},{7,3},{... | collective-permute-start | bytes 55304 | tf_op jit(solution)/shard_map/ppermute | solution.py:21
  134.2 3.9 %collective-permute-start.9 = (bf16[2,1,4608]{2,1,0:T(2,128)(2,1)S(1)}, bf16[2,1,4608]{2,1,0:T(2,128)(2,1)S(1)}, u32[]{:S(2)}, u32[]{:S(2)}) collective-permute-start(bf16[2,1,4608]{2,1,0:T(2,128)(2,1)S(1)} %get-tuple-element.34), channel_id=1, source_target_pairs={{0,4},{4,8},{8,12},{1,5},{5,9},{9,13},{2,6},{6,10},{10,14},{3,7},{... | collective-permute-start | bytes 55304 | tf_op jit(solution)/shard_map/ppermute | solution.py:19
  140.1 4.0 %copy-start.5 = (f32[4,256,128]{2,1,0:T(8,128)S(1)}, f32[4,256,128]{2,1,0:T(8,128)}, u32[]{:S(2)}) copy-start(f32[4,256,128]{2,1,0:T(8,128)} %convolution_bitcast_fusion) | copy-start | bytes 1572868
  140.4 4.0 %copy-start.1 = (f32[129,1536]{1,0:T(8,128)S(1)}, f32[129,1536]{1,0:T(8,128)}, u32[]{:S(2)}) copy-start(f32[129,1536]{1,0:T(8,128)} %reshape.283.refs_2_) | copy-start | bytes 2377732
  140.4 4.0 %copy-start.3 = (bf16[256,256]{1,0:T(8,128)(2,1)S(1)}, bf16[256,256]{1,0:T(8,128)(2,1)}, u32[]{:S(2)}) copy-start(bf16[256,256]{1,0:T(8,128)(2,1)} %constant.166.clone.refs_3_.refs_6_) | copy-start | bytes 393220
  140.4 3.8 %collective-permute-start.12 = (bf16[2,128,1536]{2,1,0:T(8,128)(2,1)S(1)}, bf16[2,128,1536]{2,1,0:T(8,128)(2,1)S(1)}, u32[]{:S(2)}, u32[]{:S(2)}) collective-permute-start(bf16[2,128,1536]{2,1,0:T(8,128)(2,1)S(1)} %get-tuple-element.29.refs_5_), channel_id=1, source_target_pairs={{0,4},{4,0},{8,12},{12,8},{1,5},{5,1},{9,13},{13,9},{2,6},{6,2},{1... | collective-permute-start | bytes 2359304 | tf_op jit(solution)/shard_map/ppermute | solution.py:347
  141.8 20.4 %collective-permute-start.11 = (bf16[2,128,1536]{2,1,0:T(8,128)(2,1)S(1)}, bf16[2,128,1536]{2,1,0:T(8,128)(2,1)S(1)}, u32[]{:S(2)}, u32[]{:S(2)}) collective-permute-start(bf16[2,128,1536]{2,1,0:T(8,128)(2,1)S(1)} %get-tuple-element.29.refs_5_), channel_id=1, source_target_pairs={{0,8},{4,12},{8,0},{12,4},{1,9},{5,13},{9,1},{13,5},{2,10},{6,14},... | collective-permute-start | bytes 2359304 | tf_op jit(solution)/shard_map/ppermute | solution.py:351
  148.8 16.0 %copy-start.2 = (f32[2,256,1536]{2,1,0:T(8,128)}, f32[2,256,1536]{2,1,0:T(8,128)S(1)}, u32[]{:S(2)}) copy-start(f32[2,256,1536]{2,1,0:T(8,128)S(1)} %shard_map.130.refs_3_) | copy-start | bytes 9437188
  162.2 2.7 %collective-permute-start.13 = (bf16[1,2,128,1536]{3,2,1,0:T(8,128)(2,1)S(1)}, bf16[1,2,128,1536]{3,2,1,0:T(8,128)(2,1)S(1)}, u32[]{:S(2)}, u32[]{:S(2)}) collective-permute-start(bf16[1,2,128,1536]{3,2,1,0:T(8,128)(2,1)S(1)} %bitcast.82), channel_id=1, source_target_pairs={{0,4},{4,0},{8,12},{12,8},{1,5},{5,1},{9,13},{13,9},{2,6},{6,2},{1... | collective-permute-start | bytes 2359304 | tf_op jit(solution)/shard_map/ppermute | solution.py:359
  164.9 0.9 copy-start.4

commit v22 on v20

--- a/solution.py
+++ b/solution.py
@@ -59,7 +59,7 @@
             chunk = jnp.where(own - step == target, from_left[step - 1], chunk)
             chunk = jnp.where(own + step == target, from_right[step - 1], chunk)
         chunks.append(chunk)
-    return jnp.concatenate(chunks, axis=0)
+    return jnp.stack(chunks)
 
 
 def permute_gather(values, axis, count, own):
@@ -319,7 +319,7 @@
     partial, basis_spec, across = lax.optimization_barrier((partial, basis_spec, across))
     gathered = lax.all_gather(across, ("groups", "seq"), axis=0, tiled=False)
     gathered = jnp.transpose(gathered, (2, 1, 0, 3)).reshape(params.shape[0], width)
-    projected = lax.all_to_all(partial, "fsdp", 0, 2, tiled=True)
+    projected = lax.all_to_all(partial, "fsdp", 0, 3, tiled=True)[0]
     projected, gathered = lax.optimization_barrier((projected, gathered))
     padded = padded_2(projected, (("seq", 1),), 1)
     shorted = (

time: 174 us -> 185 us (1.063)
  local copies, waits for them, and re-layouts: 14.1 us -> 23.4 us
  other arithmetic: 9.86 us -> 12.5 us
    squeeze x0 -> x1, local copies, waits for them, and re-layouts: none -> 4.3 us  [shards(): projected = lax.all_to_all(partial, 'fsdp', 0, 3, tiled=True)[0]]
    all_to_all x1, local copies, waits for them, and re-layouts: 1.93 us -> 4.92 us  [shards(): projected = lax.all_to_all(partial, 'fsdp', 0, 3, tiled=True)[0]]
    add x1, other arithmetic: 1.93 us -> 4.61 us  [shards(): short_weight[0] * padded[:, :-2] + short_weight[1] * padded[:, 1:-1]]
  transfers between devices with their start and end apart: 15 -> 15, of which waited for: 8 -> 7; matrix products, arithmetic and copies ran while one was open for 20% -> 19% of each run, Pallas kernels for 3% -> 2%
where the time goes in v22:
time: 185 us; the launch traced here: 184 us
  waiting for transfers between devices  68.7 us (37%)
  starting transfers between devices  30 us (16%)
  local copies, waits for them, and re-layouts  23.4 us (13%)
  matrix products  19.3 us (10%)
  blocking collectives  15.5 us (8%)
  Pallas kernels  12.7 us (7%)
  other arithmetic  12.5 us (7%)
    all_to_all x1, waiting for transfers between devices, shards(): projected = lax.all_to_all(partial, 'fsdp', 0, 3, tiled=True)[0]  25.8 us
    ppermute x3, waiting for transfers between devices, relay_gather(): lax.ppermute(leftward, axis, [(j, j - 1) for j in range(1, count - step +...  24.3 us
    all_gather x1, blocking collectives, shards(): gathered = lax.all_gather(across, ('groups', 'seq'), axis=0, tiled=False)  15.5 us
    dot_general x7, matrix products, project(): jnp.dot(block.reshape(seq_dev * block_len, width), in_weight, preferred_e...  13.8 us
    pallas_call x2, Pallas kernels, fused_conv(): pl.pallas_call(conv_body(finish), grid=(width // lanes,), in_specs=specs,...  12.7 us
    ppermute x1, waiting for transfers between devices, shards(): lax.ppermute(carried, 'seq', [(i, (i + 2 * shift) % seq_count) for i in r...  11.7 us
    ppermute x3, starting transfers between devices, relay_gather(): lax.ppermute(rightward, axis, [(j, j + 1) for j in range(step - 1, count...  8.35 us
    ppermute x3, starting transfers between devices, permute_gather(): lax.ppermute(values, axis, [(i, (i + shift) % count) for i in range(count)])  5.28 us
  transfers between devices with their start and end apart: 15, of which 7 were waited for; matrix products, arithmetic and copies ran while one was open for 19% of the time, Pallas kernels for 2%

profile of v22, /device:TPU:0, one launch (start us, length us, event | category | flops | bytes accessed | tf_op | source)
XLA Modules:
  0.0 183.9 jit_solution(16219424218102561881)
XLA Ops:
  0.0 6.1 %collective-permute-start.3 = (bf16[2,128,1536]{2,1,0:T(8,128)(2,1)}, bf16[2,128,1536]{2,1,0:T(8,128)(2,1)}, u32[]{:S(2)}, u32[]{:S(2)}) collective-permute-start(bf16[2,128,1536]{2,1,0:T(8,128)(2,1)} %param.13), channel_id=1, source_target_pairs={{0,1},{1,2},{2,3},{4,5},{5,6},{6,7},{8,9},{9,10},{10,11},{12,13},{... | collective-permute-start | bytes 2359304 | tf_op jit(solution)/shard_map/ppermute | solution.py:48
  6.1 1.3 collective-permute-start
  7.4 0.7 broadcast_in_dim.24
  8.1 1.6 fusion.19
  9.7 4.7 %collective-permute-start.6 = (f32[129,48]{1,0:T(8,128)}, f32[129,48]{1,0:T(8,128)}, u32[]{:S(2)}, u32[]{:S(2)}) collective-permute-start(f32[129,48]{1,0:T(8,128)} %fusion.19), channel_id=1, source_target_pairs={{0,3},{1,0},{2,1},{3,2},{4,7},{5,4},{6,5},{7,6},{8,11},{9,8},{10,9... | collective-permute-start | bytes 74312 | tf_op jit(solution)/shard_map/ppermute | solution.py:69
  14.4 0.6 collective-permute-start.8
  15.0 0.6 fusion.43
  17.9 2.0 %fusion.3 = f32[1024,64]{0,1:T(8,128)S(1)} fusion(f32[17,64]{1,0:T(8,128)} %param.16, f32[64]{0:T(128)} %param.17, f32[1024,8]{0,1:T(8,128)S(1)} %get-tuple-element.43, f32[1024,8]{0,1:T(8,128)S(1)} %get-tuple-element.42, f32[1024,1]{0,1:T(1,128)S(1)} %bitcast.84), kind=kOutput, calls=%fused_computation.20 | convolution fusion | flops 13469696 | bytes 336384 | tf_op jit(solution)/shard_map/dot_general | solution.py:92
  19.9 2.0 %broadcast_multiply_fusion.1 = (f32[1024,64]{0,1:T(8,128)S(1)}, f32[1024,64]{0,1:T(8,128)S(1)}) fusion(f32[1024]{0:T(1024)S(1)} %bitcast.83, f32[1024]{0:T(1024)S(1)} %broadcast_subtract_fusion, f32[64]{0:T(128)} %param.19, f32[1024,64]{0,1:T(8,128)S(1)} %fusion.3, f32[64,64]{1,0:T(8,128)} %param.18), kind=kOutput, calls=%fused_computation.50 | convolution fusion | flops 50528256 | bytes 811264 | tf_op jit(solution)/shard_map/dot_general | solution.py:93
  22.0 3.1 %convolution_convert_fusion = bf16[256,1152]{1,0:T(8,128)(2,1)} fusion(bf16[256,1536]{1,0:T(8,128)(2,1)} %bitcast.86, bf16[1536,1152]{1,0:T(8,128)(2,1)S(1)} %copy-done), kind=kOutput, calls=%fused_computation.1 | convolution fusion | flops 906264576 | bytes 4915200 | tf_op jit(solution)/shard_map/dot_general | solution.py:311
  25.7 1.6 collective-permute-start.4
  27.3 1.5 convolution_bitcast_fusion
  28.8 0.7 collective-permute-done.6
  29.5 3.9 %collective-permute-done.7 = f32[129,48]{1,0:T(8,128)} collective-permute-done((f32[129,48]{1,0:T(8,128)}, f32[129,48]{1,0:T(8,128)}, u32[]{:S(2)}, u32[]{:S(2)}) %collective-permute-start.7) | collective-permute-done | bytes 24800 | tf_op jit(solution)/shard_map/ppermute | solution.py:69
  33.4 1.1 select_bitcast_fusion.3
  34.5 1.3 collective-permute-start.1
  35.8 0.7 pad_maximum_fusion.8
  36.6 2.3 %convolution_convert_fusion.1 = bf16[256,1152]{1,0:T(8,128)(2,1)S(1)} fusion(bf16[256,1536]{1,0:T(8,128)(2,1)} %bitcast.5, bf16[1536,1152]{1,0:T(8,128)(2,1)S(1)} %copy-done), kind=kOutput, calls=%fused_computation.2 | convolution fusion | flops 906264576 | bytes 4915200 | tf_op jit(solution)/shard_map/dot_general | solution.py:311
  38.9 0.7 collective-permute-start.5
  39.6 2.3 %convolution_convert_fusion.2 = bf16[256,1152]{1,0:T(8,128)(2,1)S(1)} fusion(bf16[256,1536]{1,0:T(8,128)(2,1)} %bitcast.4, bf16[1536,1152]{1,0:T(8,128)(2,1)S(1)} %copy-done), kind=kOutput, calls=%fused_computation.3 | convolution fusion | flops 906264576 | bytes 4915200 | tf_op jit(solution)/shard_map/dot_general | solution.py:311
  41.9 12.1 %collective-permute-done.1 = bf16[2,128,1536]{2,1,0:T(8,128)(2,1)S(1)} collective-permute-done((bf16[2,128,1536]{2,1,0:T(8,128)(2,1)}, bf16[2,128,1536]{2,1,0:T(8,128)(2,1)S(1)}, u32[]{:S(2)}, u32[]{:S(2)}) %collective-permute-start.1) | collective-permute-done | bytes 786464 | tf_op jit(solution)/shard_map/ppermute | solution.py:49
  54.0 1.5 collective-permute-start.2
  55.5 2.3 %convolution_convert_fusion.3 = bf16[256,1152]{1,0:T(8,128)(2,1)S(1)} fusion(bf16[256,1536]{1,0:T(8,128)(2,1)} %bitcast.3, bf16[1536,1152]{1,0:T(8,128)(2,1)S(1)} %copy-done), kind=kOutput, calls=%fused_computation.4 | convolution fusion | flops 906264576 | bytes 4915200 | tf_op jit(solution)/shard_map/dot_general | solution.py:311
  57.8 1.2 convolution_convert_fusion.4
  59.0 1.2 convolution_convert_fusion.5
  60.2 12.2 %collective-permute-done.2 = bf16[2,128,1536]{2,1,0:T(8,128)(2,1)S(1)} collective-permute-done((bf16[2,128,1536]{2,1,0:T(8,128)(2,1)S(1)}, bf16[2,128,1536]{2,1,0:T(8,128)(2,1)S(1)}, u32[]{:S(2)}, u32[]{:S(2)}) %collective-permute-start.2) | collective-permute-done | bytes 786464 | tf_op jit(solution)/shard_map/ppermute | solution.py:49
  72.4 1.3 select_select_fusion.2
  74.1 1.8 pad_maximum_fusion.2
  75.9 4.7 %all-to-all-start = ((bf16[4,2,128,1152]{3,2,1,0:T(8,128)(2,1)}), bf16[4,2,128,1152]{3,2,1,0:T(8,128)(2,1)}, u32[]{:S(2)}, u32[]{:S(2)}) async-start(bf16[4,2,128,1152]{3,2,1,0:T(8,128)(2,1)} %pad_maximum_fusion.2), calls=%async_computation | async-start | bytes 4718592 | tf_op jit(solution)/shard_map/all_to_all | solution.py:322
  80.6 1.8 copy.42
  82.4 15.5 %all-gather = f32[32,129,48]{1,2,0:T(8,128)} all-gather(f32[4,129,48]{1,2,0:T(8,128)} %copy.42), channel_id=2, replica_groups=mesh['groups'=2,'seq'=4,'fsdp'=4] {'groups','seq'}, dimensions={0}, use_global_device_ids=true | all-gather | bytes 891648 | tf_op jit(solution)/shard_map/all_gather | solution.py:320
  98.0 3.6 %copy.43 = f32[129,4,8,48]{3,2,1,0:T(8,128)} copy(f32[129,4,8,48]{0,3,1,2:T(8,128)} %bitcast.71) | data formatting | bytes 1585152 | tf_op jit(solution)/shard_map/transpose | solution.py:321
  101.6 3.6 %reshape.552.refs_2_ = f32[129,1536]{1,0:T(8,128)} reshape(f32[129,4,8,48]{3,2,1,0:T(8,128)} %copy.43) | data formatting | bytes 1585152 | tf_op jit(solution)/shard_map/reshape | solution.py:321
  105.2 25.8 %all-to-all-done = bf16[4,2,128,1152]{3,2,1,0:T(8,128)(2,1)} async-done(((bf16[4,2,128,1152]{3,2,1,0:T(8,128)(2,1)}), bf16[4,2,128,1152]{3,2,1,0:T(8,128)(2,1)}, u32[]{:S(2)}, u32[]{:S(2)}) %all-to-all-start) | async-done | bytes 2359328 | tf_op jit(solution)/shard_map/all_to_all | solution.py:322
  131.0 4.9 %copy.41 = bf16[1,2,128,4,1152]{4,3,2,1,0:T(4,128)(2,1)} copy(bf16[1,2,128,4,1152]{4,2,1,3,0:T(8,128)(2,1)} %bitcast.20) | data formatting | bytes 4718592 | tf_op jit(solution)/shard_map/all_to_all | solution.py:322
  135.9 4.3 %squeeze.3 = bf16[2,128,4608]{2,1,0:T(8,128)(2,1)} reshape(bf16[1,2,128,4,1152]{4,3,2,1,0:T(4,128)(2,1)} %copy.41) | data formatting | bytes 4718592 | tf_op jit(solution)/shard_map/squeeze | solution.py:322
  140.2 1.0 fusion.42
  141.2 1.3 collective-permute-start.10
  142.5 3.3 %collective-permute-start.9 = (bf16[2,1,4608]{2,1,0:T(2,128)(2,1)S(1)}, bf16[2,1,4608]{2,1,0:T(2,128)(2,1)S(1)}, u32[]{:S(2)}, u32[]{:S(2)}) collective-permute-start(bf16[2,1,4608]{2,1,0:T(2,128)(2,1)S(1)} %get-tuple-element.32), channel_id=1, source_target_pairs={{0,4},{4,8},{8,12},{1,5},{5,9},{9,13},{2,6},{6,10},{10,14},{3,7},{... | collective-permute-start | bytes 55304 | tf_op jit(solution)/shard_map/ppermute | solution.py:19
  145.8 1.2 slice_reduce_fusion.2
  147.0 4.6 %multiply_add_fusion = f32[2,128,4608]{2,1,0:T(8,128)S(1)} fusion(bf16[2,128,4608]{2,1,0:T(8,128)(2,1)} %squeeze.3, bf16[2,1,4608]{2,1,0:T(2,128)(2,1)S(1)} %collective-permute-done.10, bf16[2,1,4608]{2,1,0:T(2,128)(2,1)S(1)} %collective-permute-done.9, f32[4608]{0:T(1024)S(1)} %get-tuple-element.20, f32[4608]{0:T(1024)S(1)} %get-tuple-element.21, ...), kind=kLoop, calls=%fused_computation | loop fusion | flops 16515072 | bytes 7170048 | tf_op jit(solution)/shard_map/add | solution.py:326
  151.9 1.2 collective-permute-start.12
  153.1 1.9 %collective-permute-start.11 = (bf16[2,128,1536]{2,1,0:T(8,128)(2,1)S(1)}, bf16[2,128,1536]{2,1,0:T(8,128)(2,1)S(1)}, u32[]{:S(2)}, u32[]{:S(2)}) collective-permute-start(bf16[2,128,1536]{2,1,0:T(8,128)(2,1)S(1)} %get-tuple-element.27.refs_5_), channel_id=1, source_target_pairs={{0,8},{4,12},{8,0},{12,4},{1,9},{5,13},{9,1},{13,5},{2,10},{6,14},... | collective-permute-start | bytes 2359304 | tf_op jit(solution)/shard_map/ppermute | solution.py:342
  155.3 4.4 %shard_map.130.refs_3_ = f32[2,256,1536]{2,1,0:T(8,128)S(1)} custom-call(bf16[2,2,128,1536]{3,2,1,0:T(8,128)(2,1)S(1)} %pad_maximum_fusion.3.refs_0_, bf16[2,256,384]{2,1,0:T(8,128)(2,1)S(1)} %pad_maximum_fusion.6.refs_1_, f32[129,1536]{1,0:T(8,128)S(1)} %copy-done.2, bf16[256,256]{1,0:T(8,128)(2,1)S(1)} %copy-done.3), custom_call_target="tpu_custom_call" | custom-call | tf_op jit(solution)/shard_map/pallas_call | solution.py:252
  159.8 1.6 copy-done.1
  161.4 11.7 %collective-permute-done.11 = bf16[2,128,1536]{2,1,0:T(8,128)(2,1)S(1)} collective-permute-done((bf16[2,128,1536]{2,1,0:T(8,128)(2,1)S(1)}, bf16[2,128,1536]{2,1,0:T(8,128)(2,1)S(1)}, u32[]{:S(2)}, u32[]{:S(2)}) %collective-permute-start.11) | collective-permute-done | bytes 786464 | tf_op jit(solution)/shard_map/ppermute | solution.py:342
  173.2 2.2 %collective-permute-done.13 = bf16[1,2,128,1536]{3,2,1,0:T(8,128)(2,1)S(1)} collective-permute-done((bf16[1,2,128,1536]{3,2,1,0:T(8,128)(2,1)S(1)}, bf16[1,2,128,1536]{3,2,1,0:T(8,128)(2,1)S(1)}, u32[]{:S(2)}, u32[]{:S(2)}) %collective-permute-start.13) | collective-permute-done | bytes 786464 | tf_op jit(solution)/shard_map/ppermute | solution.py:350
  175.6 8.3 %shard_map.131 = bf16[2,128,1536]{2,1,0:T(8,128)(2,1)} custom-call(bf16[2,2,128,1536]{3,2,1,0:T(8,128)(2,1)S(1)} %pad_maximum_fusion.4.refs_0_, bf16[2,256,384]{2,1,0:T(8,128)(2,1)S(1)} %pad_maximum_fusion.7.refs_1_, f32[129,1536]{1,0:T(8,128)S(1)} %copy-done.2, f32[2,256,1536]{2,1,0:T(8,128)} %copy-done.1, f32[2,128,1536]{2,1,0:T(8,128)S(1)} %get-tuple-element.26.refs_4_, ...), custom_call_target="tpu_custom_call" | custom-call | tf_op jit(solution)/shard_map/pallas_call | solution.py:252
  (50 shorter events, 2.7 us)
Async XLA Ops:
  0.0 22.0 %copy-start = (bf16[1536,1152]{1,0:T(8,128)(2,1)S(1)}, bf16[1536,1152]{1,0:T(8,128)(2,1)}, u32[]{:S(2)}) copy-start(bf16[1536,1152]{1,0:T(8,128)(2,1)} %param.14) | copy-start | bytes 10616836
  0.0 25.7 %collective-permute-start.3 = (bf16[2,128,1536]{2,1,0:T(8,128)(2,1)}, bf16[2,128,1536]{2,1,0:T(8,128)(2,1)}, u32[]{:S(2)}, u32[]{:S(2)}) collective-permute-start(bf16[2,128,1536]{2,1,0:T(8,128)(2,1)} %param.13), channel_id=1, source_target_pairs={{0,1},{1,2},{2,3},{4,5},{5,6},{6,7},{8,9},{9,10},{10,11},{12,13},{... | collective-permute-start | bytes 2359304 | tf_op jit(solution)/shard_map/ppermute | solution.py:48
  6.1 28.4 %collective-permute-start = (bf16[2,128,1536]{2,1,0:T(8,128)(2,1)}, bf16[2,128,1536]{2,1,0:T(8,128)(2,1)}, u32[]{:S(2)}, u32[]{:S(2)}) collective-permute-start(bf16[2,128,1536]{2,1,0:T(8,128)(2,1)} %param.13), channel_id=1, source_target_pairs={{1,0},{2,1},{3,2},{5,4},{6,5},{7,6},{9,8},{10,9},{11,10},{13,12},{... | collective-permute-start | bytes 2359304 | tf_op jit(solution)/shard_map/ppermute | solution.py:49
  9.7 19.8 %collective-permute-start.6 = (f32[129,48]{1,0:T(8,128)}, f32[129,48]{1,0:T(8,128)}, u32[]{:S(2)}, u32[]{:S(2)}) collective-permute-start(f32[129,48]{1,0:T(8,128)} %fusion.19), channel_id=1, source_target_pairs={{0,3},{1,0},{2,1},{3,2},{4,7},{5,4},{6,5},{7,6},{8,11},{9,8},{10,9... | collective-permute-start | bytes 74312 | tf_op jit(solution)/shard_map/ppermute | solution.py:69
  14.4 19.0 %collective-permute-start.7 = (f32[129,48]{1,0:T(8,128)}, f32[129,48]{1,0:T(8,128)}, u32[]{:S(2)}, u32[]{:S(2)}) collective-permute-start(f32[129,48]{1,0:T(8,128)} %fusion.19), channel_id=1, source_target_pairs={{0,2},{1,3},{2,0},{3,1},{4,6},{5,7},{6,4},{7,5},{8,10},{9,11},{10,... | collective-permute-start | bytes 74312 | tf_op jit(solution)/shard_map/ppermute | solution.py:69
  14.4 19.0 %collective-permute-start.8 = (f32[129,48]{1,0:T(8,128)}, f32[129,48]{1,0:T(8,128)}, u32[]{:S(2)}, u32[]{:S(2)}) collective-permute-start(f32[129,48]{1,0:T(8,128)} %fusion.19), channel_id=1, source_target_pairs={{0,1},{1,2},{2,3},{3,0},{4,5},{5,6},{6,7},{7,4},{8,9},{9,10},{10,1... | collective-permute-start | bytes 74312 | tf_op jit(solution)/shard_map/ppermute | solution.py:69
  25.7 13.2 %collective-permute-start.4 = (bf16[2,128,1536]{2,1,0:T(8,128)(2,1)}, bf16[2,128,1536]{2,1,0:T(8,128)(2,1)}, u32[]{:S(2)}, u32[]{:S(2)}) collective-permute-start(bf16[2,128,1536]{2,1,0:T(8,128)(2,1)} %collective-permute-done.3), channel_id=1, source_target_pairs={{1,2},{2,3},{5,6},{6,7},{9,10},{10,11},{13,14},{14,15},{17,18},{18... | collective-permute-start | bytes 2359304 | tf_op jit(solution)/shard_map/ppermute | solution.py:48
  34.5 19.5 %collective-permute-start.1 = (bf16[2,128,1536]{2,1,0:T(8,128)(2,1)}, bf16[2,128,1536]{2,1,0:T(8,128)(2,1)S(1)}, u32[]{:S(2)}, u32[]{:S(2)}) collective-permute-start(bf16[2,128,1536]{2,1,0:T(8,128)(2,1)} %collective-permute-done), channel_id=1, source_target_pairs={{1,0},{2,1},{5,4},{6,5},{9,8},{10,9},{13,12},{14,13},{17,16},{18,1... | collective-permute-start | bytes 2359304 | tf_op jit(solution)/shard_map/ppermute | solution.py:49
  38.9 20.2 %collective-permute-start.5 = (bf16[2,128,1536]{2,1,0:T(8,128)(2,1)}, bf16[2,128,1536]{2,1,0:T(8,128)(2,1)S(1)}, u32[]{:S(2)}, u32[]{:S(2)}) collective-permute-start(bf16[2,128,1536]{2,1,0:T(8,128)(2,1)} %collective-permute-done.4), channel_id=1, source_target_pairs={{2,3},{6,7},{10,11},{14,15},{18,19},{22,23},{26,27},{30,31}} | collective-permute-start | bytes 2359304 | tf_op jit(solution)/shard_map/ppermute | solution.py:48
  54.0 18.4 %collective-permute-start.2 = (bf16[2,128,1536]{2,1,0:T(8,128)(2,1)S(1)}, bf16[2,128,1536]{2,1,0:T(8,128)(2,1)S(1)}, u32[]{:S(2)}, u32[]{:S(2)}) collective-permute-start(bf16[2,128,1536]{2,1,0:T(8,128)(2,1)S(1)} %collective-permute-done.1), channel_id=1, source_target_pairs={{1,0},{5,4},{9,8},{13,12},{17,16},{21,20},{25,24},{29,28}} | collective-permute-start | bytes 2359304 | tf_op jit(solution)/shard_map/ppermute | solution.py:49
  59.0 13.4 %copy-start.6 = (bf16[256,1152]{1,0:T(8,128)(2,1)S(1)}, bf16[256,1152]{1,0:T(8,128)(2,1)}, u32[]{:S(2)}) copy-start(bf16[256,1152]{1,0:T(8,128)(2,1)} %convolution_convert_fusion) | copy-start | bytes 1769476
  75.9 4.7 %copy-start.7 = (s32[2,1]{0,1:T(1,128)S(1)}, s32[2,1]{0,1:T(1,128)}, u32[]{:S(2)}) copy-start(s32[2,1]{0,1:T(1,128)} %param.22) | copy-start | bytes 28
  75.9 55.1 %all-to-all-start = ((bf16[4,2,128,1152]{3,2,1,0:T(8,128)(2,1)}), bf16[4,2,128,1152]{3,2,1,0:T(8,128)(2,1)}, u32[]{:S(2)}, u32[]{:S(2)}) async-start(bf16[4,2,128,1152]{3,2,1,0:T(8,128)(2,1)} %pad_maximum_fusion.2), calls=%async_computation | async-start | bytes 4718592 | tf_op jit(solution)/shard_map/all_to_all | solution.py:322
  141.2 5.7 %collective-permute-start.10 = (bf16[2,1,4608]{2,1,0:T(2,128)(2,1)S(1)}, bf16[2,1,4608]{2,1,0:T(2,128)(2,1)S(1)}, u32[]{:S(2)}, u32[]{:S(2)}) collective-permute-start(bf16[2,1,4608]{2,1,0:T(2,128)(2,1)S(1)} %get-tuple-element.33), channel_id=1, source_target_pairs={{4,0},{8,4},{12,8},{5,1},{9,5},{13,9},{6,2},{10,6},{14,10},{7,3},{... | collective-permute-start | bytes 55304 | tf_op jit(solution)/shard_map/ppermute | solution.py:21
  142.5 4.4 %collective-permute-start.9 = (bf16[2,1,4608]{2,1,0:T(2,128)(2,1)S(1)}, bf16[2,1,4608]{2,1,0:T(2,128)(2,1)S(1)}, u32[]{:S(2)}, u32[]{:S(2)}) collective-permute-start(bf16[2,1,4608]{2,1,0:T(2,128)(2,1)S(1)} %get-tuple-element.32), channel_id=1, source_target_pairs={{0,4},{4,8},{8,12},{1,5},{5,9},{9,13},{2,6},{6,10},{10,14},{3,7},{... | collective-permute-start | bytes 55304 | tf_op jit(solution)/shard_map/ppermute | solution.py:19
  151.6 3.4 %copy-start.5 = (f32[4,256,128]{2,1,0:T(8,128)S(1)}, f32[4,256,128]{2,1,0:T(8,128)}, u32[]{:S(2)}) copy-start(f32[4,256,128]{2,1,0:T(8,128)} %convolution_bitcast_fusion) | copy-start | bytes 1572868
  151.9 3.4 %copy-start.2 = (f32[129,1536]{1,0:T(8,128)S(1)}, f32[129,1536]{1,0:T(8,128)}, u32[]{:S(2)}) copy-start(f32[129,1536]{1,0:T(8,128)} %reshape.552.refs_2_) | copy-start | bytes 2377732
  151.9 3.4 %copy-start.3 = (bf16[256,256]{1,0:T(8,128)(2,1)S(1)}, bf16[256,256]{1,0:T(8,128)(2,1)}, u32[]{:S(2)}) copy-start(bf16[256,256]{1,0:T(8,128)(2,1)} %constant.166.clone.refs_3_.refs_6_) | copy-start | bytes 393220
  151.9 3.2 %collective-permute-start.12 = (bf16[2,128,1536]{2,1,0:T(8,128)(2,1)S(1)}, bf16[2,128,1536]{2,1,0:T(8,128)(2,1)S(1)}, u32[]{:S(2)}, u32[]{:S(2)}) collective-permute-start(bf16[2,128,1536]{2,1,0:T(8,128)(2,1)S(1)} %get-tuple-element.27.refs_5_), channel_id=1, source_target_pairs={{0,4},{4,0},{8,12},{12,8},{1,5},{5,1},{9,13},{13,9},{2,6},{6,2},{1... | collective-permute-start | bytes 2359304 | tf_op jit(solution)/shard_map/ppermute | solution.py:338
  153.1 20.1 %collective-permute-start.11 = (bf16[2,128,1536]{2,1,0:T(8,128)(2,1)S(1)}, bf16[2,128,1536]{2,1,0:T(8,128)(2,1)S(1)}, u32[]{:S(2)}, u32[]{:S(2)}) collective-permute-start(bf16[2,128,1536]{2,1,0:T(8,128)(2,1)S(1)} %get-tuple-element.27.refs_5_), channel_id=1, source_target_pairs={{0,8},{4,12},{8,0},{12,4},{1,9},{5,13},{9,1},{13,5},{2,10},{6,14},... | collective-permute-start | bytes 2359304 | tf_op jit(solution)/shard_map/ppermute | solution.py:342
  159.8 1.6 copy-start.1
  161.4 14.2 %copy-start.4 = (bf16[128,768]{1,0:T(8,128)(2,1)S(1)}, bf16[128,768]{1,0:T(8,128)(2,1)}, u32[]{:S(2)}) copy-start(bf16[128,768]{1,0:T(8,128)(2,1)} %constant.167.clone.refs_7_) | copy-start | bytes 589828
  173.2 2.3 %collective-permute-start.13 = (bf16[1,2,128,1536]{3,2,1,0:T(8,128)(2,1)S(1)}, bf16[1,2,128,1536]{3,2,1,0:T(8,128)(2,1)S(1)}, u32[]{:S(2)}, u32[]{:S(2)}) collective-permute-start(bf16[1,2,128,1536]{3,2,1,0:T(8,128)(2,1)S(1)} %bitcast.75), channel_id=1, source_target_pairs={{0,4},{4,0},{8,12},{12,8},{1,5},{5,1},{9,13},{13,9},{2,6},{6,2},{1... | collective-permute-start | bytes 2359304 | tf_op jit(solution)/shard_map/ppermute | solution.py:350

commit v23 on v20

--- a/solution.py
+++ b/solution.py
@@ -224,7 +224,7 @@
     fwd, inv = dft_tables(rows)
     fwd = np.concatenate([fwd[0], fwd[1]], axis=1)
     inv = np.concatenate([inv[0], inv[0], inv[1]], axis=1)
-    lanes = width if block_total <= 4 or width % 768 else 768
+    lanes = width if (block_total <= 4 and not finish) or width % 768 else 768
     tile3 = lambda i: (0, 0, i)
     specs = [
         pl.BlockSpec((block_total, tables, rows, lanes), lambda i: (0, 0, 0, i)),

time: 174 us -> 174 us (level)
  transfers between devices with their start and end apart: 15 -> 15, of which waited for: 8 -> 8; matrix products, arithmetic and copies ran while one was open for 20% -> 19% of each run, Pallas kernels for 3% -> 3%
where the time goes in v23:
time: 174 us; the launch traced here: 173 us
  waiting for transfers between devices  69.3 us (40%)
  starting transfers between devices  30.5 us (18%)
  matrix products  19.3 us (11%)
  blocking collectives  15.5 us (9%)
  local copies, waits for them, and re-layouts  14.1 us (8%)
  Pallas kernels  13.1 us (8%)
  other arithmetic  9.86 us (6%)
    all_to_all x1, waiting for transfers between devices, shards(): projected = lax.all_to_all(partial, 'fsdp', 0, 2, tiled=True)  25.8 us
    ppermute x3, waiting for transfers between devices, relay_gather(): lax.ppermute(leftward, axis, [(j, j - 1) for j in range(1, count - step +...  24.3 us
    all_gather x1, blocking collectives, shards(): gathered = lax.all_gather(across, ('groups', 'seq'), axis=0, tiled=False)  15.5 us
    dot_general x7, matrix products, project(): jnp.dot(block.reshape(seq_dev * block_len, width), in_weight, preferred_e...  13.8 us
    pallas_call x2, Pallas kernels, fused_conv(): pl.pallas_call(conv_body(finish), grid=(width // lanes,), in_specs=specs,...  13.1 us
    ppermute x1, waiting for transfers between devices, shards(): lax.ppermute(carried, 'seq', [(i, (i + 2 * shift) % seq_count) for i in r...  11.7 us
    ppermute x3, starting transfers between devices, relay_gather(): lax.ppermute(rightward, axis, [(j, j + 1) for j in range(step - 1, count...  8.37 us
    ppermute x3, starting transfers between devices, permute_gather(): lax.ppermute(values, axis, [(i, (i + shift) % count) for i in range(count)])  5.26 us
  transfers between devices with their start and end apart: 15, of which 8 were waited for; matrix products, arithmetic and copies ran while one was open for 19% of the time, Pallas kernels for 3%

profile of v23, /device:TPU:0, one launch (start us, length us, event | category | flops | bytes accessed | tf_op | source)
XLA Modules:
  0.0 173.3 jit_solution(3416787055685734477)
XLA Ops:
  0.0 6.1 %collective-permute-start.3 = (bf16[2,128,1536]{2,1,0:T(8,128)(2,1)}, bf16[2,128,1536]{2,1,0:T(8,128)(2,1)}, u32[]{:S(2)}, u32[]{:S(2)}) collective-permute-start(bf16[2,128,1536]{2,1,0:T(8,128)(2,1)} %param.13), channel_id=1, source_target_pairs={{0,1},{1,2},{2,3},{4,5},{5,6},{6,7},{8,9},{9,10},{10,11},{12,13},{... | collective-permute-start | bytes 2359304 | tf_op jit(solution)/shard_map/ppermute | solution.py:48
  6.1 1.3 collective-permute-start
  7.4 0.7 broadcast_in_dim.24
  8.1 1.6 fusion.19
  9.7 4.7 %collective-permute-start.6 = (f32[129,48]{1,0:T(8,128)}, f32[129,48]{1,0:T(8,128)}, u32[]{:S(2)}, u32[]{:S(2)}) collective-permute-start(f32[129,48]{1,0:T(8,128)} %fusion.19), channel_id=1, source_target_pairs={{0,3},{1,0},{2,1},{3,2},{4,7},{5,4},{6,5},{7,6},{8,11},{9,8},{10,9... | collective-permute-start | bytes 74312 | tf_op jit(solution)/shard_map/ppermute | solution.py:69
  14.4 0.6 collective-permute-start.8
  15.0 0.6 fusion.43
  17.1 0.6 fusion.27
  17.7 2.0 %fusion.3 = f32[1024,64]{0,1:T(8,128)S(1)} fusion(f32[17,64]{1,0:T(8,128)} %param.16, f32[64]{0:T(128)} %param.17, f32[1024,8]{0,1:T(8,128)S(1)} %get-tuple-element.43, f32[1024,8]{0,1:T(8,128)S(1)} %get-tuple-element.42, f32[1024,1]{0,1:T(1,128)S(1)} %bitcast.88), kind=kOutput, calls=%fused_computation.20 | convolution fusion | flops 13469696 | bytes 336384 | tf_op jit(solution)/shard_map/dot_general | solution.py:92
  19.7 2.0 %broadcast_multiply_fusion.1 = (f32[1024,64]{0,1:T(8,128)S(1)}, f32[1024,64]{0,1:T(8,128)S(1)}) fusion(f32[1024]{0:T(1024)S(1)} %bitcast.87, f32[1024]{0:T(1024)S(1)} %broadcast_subtract_fusion, f32[64]{0:T(128)} %param.19, f32[1024,64]{0,1:T(8,128)S(1)} %fusion.3, f32[64,64]{1,0:T(8,128)} %param.18), kind=kOutput, calls=%fused_computation.50 | convolution fusion | flops 50528256 | bytes 811264 | tf_op jit(solution)/shard_map/dot_general | solution.py:93
  21.8 3.1 %convolution_convert_fusion = bf16[256,1152]{1,0:T(8,128)(2,1)} fusion(bf16[256,1536]{1,0:T(8,128)(2,1)} %bitcast.90, bf16[1536,1152]{1,0:T(8,128)(2,1)S(1)} %copy-done), kind=kOutput, calls=%fused_computation.1 | convolution fusion | flops 906264576 | bytes 4915200 | tf_op jit(solution)/shard_map/dot_general | solution.py:311
  24.9 0.5 negate_select_fusion.2
  25.5 1.6 collective-permute-start.4
  27.1 1.5 convolution_bitcast_fusion
  28.6 1.0 collective-permute-done.6
  29.5 3.9 %collective-permute-done.7 = f32[129,48]{1,0:T(8,128)} collective-permute-done((f32[129,48]{1,0:T(8,128)}, f32[129,48]{1,0:T(8,128)}, u32[]{:S(2)}, u32[]{:S(2)}) %collective-permute-start.7) | collective-permute-done | bytes 24800 | tf_op jit(solution)/shard_map/ppermute | solution.py:69
  33.4 1.1 select_bitcast_fusion.3
  34.5 1.3 collective-permute-start.1
  35.8 0.7 pad_maximum_fusion.8
  36.6 2.3 %convolution_convert_fusion.1 = bf16[256,1152]{1,0:T(8,128)(2,1)S(1)} fusion(bf16[256,1536]{1,0:T(8,128)(2,1)} %bitcast.5, bf16[1536,1152]{1,0:T(8,128)(2,1)S(1)} %copy-done), kind=kOutput, calls=%fused_computation.2 | convolution fusion | flops 906264576 | bytes 4915200 | tf_op jit(solution)/shard_map/dot_general | solution.py:311
  38.9 0.7 collective-permute-start.5
  39.6 2.3 %convolution_convert_fusion.2 = bf16[256,1152]{1,0:T(8,128)(2,1)S(1)} fusion(bf16[256,1536]{1,0:T(8,128)(2,1)} %bitcast.4, bf16[1536,1152]{1,0:T(8,128)(2,1)S(1)} %copy-done), kind=kOutput, calls=%fused_computation.3 | convolution fusion | flops 906264576 | bytes 4915200 | tf_op jit(solution)/shard_map/dot_general | solution.py:311
  41.9 12.1 %collective-permute-done.1 = bf16[2,128,1536]{2,1,0:T(8,128)(2,1)S(1)} collective-permute-done((bf16[2,128,1536]{2,1,0:T(8,128)(2,1)}, bf16[2,128,1536]{2,1,0:T(8,128)(2,1)S(1)}, u32[]{:S(2)}, u32[]{:S(2)}) %collective-permute-start.1) | collective-permute-done | bytes 786464 | tf_op jit(solution)/shard_map/ppermute | solution.py:49
  54.0 1.5 collective-permute-start.2
  55.5 2.3 %convolution_convert_fusion.3 = bf16[256,1152]{1,0:T(8,128)(2,1)S(1)} fusion(bf16[256,1536]{1,0:T(8,128)(2,1)} %bitcast.3, bf16[1536,1152]{1,0:T(8,128)(2,1)S(1)} %copy-done), kind=kOutput, calls=%fused_computation.4 | convolution fusion | flops 906264576 | bytes 4915200 | tf_op jit(solution)/shard_map/dot_general | solution.py:311
  57.8 1.2 convolution_convert_fusion.4
  59.1 1.2 convolution_convert_fusion.5
  60.3 12.1 %collective-permute-done.2 = bf16[2,128,1536]{2,1,0:T(8,128)(2,1)S(1)} collective-permute-done((bf16[2,128,1536]{2,1,0:T(8,128)(2,1)S(1)}, bf16[2,128,1536]{2,1,0:T(8,128)(2,1)S(1)}, u32[]{:S(2)}, u32[]{:S(2)}) %collective-permute-start.2) | collective-permute-done | bytes 786464 | tf_op jit(solution)/shard_map/ppermute | solution.py:49
  72.4 1.3 select_select_fusion.2
  74.0 1.8 %pad_maximum_fusion.2 = bf16[8,128,1152]{2,1,0:T(8,128)(2,1)} fusion(bf16[2,128,1152]{2,1,0:T(8,128)(2,1)S(1)} %bitcast.85, bf16[2,128,1152]{2,1,0:T(8,128)(2,1)S(1)} %bitcast.77, bf16[2,128,1152]{2,1,0:T(8,128)(2,1)S(1)} %bitcast.84, bf16[2,128,1152]{2,1,0:T(8,128)(2,1)S(1)} %bitcast.76), kind=kLoop, calls=%fused_computation.10 | loop fusion | flops 3538944 | bytes 4718592 | tf_op jit(solution)/shard_map/concatenate | solution.py:62
  75.8 4.7 %all-to-all-start = ((bf16[8,128,1152]{2,1,0:T(8,128)(2,1)}), bf16[8,128,1152]{2,1,0:T(8,128)(2,1)}, u32[]{:S(2)}, u32[]{:S(2)}) async-start(bf16[8,128,1152]{2,1,0:T(8,128)(2,1)} %pad_maximum_fusion.2), calls=%async_computation | async-start | bytes 4718592 | tf_op jit(solution)/shard_map/all_to_all | solution.py:322
  80.6 1.8 %copy.32 = f32[4,129,48]{1,2,0:T(8,128)} copy(f32[4,129,48]{2,1,0:T(8,128)} %pad_maximum_fusion.8) | data formatting | bytes 198144 | tf_op jit(solution)/shard_map/optimization_barrier | solution.py:319
  82.4 15.5 %all-gather = f32[32,129,48]{1,2,0:T(8,128)} all-gather(f32[4,129,48]{1,2,0:T(8,128)} %copy.32), channel_id=2, replica_groups=mesh['groups'=2,'seq'=4,'fsdp'=4] {'groups','seq'}, dimensions={0}, use_global_device_ids=true | all-gather | bytes 891648 | tf_op jit(solution)/shard_map/all_gather | solution.py:320
  97.9 3.6 %copy.33 = f32[129,4,8,48]{3,2,1,0:T(8,128)} copy(f32[129,4,8,48]{0,3,1,2:T(8,128)} %bitcast.75) | data formatting | bytes 1585152 | tf_op jit(solution)/shard_map/transpose | solution.py:321
  101.5 3.6 %reshape.283.refs_2_ = f32[129,1536]{1,0:T(8,128)} reshape(f32[129,4,8,48]{3,2,1,0:T(8,128)} %copy.33) | data formatting | bytes 1585152 | tf_op jit(solution)/shard_map/reshape | solution.py:321
  105.1 25.8 %all-to-all-done = bf16[8,128,1152]{2,1,0:T(8,128)(2,1)} async-done(((bf16[8,128,1152]{2,1,0:T(8,128)(2,1)}), bf16[8,128,1152]{2,1,0:T(8,128)(2,1)}, u32[]{:S(2)}, u32[]{:S(2)}) %all-to-all-start) | async-done | bytes 2359328 | tf_op jit(solution)/shard_map/all_to_all | solution.py:322
  131.0 1.9 %copy.36 = bf16[4,2,16,8,1152]{4,3,0,2,1:T(8,128)(2,1)S(1)} copy(bf16[4,2,16,8,1152]{4,3,2,1,0:T(8,128)(2,1)} %bitcast.31) | data formatting | bytes 4718592 | tf_op jit(solution)/shard_map/all_to_all | solution.py:322
  133.0 1.3 collective-permute-start.10
  134.3 3.3 %collective-permute-start.9 = (bf16[2,1,4608]{2,1,0:T(2,128)(2,1)S(1)}, bf16[2,1,4608]{2,1,0:T(2,128)(2,1)S(1)}, u32[]{:S(2)}, u32[]{:S(2)}) collective-permute-start(bf16[2,1,4608]{2,1,0:T(2,128)(2,1)S(1)} %get-tuple-element.32), channel_id=1, source_target_pairs={{0,4},{4,8},{8,12},{1,5},{5,9},{9,13},{2,6},{6,10},{10,14},{3,7},{... | collective-permute-start | bytes 55304 | tf_op jit(solution)/shard_map/ppermute | solution.py:19
  137.7 0.5 collective-permute-done.9
  138.1 1.9 %multiply_add_fusion = f32[2,128,4608]{2,1,0:T(8,128)S(1)} fusion(bf16[2,128,4608]{2,1,0:T(8,128)(2,1)S(1)} %bitcast.74, bf16[2,1,4608]{2,1,0:T(2,128)(2,1)S(1)} %collective-permute-done.10, bf16[2,1,4608]{2,1,0:T(2,128)(2,1)S(1)} %collective-permute-done.9, f32[4608]{0:T(1024)S(1)} %get-tuple-element.20, f32[4608]{0:T(1024)S(1)} %get-tuple-element.21, ...), kind=kLoop, calls=%fused_computation | loop fusion | flops 16515072 | bytes 7170048 | tf_op jit(solution)/shard_map/add | solution.py:326
  140.4 1.4 collective-permute-start.12
  141.8 2.3 %collective-permute-start.11 = (bf16[2,128,1536]{2,1,0:T(8,128)(2,1)S(1)}, bf16[2,128,1536]{2,1,0:T(8,128)(2,1)S(1)}, u32[]{:S(2)}, u32[]{:S(2)}) collective-permute-start(bf16[2,128,1536]{2,1,0:T(8,128)(2,1)S(1)} %get-tuple-element.27.refs_5_), channel_id=1, source_target_pairs={{0,8},{4,12},{8,0},{12,4},{1,9},{5,13},{9,1},{13,5},{2,10},{6,14},... | collective-permute-start | bytes 2359304 | tf_op jit(solution)/shard_map/ppermute | solution.py:342
  144.4 4.4 %shard_map.130.refs_3_ = f32[2,256,1536]{2,1,0:T(8,128)S(1)} custom-call(bf16[2,2,128,1536]{3,2,1,0:T(8,128)(2,1)S(1)} %pad_maximum_fusion.3.refs_0_, bf16[2,256,384]{2,1,0:T(8,128)(2,1)S(1)} %pad_maximum_fusion.6.refs_1_, f32[129,1536]{1,0:T(8,128)S(1)} %copy-done.2, bf16[256,256]{1,0:T(8,128)(2,1)S(1)} %copy-done.3), custom_call_target="tpu_custom_call" | custom-call | tf_op jit(solution)/shard_map/pallas_call | solution.py:252
  148.9 1.6 copy-done.1
  150.5 11.7 %collective-permute-done.11 = bf16[2,128,1536]{2,1,0:T(8,128)(2,1)S(1)} collective-permute-done((bf16[2,128,1536]{2,1,0:T(8,128)(2,1)S(1)}, bf16[2,128,1536]{2,1,0:T(8,128)(2,1)S(1)}, u32[]{:S(2)}, u32[]{:S(2)}) %collective-permute-start.11) | collective-permute-done | bytes 786464 | tf_op jit(solution)/shard_map/ppermute | solution.py:342
  162.3 2.2 %collective-permute-done.13 = bf16[1,2,128,1536]{3,2,1,0:T(8,128)(2,1)S(1)} collective-permute-done((bf16[1,2,128,1536]{3,2,1,0:T(8,128)(2,1)S(1)}, bf16[1,2,128,1536]{3,2,1,0:T(8,128)(2,1)S(1)}, u32[]{:S(2)}, u32[]{:S(2)}) %collective-permute-start.13) | collective-permute-done | bytes 786464 | tf_op jit(solution)/shard_map/ppermute | solution.py:350
  164.7 8.6 %shard_map.131 = bf16[2,128,1536]{2,1,0:T(8,128)(2,1)} custom-call(bf16[2,2,128,1536]{3,2,1,0:T(8,128)(2,1)S(1)} %pad_maximum_fusion.4.refs_0_, bf16[2,256,384]{2,1,0:T(8,128)(2,1)S(1)} %pad_maximum_fusion.7.refs_1_, f32[129,1536]{1,0:T(8,128)S(1)} %copy-done.2, f32[2,256,1536]{2,1,0:T(8,128)} %copy-done.1, f32[2,128,1536]{2,1,0:T(8,128)S(1)} %get-tuple-element.26.refs_4_, ...), custom_call_target="tpu_custom_call" | custom-call | tf_op jit(solution)/shard_map/pallas_call | solution.py:252
  (51 shorter events, 1.8 us)
Async XLA Ops:
  0.0 21.8 %copy-start = (bf16[1536,1152]{1,0:T(8,128)(2,1)S(1)}, bf16[1536,1152]{1,0:T(8,128)(2,1)}, u32[]{:S(2)}) copy-start(bf16[1536,1152]{1,0:T(8,128)(2,1)} %param.14) | copy-start | bytes 10616836
  0.0 25.5 %collective-permute-start.3 = (bf16[2,128,1536]{2,1,0:T(8,128)(2,1)}, bf16[2,128,1536]{2,1,0:T(8,128)(2,1)}, u32[]{:S(2)}, u32[]{:S(2)}) collective-permute-start(bf16[2,128,1536]{2,1,0:T(8,128)(2,1)} %param.13), channel_id=1, source_target_pairs={{0,1},{1,2},{2,3},{4,5},{5,6},{6,7},{8,9},{9,10},{10,11},{12,13},{... | collective-permute-start | bytes 2359304 | tf_op jit(solution)/shard_map/ppermute | solution.py:48
  6.1 28.4 %collective-permute-start = (bf16[2,128,1536]{2,1,0:T(8,128)(2,1)}, bf16[2,128,1536]{2,1,0:T(8,128)(2,1)}, u32[]{:S(2)}, u32[]{:S(2)}) collective-permute-start(bf16[2,128,1536]{2,1,0:T(8,128)(2,1)} %param.13), channel_id=1, source_target_pairs={{1,0},{2,1},{3,2},{5,4},{6,5},{7,6},{9,8},{10,9},{11,10},{13,12},{... | collective-permute-start | bytes 2359304 | tf_op jit(solution)/shard_map/ppermute | solution.py:49
  9.7 19.8 %collective-permute-start.6 = (f32[129,48]{1,0:T(8,128)}, f32[129,48]{1,0:T(8,128)}, u32[]{:S(2)}, u32[]{:S(2)}) collective-permute-start(f32[129,48]{1,0:T(8,128)} %fusion.19), channel_id=1, source_target_pairs={{0,3},{1,0},{2,1},{3,2},{4,7},{5,4},{6,5},{7,6},{8,11},{9,8},{10,9... | collective-permute-start | bytes 74312 | tf_op jit(solution)/shard_map/ppermute | solution.py:69
  14.4 19.0 %collective-permute-start.7 = (f32[129,48]{1,0:T(8,128)}, f32[129,48]{1,0:T(8,128)}, u32[]{:S(2)}, u32[]{:S(2)}) collective-permute-start(f32[129,48]{1,0:T(8,128)} %fusion.19), channel_id=1, source_target_pairs={{0,2},{1,3},{2,0},{3,1},{4,6},{5,7},{6,4},{7,5},{8,10},{9,11},{10,... | collective-permute-start | bytes 74312 | tf_op jit(solution)/shard_map/ppermute | solution.py:69
  14.4 19.0 %collective-permute-start.8 = (f32[129,48]{1,0:T(8,128)}, f32[129,48]{1,0:T(8,128)}, u32[]{:S(2)}, u32[]{:S(2)}) collective-permute-start(f32[129,48]{1,0:T(8,128)} %fusion.19), channel_id=1, source_target_pairs={{0,1},{1,2},{2,3},{3,0},{4,5},{5,6},{6,7},{7,4},{8,9},{9,10},{10,1... | collective-permute-start | bytes 74312 | tf_op jit(solution)/shard_map/ppermute | solution.py:69
  25.5 13.4 %collective-permute-start.4 = (bf16[2,128,1536]{2,1,0:T(8,128)(2,1)}, bf16[2,128,1536]{2,1,0:T(8,128)(2,1)}, u32[]{:S(2)}, u32[]{:S(2)}) collective-permute-start(bf16[2,128,1536]{2,1,0:T(8,128)(2,1)} %collective-permute-done.3), channel_id=1, source_target_pairs={{1,2},{2,3},{5,6},{6,7},{9,10},{10,11},{13,14},{14,15},{17,18},{18... | collective-permute-start | bytes 2359304 | tf_op jit(solution)/shard_map/ppermute | solution.py:48
  34.5 19.5 %collective-permute-start.1 = (bf16[2,128,1536]{2,1,0:T(8,128)(2,1)}, bf16[2,128,1536]{2,1,0:T(8,128)(2,1)S(1)}, u32[]{:S(2)}, u32[]{:S(2)}) collective-permute-start(bf16[2,128,1536]{2,1,0:T(8,128)(2,1)} %collective-permute-done), channel_id=1, source_target_pairs={{1,0},{2,1},{5,4},{6,5},{9,8},{10,9},{13,12},{14,13},{17,16},{18,1... | collective-permute-start | bytes 2359304 | tf_op jit(solution)/shard_map/ppermute | solution.py:49
  38.9 20.2 %collective-permute-start.5 = (bf16[2,128,1536]{2,1,0:T(8,128)(2,1)}, bf16[2,128,1536]{2,1,0:T(8,128)(2,1)S(1)}, u32[]{:S(2)}, u32[]{:S(2)}) collective-permute-start(bf16[2,128,1536]{2,1,0:T(8,128)(2,1)} %collective-permute-done.4), channel_id=1, source_target_pairs={{2,3},{6,7},{10,11},{14,15},{18,19},{22,23},{26,27},{30,31}} | collective-permute-start | bytes 2359304 | tf_op jit(solution)/shard_map/ppermute | solution.py:48
  54.0 18.4 %collective-permute-start.2 = (bf16[2,128,1536]{2,1,0:T(8,128)(2,1)S(1)}, bf16[2,128,1536]{2,1,0:T(8,128)(2,1)S(1)}, u32[]{:S(2)}, u32[]{:S(2)}) collective-permute-start(bf16[2,128,1536]{2,1,0:T(8,128)(2,1)S(1)} %collective-permute-done.1), channel_id=1, source_target_pairs={{1,0},{5,4},{9,8},{13,12},{17,16},{21,20},{25,24},{29,28}} | collective-permute-start | bytes 2359304 | tf_op jit(solution)/shard_map/ppermute | solution.py:49
  59.0 13.4 %copy-start.6 = (bf16[256,1152]{1,0:T(8,128)(2,1)S(1)}, bf16[256,1152]{1,0:T(8,128)(2,1)}, u32[]{:S(2)}) copy-start(bf16[256,1152]{1,0:T(8,128)(2,1)} %convolution_convert_fusion) | copy-start | bytes 1769476
  75.8 4.7 %copy-start.8 = (s32[2,1]{0,1:T(1,128)S(1)}, s32[2,1]{0,1:T(1,128)}, u32[]{:S(2)}) copy-start(s32[2,1]{0,1:T(1,128)} %param.22) | copy-start | bytes 28
  75.8 55.1 %all-to-all-start = ((bf16[8,128,1152]{2,1,0:T(8,128)(2,1)}), bf16[8,128,1152]{2,1,0:T(8,128)(2,1)}, u32[]{:S(2)}, u32[]{:S(2)}) async-start(bf16[8,128,1152]{2,1,0:T(8,128)(2,1)} %pad_maximum_fusion.2), calls=%async_computation | async-start | bytes 4718592 | tf_op jit(solution)/shard_map/all_to_all | solution.py:322
  130.9 6.6 %copy-start.7 = (f32[3,4608]{1,0:T(4,128)S(1)}, f32[3,4608]{1,0:T(4,128)}, u32[]{:S(2)}) copy-start(f32[3,4608]{1,0:T(4,128)} %param.15) | copy-start | bytes 165892
  133.0 4.7 %collective-permute-start.10 = (bf16[2,1,4608]{2,1,0:T(2,128)(2,1)S(1)}, bf16[2,1,4608]{2,1,0:T(2,128)(2,1)S(1)}, u32[]{:S(2)}, u32[]{:S(2)}) collective-permute-start(bf16[2,1,4608]{2,1,0:T(2,128)(2,1)S(1)} %get-tuple-element.33), channel_id=1, source_target_pairs={{4,0},{8,4},{12,8},{5,1},{9,5},{13,9},{6,2},{10,6},{14,10},{7,3},{... | collective-permute-start | bytes 55304 | tf_op jit(solution)/shard_map/ppermute | solution.py:21
  134.3 3.9 %collective-permute-start.9 = (bf16[2,1,4608]{2,1,0:T(2,128)(2,1)S(1)}, bf16[2,1,4608]{2,1,0:T(2,128)(2,1)S(1)}, u32[]{:S(2)}, u32[]{:S(2)}) collective-permute-start(bf16[2,1,4608]{2,1,0:T(2,128)(2,1)S(1)} %get-tuple-element.32), channel_id=1, source_target_pairs={{0,4},{4,8},{8,12},{1,5},{5,9},{9,13},{2,6},{6,10},{10,14},{3,7},{... | collective-permute-start | bytes 55304 | tf_op jit(solution)/shard_map/ppermute | solution.py:19
  140.1 4.0 %copy-start.5 = (f32[4,256,128]{2,1,0:T(8,128)S(1)}, f32[4,256,128]{2,1,0:T(8,128)}, u32[]{:S(2)}) copy-start(f32[4,256,128]{2,1,0:T(8,128)} %convolution_bitcast_fusion) | copy-start | bytes 1572868
  140.4 4.0 %copy-start.2 = (f32[129,1536]{1,0:T(8,128)S(1)}, f32[129,1536]{1,0:T(8,128)}, u32[]{:S(2)}) copy-start(f32[129,1536]{1,0:T(8,128)} %reshape.283.refs_2_) | copy-start | bytes 2377732
  140.4 4.0 %copy-start.3 = (bf16[256,256]{1,0:T(8,128)(2,1)S(1)}, bf16[256,256]{1,0:T(8,128)(2,1)}, u32[]{:S(2)}) copy-start(bf16[256,256]{1,0:T(8,128)(2,1)} %constant.166.clone.refs_3_.refs_6_) | copy-start | bytes 393220
  140.4 3.8 %collective-permute-start.12 = (bf16[2,128,1536]{2,1,0:T(8,128)(2,1)S(1)}, bf16[2,128,1536]{2,1,0:T(8,128)(2,1)S(1)}, u32[]{:S(2)}, u32[]{:S(2)}) collective-permute-start(bf16[2,128,1536]{2,1,0:T(8,128)(2,1)S(1)} %get-tuple-element.27.refs_5_), channel_id=1, source_target_pairs={{0,4},{4,0},{8,12},{12,8},{1,5},{5,1},{9,13},{13,9},{2,6},{6,2},{1... | collective-permute-start | bytes 2359304 | tf_op jit(solution)/shard_map/ppermute | solution.py:338
  141.8 20.4 %collective-permute-start.11 = (bf16[2,128,1536]{2,1,0:T(8,128)(2,1)S(1)}, bf16[2,128,1536]{2,1,0:T(8,128)(2,1)S(1)}, u32[]{:S(2)}, u32[]{:S(2)}) collective-permute-start(bf16[2,128,1536]{2,1,0:T(8,128)(2,1)S(1)} %get-tuple-element.27.refs_5_), channel_id=1, source_target_pairs={{0,8},{4,12},{8,0},{12,4},{1,9},{5,13},{9,1},{13,5},{2,10},{6,14},... | collective-permute-start | bytes 2359304 | tf_op jit(solution)/shard_map/ppermute | solution.py:342
  144.4 20.3 %copy-start.4 = (bf16[128,768]{1,0:T(8,128)(2,1)S(1)}, bf16[128,768]{1,0:T(8,128)(2,1)}, u32[]{:S(2)}) copy-start(bf16[128,768]{1,0:T(8,128)(2,1)} %constant.167.clone.refs_7_) | copy-start | bytes 589828
  148.9 1.6 copy-start.1
  162.2 2.3 %collective-permute-start.13 = (bf16[1,2,128,1536]{3,2,1,0:T(8,128)(2,1)S(1)}, bf16[1,2,128,1536]{3,2,1,0:T(8,128)(2,1)S(1)}, u32[]{:S(2)}, u32[]{:S(2)}) collective-permute-start(bf16[1,2,128,1536]{3,2,1,0:T(8,128)(2,1)S(1)} %bitcast.79), channel_id=1, source_target_pairs={{0,4},{4,0},{8,12},{12,8},{1,5},{5,1},{9,13},{13,9},{2,6},{6,2},{1... | collective-permute-start | bytes 2359304 | tf_op jit(solution)/shard_map/ppermute | solution.py:350
